TPU v7x, 512 devices: a whole 4x4x16 slice. The times are simulated.
512 devices in a mesh: section: 4 (over y), ctx: 16 (over z), dp: 8 (over x, core).
Axes of the slice: x: 4, y: 4, z: 16, core: 2. Of those that a mesh axis runs over, the one named last changes fastest.
Arguments:
- query_input: bfloat16 [4, 8, 2048, 4096], P('section', 'dp', 'ctx'), may hold values from -6 to 6
- key_states: bfloat16 [4, 8, 2048, 512], P('section', 'dp', 'ctx'), may hold values from -4 to 4
- value_states: bfloat16 [4, 8, 2048, 512], P('section', 'dp', 'ctx'), may hold values from -16 to 16
- query_gain: float32 [4, 4096], P('section', 'ctx'), may hold values from 0.5 to 1.5
- top_grad: bfloat16 [8, 2048, 4096], P('dp', 'ctx'), may hold values from -6 to 6
- block_lists: int32 [16, 4], replicated, may hold values from 0 to 15, as said below
Outputs:
- stream_grad: bfloat16 [4, 8, 2048, 4096], P('section', 'dp', 'ctx')
- key_grad: bfloat16 [4, 8, 2048, 512], P('section', 'dp', 'ctx')
- value_grad: bfloat16 [4, 8, 2048, 512], P('section', 'dp', 'ctx')
- gain_grad: float32 [4, 4096], P('section', 'ctx')
Inputs may be any that keep to these rules, and one draw needn't show every extreme that they name: `block_lists`: row b names 4 different blocks; the window blocks b - 1, b, b + 1 that exist come first, then block 0, then block 15, then blocks drawn at random, as far as 4 allows.
All inputs are finite; a program needn't handle non-finite values.
Results may differ from a plain program's by a relative error of at most 0.03.
Values may be sent and summed in bfloat16 or wider, within the bound.
No kernel may reach another device: no remote copies, remote signals or barrier semaphores. Data moves between devices by JAX's collectives and lax.ppermute only.
A program may use at most 64 MiB of HBM per device.

v0:
```python
import math

import jax
import jax.numpy as jnp
import numpy as np
from jax import lax
from jax.sharding import PartitionSpec as P

HEAD_FEATURES = 128


def passed_along(block, axis, distance):
    devices = range(lax.axis_size(axis))
    route = [(i - distance, i) for i in devices if i - distance in devices]
    return lax.ppermute(block, axis, route)


def shards(query_input, key_states, value_states, query_gain, top_grad, block_lists):
    ctx_count = lax.axis_size("ctx")
    section_count = lax.axis_size("section")
    section_pos = lax.axis_index("section")
    layer_input = query_input[0, 0]
    tok_local, feature_count = layer_input.shape
    kv_width = key_states.shape[-1]
    kv_heads = kv_width // HEAD_FEATURES
    head_count = feature_count // HEAD_FEATURES
    local_heads = head_count // ctx_count
    group_width = head_count // kv_heads
    local_kv = max(1, local_heads // group_width)
    per_kv = local_heads // local_kv
    repeats = ctx_count * local_kv // kv_heads
    local_width = local_heads * HEAD_FEATURES
    slot_width = local_kv * HEAD_FEATURES
    total_rows = tok_local * ctx_count
    block_count, listed = block_lists.shape
    block_rows = total_rows // block_count
    scale_factor = 1.0 / math.sqrt(HEAD_FEATURES)
    slot_index = np.arange(ctx_count * local_kv)
    slot_heads = slot_index // local_kv * local_heads // group_width + slot_index % local_kv
    sent_keys = (
        key_states[0, 0]
        .reshape(tok_local, kv_heads, HEAD_FEATURES)[:, slot_heads]
        .reshape(tok_local, ctx_count * slot_width)
    )
    sent_values = (
        value_states[0, 0]
        .reshape(tok_local, kv_heads, HEAD_FEATURES)[:, slot_heads]
        .reshape(tok_local, ctx_count * slot_width)
    )
    head_input, head_keys, head_values, head_top = (
        lax.all_to_all(layer_input, "ctx", split_axis=1, concat_axis=0, tiled=True),
        lax.all_to_all(sent_keys, "ctx", split_axis=1, concat_axis=0, tiled=True),
        lax.all_to_all(sent_values, "ctx", split_axis=1, concat_axis=0, tiled=True),
        lax.all_to_all(top_grad[0], "ctx", split_axis=1, concat_axis=0, tiled=True),
    )
    gain_row = query_gain[0]
    query_rows = (head_input.astype(jnp.float32) * gain_row).astype(jnp.bfloat16)
    blocked_keys = head_keys.reshape(block_count, block_rows, local_kv, HEAD_FEATURES)
    blocked_values = head_values.reshape(block_count, block_rows, local_kv, HEAD_FEATURES)
    per_turn = 2
    unit_count = block_count // per_turn
    turn_rows = per_turn * block_rows
    token_rows = turn_rows // ctx_count
    turn_count = unit_count + section_count - 1
    grid_shape = (per_turn, block_rows, local_kv, per_kv, HEAD_FEATURES)

    def attend(unit, head_grad):
        first_row = unit * turn_rows
        query_now = lax.dynamic_slice_in_dim(query_rows, first_row, turn_rows, 0).reshape(
            grid_shape
        )
        input_now = lax.dynamic_slice_in_dim(head_input, first_row, turn_rows, 0)
        grad_now = head_grad.reshape(grid_shape)
        lists_now = lax.dynamic_slice_in_dim(block_lists, unit * per_turn, per_turn, 0)
        neighbor_keys = blocked_keys[lists_now].reshape(
            per_turn, listed * block_rows, local_kv, HEAD_FEATURES
        )
        neighbor_values = blocked_values[lists_now].reshape(
            per_turn, listed * block_rows, local_kv, HEAD_FEATURES
        )
        scores = (
            jnp.einsum(
                "pbkgd,pjkd->pkgbj", query_now, neighbor_keys, preferred_element_type=jnp.float32
            )
            * scale_factor
        )
        row_max = jnp.max(scores, axis=-1, keepdims=True)
        weights = jnp.exp(scores - row_max)
        probs = weights / jnp.sum(weights, axis=-1, keepdims=True)
        probs_low = probs.astype(jnp.bfloat16)
        prob_grad = jnp.einsum(
            "pbkgd,pjkd->pkgbj", grad_now, neighbor_values, preferred_element_type=jnp.float32
        )
        row_dot = jnp.sum(probs * prob_grad, axis=-1, keepdims=True)
        score_grad = (probs * (prob_grad - row_dot)).astype(jnp.bfloat16)
        query_grad = (
            jnp.einsum(
                "pkgbj,pjkd->pbkgd", score_grad, neighbor_keys, preferred_element_type=jnp.float32
            )
            * scale_factor
        )
        key_part = (
            jnp.einsum(
                "pkgbj,pbkgd->pjkd", score_grad, query_now, preferred_element_type=jnp.float32
            )
            * scale_factor
        )
        value_part = jnp.einsum(
            "pkgbj,pbkgd->pjkd", probs_low, grad_now, preferred_element_type=jnp.float32
        )
        query_grad = query_grad.reshape(turn_rows, local_width)
        gain_part = jnp.sum(input_now.astype(jnp.float32) * query_grad, axis=0)
        return (
            query_grad,
            key_part.reshape(per_turn, listed * block_rows, slot_width),
            value_part.reshape(per_turn, listed * block_rows, slot_width),
            gain_part,
        )

    def spare(unit, head_grad):
        empty_part = jnp.zeros((per_turn, listed * block_rows, slot_width), jnp.float32)
        return (
            jnp.zeros((turn_rows, local_width), jnp.float32),
            empty_part,
            empty_part,
            jnp.zeros((local_width,), jnp.float32),
        )

    on_top = section_pos == section_count - 1

    def turn_step(turn, carry):
        incoming, result_heads, key_slots, value_slots, gain_acc = carry
        unit = turn - (section_count - 1 - section_pos)
        active = (unit >= 0) & (unit < unit_count)
        safe_index = jnp.clip(unit, 0, unit_count - 1)
        target = jnp.where(active, safe_index, unit_count)
        from_top = lax.dynamic_slice_in_dim(head_top, safe_index * turn_rows, turn_rows, 0)
        arrived = lax.all_to_all(incoming, "ctx", split_axis=1, concat_axis=0, tiled=True)
        head_grad = jnp.where(on_top, from_top, arrived)
        query_grad, key_part, value_part, gain_part = lax.cond(
            active, attend, spare, safe_index, head_grad
        )
        moved_grad = (gain_row * query_grad).astype(jnp.bfloat16)
        handed = (head_grad.astype(jnp.float32) + moved_grad.astype(jnp.float32)).astype(
            jnp.bfloat16
        )
        result_heads = lax.dynamic_update_slice_in_dim(result_heads, handed, target * turn_rows, 0)
        key_slots = lax.dynamic_update_slice_in_dim(key_slots, key_part, target * per_turn, 0)
        value_slots = lax.dynamic_update_slice_in_dim(value_slots, value_part, target * per_turn, 0)
        gain_acc = gain_acc + gain_part
        outgoing = lax.all_to_all(handed, "ctx", split_axis=0, concat_axis=1, tiled=True)
        incoming = passed_along(outgoing, "section", -1)
        return (incoming, result_heads, key_slots, value_slots, gain_acc)

    first_incoming = jnp.zeros((token_rows, feature_count), jnp.bfloat16)
    slot_zeros = jnp.zeros(
        ((unit_count + 1) * per_turn, listed * block_rows, slot_width), jnp.float32
    )
    start_carry = (
        first_incoming,
        jnp.zeros(((unit_count + 1) * turn_rows, local_width), jnp.bfloat16),
        slot_zeros,
        slot_zeros,
        jnp.zeros((local_width,), jnp.float32),
    )
    final_carry = lax.fori_loop(0, turn_count, turn_step, start_carry)
    incoming, result_heads, key_slots, value_slots, gain_acc = final_carry
    result_rows = lax.all_to_all(
        result_heads[:total_rows], "ctx", split_axis=0, concat_axis=1, tiled=True
    )
    target_labels = block_lists.reshape(-1)
    key_pieces = key_slots[:block_count].reshape(block_count * listed, block_rows, slot_width)
    value_pieces = value_slots[:block_count].reshape(block_count * listed, block_rows, slot_width)
    key_acc = (
        jnp.zeros((block_count, block_rows, slot_width), jnp.float32)
        .at[target_labels]
        .add(key_pieces)
    )
    value_acc = (
        jnp.zeros((block_count, block_rows, slot_width), jnp.float32)
        .at[target_labels]
        .add(value_pieces)
    )
    key_back, value_back = (
        lax.all_to_all(
            key_acc.reshape(total_rows, slot_width).astype(jnp.bfloat16),
            "ctx",
            split_axis=0,
            concat_axis=1,
            tiled=True,
        ).astype(jnp.float32),
        lax.all_to_all(
            value_acc.reshape(total_rows, slot_width).astype(jnp.bfloat16),
            "ctx",
            split_axis=0,
            concat_axis=1,
            tiled=True,
        ).astype(jnp.float32),
    )
    key_out = (
        key_back.reshape(tok_local, kv_heads, repeats, HEAD_FEATURES)
        .sum(axis=2)
        .reshape(tok_local, kv_width)
        .astype(jnp.bfloat16)
    )
    value_out = (
        value_back.reshape(tok_local, kv_heads, repeats, HEAD_FEATURES)
        .sum(axis=2)
        .reshape(tok_local, kv_width)
        .astype(jnp.bfloat16)
    )
    gain_total = lax.psum(gain_acc, "dp")
    return (result_rows[None, None], key_out[None, None], value_out[None, None], gain_total[None])


def solution(mesh):
    placed = (
        P("section", "dp", "ctx", None),
        P("section", "dp", "ctx", None),
        P("section", "dp", "ctx", None),
        P("section", "ctx"),
        P("dp", "ctx", None),
        P(),
    )
    return jax.shard_map(
        shards,
        mesh=mesh,
        in_specs=placed,
        out_specs=(
            P("section", "dp", "ctx", None),
            P("section", "dp", "ctx", None),
            P("section", "dp", "ctx", None),
            P("section", "ctx"),
        ),
        check_vma=False,
    )
```

profile of v0, /device:TPU:6, one launch (start us, length us, event | category | flops | bytes accessed | tf_op | source)
XLA Modules:
  0.0 878.3 jit_solution(11381921271365920453)
XLA Ops:
  4.0 15.2 %all-to-all-start.3 = ((bf16[128,16,128]{2,0,1:T(8,128)(2,1)}), bf16[128,16,128]{2,0,1:T(8,128)(2,1)S(1)}, u32[]{:S(2)}, u32[]{:S(2)}) async-start(bf16[128,16,128]{2,0,1:T(8,128)(2,1)} %bitcast.29), calls=%async_computation.3 | async-start | bytes 1048576 | tf_op jit(solution)/shard_map/all_to_all | solution.py:52
  21.8 26.5 %all-to-all-done.3 = bf16[128,16,128]{2,0,1:T(8,128)(2,1)S(1)} async-done(((bf16[128,16,128]{2,0,1:T(8,128)(2,1)}), bf16[128,16,128]{2,0,1:T(8,128)(2,1)S(1)}, u32[]{:S(2)}, u32[]{:S(2)}) %all-to-all-start.3) | async-done | bytes 524320 | tf_op jit(solution)/shard_map/all_to_all | solution.py:52
  48.3 6.3 all-to-all-start.5
  56.2 27.6 %all-to-all-done.5 = bf16[128,16,128]{2,0,1:T(8,128)(2,1)} async-done(((bf16[128,16,128]{2,0,1:T(8,128)(2,1)}), bf16[128,16,128]{2,0,1:T(8,128)(2,1)}, u32[]{:S(2)}, u32[]{:S(2)}) %all-to-all-start.5) | async-done | bytes 524320 | tf_op jit(solution)/shard_map/all_to_all | solution.py:53
  83.8 6.3 all-to-all-start.4
  91.7 48.5 %all-to-all-done.4 = bf16[128,16,256]{2,0,1:T(8,128)(2,1)} async-done(((bf16[128,16,256]{2,0,1:T(8,128)(2,1)}), bf16[128,16,256]{2,0,1:T(8,128)(2,1)}, u32[]{:S(2)}, u32[]{:S(2)}) %all-to-all-start.4) | async-done | bytes 1048608 | tf_op jit(solution)/shard_map/all_to_all | solution.py:51
  140.2 7.9 all-to-all-start.2
  150.8 47.5 %all-to-all-done.2 = bf16[128,16,256]{2,0,1:T(8,128)(2,1)} async-done(((bf16[128,16,256]{2,0,1:T(8,128)(2,1)}), bf16[128,16,256]{2,0,1:T(8,128)(2,1)}, u32[]{:S(2)}, u32[]{:S(2)}) %all-to-all-start.2) | async-done | bytes 1048608 | tf_op jit(solution)/shard_map/all_to_all | solution.py:54
  204.7 561.9 %while.24 = (s32[]{:T(128)}, bf16[16,4096]{1,0:T(8,128)(2,1)S(1)}, bf16[2304,256]{1,0:T(8,128)(2,1)}, f32[18,512,128]{2,1,0:T(8,128)}, f32[18,512,128]{2,1,0:T(8...) while((s32[]{:T(128)}, bf16[16,4096]{1,0:T(8,128)(2,1)S(1)}, ...), condition=%wide.region_7.8_spmd.clone, body=%wide.region_0.7_spmd.clone.sunk | while | flops 340590400 | bytes 20873156 | solution.py:166
  205.4 7.9 all-to-all-start
  213.4 14.6 %all-to-all-done = bf16[16,16,256]{2,0,1:T(8,128)(2,1)S(1)} async-done(((bf16[16,16,256]{2,0,1:T(8,128)(2,1)}), bf16[16,16,256]{2,0,1:T(8,128)(2,1)S(1)}, u32[]{:S(2)}, u32[]{:S(2)}) %all-to-all-start) | async-done | bytes 131104 | tf_op jit(solution)/shard_map/while/body/eval_jaxpr/all_to_all | solution.py:138
  234.1 14.3 %all-to-all-done.1 = bf16[16,16,256]{2,1,0:T(8,128)(2,1)S(1)} async-done(((bf16[16,16,256]{2,1,0:T(8,128)(2,1)}), bf16[16,16,256]{2,1,0:T(8,128)(2,1)S(1)}, u32[]{:S(2)}, u32[]{:S(2)}) %all-to-all-start.1) | async-done | bytes 131104 | tf_op jit(solution)/shard_map/while/body/eval_jaxpr/all_to_all | solution.py:151
  250.9 4.5 collective-permute-done
  259.9 13.2 %all-to-all-done = bf16[16,16,256]{2,0,1:T(8,128)(2,1)S(1)} async-done(((bf16[16,16,256]{2,0,1:T(8,128)(2,1)}), bf16[16,16,256]{2,0,1:T(8,128)(2,1)S(1)}, u32[]{:S(2)}, u32[]{:S(2)}) %all-to-all-start) | async-done | bytes 131104 | tf_op jit(solution)/shard_map/while/body/eval_jaxpr/all_to_all | solution.py:138
  279.1 12.9 %all-to-all-done.1 = bf16[16,16,256]{2,1,0:T(8,128)(2,1)S(1)} async-done(((bf16[16,16,256]{2,1,0:T(8,128)(2,1)}), bf16[16,16,256]{2,1,0:T(8,128)(2,1)S(1)}, u32[]{:S(2)}, u32[]{:S(2)}) %all-to-all-start.1) | async-done | bytes 131104 | tf_op jit(solution)/shard_map/while/body/eval_jaxpr/all_to_all | solution.py:151
  294.4 4.5 collective-permute-done
  303.6 13.2 %all-to-all-done = bf16[16,16,256]{2,0,1:T(8,128)(2,1)S(1)} async-done(((bf16[16,16,256]{2,0,1:T(8,128)(2,1)}), bf16[16,16,256]{2,0,1:T(8,128)(2,1)S(1)}, u32[]{:S(2)}, u32[]{:S(2)}) %all-to-all-start) | async-done | bytes 131104 | tf_op jit(solution)/shard_map/while/body/eval_jaxpr/all_to_all | solution.py:138
  322.8 13.0 %all-to-all-done.1 = bf16[16,16,256]{2,1,0:T(8,128)(2,1)S(1)} async-done(((bf16[16,16,256]{2,1,0:T(8,128)(2,1)}), bf16[16,16,256]{2,1,0:T(8,128)(2,1)S(1)}, u32[]{:S(2)}, u32[]{:S(2)}) %all-to-all-start.1) | async-done | bytes 131104 | tf_op jit(solution)/shard_map/while/body/eval_jaxpr/all_to_all | solution.py:151
  338.1 21.7 %collective-permute-done = bf16[16,4096]{1,0:T(8,128)(2,1)S(1)} collective-permute-done((bf16[16,4096]{1,0:T(8,128)(2,1)S(1)}, bf16[16,4096]{1,0:T(8,128)(2,1)S(1)}, u32[]{:S(2)}, u32[]{:S(2)}) %collective-permute-start) | collective-permute-done | bytes 131104 | tf_op jit(solution)/shard_map/while/body/eval_jaxpr/ppermute | solution.py:15
  364.4 13.1 %all-to-all-done = bf16[16,16,256]{2,0,1:T(8,128)(2,1)S(1)} async-done(((bf16[16,16,256]{2,0,1:T(8,128)(2,1)}), bf16[16,16,256]{2,0,1:T(8,128)(2,1)S(1)}, u32[]{:S(2)}, u32[]{:S(2)}) %all-to-all-start) | async-done | bytes 131104 | tf_op jit(solution)/shard_map/while/body/eval_jaxpr/all_to_all | solution.py:138
  378.4 6.6 conditional.3
  390.0 12.9 %all-to-all-done.1 = bf16[16,16,256]{2,1,0:T(8,128)(2,1)S(1)} async-done(((bf16[16,16,256]{2,1,0:T(8,128)(2,1)}), bf16[16,16,256]{2,1,0:T(8,128)(2,1)S(1)}, u32[]{:S(2)}, u32[]{:S(2)}) %all-to-all-start.1) | async-done | bytes 131104 | tf_op jit(solution)/shard_map/while/body/eval_jaxpr/all_to_all | solution.py:151
  405.3 4.5 collective-permute-done
  414.5 13.1 %all-to-all-done = bf16[16,16,256]{2,0,1:T(8,128)(2,1)S(1)} async-done(((bf16[16,16,256]{2,0,1:T(8,128)(2,1)}), bf16[16,16,256]{2,0,1:T(8,128)(2,1)S(1)}, u32[]{:S(2)}, u32[]{:S(2)}) %all-to-all-start) | async-done | bytes 131104 | tf_op jit(solution)/shard_map/while/body/eval_jaxpr/all_to_all | solution.py:138
  428.5 6.6 conditional.3
  440.2 12.9 %all-to-all-done.1 = bf16[16,16,256]{2,1,0:T(8,128)(2,1)S(1)} async-done(((bf16[16,16,256]{2,1,0:T(8,128)(2,1)}), bf16[16,16,256]{2,1,0:T(8,128)(2,1)S(1)}, u32[]{:S(2)}, u32[]{:S(2)}) %all-to-all-start.1) | async-done | bytes 131104 | tf_op jit(solution)/shard_map/while/body/eval_jaxpr/all_to_all | solution.py:151
  455.4 4.5 collective-permute-done
  464.6 13.1 %all-to-all-done = bf16[16,16,256]{2,0,1:T(8,128)(2,1)S(1)} async-done(((bf16[16,16,256]{2,0,1:T(8,128)(2,1)}), bf16[16,16,256]{2,0,1:T(8,128)(2,1)S(1)}, u32[]{:S(2)}, u32[]{:S(2)}) %all-to-all-start) | async-done | bytes 131104 | tf_op jit(solution)/shard_map/while/body/eval_jaxpr/all_to_all | solution.py:138
  478.7 6.6 conditional.3
  490.3 12.9 %all-to-all-done.1 = bf16[16,16,256]{2,1,0:T(8,128)(2,1)S(1)} async-done(((bf16[16,16,256]{2,1,0:T(8,128)(2,1)}), bf16[16,16,256]{2,1,0:T(8,128)(2,1)S(1)}, u32[]{:S(2)}, u32[]{:S(2)}) %all-to-all-start.1) | async-done | bytes 131104 | tf_op jit(solution)/shard_map/while/body/eval_jaxpr/all_to_all | solution.py:151
  505.5 4.5 collective-permute-done
  514.8 13.1 %all-to-all-done = bf16[16,16,256]{2,0,1:T(8,128)(2,1)S(1)} async-done(((bf16[16,16,256]{2,0,1:T(8,128)(2,1)}), bf16[16,16,256]{2,0,1:T(8,128)(2,1)S(1)}, u32[]{:S(2)}, u32[]{:S(2)}) %all-to-all-start) | async-done | bytes 131104 | tf_op jit(solution)/shard_map/while/body/eval_jaxpr/all_to_all | solution.py:138
  528.8 6.6 conditional.3
  536.1 4.1 all-to-all-start.1
  540.5 13.7 %all-to-all-done.1 = bf16[16,16,256]{2,1,0:T(8,128)(2,1)S(1)} async-done(((bf16[16,16,256]{2,1,0:T(8,128)(2,1)}), bf16[16,16,256]{2,1,0:T(8,128)(2,1)S(1)}, u32[]{:S(2)}, u32[]{:S(2)}) %all-to-all-start.1) | async-done | bytes 131104 | tf_op jit(solution)/shard_map/while/body/eval_jaxpr/all_to_all | solution.py:151
  556.6 4.5 collective-permute-done
  561.7 5.9 all-to-all-start
  567.7 13.9 %all-to-all-done = bf16[16,16,256]{2,0,1:T(8,128)(2,1)S(1)} async-done(((bf16[16,16,256]{2,0,1:T(8,128)(2,1)}), bf16[16,16,256]{2,0,1:T(8,128)(2,1)S(1)}, u32[]{:S(2)}, u32[]{:S(2)}) %all-to-all-start) | async-done | bytes 131104 | tf_op jit(solution)/shard_map/while/body/eval_jaxpr/all_to_all | solution.py:138
  582.5 6.6 conditional.3
  589.9 5.6 all-to-all-start.1
  595.7 13.6 %all-to-all-done.1 = bf16[16,16,256]{2,1,0:T(8,128)(2,1)S(1)} async-done(((bf16[16,16,256]{2,1,0:T(8,128)(2,1)}), bf16[16,16,256]{2,1,0:T(8,128)(2,1)S(1)}, u32[]{:S(2)}, u32[]{:S(2)}) %all-to-all-start.1) | async-done | bytes 131104 | tf_op jit(solution)/shard_map/while/body/eval_jaxpr/all_to_all | solution.py:151
  611.7 4.5 collective-permute-done
  620.4 13.5 %all-to-all-done = bf16[16,16,256]{2,0,1:T(8,128)(2,1)S(1)} async-done(((bf16[16,16,256]{2,0,1:T(8,128)(2,1)}), bf16[16,16,256]{2,0,1:T(8,128)(2,1)S(1)}, u32[]{:S(2)}, u32[]{:S(2)}) %all-to-all-start) | async-done | bytes 131104 | tf_op jit(solution)/shard_map/while/body/eval_jaxpr/all_to_all | solution.py:138
  634.9 6.6 conditional.3
  646.0 12.9 %all-to-all-done.1 = bf16[16,16,256]{2,1,0:T(8,128)(2,1)S(1)} async-done(((bf16[16,16,256]{2,1,0:T(8,128)(2,1)}), bf16[16,16,256]{2,1,0:T(8,128)(2,1)S(1)}, u32[]{:S(2)}, u32[]{:S(2)}) %all-to-all-start.1) | async-done | bytes 131104 | tf_op jit(solution)/shard_map/while/body/eval_jaxpr/all_to_all | solution.py:151
  661.3 4.5 collective-permute-done
  670.5 13.1 %all-to-all-done = bf16[16,16,256]{2,0,1:T(8,128)(2,1)S(1)} async-done(((bf16[16,16,256]{2,0,1:T(8,128)(2,1)}), bf16[16,16,256]{2,0,1:T(8,128)(2,1)S(1)}, u32[]{:S(2)}, u32[]{:S(2)}) %all-to-all-start) | async-done | bytes 131104 | tf_op jit(solution)/shard_map/while/body/eval_jaxpr/all_to_all | solution.py:138
  684.5 6.6 conditional.3
  696.1 12.9 %all-to-all-done.1 = bf16[16,16,256]{2,1,0:T(8,128)(2,1)S(1)} async-done(((bf16[16,16,256]{2,1,0:T(8,128)(2,1)}), bf16[16,16,256]{2,1,0:T(8,128)(2,1)S(1)}, u32[]{:S(2)}, u32[]{:S(2)}) %all-to-all-start.1) | async-done | bytes 131104 | tf_op jit(solution)/shard_map/while/body/eval_jaxpr/all_to_all | solution.py:151
  711.5 4.5 collective-permute-done
  720.6 13.1 %all-to-all-done = bf16[16,16,256]{2,0,1:T(8,128)(2,1)S(1)} async-done(((bf16[16,16,256]{2,0,1:T(8,128)(2,1)}), bf16[16,16,256]{2,0,1:T(8,128)(2,1)S(1)}, u32[]{:S(2)}, u32[]{:S(2)}) %all-to-all-start) | async-done | bytes 131104 | tf_op jit(solution)/shard_map/while/body/eval_jaxpr/all_to_all | solution.py:138
  734.7 6.6 conditional.3
  746.3 13.4 %all-to-all-done.1 = bf16[16,16,256]{2,1,0:T(8,128)(2,1)S(1)} async-done(((bf16[16,16,256]{2,1,0:T(8,128)(2,1)}), bf16[16,16,256]{2,1,0:T(8,128)(2,1)S(1)}, u32[]{:S(2)}, u32[]{:S(2)}) %all-to-all-start.1) | async-done | bytes 131104 | tf_op jit(solution)/shard_map/while/body/eval_jaxpr/all_to_all | solution.py:151
  762.1 4.5 collective-permute-done
  766.6 4.7 slice.10
  771.3 8.8 %scatter_fusion = f32[16,128,128]{2,1,0:T(8,128)S(1)} fusion(f32[16,128,128]{2,1,0:T(8,128)S(1)} %broadcast.75.clone, s32[64]{0:T(128)S(1)} %fusion.12, f32[64,128,128]{2,1,0:T(8,128)} %bitcast.136), kind=kCustom, calls=%fused_computation.4 | custom fusion | flops 1048576 | bytes 12583168 | tf_op jit(solution)/shard_map/scatter-add | solution.py:177
  781.0 7.7 all-to-all-start.7
  788.7 4.5 slice.11
  793.4 8.8 %scatter_fusion.1 = f32[16,128,128]{2,1,0:T(8,128)S(1)} fusion(f32[16,128,128]{2,1,0:T(8,128)S(1)} %broadcast.75.clone.1, s32[64]{0:T(128)S(1)} %fusion.12, f32[64,128,128]{2,1,0:T(8,128)} %bitcast.135), kind=kCustom, calls=%fused_computation.5 | custom fusion | flops 1048576 | bytes 12583168 | tf_op jit(solution)/shard_map/scatter-add | solution.py:182
  806.7 15.4 %all-to-all-start.8 = ((bf16[16,128,128]{2,1,0:T(8,128)(2,1)}), bf16[16,128,128]{2,1,0:T(8,128)(2,1)S(1)}, u32[]{:S(2)}, u32[]{:S(2)}) async-start(bf16[16,128,128]{2,1,0:T(8,128)(2,1)} %convert_element_type.122), calls=%async_computation.8 | async-start | bytes 1048576 | tf_op jit(solution)/shard_map/all_to_all | solution.py:192
  823.2 20.6 %all-to-all-done.8 = bf16[16,128,128]{2,1,0:T(8,128)(2,1)S(1)} async-done(((bf16[16,128,128]{2,1,0:T(8,128)(2,1)}), bf16[16,128,128]{2,1,0:T(8,128)(2,1)S(1)}, u32[]{:S(2)}, u32[]{:S(2)}) %all-to-all-start.8) | async-done | bytes 524320 | tf_op jit(solution)/shard_map/all_to_all | solution.py:192
  843.8 4.3 all-to-all-start.6
  848.0 10.9 %psum.7 = f32[1,256]{1,0:T(1,128)} all-reduce(f32[1,256]{1,0:T(1,128)S(1)} %bitcast.154), channel_id=1, replica_groups=mesh['section'=4,'ctx'=16,'dp'=8] {'dp'}, use_global_device_ids=true, to_apply=%region_12.13 | all-reduce | flops 256 | bytes 2048 | tf_op jit(solution)/shard_map/psum | solution.py:212
  860.9 15.5 %all-to-all-done.6 = bf16[16,128,256]{2,1,0:T(8,128)(2,1)S(1)} async-done(((bf16[16,128,256]{2,1,0:T(8,128)(2,1)}), bf16[16,128,256]{2,1,0:T(8,128)(2,1)S(1)}, u32[]{:S(2)}, u32[]{:S(2)}) %all-to-all-start.6) | async-done | bytes 1048608 | tf_op jit(solution)/shard_map/all_to_all | solution.py:168
  (309 shorter events, 206.6 us)
Async XLA Ops:
  0.6 54.0 %copy-start.1 = (bf16[1,1,128,4096]{3,2,1,0:T(8,128)(2,1)S(1)}, bf16[1,1,128,4096]{3,2,1,0:T(8,128)(2,1)}, u32[]{:S(2)}) copy-start(bf16[1,1,128,4096]{3,2,1,0:T(8,128)(2,1)} %param.13) | copy-start | bytes 3145732
  4.0 44.3 %all-to-all-start.3 = ((bf16[128,16,128]{2,0,1:T(8,128)(2,1)}), bf16[128,16,128]{2,0,1:T(8,128)(2,1)S(1)}, u32[]{:S(2)}, u32[]{:S(2)}) async-start(bf16[128,16,128]{2,0,1:T(8,128)(2,1)} %bitcast.29), calls=%async_computation.3 | async-start | bytes 1048576 | tf_op jit(solution)/shard_map/all_to_all | solution.py:52
  20.3 69.8 %copy-start.2 = (bf16[1,128,4096]{2,1,0:T(8,128)(2,1)S(1)}, bf16[1,128,4096]{2,1,0:T(8,128)(2,1)}, u32[]{:S(2)}) copy-start(bf16[1,128,4096]{2,1,0:T(8,128)(2,1)} %param.17) | copy-start | bytes 3145732
  48.3 35.5 %all-to-all-start.5 = ((bf16[128,16,128]{2,0,1:T(8,128)(2,1)}), bf16[128,16,128]{2,0,1:T(8,128)(2,1)}, u32[]{:S(2)}, u32[]{:S(2)}) async-start(bf16[128,16,128]{2,0,1:T(8,128)(2,1)} %bitcast.36), calls=%async_computation.5 | async-start | bytes 1048576 | tf_op jit(solution)/shard_map/all_to_all | solution.py:53
  56.2 92.0 %copy-start.4 = (s32[16,4]{0,1:T(4,128)S(1)}, s32[16,4]{0,1:T(4,128)}, u32[]{:S(2)}) copy-start(s32[16,4]{0,1:T(4,128)} %param.18) | copy-start | bytes 772
  56.2 92.2 %copy-start.3 = (f32[1,256]{1,0:T(1,128)S(1)}, f32[1,256]{1,0:T(1,128)}, u32[]{:S(2)}) copy-start(f32[1,256]{1,0:T(1,128)} %param.16) | copy-start | bytes 3076
  83.8 56.4 %all-to-all-start.4 = ((bf16[128,16,256]{2,0,1:T(8,128)(2,1)}), bf16[128,16,256]{2,0,1:T(8,128)(2,1)}, u32[]{:S(2)}, u32[]{:S(2)}) async-start(bf16[128,16,256]{2,0,1:T(8,128)(2,1)} %copy.149), calls=%async_computation.4 | async-start | bytes 2097152 | tf_op jit(solution)/shard_map/all_to_all | solution.py:51
  140.2 58.1 %all-to-all-start.2 = ((bf16[128,16,256]{2,0,1:T(8,128)(2,1)}), bf16[128,16,256]{2,0,1:T(8,128)(2,1)}, u32[]{:S(2)}, u32[]{:S(2)}) async-start(bf16[128,16,256]{2,0,1:T(8,128)(2,1)} %copy.146), calls=%async_computation.2 | async-start | bytes 2097152 | tf_op jit(solution)/shard_map/all_to_all | solution.py:54
  205.4 22.6 %all-to-all-start = ((bf16[16,16,256]{2,0,1:T(8,128)(2,1)}), bf16[16,16,256]{2,0,1:T(8,128)(2,1)S(1)}, u32[]{:S(2)}, u32[]{:S(2)}) async-start(bf16[16,16,256]{2,0,1:T(8,128)(2,1)} %bitcast.127), calls=%async_computation | async-start | bytes 262144 | tf_op jit(solution)/shard_map/while/body/eval_jaxpr/all_to_all | solution.py:138
  229.8 18.6 %all-to-all-start.1 = ((bf16[16,16,256]{2,1,0:T(8,128)(2,1)}), bf16[16,16,256]{2,1,0:T(8,128)(2,1)S(1)}, u32[]{:S(2)}, u32[]{:S(2)}) async-start(bf16[16,16,256]{2,1,0:T(8,128)(2,1)} %bitcast.129), calls=%async_computation.1 | async-start | bytes 262144 | tf_op jit(solution)/shard_map/while/body/eval_jaxpr/all_to_all | solution.py:151
  248.5 6.9 collective-permute-start
  256.0 17.1 %all-to-all-start = ((bf16[16,16,256]{2,0,1:T(8,128)(2,1)}), bf16[16,16,256]{2,0,1:T(8,128)(2,1)S(1)}, u32[]{:S(2)}, u32[]{:S(2)}) async-start(bf16[16,16,256]{2,0,1:T(8,128)(2,1)} %bitcast.127), calls=%async_computation | async-start | bytes 262144 | tf_op jit(solution)/shard_map/while/body/eval_jaxpr/all_to_all | solution.py:138
  275.0 17.0 %all-to-all-start.1 = ((bf16[16,16,256]{2,1,0:T(8,128)(2,1)}), bf16[16,16,256]{2,1,0:T(8,128)(2,1)S(1)}, u32[]{:S(2)}, u32[]{:S(2)}) async-start(bf16[16,16,256]{2,1,0:T(8,128)(2,1)} %bitcast.129), calls=%async_computation.1 | async-start | bytes 262144 | tf_op jit(solution)/shard_map/while/body/eval_jaxpr/all_to_all | solution.py:151
  292.0 6.9 collective-permute-start
  299.5 17.2 %all-to-all-start = ((bf16[16,16,256]{2,0,1:T(8,128)(2,1)}), bf16[16,16,256]{2,0,1:T(8,128)(2,1)S(1)}, u32[]{:S(2)}, u32[]{:S(2)}) async-start(bf16[16,16,256]{2,0,1:T(8,128)(2,1)} %bitcast.127), calls=%async_computation | async-start | bytes 262144 | tf_op jit(solution)/shard_map/while/body/eval_jaxpr/all_to_all | solution.py:138
  318.6 17.1 %all-to-all-start.1 = ((bf16[16,16,256]{2,1,0:T(8,128)(2,1)}), bf16[16,16,256]{2,1,0:T(8,128)(2,1)S(1)}, u32[]{:S(2)}, u32[]{:S(2)}) async-start(bf16[16,16,256]{2,1,0:T(8,128)(2,1)} %bitcast.129), calls=%async_computation.1 | async-start | bytes 262144 | tf_op jit(solution)/shard_map/while/body/eval_jaxpr/all_to_all | solution.py:151
  335.7 24.1 %collective-permute-start = (bf16[16,4096]{1,0:T(8,128)(2,1)S(1)}, bf16[16,4096]{1,0:T(8,128)(2,1)S(1)}, u32[]{:S(2)}, u32[]{:S(2)}) collective-permute-start(bf16[16,4096]{1,0:T(8,128)(2,1)S(1)} %bitcast.145), channel_id=1, source_target_pairs={{128,0},{256,128},{384,256},{129,1},{257,129},{385,257},{130,2},{2... | collective-permute-start | bytes 393224 | tf_op jit(solution)/shard_map/while/body/eval_jaxpr/ppermute | solution.py:15
  360.5 17.0 %all-to-all-start = ((bf16[16,16,256]{2,0,1:T(8,128)(2,1)}), bf16[16,16,256]{2,0,1:T(8,128)(2,1)S(1)}, u32[]{:S(2)}, u32[]{:S(2)}) async-start(bf16[16,16,256]{2,0,1:T(8,128)(2,1)} %bitcast.127), calls=%async_computation | async-start | bytes 262144 | tf_op jit(solution)/shard_map/while/body/eval_jaxpr/all_to_all | solution.py:138
  385.8 17.2 %all-to-all-start.1 = ((bf16[16,16,256]{2,1,0:T(8,128)(2,1)}), bf16[16,16,256]{2,1,0:T(8,128)(2,1)S(1)}, u32[]{:S(2)}, u32[]{:S(2)}) async-start(bf16[16,16,256]{2,1,0:T(8,128)(2,1)} %bitcast.129), calls=%async_computation.1 | async-start | bytes 262144 | tf_op jit(solution)/shard_map/while/body/eval_jaxpr/all_to_all | solution.py:151
  402.9 6.9 collective-permute-start
  410.4 17.1 %all-to-all-start = ((bf16[16,16,256]{2,0,1:T(8,128)(2,1)}), bf16[16,16,256]{2,0,1:T(8,128)(2,1)S(1)}, u32[]{:S(2)}, u32[]{:S(2)}) async-start(bf16[16,16,256]{2,0,1:T(8,128)(2,1)} %bitcast.127), calls=%async_computation | async-start | bytes 262144 | tf_op jit(solution)/shard_map/while/body/eval_jaxpr/all_to_all | solution.py:138
  435.9 17.2 %all-to-all-start.1 = ((bf16[16,16,256]{2,1,0:T(8,128)(2,1)}), bf16[16,16,256]{2,1,0:T(8,128)(2,1)S(1)}, u32[]{:S(2)}, u32[]{:S(2)}) async-start(bf16[16,16,256]{2,1,0:T(8,128)(2,1)} %bitcast.129), calls=%async_computation.1 | async-start | bytes 262144 | tf_op jit(solution)/shard_map/while/body/eval_jaxpr/all_to_all | solution.py:151
  453.1 6.9 collective-permute-start
  460.6 17.1 %all-to-all-start = ((bf16[16,16,256]{2,0,1:T(8,128)(2,1)}), bf16[16,16,256]{2,0,1:T(8,128)(2,1)S(1)}, u32[]{:S(2)}, u32[]{:S(2)}) async-start(bf16[16,16,256]{2,0,1:T(8,128)(2,1)} %bitcast.127), calls=%async_computation | async-start | bytes 262144 | tf_op jit(solution)/shard_map/while/body/eval_jaxpr/all_to_all | solution.py:138
  486.0 17.1 %all-to-all-start.1 = ((bf16[16,16,256]{2,1,0:T(8,128)(2,1)}), bf16[16,16,256]{2,1,0:T(8,128)(2,1)S(1)}, u32[]{:S(2)}, u32[]{:S(2)}) async-start(bf16[16,16,256]{2,1,0:T(8,128)(2,1)} %bitcast.129), calls=%async_computation.1 | async-start | bytes 262144 | tf_op jit(solution)/shard_map/while/body/eval_jaxpr/all_to_all | solution.py:151
  503.2 6.9 collective-permute-start
  510.7 17.2 %all-to-all-start = ((bf16[16,16,256]{2,0,1:T(8,128)(2,1)}), bf16[16,16,256]{2,0,1:T(8,128)(2,1)S(1)}, u32[]{:S(2)}, u32[]{:S(2)}) async-start(bf16[16,16,256]{2,0,1:T(8,128)(2,1)} %bitcast.127), calls=%async_computation | async-start | bytes 262144 | tf_op jit(solution)/shard_map/while/body/eval_jaxpr/all_to_all | solution.py:138
  536.1 18.0 %all-to-all-start.1 = ((bf16[16,16,256]{2,1,0:T(8,128)(2,1)}), bf16[16,16,256]{2,1,0:T(8,128)(2,1)S(1)}, u32[]{:S(2)}, u32[]{:S(2)}) async-start(bf16[16,16,256]{2,1,0:T(8,128)(2,1)} %bitcast.129), calls=%async_computation.1 | async-start | bytes 262144 | tf_op jit(solution)/shard_map/while/body/eval_jaxpr/all_to_all | solution.py:151
  554.2 6.9 collective-permute-start
  561.7 19.9 %all-to-all-start = ((bf16[16,16,256]{2,0,1:T(8,128)(2,1)}), bf16[16,16,256]{2,0,1:T(8,128)(2,1)S(1)}, u32[]{:S(2)}, u32[]{:S(2)}) async-start(bf16[16,16,256]{2,0,1:T(8,128)(2,1)} %bitcast.127), calls=%async_computation | async-start | bytes 262144 | tf_op jit(solution)/shard_map/while/body/eval_jaxpr/all_to_all | solution.py:138
  589.9 19.4 %all-to-all-start.1 = ((bf16[16,16,256]{2,1,0:T(8,128)(2,1)}), bf16[16,16,256]{2,1,0:T(8,128)(2,1)S(1)}, u32[]{:S(2)}, u32[]{:S(2)}) async-start(bf16[16,16,256]{2,1,0:T(8,128)(2,1)} %bitcast.129), calls=%async_computation.1 | async-start | bytes 262144 | tf_op jit(solution)/shard_map/while/body/eval_jaxpr/all_to_all | solution.py:151
  609.4 6.9 collective-permute-start
  616.9 17.1 %all-to-all-start = ((bf16[16,16,256]{2,0,1:T(8,128)(2,1)}), bf16[16,16,256]{2,0,1:T(8,128)(2,1)S(1)}, u32[]{:S(2)}, u32[]{:S(2)}) async-start(bf16[16,16,256]{2,0,1:T(8,128)(2,1)} %bitcast.127), calls=%async_computation | async-start | bytes 262144 | tf_op jit(solution)/shard_map/while/body/eval_jaxpr/all_to_all | solution.py:138
  642.3 16.6 %all-to-all-start.1 = ((bf16[16,16,256]{2,1,0:T(8,128)(2,1)}), bf16[16,16,256]{2,1,0:T(8,128)(2,1)S(1)}, u32[]{:S(2)}, u32[]{:S(2)}) async-start(bf16[16,16,256]{2,1,0:T(8,128)(2,1)} %bitcast.129), calls=%async_computation.1 | async-start | bytes 262144 | tf_op jit(solution)/shard_map/while/body/eval_jaxpr/all_to_all | solution.py:151
  658.9 6.9 collective-permute-start
  666.4 17.1 %all-to-all-start = ((bf16[16,16,256]{2,0,1:T(8,128)(2,1)}), bf16[16,16,256]{2,0,1:T(8,128)(2,1)S(1)}, u32[]{:S(2)}, u32[]{:S(2)}) async-start(bf16[16,16,256]{2,0,1:T(8,128)(2,1)} %bitcast.127), calls=%async_computation | async-start | bytes 262144 | tf_op jit(solution)/shard_map/while/body/eval_jaxpr/all_to_all | solution.py:138
  691.9 17.2 %all-to-all-start.1 = ((bf16[16,16,256]{2,1,0:T(8,128)(2,1)}), bf16[16,16,256]{2,1,0:T(8,128)(2,1)S(1)}, u32[]{:S(2)}, u32[]{:S(2)}) async-start(bf16[16,16,256]{2,1,0:T(8,128)(2,1)} %bitcast.129), calls=%async_computation.1 | async-start | bytes 262144 | tf_op jit(solution)/shard_map/while/body/eval_jaxpr/all_to_all | solution.py:151
  709.0 6.9 collective-permute-start
  716.6 17.1 %all-to-all-start = ((bf16[16,16,256]{2,0,1:T(8,128)(2,1)}), bf16[16,16,256]{2,0,1:T(8,128)(2,1)S(1)}, u32[]{:S(2)}, u32[]{:S(2)}) async-start(bf16[16,16,256]{2,0,1:T(8,128)(2,1)} %bitcast.127), calls=%async_computation | async-start | bytes 262144 | tf_op jit(solution)/shard_map/while/body/eval_jaxpr/all_to_all | solution.py:138
  742.0 17.7 %all-to-all-start.1 = ((bf16[16,16,256]{2,1,0:T(8,128)(2,1)}), bf16[16,16,256]{2,1,0:T(8,128)(2,1)S(1)}, u32[]{:S(2)}, u32[]{:S(2)}) async-start(bf16[16,16,256]{2,1,0:T(8,128)(2,1)} %bitcast.129), calls=%async_computation.1 | async-start | bytes 262144 | tf_op jit(solution)/shard_map/while/body/eval_jaxpr/all_to_all | solution.py:151
  759.7 6.9 collective-permute-start
  781.0 25.7 %all-to-all-start.7 = ((bf16[16,128,128]{2,1,0:T(8,128)(2,1)}), bf16[16,128,128]{2,1,0:T(8,128)(2,1)S(1)}, u32[]{:S(2)}, u32[]{:S(2)}) async-start(bf16[16,128,128]{2,1,0:T(8,128)(2,1)} %convert_element_type.116), calls=%async_computation.7 | async-start | bytes 1048576 | tf_op jit(solution)/shard_map/all_to_all | solution.py:185
  793.4 28.8 %copy-start = (bf16[2304,256]{1,0:T(8,128)(2,1)S(1)}, bf16[2304,256]{1,0:T(8,128)(2,1)}, u32[]{:S(2)}) copy-start(bf16[2304,256]{1,0:T(8,128)(2,1)} %get-tuple-element.370) | copy-start | bytes 3538948
  806.7 37.1 %all-to-all-start.8 = ((bf16[16,128,128]{2,1,0:T(8,128)(2,1)}), bf16[16,128,128]{2,1,0:T(8,128)(2,1)S(1)}, u32[]{:S(2)}, u32[]{:S(2)}) async-start(bf16[16,128,128]{2,1,0:T(8,128)(2,1)} %convert_element_type.122), calls=%async_computation.8 | async-start | bytes 1048576 | tf_op jit(solution)/shard_map/all_to_all | solution.py:192
  843.8 32.6 %all-to-all-start.6 = ((bf16[16,128,256]{2,1,0:T(8,128)(2,1)}), bf16[16,128,256]{2,1,0:T(8,128)(2,1)S(1)}, u32[]{:S(2)}, u32[]{:S(2)}) async-start(bf16[16,128,256]{2,1,0:T(8,128)(2,1)} %bitcast.39), calls=%async_computation.6 | async-start | bytes 2097152 | tf_op jit(solution)/shard_map/all_to_all | solution.py:168
where the time goes:
time: 882 us; the launch traced here: 878 us
  waiting for transfers between devices  548 us (62%)
  starting transfers between devices  172 us (20%)
  local copies, waits for them, and re-layouts  79.6 us (9%)
  other arithmetic  52.4 us (6%)
  matrix products  12.1 us (1%)
  blocking collectives  10.9 us (1%)
    all_to_all x11, waiting for transfers between devices, turn_step(): lax.all_to_all(incoming, 'ctx', split_axis=1, concat_axis=0, tiled=True)  147 us
    all_to_all x11, waiting for transfers between devices, turn_step(): lax.all_to_all(handed, 'ctx', split_axis=0, concat_axis=1, tiled=True)  145 us
    ppermute x11, waiting for transfers between devices, passed_along(): return lax.ppermute(block, axis, route)  66.5 us
    all_to_all x11, starting transfers between devices, turn_step(): lax.all_to_all(incoming, 'ctx', split_axis=1, concat_axis=0, tiled=True)  49.3 us
    all_to_all x1, waiting for transfers between devices, shards(): lax.all_to_all(layer_input, 'ctx', split_axis=1, concat_axis=0, tiled=True)  48.5 us
    all_to_all x1, waiting for transfers between devices, shards(): lax.all_to_all(top_grad[0], 'ctx', split_axis=1, concat_axis=0, tiled=True)  47.5 us
    all_to_all x11, starting transfers between devices, turn_step(): lax.all_to_all(handed, 'ctx', split_axis=0, concat_axis=1, tiled=True)  45.3 us
    all_to_all x1, waiting for transfers between devices, shards(): lax.all_to_all(sent_values, 'ctx', split_axis=1, concat_axis=0, tiled=True)  27.6 us
  transfers between devices with their start and end apart: 40, of which 40 were waited for; matrix products, arithmetic and copies ran while one was open for 5% of the time, Pallas kernels for 0%

commit v1 on v0

v1 whole, which is shorter than its diff:
```python
import math

import jax
import jax.numpy as jnp
from jax import lax
from jax.sharding import PartitionSpec as P

HEAD_FEATURES = 128


def passed_along(block, axis, distance):
    devices = range(lax.axis_size(axis))
    route = [(i - distance, i) for i in devices if i - distance in devices]
    return lax.ppermute(block, axis, route)


def shards(query_input, key_states, value_states, query_gain, top_grad, block_lists):
    ctx_count = lax.axis_size("ctx")
    section_count = lax.axis_size("section")
    section_pos = lax.axis_index("section")
    ctx_pos = lax.axis_index("ctx")
    layer_input = query_input[0, 0]
    tok_local, feature_count = layer_input.shape
    kv_width = key_states.shape[-1]
    kv_heads = kv_width // HEAD_FEATURES
    head_count = feature_count // HEAD_FEATURES
    group_width = head_count // kv_heads
    group_features = group_width * HEAD_FEATURES
    block_count, listed = block_lists.shape
    block_rows = tok_local * ctx_count // block_count
    assert block_rows == tok_local
    scale_factor = 1.0 / math.sqrt(HEAD_FEATURES)
    turn_count = kv_heads + section_count - 1

    gain_row = lax.all_gather(query_gain[0], "ctx", tiled=True)
    query_rows = (layer_input.astype(jnp.float32) * gain_row).astype(jnp.bfloat16)
    own_top = top_grad[0]
    own_keys = key_states[0, 0]
    own_values = value_states[0, 0]
    own_list = lax.dynamic_index_in_dim(block_lists, ctx_pos, 0, keepdims=False)
    on_top = section_pos == section_count - 1
    lag = section_count - 1 - section_pos

    def group_cols(array, group, width):
        return lax.dynamic_slice_in_dim(array, group * width, width, 1)

    def attend(group, head_grad):
        keys_now = lax.all_gather(group_cols(own_keys, group, HEAD_FEATURES), "ctx", tiled=True)
        values_now = lax.all_gather(group_cols(own_values, group, HEAD_FEATURES), "ctx", tiled=True)
        neighbor_keys = keys_now.reshape(block_count, block_rows, HEAD_FEATURES)[own_list].reshape(
            listed * block_rows, HEAD_FEATURES
        )
        neighbor_values = values_now.reshape(block_count, block_rows, HEAD_FEATURES)[
            own_list
        ].reshape(listed * block_rows, HEAD_FEATURES)
        query_now = group_cols(query_rows, group, group_features).reshape(
            tok_local, group_width, HEAD_FEATURES
        )
        input_now = group_cols(layer_input, group, group_features)
        gain_now = lax.dynamic_slice_in_dim(gain_row, group * group_features, group_features, 0)
        grad_now = head_grad.reshape(tok_local, group_width, HEAD_FEATURES)
        scores = (
            jnp.einsum("bhd,jd->hbj", query_now, neighbor_keys, preferred_element_type=jnp.float32)
            * scale_factor
        )
        row_max = jnp.max(scores, axis=-1, keepdims=True)
        weights = jnp.exp(scores - row_max)
        probs = weights / jnp.sum(weights, axis=-1, keepdims=True)
        probs_low = probs.astype(jnp.bfloat16)
        prob_grad = jnp.einsum(
            "bhd,jd->hbj", grad_now, neighbor_values, preferred_element_type=jnp.float32
        )
        row_dot = jnp.sum(probs * prob_grad, axis=-1, keepdims=True)
        score_grad = (probs * (prob_grad - row_dot)).astype(jnp.bfloat16)
        query_grad = (
            jnp.einsum("hbj,jd->bhd", score_grad, neighbor_keys, preferred_element_type=jnp.float32)
            * scale_factor
        ).reshape(tok_local, group_features)
        key_part = (
            jnp.einsum("hbj,bhd->jd", score_grad, query_now, preferred_element_type=jnp.float32)
            * scale_factor
        )
        value_part = jnp.einsum(
            "hbj,bhd->jd", probs_low, grad_now, preferred_element_type=jnp.float32
        )
        moved_grad = (gain_now * query_grad).astype(jnp.bfloat16)
        handed = (head_grad.astype(jnp.float32) + moved_grad.astype(jnp.float32)).astype(
            jnp.bfloat16
        )
        gain_part = jnp.sum(input_now.astype(jnp.float32) * query_grad, axis=0)
        key_blocks = (
            jnp.zeros((block_count, block_rows, HEAD_FEATURES), jnp.float32)
            .at[own_list]
            .add(key_part.reshape(listed, block_rows, HEAD_FEATURES))
        )
        value_blocks = (
            jnp.zeros((block_count, block_rows, HEAD_FEATURES), jnp.float32)
            .at[own_list]
            .add(value_part.reshape(listed, block_rows, HEAD_FEATURES))
        )
        key_own = lax.psum_scatter(
            key_blocks.reshape(block_count * block_rows, HEAD_FEATURES),
            "ctx",
            scatter_dimension=0,
            tiled=True,
        )
        value_own = lax.psum_scatter(
            value_blocks.reshape(block_count * block_rows, HEAD_FEATURES),
            "ctx",
            scatter_dimension=0,
            tiled=True,
        )
        return handed, key_own, value_own, gain_part

    incoming = jnp.zeros((tok_local, group_features), jnp.bfloat16)
    handed_turns, key_turns, value_turns, gain_turns = [], [], [], []
    for turn in range(turn_count):
        group = jnp.clip(turn - lag, 0, kv_heads - 1)
        from_top = group_cols(own_top, group, group_features)
        head_grad = jnp.where(on_top, from_top, incoming)
        handed, key_own, value_own, gain_part = attend(group, head_grad)
        handed_turns.append(handed)
        key_turns.append(key_own)
        value_turns.append(value_own)
        gain_turns.append(gain_part)
        if turn + 1 < turn_count:
            incoming = passed_along(handed, "section", -1)

    def own_turns(parts):
        stacked = jnp.stack(parts)
        return lax.dynamic_slice_in_dim(stacked, lag, kv_heads, 0)

    stream_out = (
        own_turns(handed_turns).transpose(1, 0, 2).reshape(tok_local, feature_count)
    )
    key_out = (
        own_turns(key_turns).transpose(1, 0, 2).reshape(tok_local, kv_width).astype(jnp.bfloat16)
    )
    value_out = (
        own_turns(value_turns)
        .transpose(1, 0, 2)
        .reshape(tok_local, kv_width)
        .astype(jnp.bfloat16)
    )
    gain_full = own_turns(gain_turns).reshape(feature_count)
    gain_total = lax.psum(
        lax.psum_scatter(gain_full, "ctx", scatter_dimension=0, tiled=True), "dp"
    )
    return (stream_out[None, None], key_out[None, None], value_out[None, None], gain_total[None])


def solution(mesh):
    placed = (
        P("section", "dp", "ctx", None),
        P("section", "dp", "ctx", None),
        P("section", "dp", "ctx", None),
        P("section", "ctx"),
        P("dp", "ctx", None),
        P(),
    )
    return jax.shard_map(
        shards,
        mesh=mesh,
        in_specs=placed,
        out_specs=(
            P("section", "dp", "ctx", None),
            P("section", "dp", "ctx", None),
            P("section", "dp", "ctx", None),
            P("section", "ctx"),
        ),
        check_vma=False,
    )
```

time: 882 us -> 1450 us (1.64)
  blocking collectives: 10.9 us -> 539 us
  starting transfers between devices: 172 us -> 8.64 us
  waiting for transfers between devices: 548 us -> 698 us
  matrix products: 12.1 us -> 42.1 us
  other arithmetic: 52.4 us -> 73 us
  between operations: 0.88 us -> 16.5 us
    reduce_scatter x0 -> x14, waiting for transfers between devices: none -> 690 us  [the longest x7 495 us: attend(): lax.psum_scatter(value_blocks.reshape(block_count * block_rows, HEAD_FEAT...]
    all_to_all x29 -> x0, waiting for transfers between devices: 482 us -> none  [the longest x11 147 us: turn_step(): lax.all_to_all(incoming, 'ctx', split_axis=1, concat_axis=0, tiled=True)]
    all_gather x0 -> x15, blocking collectives: none -> 475 us  [the longest x7 226 us: attend(): lax.all_gather(group_cols(own_keys, group, HEAD_FEATURES), 'ctx', tiled=T...]
    all_to_all x29 -> x0, starting transfers between devices: 158 us -> none  [the longest x11 49.3 us: turn_step(): lax.all_to_all(incoming, 'ctx', split_axis=1, concat_axis=0, tiled=True)]
    ppermute x11 -> x6, waiting for transfers between devices: 66.5 us -> 7.94 us  [passed_along(): return lax.ppermute(block, axis, route)]
    unnamed x0 -> x1, blocking collectives: none -> 53.1 us
    dot_general x40 -> x35, matrix products: 12.1 us -> 42.1 us  [the longest x7 13.1 us: attend(): jnp.einsum('bhd,jd->hbj', query_now, neighbor_keys, preferred_element_typ...]
  transfers between devices with their start and end apart: 40 -> 20, of which waited for: 40 -> 13; matrix products, arithmetic and copies ran while one was open for 5% -> 10% of each run, Pallas kernels for 0% -> 0%
where the time goes in v1:
time: 1450 us
  waiting for transfers between devices  698 us (48%)
  blocking collectives  539 us (37%)
  other arithmetic  73 us (5%)
  local copies, waits for them, and re-layouts  67.9 us (5%)
  matrix products  42.1 us (3%)
  between operations  16.5 us (1%)
    reduce_scatter x7, waiting for transfers between devices, attend(): lax.psum_scatter(value_blocks.reshape(block_count * block_rows, HEAD_FEAT...  495 us
    all_gather x7, blocking collectives, attend(): lax.all_gather(group_cols(own_keys, group, HEAD_FEATURES), 'ctx', tiled=T...  226 us
    all_gather x7, blocking collectives, attend(): lax.all_gather(group_cols(own_values, group, HEAD_FEATURES), 'ctx', tiled...  224 us
    reduce_scatter x7, waiting for transfers between devices, attend(): lax.psum_scatter(key_blocks.reshape(block_count * block_rows, HEAD_FEATUR...  195 us
    unnamed x1, blocking collectives  53.1 us
  transfers between devices with their start and end apart: 20, of which 13 were waited for; matrix products, arithmetic and copies ran while one was open for 10% of the time, Pallas kernels for 0%

profile of v1, /device:TPU:6, one launch (start us, length us, event | category | flops | bytes accessed | tf_op | source)
XLA Modules:
  0.0 1445.5 jit_solution(15006722407481758809)
XLA Ops:
  9.0 1.8 dynamic-slice_convert_fusion
  12.4 40.5 %all-gather.1 = bf16[1,1,2048,128]{3,2,1,0:T(8,128)(2,1)} all-gather(bf16[1,1,128,128]{3,2,1,0:T(8,128)(2,1)S(1)} %get-tuple-element.45), channel_id=3, replica_groups=mesh['section'=4,'ctx'=16,'dp'=8] {'ctx'}, dimensions={2}, use_global_device_ids=true | all-gather | bytes 557056 | tf_op jit(solution)/shard_map/all_gather | solution.py:48
  53.2 26.0 %all-gather = f32[1,4096]{1,0:T(1,128)S(1)} all-gather(f32[1,256]{1,0:T(1,128)S(1)} %copy-done.116), channel_id=2, replica_groups=mesh['section'=4,'ctx'=16,'dp'=8] {'ctx'}, dimensions={1}, use_global_device_ids=true | all-gather | bytes 17408 | tf_op jit(solution)/shard_map/all_gather | solution.py:35
  82.3 31.5 %all-gather.2 = bf16[1,1,2048,128]{3,2,1,0:T(8,128)(2,1)S(1)} all-gather(bf16[1,1,128,128]{3,2,1,0:T(8,128)(2,1)S(1)} %get-tuple-element.38), channel_id=4, replica_groups=mesh['section'=4,'ctx'=16,'dp'=8] {'ctx'}, dimensions={2}, use_global_device_ids=true | all-gather | bytes 557056 | tf_op jit(solution)/shard_map/all_gather | solution.py:49
  128.4 29.4 %all-gather.3 = bf16[1,1,2048,128]{3,2,1,0:T(8,128)(2,1)S(1)} all-gather(bf16[1,1,128,128]{3,2,1,0:T(8,128)(2,1)S(1)} %copy-done.73), channel_id=5, replica_groups=mesh['section'=4,'ctx'=16,'dp'=8] {'ctx'}, dimensions={2}, use_global_device_ids=true | all-gather | bytes 557056 | tf_op jit(solution)/shard_map/all_gather | solution.py:48
  158.4 34.3 %all-gather.4 = bf16[1,1,2048,128]{3,2,1,0:T(8,128)(2,1)} all-gather(bf16[1,1,128,128]{3,2,1,0:T(8,128)(2,1)S(1)} %copy-done.78), channel_id=6, replica_groups=mesh['section'=4,'ctx'=16,'dp'=8] {'ctx'}, dimensions={2}, use_global_device_ids=true | all-gather | bytes 557056 | tf_op jit(solution)/shard_map/all_gather | solution.py:49
  192.8 30.4 %all-gather.5 = bf16[1,1,2048,128]{3,2,1,0:T(8,128)(2,1)S(1)} all-gather(bf16[1,1,128,128]{3,2,1,0:T(8,128)(2,1)S(1)} %copy-done.72), channel_id=7, replica_groups=mesh['section'=4,'ctx'=16,'dp'=8] {'ctx'}, dimensions={2}, use_global_device_ids=true | all-gather | bytes 557056 | tf_op jit(solution)/shard_map/all_gather | solution.py:48
  223.7 32.2 %all-gather.6 = bf16[1,1,2048,128]{3,2,1,0:T(8,128)(2,1)} all-gather(bf16[1,1,128,128]{3,2,1,0:T(8,128)(2,1)S(1)} %copy-done.77), channel_id=8, replica_groups=mesh['section'=4,'ctx'=16,'dp'=8] {'ctx'}, dimensions={2}, use_global_device_ids=true | all-gather | bytes 557056 | tf_op jit(solution)/shard_map/all_gather | solution.py:49
  255.9 30.8 %all-gather.7 = bf16[1,1,2048,128]{3,2,1,0:T(8,128)(2,1)S(1)} all-gather(bf16[1,1,128,128]{3,2,1,0:T(8,128)(2,1)S(1)} %copy-done.71), channel_id=9, replica_groups=mesh['section'=4,'ctx'=16,'dp'=8] {'ctx'}, dimensions={2}, use_global_device_ids=true | all-gather | bytes 557056 | tf_op jit(solution)/shard_map/all_gather | solution.py:48
  287.3 31.7 %all-gather.8 = bf16[1,1,2048,128]{3,2,1,0:T(8,128)(2,1)} all-gather(bf16[1,1,128,128]{3,2,1,0:T(8,128)(2,1)S(1)} %copy-done.76), channel_id=10, replica_groups=mesh['section'=4,'ctx'=16,'dp'=8] {'ctx'}, dimensions={2}, use_global_device_ids=true | all-gather | bytes 557056 | tf_op jit(solution)/shard_map/all_gather | solution.py:49
  319.0 30.7 %all-gather.9 = bf16[1,1,2048,128]{3,2,1,0:T(8,128)(2,1)S(1)} all-gather(bf16[1,1,128,128]{3,2,1,0:T(8,128)(2,1)S(1)} %copy-done.70), channel_id=11, replica_groups=mesh['section'=4,'ctx'=16,'dp'=8] {'ctx'}, dimensions={2}, use_global_device_ids=true | all-gather | bytes 557056 | tf_op jit(solution)/shard_map/all_gather | solution.py:48
  350.3 31.6 %all-gather.10 = bf16[1,1,2048,128]{3,2,1,0:T(8,128)(2,1)} all-gather(bf16[1,1,128,128]{3,2,1,0:T(8,128)(2,1)S(1)} %copy-done.75), channel_id=12, replica_groups=mesh['section'=4,'ctx'=16,'dp'=8] {'ctx'}, dimensions={2}, use_global_device_ids=true | all-gather | bytes 557056 | tf_op jit(solution)/shard_map/all_gather | solution.py:49
  381.8 30.7 %all-gather.11 = bf16[1,1,2048,128]{3,2,1,0:T(8,128)(2,1)S(1)} all-gather(bf16[1,1,128,128]{3,2,1,0:T(8,128)(2,1)S(1)} %copy-done.69), channel_id=13, replica_groups=mesh['section'=4,'ctx'=16,'dp'=8] {'ctx'}, dimensions={2}, use_global_device_ids=true | all-gather | bytes 557056 | tf_op jit(solution)/shard_map/all_gather | solution.py:48
  413.1 31.3 %all-gather.12 = bf16[1,1,2048,128]{3,2,1,0:T(8,128)(2,1)} all-gather(bf16[1,1,128,128]{3,2,1,0:T(8,128)(2,1)S(1)} %copy-done.74), channel_id=14, replica_groups=mesh['section'=4,'ctx'=16,'dp'=8] {'ctx'}, dimensions={2}, use_global_device_ids=true | all-gather | bytes 557056 | tf_op jit(solution)/shard_map/all_gather | solution.py:49
  444.5 2.4 bitcast_reduce_fusion.5
  446.9 2.4 bitcast_reduce_fusion.4
  449.3 2.4 bitcast_reduce_fusion.3
  453.8 33.3 %all-gather.13 = bf16[1,1,2048,128]{3,2,1,0:T(8,128)(2,1)} all-gather(bf16[1,1,128,128]{3,2,1,0:T(8,128)(2,1)S(1)} %copy-done.68), channel_id=15, replica_groups=mesh['section'=4,'ctx'=16,'dp'=8] {'ctx'}, dimensions={2}, use_global_device_ids=true | all-gather | bytes 557056 | tf_op jit(solution)/shard_map/all_gather | solution.py:48
  487.2 2.0 copy.196
  489.2 2.4 gather_fusion.3
  491.6 1.8 copy.145
  494.4 2.4 gather_fusion.5
  496.8 1.8 copy.151
  499.6 1.8 gather_fusion.7
  502.2 2.1 fusion.32
  514.5 2.1 fusion.34
  528.3 2.1 fusion.36
  541.9 2.6 fusion.38
  545.5 2.4 gather_fusion.9
  550.0 2.4 gather_fusion.11
  560.9 2.4 scatter_fusion.4
  563.4 2.8 fusion.63
  566.3 2.1 bitcast_dynamic-update-slice_fusion.1
  569.7 2.3 bitcast_reduce_fusion
  572.0 5.2 collective-permute-done.4
  581.2 2.5 scatter_fusion.5
  583.6 2.8 fusion.62
  586.6 2.1 bitcast_dynamic-update-slice_fusion
  590.0 31.1 %all-gather.14 = bf16[1,1,2048,128]{3,2,1,0:T(8,128)(2,1)S(1)} all-gather(bf16[1,1,128,128]{3,2,1,0:T(8,128)(2,1)S(1)} %copy-done.67), channel_id=16, replica_groups=mesh['section'=4,'ctx'=16,'dp'=8] {'ctx'}, dimensions={2}, use_global_device_ids=true | all-gather | bytes 557056 | tf_op jit(solution)/shard_map/all_gather | solution.py:49
  622.0 2.1 fusion.42
  629.0 2.5 scatter_fusion.6
  631.6 2.1 divide_convert_fusion.6
  635.9 2.5 scatter_fusion.7
  638.4 2.0 divide_convert_fusion.5
  642.7 2.5 scatter_fusion.8
  645.4 2.0 divide_convert_fusion.4
  649.7 2.5 scatter_fusion.9
  652.2 2.0 divide_convert_fusion.3
  656.5 2.5 scatter_fusion.10
  659.1 2.0 divide_convert_fusion.2
  663.3 2.5 scatter_fusion.11
  669.0 2.5 scatter_fusion.12
  680.2 53.1 %all-reduce = f32[4096]{0:T(1024)S(1)} all-reduce(f32[4096]{0:T(1024)S(1)} %bitcast.698), channel_id=31, replica_groups=mesh['section'=4,'ctx'=16,'dp'=8] {'ctx'}, use_global_device_ids=true, to_apply=%region_56.57.clone | all-reduce | flops 4096 | bytes 32768
  733.4 10.5 psum.7
  744.0 52.7 %reduce-scatter.23.cloned.1.call-done = f32[128,128]{1,0:T(8,128)} async-done(((f32[2048,128]{1,0:T(8,128)}), f32[128,128]{1,0:T(8,128)}) %reduce-scatter.23.cloned.1.call-update) | async-done | bytes 65552 | tf_op jit(solution)/shard_map/reduce_scatter | solution.py:101
  796.7 71.0 %reduce-scatter.25.cloned.1.call-done = f32[128,128]{1,0:T(8,128)} async-done(((f32[2048,128]{1,0:T(8,128)}), f32[128,128]{1,0:T(8,128)}) %reduce-scatter.25.cloned.1.call-update) | async-done | bytes 65552 | tf_op jit(solution)/shard_map/reduce_scatter | solution.py:101
  867.7 70.9 %reduce-scatter.27.cloned.1.call-done = f32[128,128]{1,0:T(8,128)} async-done(((f32[2048,128]{1,0:T(8,128)}), f32[128,128]{1,0:T(8,128)}) %reduce-scatter.27.cloned.1.call-update) | async-done | bytes 65552 | tf_op jit(solution)/shard_map/reduce_scatter | solution.py:101
  940.1 69.6 %reduce-scatter.29.cloned.1.call-done = f32[128,128]{1,0:T(8,128)} async-done(((f32[2048,128]{1,0:T(8,128)}), f32[128,128]{1,0:T(8,128)}) %reduce-scatter.29.cloned.1.call-update) | async-done | bytes 65552 | tf_op jit(solution)/shard_map/reduce_scatter | solution.py:107
  1009.7 71.0 %reduce-scatter.31.cloned.1.call-done = f32[128,128]{1,0:T(8,128)} async-done(((f32[2048,128]{1,0:T(8,128)}), f32[128,128]{1,0:T(8,128)}) %reduce-scatter.31.cloned.1.call-update) | async-done | bytes 65552 | tf_op jit(solution)/shard_map/reduce_scatter | solution.py:107
  1080.7 71.0 %reduce-scatter.33.cloned.1.call-done = f32[128,128]{1,0:T(8,128)} async-done(((f32[2048,128]{1,0:T(8,128)}), f32[128,128]{1,0:T(8,128)}) %reduce-scatter.33.cloned.1.call-update) | async-done | bytes 65552 | tf_op jit(solution)/shard_map/reduce_scatter | solution.py:107
  1151.7 70.9 %reduce-scatter.35.cloned.1.call-done = f32[128,128]{1,0:T(8,128)} async-done(((f32[2048,128]{1,0:T(8,128)}), f32[128,128]{1,0:T(8,128)}) %reduce-scatter.35.cloned.1.call-update) | async-done | bytes 65552 | tf_op jit(solution)/shard_map/reduce_scatter | solution.py:107
  1222.6 71.0 %reduce-scatter.37.cloned.1.call-done = f32[128,128]{1,0:T(8,128)} async-done(((f32[2048,128]{1,0:T(8,128)}), f32[128,128]{1,0:T(8,128)}) %reduce-scatter.37.cloned.1.call-update) | async-done | bytes 65552 | tf_op jit(solution)/shard_map/reduce_scatter | solution.py:107
  1293.6 70.9 %reduce-scatter.39.cloned.1.call-done = f32[128,128]{1,0:T(8,128)} async-done(((f32[2048,128]{1,0:T(8,128)}), f32[128,128]{1,0:T(8,128)}) %reduce-scatter.39.cloned.1.call-update) | async-done | bytes 65552 | tf_op jit(solution)/shard_map/reduce_scatter | solution.py:107
  1364.6 71.0 %reduce-scatter.41.cloned.1.call-done = f32[128,128]{1,0:T(8,128)} async-done(((f32[2048,128]{1,0:T(8,128)}), f32[128,128]{1,0:T(8,128)}) %reduce-scatter.41.cloned.1.call-update) | async-done | bytes 65552 | tf_op jit(solution)/shard_map/reduce_scatter | solution.py:107
  (391 shorter events, 113.1 us)
Async XLA Ops:
  7.2 45.8 %copy-start = (s32[16,4]{0,1:T(4,128)S(1)}, s32[16,4]{0,1:T(4,128)}, u32[]{:S(2)}) copy-start(s32[16,4]{0,1:T(4,128)} %param.11) | copy-start | bytes 772
  7.2 736.8 %reduce-scatter.15.cloned.1.call-start = ((), (), s32[]{:S(2)}) async-start(), calls=%async_computation.14 | async-start | bytes 1114112 | tf_op jit(solution)/shard_map/reduce_scatter | solution.py:101
  10.8 42.4 %copy-start.116 = (f32[1,256]{1,0:T(1,128)S(1)}, f32[1,256]{1,0:T(1,128)}, u32[]{:S(2)}) copy-start(f32[1,256]{1,0:T(1,128)} %param.9) | copy-start | bytes 3076
  53.2 359.4 %copy-start.105 = (s32[1024]{0:T(1024)}, s32[1024]{0:T(1024)S(1)}, u32[]{:S(2)}) copy-start(s32[1024]{0:T(1024)S(1)} %pad_clamp_fusion) | copy-start | bytes 12292
  80.5 36.1 %copy-start.15 = (bf16[1,128,4096]{2,1,0:T(8,128)(2,1)S(1)}, bf16[1,128,4096]{2,1,0:T(8,128)(2,1)}, u32[]{:S(2)}) copy-start(bf16[1,128,4096]{2,1,0:T(8,128)(2,1)} %param.10) | copy-start | bytes 3145732
  81.4 365.5 %copy-start.32 = (bf16[128,1024]{0,1:T(8,128)(2,1)}, bf16[128,1024]{0,1:T(8,128)(2,1)S(1)}, u32[]{:S(2)}) copy-start(bf16[128,1024]{0,1:T(8,128)(2,1)S(1)} %get-tuple-element.23) | copy-start | bytes 786436
  81.4 367.8 %copy-start.30 = (bf16[128,1024]{0,1:T(8,128)(2,1)}, bf16[128,1024]{0,1:T(8,128)(2,1)S(1)}, u32[]{:S(2)}) copy-start(bf16[128,1024]{0,1:T(8,128)(2,1)S(1)} %get-tuple-element.22) | copy-start | bytes 786436
  81.4 370.2 %copy-start.28 = (bf16[128,1024]{0,1:T(8,128)(2,1)}, bf16[128,1024]{0,1:T(8,128)(2,1)S(1)}, u32[]{:S(2)}) copy-start(bf16[128,1024]{0,1:T(8,128)(2,1)S(1)} %get-tuple-element.21) | copy-start | bytes 786436
  81.4 372.0 %copy-start.26 = (bf16[128,1024]{0,1:T(8,128)(2,1)}, bf16[128,1024]{0,1:T(8,128)(2,1)S(1)}, u32[]{:S(2)}) copy-start(bf16[128,1024]{0,1:T(8,128)(2,1)S(1)} %get-tuple-element.20) | copy-start | bytes 786436
  123.7 380.6 %collective-permute-start = (bf16[128,1024]{0,1:T(8,128)(2,1)}, bf16[128,1024]{0,1:T(8,128)(2,1)}, u32[]{:S(2)}, u32[]{:S(2)}) collective-permute-start(bf16[128,1024]{0,1:T(8,128)(2,1)} %fusion.52), channel_id=1, source_target_pairs={{128,0},{256,128},{384,256},{129,1},{257,129},{385,257},{130,2},{2... | collective-permute-start | bytes 786440 | tf_op jit(solution)/shard_map/ppermute | solution.py:14
  125.6 32.8 %copy-start.78 = (bf16[1,1,128,128]{3,2,1,0:T(8,128)(2,1)S(1)}, bf16[1,1,128,128]{3,2,1,0:T(8,128)(2,1)}, u32[]{:S(2)}) copy-start(bf16[1,1,128,128]{3,2,1,0:T(8,128)(2,1)} %get-tuple-element.37) | copy-start | bytes 98308
  125.6 67.2 %copy-start.72 = (bf16[1,1,128,128]{3,2,1,0:T(8,128)(2,1)S(1)}, bf16[1,1,128,128]{3,2,1,0:T(8,128)(2,1)}, u32[]{:S(2)}) copy-start(bf16[1,1,128,128]{3,2,1,0:T(8,128)(2,1)} %get-tuple-element.43) | copy-start | bytes 98308
  126.4 97.3 %copy-start.77 = (bf16[1,1,128,128]{3,2,1,0:T(8,128)(2,1)S(1)}, bf16[1,1,128,128]{3,2,1,0:T(8,128)(2,1)}, u32[]{:S(2)}) copy-start(bf16[1,1,128,128]{3,2,1,0:T(8,128)(2,1)} %get-tuple-element.36) | copy-start | bytes 98308
  127.4 128.5 %copy-start.71 = (bf16[1,1,128,128]{3,2,1,0:T(8,128)(2,1)S(1)}, bf16[1,1,128,128]{3,2,1,0:T(8,128)(2,1)}, u32[]{:S(2)}) copy-start(bf16[1,1,128,128]{3,2,1,0:T(8,128)(2,1)} %get-tuple-element.42) | copy-start | bytes 98308
  127.4 159.9 %copy-start.76 = (bf16[1,1,128,128]{3,2,1,0:T(8,128)(2,1)S(1)}, bf16[1,1,128,128]{3,2,1,0:T(8,128)(2,1)}, u32[]{:S(2)}) copy-start(bf16[1,1,128,128]{3,2,1,0:T(8,128)(2,1)} %get-tuple-element.35) | copy-start | bytes 98308
  127.4 616.6 %reduce-scatter.17.cloned.1.call-start = ((), (), s32[]{:S(2)}) async-start(), calls=%async_computation.15 | async-start | bytes 1114112 | tf_op jit(solution)/shard_map/reduce_scatter | solution.py:101
  128.4 190.6 %copy-start.70 = (bf16[1,1,128,128]{3,2,1,0:T(8,128)(2,1)S(1)}, bf16[1,1,128,128]{3,2,1,0:T(8,128)(2,1)}, u32[]{:S(2)}) copy-start(bf16[1,1,128,128]{3,2,1,0:T(8,128)(2,1)} %get-tuple-element.41) | copy-start | bytes 98308
  158.4 286.1 %copy-start.53 = (bf16[4,128,128]{2,1,0:T(8,128)(2,1)}, bf16[4,128,128]{2,1,0:T(8,128)(2,1)S(1)}, u32[]{:S(2)}) copy-start(bf16[4,128,128]{2,1,0:T(8,128)(2,1)S(1)} %gather_fusion.2) | copy-start | bytes 393220
  158.4 191.9 %copy-start.75 = (bf16[1,1,128,128]{3,2,1,0:T(8,128)(2,1)S(1)}, bf16[1,1,128,128]{3,2,1,0:T(8,128)(2,1)}, u32[]{:S(2)}) copy-start(bf16[1,1,128,128]{3,2,1,0:T(8,128)(2,1)} %get-tuple-element.34) | copy-start | bytes 98308
  192.8 189.1 %copy-start.69 = (bf16[1,1,128,128]{3,2,1,0:T(8,128)(2,1)S(1)}, bf16[1,1,128,128]{3,2,1,0:T(8,128)(2,1)}, u32[]{:S(2)}) copy-start(bf16[1,1,128,128]{3,2,1,0:T(8,128)(2,1)} %get-tuple-element.46) | copy-start | bytes 98308
  223.7 223.2 %copy-start.51 = (bf16[4,128,128]{2,1,0:T(8,128)(2,1)}, bf16[4,128,128]{2,1,0:T(8,128)(2,1)S(1)}, u32[]{:S(2)}) copy-start(bf16[4,128,128]{2,1,0:T(8,128)(2,1)S(1)} %gather_fusion.4) | copy-start | bytes 393220
  223.7 189.4 %copy-start.74 = (bf16[1,1,128,128]{3,2,1,0:T(8,128)(2,1)S(1)}, bf16[1,1,128,128]{3,2,1,0:T(8,128)(2,1)}, u32[]{:S(2)}) copy-start(bf16[1,1,128,128]{3,2,1,0:T(8,128)(2,1)} %get-tuple-element.39) | copy-start | bytes 98308
  255.9 188.6 %copy-start.36 = (bf16[128,1024]{0,1:T(8,128)(2,1)S(1)}, bf16[128,1024]{0,1:T(8,128)(2,1)}, u32[]{:S(2)}) copy-start(bf16[128,1024]{0,1:T(8,128)(2,1)} %get-tuple-element.24) | copy-start | bytes 786436
  287.3 162.0 %copy-start.49 = (bf16[4,128,128]{2,1,0:T(8,128)(2,1)}, bf16[4,128,128]{2,1,0:T(8,128)(2,1)S(1)}, u32[]{:S(2)}) copy-start(bf16[4,128,128]{2,1,0:T(8,128)(2,1)S(1)} %gather_fusion.6) | copy-start | bytes 393220
  350.3 101.4 %copy-start.48 = (bf16[4,128,128]{2,1,0:T(8,128)(2,1)}, bf16[4,128,128]{2,1,0:T(8,128)(2,1)S(1)}, u32[]{:S(2)}) copy-start(bf16[4,128,128]{2,1,0:T(8,128)(2,1)S(1)} %gather_fusion.8) | copy-start | bytes 393220
  413.1 40.3 %copy-start.47 = (bf16[4,128,128]{2,1,0:T(8,128)(2,1)}, bf16[4,128,128]{2,1,0:T(8,128)(2,1)S(1)}, u32[]{:S(2)}) copy-start(bf16[4,128,128]{2,1,0:T(8,128)(2,1)S(1)} %gather_fusion.10) | copy-start | bytes 393220
  453.4 40.0 %copy-start.42 = (f32[1,1,128,1024]{3,2,1,0:T(8,128)S(1)}, f32[1,1,128,1024]{3,2,1,0:T(8,128)}, u32[]{:S(2)}) copy-start(f32[1,1,128,1024]{3,2,1,0:T(8,128)} %get-tuple-element.15) | copy-start | bytes 1572868
  453.8 44.8 %copy-start.41 = (f32[1,1,128,1024]{3,2,1,0:T(8,128)S(1)}, f32[1,1,128,1024]{3,2,1,0:T(8,128)}, u32[]{:S(2)}) copy-start(f32[1,1,128,1024]{3,2,1,0:T(8,128)} %get-tuple-element.14) | copy-start | bytes 1572868
  494.4 7.0 copy-start.63
  498.6 5.7 copy-start.60
  499.6 5.7 copy-start.82
  499.6 5.8 copy-start.88
  509.2 9.0 collective-permute-start.1
  514.4 229.6 %reduce-scatter.19.cloned.1.call-start = ((), (), s32[]{:S(2)}) async-start(), calls=%async_computation.16 | async-start | bytes 1114112 | tf_op jit(solution)/shard_map/reduce_scatter | solution.py:101
  523.0 8.6 collective-permute-start.2
  528.2 215.8 %reduce-scatter.21.cloned.1.call-start = ((), (), s32[]{:S(2)}) async-start(), calls=%async_computation.17 | async-start | bytes 1114112 | tf_op jit(solution)/shard_map/reduce_scatter | solution.py:101
  536.4 19.6 %collective-permute-start.3 = (bf16[128,1024]{0,1:T(8,128)(2,1)}, bf16[128,1024]{0,1:T(8,128)(2,1)}, u32[]{:S(2)}, u32[]{:S(2)}) collective-permute-start(bf16[128,1024]{0,1:T(8,128)(2,1)} %get-tuple-element.75), channel_id=1, source_target_pairs={{128,0},{256,128},{384,256},{129,1},{257,129},{385,257},{130,2},{2... | collective-permute-start | bytes 786440 | tf_op jit(solution)/shard_map/ppermute | solution.py:14
  541.6 7.4 copy-start.39
  541.6 255.1 %reduce-scatter.23.cloned.1.call-start = ((), (), s32[]{:S(2)}) async-start(), calls=%async_computation.18 | async-start | bytes 1114112 | tf_op jit(solution)/shard_map/reduce_scatter | solution.py:101
  545.5 7.0 copy-start.62
  550.0 7.0 copy-start.83
  550.0 7.0 copy-start.100
  566.2 11.0 copy-start.59
  566.2 301.4 %reduce-scatter.25.cloned.1.call-start = ((), (), s32[]{:S(2)}) async-start(), calls=%async_computation.19 | async-start | bytes 1114112 | tf_op jit(solution)/shard_map/reduce_scatter | solution.py:101
  566.3 11.0 copy-start.80
  566.3 11.0 copy-start.98
  568.4 8.9 collective-permute-start.4
  586.5 34.6 %copy-start.61 = (bf16[1,128,1024]{2,1,0:T(8,128)(2,1)S(1)}, bf16[1,128,1024]{2,1,0:T(8,128)(2,1)}, u32[]{:S(2)}) copy-start(bf16[1,128,1024]{2,1,0:T(8,128)(2,1)} %get-tuple-element.26) | copy-start | bytes 786436
  586.5 352.0 %reduce-scatter.27.cloned.1.call-start = ((), (), s32[]{:S(2)}) async-start(), calls=%async_computation.20 | async-start | bytes 1114112 | tf_op jit(solution)/shard_map/reduce_scatter | solution.py:101
  588.7 35.5 %collective-permute-start.5 = (bf16[128,1024]{0,1:T(8,128)(2,1)}, bf16[128,1024]{0,1:T(8,128)(2,1)}, u32[]{:S(2)}, u32[]{:S(2)}) collective-permute-start(bf16[128,1024]{0,1:T(8,128)(2,1)} %get-tuple-element.87), channel_id=1, source_target_pairs={{128,0},{256,128},{384,256},{129,1},{257,129},{385,257},{130,2},{2... | collective-permute-start | bytes 786440 | tf_op jit(solution)/shard_map/ppermute | solution.py:14
  631.5 378.2 %reduce-scatter.29.cloned.1.call-start = ((), (), s32[]{:S(2)}) async-start(), calls=%async_computation.21 | async-start | bytes 1114112 | tf_op jit(solution)/shard_map/reduce_scatter | solution.py:107
  638.4 442.4 %reduce-scatter.31.cloned.1.call-start = ((), (), s32[]{:S(2)}) async-start(), calls=%async_computation.22 | async-start | bytes 1114112 | tf_op jit(solution)/shard_map/reduce_scatter | solution.py:107
  640.4 5.0 copy-start.87
  645.2 506.6 %reduce-scatter.33.cloned.1.call-start = ((), (), s32[]{:S(2)}) async-start(), calls=%async_computation.23 | async-start | bytes 1114112 | tf_op jit(solution)/shard_map/reduce_scatter | solution.py:107
  647.5 4.8 copy-start.85
  652.2 570.4 %reduce-scatter.35.cloned.1.call-start = ((), (), s32[]{:S(2)}) async-start(), calls=%async_computation.24 | async-start | bytes 1114112 | tf_op jit(solution)/shard_map/reduce_scatter | solution.py:107
  654.3 4.8 copy-start.102
  659.0 634.6 %reduce-scatter.37.cloned.1.call-start = ((), (), s32[]{:S(2)}) async-start(), calls=%async_computation.25 | async-start | bytes 1114112 | tf_op jit(solution)/shard_map/reduce_scatter | solution.py:107
  665.8 698.7 %reduce-scatter.39.cloned.1.call-start = ((), (), s32[]{:S(2)}) async-start(), calls=%async_computation.26 | async-start | bytes 1114112 | tf_op jit(solution)/shard_map/reduce_scatter | solution.py:107
  666.7 4.8 copy-start.8
  666.7 4.8 copy-start.93
  666.7 4.8 copy-start.104
  671.5 764.1 %reduce-scatter.41.cloned.1.call-start = ((), (), s32[]{:S(2)}) async-start(), calls=%async_computation.27 | async-start | bytes 1114112 | tf_op jit(solution)/shard_map/reduce_scatter | solution.py:107
  678.8 760.0 %copy-start.1 = (s32[16,4]{0,1:T(4,128)S(1)}, s32[16,4]{0,1:T(4,128)}, u32[]{:S(2)}) copy-start(s32[16,4]{0,1:T(4,128)} %param.11) | copy-start | bytes 772
  (73 other events, 154.5 us)
Sparse Core Ops, SparseCore 0:
  127.5 68.3 reduce-scatter.14
  514.5 68.8 reduce-scatter.16
  586.2 68.1 reduce-scatter.18
  657.3 68.4 reduce-scatter.20
  728.4 68.1 reduce-scatter.22
  799.6 68.0 reduce-scatter.24
  870.5 68.0 reduce-scatter.26
  941.6 68.1 reduce-scatter.28
  1012.6 68.1 reduce-scatter.30
  1083.6 68.0 reduce-scatter.32
  1154.5 68.0 reduce-scatter.34
  1225.5 68.0 reduce-scatter.36
  1296.4 68.0 reduce-scatter.38
  1367.5 68.0 reduce-scatter.40

commit v2 on v1

v2 whole, which is shorter than its diff:
```python
import math

import jax
import jax.numpy as jnp
from jax import lax
from jax.sharding import PartitionSpec as P

HEAD_FEATURES = 128


def passed_along(block, axis, distance):
    devices = range(lax.axis_size(axis))
    route = [(i - distance, i) for i in devices if i - distance in devices]
    return lax.ppermute(block, axis, route)


def cyclic_shift(block, axis, distance):
    count = lax.axis_size(axis)
    return lax.ppermute(block, axis, [(i, (i + distance) % count) for i in range(count)])


def checked_pairs(pairs):
    pairs = sorted(set(pairs))
    assert len({a for a, _ in pairs}) == len(pairs)
    assert len({b for _, b in pairs}) == len(pairs)
    return pairs


def forward_pairs(count, hop):
    spread = [(m, m + hop) for m in range(0, count, 2 * hop)]
    to_last = [(c - hop, c) for c in range(count - hop, count)]
    to_first = [(c + hop, c) for c in range(hop)]
    return checked_pairs(spread + to_last + to_first)


def reverse_pairs(count, hop):
    gather = [(m + hop, m) for m in range(0, count, 2 * hop)]
    from_last = [(c, c - hop) for c in range(count - hop, count)]
    from_first = [(c, c + hop) for c in range(hop)]
    return checked_pairs(gather + from_last + from_first)


def shards(query_input, key_states, value_states, query_gain, top_grad, block_lists):
    ctx_count = lax.axis_size("ctx")
    section_count = lax.axis_size("section")
    section_pos = lax.axis_index("section")
    ctx_pos = lax.axis_index("ctx")
    layer_input = query_input[0, 0]
    tok_local, feature_count = layer_input.shape
    kv_width = key_states.shape[-1]
    kv_heads = kv_width // HEAD_FEATURES
    head_count = feature_count // HEAD_FEATURES
    group_width = head_count // kv_heads
    group_features = group_width * HEAD_FEATURES
    block_count, listed = block_lists.shape
    block_rows = tok_local
    assert block_count == ctx_count and listed == 4
    hops = []
    hop = ctx_count // 2
    while hop >= 1:
        hops.append(hop)
        hop //= 2
    assert 2 * hops[0] == ctx_count
    scale_factor = 1.0 / math.sqrt(HEAD_FEATURES)
    turn_count = kv_heads + section_count - 1
    last = ctx_count - 1

    first_row = block_lists[0]
    first_extra = jnp.sum(
        jnp.where((first_row != last) & (first_row != 0) & (first_row != 1), first_row, 0)
    )
    last_row = block_lists[last]
    last_extra = jnp.sum(
        jnp.where((last_row != last - 1) & (last_row != last) & (last_row != 0), last_row, 0)
    )
    to_first_shift = first_extra
    to_last_shift = (last - last_extra) % ctx_count

    def bit_of(value, hop):
        return (value // hop) % 2 == 1

    is_first = ctx_pos == 0
    is_last = ctx_pos == last
    is_second = ctx_pos == 1
    uses_spread = ~(is_first | is_last | is_second)

    gain_row = lax.all_gather(query_gain[0], "ctx", tiled=True)
    query_rows = (layer_input.astype(jnp.float32) * gain_row).astype(jnp.bfloat16)
    own_top = top_grad[0]
    own_kv = jnp.stack([key_states[0, 0], value_states[0, 0]])
    on_top = section_pos == section_count - 1
    lag = section_count - 1 - section_pos

    def group_cols(array, group, width):
        return lax.dynamic_slice_in_dim(array, group * width, width, array.ndim - 1)

    def fetch_pool(group):
        own = group_cols(own_kv, group, HEAD_FEATURES)
        prev_blk = cyclic_shift(own, "ctx", 1)
        next_blk = cyclic_shift(own, "ctx", -1)
        second_blk = lax.ppermute(own, "ctx", [(last, 1)])
        lanes = jnp.stack([own, own, own])
        for hop in hops:
            got = lax.ppermute(lanes, "ctx", forward_pairs(ctx_count, hop))
            spread_lane = jnp.where(ctx_pos % (2 * hop) == hop, got[0], lanes[0])
            first_lane = jnp.where(
                (ctx_pos < hop) & bit_of(to_first_shift, hop), got[1], lanes[1]
            )
            last_lane = jnp.where(
                (ctx_pos >= ctx_count - hop) & bit_of(to_last_shift, hop), got[2], lanes[2]
            )
            lanes = jnp.stack([spread_lane, first_lane, last_lane])
        extra = jnp.where(
            is_first, lanes[1], jnp.where(is_last, lanes[2], jnp.where(is_second, second_blk, lanes[0]))
        )
        return jnp.stack([prev_blk, own, next_blk, extra], axis=1)

    def return_parts(parts):
        prev_part, own_part, next_part, extra_part = parts[:, 0], parts[:, 1], parts[:, 2], parts[:, 3]
        total = own_part + cyclic_shift(prev_part, "ctx", -1) + cyclic_shift(next_part, "ctx", 1)
        total = total + lax.ppermute(extra_part, "ctx", [(1, last)])
        zero = jnp.zeros_like(extra_part)
        lanes = jnp.stack(
            [
                jnp.where(uses_spread, extra_part, zero),
                jnp.where(is_first, extra_part, zero),
                jnp.where(is_last, extra_part, zero),
            ]
        )
        for hop in reversed(hops):
            got = lax.ppermute(lanes, "ctx", reverse_pairs(ctx_count, hop))
            spread_lane = jnp.where(ctx_pos % (2 * hop) == 0, lanes[0] + got[0], lanes[0])
            first_lane = jnp.where(
                bit_of(to_first_shift, hop),
                jnp.where((ctx_pos >= hop) & (ctx_pos < 2 * hop), got[1], zero),
                lanes[1],
            )
            last_lane = jnp.where(
                bit_of(to_last_shift, hop),
                jnp.where(
                    (ctx_pos >= ctx_count - 2 * hop) & (ctx_pos < ctx_count - hop), got[2], zero
                ),
                lanes[2],
            )
            lanes = jnp.stack([spread_lane, first_lane, last_lane])
        return total + jnp.where(is_first, lanes[0], zero) + lanes[1] + lanes[2]

    def attend(group, head_grad):
        pool = fetch_pool(group)
        neighbor_keys = pool[0].reshape(listed * block_rows, HEAD_FEATURES)
        neighbor_values = pool[1].reshape(listed * block_rows, HEAD_FEATURES)
        query_now = group_cols(query_rows, group, group_features).reshape(
            tok_local, group_width, HEAD_FEATURES
        )
        input_now = group_cols(layer_input, group, group_features)
        gain_now = lax.dynamic_slice_in_dim(gain_row, group * group_features, group_features, 0)
        grad_now = head_grad.reshape(tok_local, group_width, HEAD_FEATURES)
        scores = (
            jnp.einsum("bhd,jd->hbj", query_now, neighbor_keys, preferred_element_type=jnp.float32)
            * scale_factor
        )
        row_max = jnp.max(scores, axis=-1, keepdims=True)
        weights = jnp.exp(scores - row_max)
        probs = weights / jnp.sum(weights, axis=-1, keepdims=True)
        probs_low = probs.astype(jnp.bfloat16)
        prob_grad = jnp.einsum(
            "bhd,jd->hbj", grad_now, neighbor_values, preferred_element_type=jnp.float32
        )
        row_dot = jnp.sum(probs * prob_grad, axis=-1, keepdims=True)
        score_grad = (probs * (prob_grad - row_dot)).astype(jnp.bfloat16)
        query_grad = (
            jnp.einsum("hbj,jd->bhd", score_grad, neighbor_keys, preferred_element_type=jnp.float32)
            * scale_factor
        ).reshape(tok_local, group_features)
        key_part = (
            jnp.einsum("hbj,bhd->jd", score_grad, query_now, preferred_element_type=jnp.float32)
            * scale_factor
        )
        value_part = jnp.einsum(
            "hbj,bhd->jd", probs_low, grad_now, preferred_element_type=jnp.float32
        )
        moved_grad = (gain_now * query_grad).astype(jnp.bfloat16)
        handed = (head_grad.astype(jnp.float32) + moved_grad.astype(jnp.float32)).astype(
            jnp.bfloat16
        )
        gain_part = jnp.sum(input_now.astype(jnp.float32) * query_grad, axis=0)
        parts = jnp.stack([key_part, value_part]).reshape(2, listed, block_rows, HEAD_FEATURES)
        return handed, return_parts(parts), gain_part

    incoming = jnp.zeros((tok_local, group_features), jnp.bfloat16)
    handed_turns, kv_turns, gain_turns = [], [], []
    for turn in range(turn_count):
        group = jnp.clip(turn - lag, 0, kv_heads - 1)
        from_top = group_cols(own_top, group, group_features)
        head_grad = jnp.where(on_top, from_top, incoming)
        handed, kv_own, gain_part = attend(group, head_grad)
        handed_turns.append(handed)
        kv_turns.append(kv_own)
        gain_turns.append(gain_part)
        if turn + 1 < turn_count:
            incoming = passed_along(handed, "section", -1)

    def own_turns(parts):
        stacked = jnp.stack(parts)
        return lax.dynamic_slice_in_dim(stacked, lag, kv_heads, 0)

    stream_out = own_turns(handed_turns).transpose(1, 0, 2).reshape(tok_local, feature_count)
    kv_out = own_turns(kv_turns).transpose(1, 2, 0, 3).reshape(2, tok_local, kv_width)
    kv_out = kv_out.astype(jnp.bfloat16)
    gain_full = own_turns(gain_turns).reshape(feature_count)
    gain_total = lax.psum(
        lax.psum_scatter(gain_full, "ctx", scatter_dimension=0, tiled=True), "dp"
    )
    return (stream_out[None, None], kv_out[0][None, None], kv_out[1][None, None], gain_total[None])


def solution(mesh):
    placed = (
        P("section", "dp", "ctx", None),
        P("section", "dp", "ctx", None),
        P("section", "dp", "ctx", None),
        P("section", "ctx"),
        P("dp", "ctx", None),
        P(),
    )
    return jax.shard_map(
        shards,
        mesh=mesh,
        in_specs=placed,
        out_specs=(
            P("section", "dp", "ctx", None),
            P("section", "dp", "ctx", None),
            P("section", "dp", "ctx", None),
            P("section", "ctx"),
        ),
        check_vma=False,
    )
```

time: 1450 us -> 1320 us (0.910)
  starting transfers between devices: 8.64 us -> 625 us
  blocking collectives: 539 us -> 98.6 us
  waiting for transfers between devices: 698 us -> 380 us
  other arithmetic: 73 us -> 92.1 us
    reduce_scatter x14 -> x0, waiting for transfers between devices: 690 us -> none  [the longest x7 495 us: attend(): lax.psum_scatter(value_blocks.reshape(block_count * block_rows, HEAD_FEAT...]
    ppermute x0 -> x98, starting transfers between devices: none -> 617 us  [the longest x28 320 us: return_parts(): got = lax.ppermute(lanes, 'ctx', reverse_pairs(ctx_count, hop))]
    all_gather x14 -> x0, blocking collectives: 449 us -> none  [the longest x7 226 us: attend(): lax.all_gather(group_cols(own_keys, group, HEAD_FEATURES), 'ctx', tiled=T...]
    ppermute x0 -> x98, waiting for transfers between devices: none -> 360 us  [the longest x28 261 us: fetch_pool(): got = lax.ppermute(lanes, 'ctx', forward_pairs(ctx_count, hop))]
    another operation x0 -> x80, other arithmetic: none -> 29.7 us  [the longest x21 8.62 us: return_parts(): lanes = jnp.stack([spread_lane, first_lane, last_lane])]
    scatter-add x14 -> x0, other arithmetic: 28.7 us -> none  [the longest x7 15.6 us: attend(): value_blocks = jnp.zeros((block_count, block_rows, HEAD_FEATURES), jnp.fl...]
    select_n x1 -> x43, other arithmetic: 0.01 us -> 21.9 us  [the longest x21 10.4 us: return_parts(): jnp.where(ctx_pos % (2 * hop) == 0, lanes[0] + got[0], lanes[0])]
    gather x14 -> x0, local copies, waits for them, and re-layouts: 19.5 us -> none  [the longest x7 13.3 us: attend(): values_now.reshape(block_count, block_rows, HEAD_FEATURES)[own_list]]
  transfers between devices with their start and end apart: 20 -> 104, of which waited for: 13 -> 32; matrix products, arithmetic and copies ran while one was open for 10% -> 14% of each run, Pallas kernels for 0% -> 0%
where the time goes in v2:
time: 1320 us; the launch traced here: 1300 us
  starting transfers between devices  625 us (47%)
  waiting for transfers between devices  380 us (29%)
  blocking collectives  98.6 us (7%)
  other arithmetic  92.1 us (7%)
  local copies, waits for them, and re-layouts  63.6 us (5%)
  matrix products  32.8 us (2%)
    ppermute x28, starting transfers between devices, return_parts(): got = lax.ppermute(lanes, 'ctx', reverse_pairs(ctx_count, hop))  320 us
    ppermute x28, waiting for transfers between devices, fetch_pool(): got = lax.ppermute(lanes, 'ctx', forward_pairs(ctx_count, hop))  261 us
    ppermute x28, starting transfers between devices, cyclic_shift(): lax.ppermute(block, axis, [(i, (i + distance) % count) for i in range(cou...  192 us
    ppermute x28, starting transfers between devices, fetch_pool(): got = lax.ppermute(lanes, 'ctx', forward_pairs(ctx_count, hop))  93.5 us
    ppermute x28, waiting for transfers between devices, return_parts(): got = lax.ppermute(lanes, 'ctx', reverse_pairs(ctx_count, hop))  67 us
    unnamed x1, blocking collectives  52.7 us
    all_gather x1, blocking collectives, shards(): gain_row = lax.all_gather(query_gain[0], 'ctx', tiled=True)  35.3 us
    ppermute x28, waiting for transfers between devices, cyclic_shift(): lax.ppermute(block, axis, [(i, (i + distance) % count) for i in range(cou...  31.4 us
  transfers between devices with their start and end apart: 104, of which 32 were waited for; matrix products, arithmetic and copies ran while one was open for 14% of the time, Pallas kernels for 0%

profile of v2, /device:TPU:6, one launch (start us, length us, event | category | flops | bytes accessed | tf_op | source)
XLA Modules:
  0.0 1302.9 jit_solution(1142133523175414043)
XLA Ops:
  4.1 12.0 collective-permute-start.1
  18.8 7.6 collective-permute-start.2
  30.3 35.3 %all-gather = f32[1,4096]{1,0:T(1,128)S(1)} all-gather(f32[1,256]{1,0:T(1,128)S(1)} %copy-done.283), channel_id=2, replica_groups=mesh['section'=4,'ctx'=16,'dp'=8] {'ctx'}, dimensions={1}, use_global_device_ids=true | all-gather | bytes 17408 | tf_op jit(solution)/shard_map/all_gather | solution.py:87
  99.1 7.4 collective-permute-start.10
  107.5 13.9 %collective-permute-done.10 = bf16[3,2,128,128]{2,3,1,0:T(8,128)(2,1)S(1)} collective-permute-done((bf16[3,2,128,128]{2,3,1,0:T(8,128)(2,1)S(1)}, bf16[3,2,128,128]{2,3,1,0:T(8,128)(2,1)S(1)}, u32[]{:S(2)}, u32[]{:S(2)}) %collective-permute-start.10) | collective-permute-done | bytes 196640 | tf_op jit(solution)/shard_map/ppermute | solution.py:104
  121.5 7.1 collective-permute-start.18
  128.6 13.5 %collective-permute-done.18 = bf16[3,2,128,128]{2,3,1,0:T(8,128)(2,1)S(1)} collective-permute-done((bf16[3,2,128,128]{2,3,1,0:T(8,128)(2,1)S(1)}, bf16[3,2,128,128]{2,3,1,0:T(8,128)(2,1)S(1)}, u32[]{:S(2)}, u32[]{:S(2)}) %collective-permute-start.18) | collective-permute-done | bytes 196640 | tf_op jit(solution)/shard_map/ppermute | solution.py:104
  142.2 7.5 collective-permute-start.26
  149.8 14.1 %collective-permute-done.26 = bf16[3,2,128,128]{2,3,1,0:T(8,128)(2,1)S(1)} collective-permute-done((bf16[3,2,128,128]{2,3,1,0:T(8,128)(2,1)S(1)}, bf16[3,2,128,128]{2,3,1,0:T(8,128)(2,1)S(1)}, u32[]{:S(2)}, u32[]{:S(2)}) %collective-permute-start.26) | collective-permute-done | bytes 196640 | tf_op jit(solution)/shard_map/ppermute | solution.py:104
  164.0 7.1 collective-permute-start.34
  171.1 14.2 %collective-permute-done.34 = bf16[3,2,128,128]{2,3,1,0:T(8,128)(2,1)S(1)} collective-permute-done((bf16[3,2,128,128]{2,3,1,0:T(8,128)(2,1)S(1)}, bf16[3,2,128,128]{2,3,1,0:T(8,128)(2,1)S(1)}, u32[]{:S(2)}, u32[]{:S(2)}) %collective-permute-start.34) | collective-permute-done | bytes 196640 | tf_op jit(solution)/shard_map/ppermute | solution.py:104
  186.2 7.5 collective-permute-start.42
  193.7 13.4 %collective-permute-done.42 = bf16[3,2,128,128]{2,3,1,0:T(8,128)(2,1)S(1)} collective-permute-done((bf16[3,2,128,128]{2,3,1,0:T(8,128)(2,1)S(1)}, bf16[3,2,128,128]{2,3,1,0:T(8,128)(2,1)S(1)}, u32[]{:S(2)}, u32[]{:S(2)}) %collective-permute-start.42) | collective-permute-done | bytes 196640 | tf_op jit(solution)/shard_map/ppermute | solution.py:104
  208.0 7.1 collective-permute-start.50
  215.2 13.4 %collective-permute-done.50 = bf16[3,2,128,128]{2,3,1,0:T(8,128)(2,1)S(1)} collective-permute-done((bf16[3,2,128,128]{2,3,1,0:T(8,128)(2,1)S(1)}, bf16[3,2,128,128]{2,3,1,0:T(8,128)(2,1)S(1)}, u32[]{:S(2)}, u32[]{:S(2)}) %collective-permute-start.50) | collective-permute-done | bytes 196640 | tf_op jit(solution)/shard_map/ppermute | solution.py:104
  231.5 50.7 %collective-permute-done.3 = bf16[3,2,128,128]{2,3,1,0:T(8,128)(2,1)S(1)} collective-permute-done((bf16[3,2,128,128]{2,3,1,0:T(8,128)(2,1)S(1)}, bf16[3,2,128,128]{2,3,1,0:T(8,128)(2,1)S(1)}, u32[]{:S(2)}, u32[]{:S(2)}) %collective-permute-start.3) | collective-permute-done | bytes 196640 | tf_op jit(solution)/shard_map/ppermute | solution.py:104
  285.0 29.1 %collective-permute-done.11 = bf16[3,2,128,128]{2,3,1,0:T(8,128)(2,1)S(1)} collective-permute-done((bf16[3,2,128,128]{2,3,1,0:T(8,128)(2,1)S(1)}, bf16[3,2,128,128]{2,3,1,0:T(8,128)(2,1)S(1)}, u32[]{:S(2)}, u32[]{:S(2)}) %collective-permute-start.11) | collective-permute-done | bytes 196640 | tf_op jit(solution)/shard_map/ppermute | solution.py:104
  316.2 13.9 %collective-permute-done.19 = bf16[3,2,128,128]{2,3,1,0:T(8,128)(2,1)S(1)} collective-permute-done((bf16[3,2,128,128]{2,3,1,0:T(8,128)(2,1)S(1)}, bf16[3,2,128,128]{2,3,1,0:T(8,128)(2,1)S(1)}, u32[]{:S(2)}, u32[]{:S(2)}) %collective-permute-start.19) | collective-permute-done | bytes 196640 | tf_op jit(solution)/shard_map/ppermute | solution.py:104
  332.1 10.7 collective-permute-done.27
  344.9 9.6 collective-permute-done.35
  357.1 9.0 collective-permute-done.43
  368.5 9.1 collective-permute-done.51
  380.5 5.6 collective-permute-done.4
  388.1 7.5 collective-permute-done.12
  397.6 8.8 collective-permute-done.20
  416.9 6.6 collective-permute-done.36
  426.8 6.4 collective-permute-done.44
  435.1 6.6 collective-permute-done.52
  445.1 8.4 collective-permute-start.9
  464.8 6.7 collective-permute-start.17
  480.3 5.8 collective-permute-start.25
  494.4 5.8 collective-permute-start.33
  508.4 5.8 collective-permute-start.41
  524.7 5.3 collective-permute-start.49
  550.8 6.5 collective-permute-start.56
  619.7 6.2 collective-permute-done.23
  664.8 5.5 collective-permute-start.79
  673.3 7.0 collective-permute-done.79
  703.5 5.1 collective-permute-start.86
  711.5 11.7 collective-permute-done.67
  723.2 13.7 %collective-permute-start.61 = (f32[3,2,128,128]{2,3,1,0:T(8,128)}, f32[3,2,128,128]{2,3,1,0:T(8,128)}, u32[]{:S(2)}, u32[]{:S(2)}) collective-permute-start(f32[3,2,128,128]{2,3,1,0:T(8,128)} %pad_maximum_fusion.3), channel_id=1, source_target_pairs={{0,64},{8,72},{16,80},{24,88},{32,96},{40,104},{48,112},{56,120},{... | collective-permute-start | bytes 1179656 | tf_op jit(solution)/shard_map/ppermute | solution.py:131
  741.2 5.2 collective-permute-done.47
  746.4 22.3 %collective-permute-start.80 = (f32[3,2,128,128]{2,3,1,0:T(8,128)}, f32[3,2,128,128]{2,3,1,0:T(8,128)}, u32[]{:S(2)}, u32[]{:S(2)}) collective-permute-start(f32[3,2,128,128]{2,3,1,0:T(8,128)} %pad_maximum_fusion.13), channel_id=1, source_target_pairs={{0,16},{8,24},{16,0},{48,32},{80,64},{112,96},{120,104},{1,17},{9,... | collective-permute-start | bytes 1179656 | tf_op jit(solution)/shard_map/ppermute | solution.py:131
  778.0 52.7 %all-reduce = f32[4096]{0:T(1024)S(1)} all-reduce(f32[4096]{0:T(1024)S(1)} %bitcast.1926), channel_id=3, replica_groups=mesh['section'=4,'ctx'=16,'dp'=8] {'ctx'}, use_global_device_ids=true, to_apply=%region_30.31.clone | all-reduce | flops 4096 | bytes 32768
  832.1 10.7 psum.7
  844.4 5.3 collective-permute-start.63
  860.5 7.8 collective-permute-done.74
  868.3 29.3 %collective-permute-start.68 = (f32[3,2,128,128]{2,3,1,0:T(8,128)S(1)}, f32[3,2,128,128]{2,3,1,0:T(8,128)S(1)}, u32[]{:S(2)}, u32[]{:S(2)}) collective-permute-start(f32[3,2,128,128]{2,3,1,0:T(8,128)S(1)} %copy-done.232), channel_id=1, source_target_pairs={{0,64},{8,72},{16,80},{24,88},{32,96},{40,104},{48,112},{56,120},{... | collective-permute-start | bytes 1179656 | tf_op jit(solution)/shard_map/ppermute | solution.py:131
  900.0 31.4 %collective-permute-done.87 = f32[3,2,128,128]{2,3,1,0:T(8,128)S(1)} collective-permute-done((f32[3,2,128,128]{2,3,1,0:T(8,128)S(1)}, f32[3,2,128,128]{2,3,1,0:T(8,128)S(1)}, u32[]{:S(2)}, u32[]{:S(2)}) %collective-permute-start.87) | collective-permute-done | bytes 393248 | tf_op jit(solution)/shard_map/ppermute | solution.py:131
  931.3 11.5 collective-permute-start.100
  943.6 5.6 collective-permute-start.70
  958.1 9.2 collective-permute-done.81
  967.3 27.7 %collective-permute-start.75 = (f32[3,2,128,128]{2,3,1,0:T(8,128)S(1)}, f32[3,2,128,128]{2,3,1,0:T(8,128)S(1)}, u32[]{:S(2)}, u32[]{:S(2)}) collective-permute-start(f32[3,2,128,128]{2,3,1,0:T(8,128)S(1)} %pad_maximum_fusion.11), channel_id=1, source_target_pairs={{0,64},{8,72},{16,80},{24,88},{32,96},{40,104},{48,112},{56,120},{... | collective-permute-start | bytes 1179656 | tf_op jit(solution)/shard_map/ppermute | solution.py:131
  997.8 48.4 %collective-permute-start.77 = (f32[2,128,128]{1,2,0:T(8,128)S(1)}, f32[2,128,128]{1,2,0:T(8,128)S(1)}, u32[]{:S(2)}, u32[]{:S(2)}) collective-permute-start(f32[2,128,128]{1,2,0:T(8,128)S(1)} %copy-done.247), channel_id=1, source_target_pairs={{0,8},{8,16},{16,24},{24,32},{32,40},{40,48},{48,56},{56,64},{64,7... | collective-permute-start | bytes 393224 | tf_op jit(solution)/shard_map/ppermute | solution.py:19
  1053.1 29.2 %collective-permute-start.82 = (f32[3,2,128,128]{2,3,1,0:T(8,128)S(1)}, f32[3,2,128,128]{2,3,1,0:T(8,128)S(1)}, u32[]{:S(2)}, u32[]{:S(2)}) collective-permute-start(f32[3,2,128,128]{2,3,1,0:T(8,128)S(1)} %pad_maximum_fusion.15), channel_id=1, source_target_pairs={{0,64},{8,72},{16,80},{24,88},{32,96},{40,104},{48,112},{56,120},{... | collective-permute-start | bytes 1179656 | tf_op jit(solution)/shard_map/ppermute | solution.py:131
  1085.1 28.5 %collective-permute-start.84 = (f32[2,128,128]{1,2,0:T(8,128)S(1)}, f32[2,128,128]{1,2,0:T(8,128)S(1)}, u32[]{:S(2)}, u32[]{:S(2)}) collective-permute-start(f32[2,128,128]{1,2,0:T(8,128)S(1)} %copy-done.249), channel_id=1, source_target_pairs={{0,8},{8,16},{16,24},{24,32},{32,40},{40,48},{48,56},{56,64},{64,7... | collective-permute-start | bytes 393224 | tf_op jit(solution)/shard_map/ppermute | solution.py:19
  1115.6 6.8 collective-permute-start.102
  1123.7 79.9 %collective-permute-start.89 = (f32[3,2,128,128]{2,3,1,0:T(8,128)S(1)}, f32[3,2,128,128]{2,3,1,0:T(8,128)S(1)}, u32[]{:S(2)}, u32[]{:S(2)}) collective-permute-start(f32[3,2,128,128]{2,3,1,0:T(8,128)S(1)} %pad_maximum_fusion.19), channel_id=1, source_target_pairs={{0,64},{8,72},{16,80},{24,88},{32,96},{40,104},{48,112},{56,120},{... | collective-permute-start | bytes 1179656 | tf_op jit(solution)/shard_map/ppermute | solution.py:131
  1203.8 44.2 %collective-permute-start.96 = (f32[3,2,128,128]{2,3,1,0:T(8,128)S(1)}, f32[3,2,128,128]{2,3,1,0:T(8,128)S(1)}, u32[]{:S(2)}, u32[]{:S(2)}) collective-permute-start(f32[3,2,128,128]{2,3,1,0:T(8,128)S(1)} %pad_maximum_fusion.23), channel_id=1, source_target_pairs={{0,64},{8,72},{16,80},{24,88},{32,96},{40,104},{48,112},{56,120},{... | collective-permute-start | bytes 1179656 | tf_op jit(solution)/shard_map/ppermute | solution.py:131
  1250.7 5.3 collective-permute-start.90
  1258.9 9.0 collective-permute-done.91
  1272.4 14.2 %collective-permute-done.90 = f32[2,128,128]{1,2,0:T(8,128)S(1)} collective-permute-done((f32[2,128,128]{1,2,0:T(8,128)S(1)}, f32[2,128,128]{1,2,0:T(8,128)S(1)}, u32[]{:S(2)}, u32[]{:S(2)}) %collective-permute-start.90) | collective-permute-done | bytes 131104 | tf_op jit(solution)/shard_map/ppermute | solution.py:19
  1286.7 5.8 collective-permute-start.97
  1292.8 8.1 collective-permute-done.97
  (987 shorter events, 346.4 us)
Async XLA Ops:
  3.5 441.6 %collective-permute-start.6 = (bf16[2,128,128]{1,2,0:T(8,128)(2,1)S(1)}, bf16[2,128,128]{1,2,0:T(8,128)(2,1)S(1)}, u32[]{:S(2)}, u32[]{:S(2)}) collective-permute-start(bf16[2,128,128]{1,2,0:T(8,128)(2,1)S(1)} %get-tuple-element.159), channel_id=1, source_target_pairs={{120,8},{121,9},{122,10},{123,11},{124,12},{125,13},{126,14},{127,... | collective-permute-start | bytes 196616 | tf_op jit(solution)/shard_map/ppermute | solution.py:101
  4.1 451.4 %collective-permute-start.1 = (bf16[2,128,128]{1,2,0:T(8,128)(2,1)S(1)}, bf16[2,128,128]{1,2,0:T(8,128)(2,1)}, u32[]{:S(2)}, u32[]{:S(2)}) collective-permute-start(bf16[2,128,128]{1,2,0:T(8,128)(2,1)S(1)} %get-tuple-element.159), channel_id=1, source_target_pairs={{0,120},{8,0},{16,8},{24,16},{32,24},{40,32},{48,40},{56,48},{64,5... | collective-permute-start | bytes 196616 | tf_op jit(solution)/shard_map/ppermute | solution.py:19
  16.2 440.6 %collective-permute-start = (bf16[2,128,128]{1,2,0:T(8,128)(2,1)S(1)}, bf16[2,128,128]{1,2,0:T(8,128)(2,1)}, u32[]{:S(2)}, u32[]{:S(2)}) collective-permute-start(bf16[2,128,128]{1,2,0:T(8,128)(2,1)S(1)} %get-tuple-element.159), channel_id=1, source_target_pairs={{0,8},{8,16},{16,24},{24,32},{32,40},{40,48},{48,56},{56,64},{64,7... | collective-permute-start | bytes 196616 | tf_op jit(solution)/shard_map/ppermute | solution.py:19
  18.8 80.3 %collective-permute-start.2 = (bf16[3,2,128,128]{2,3,1,0:T(8,128)(2,1)}, bf16[3,2,128,128]{2,3,1,0:T(8,128)(2,1)}, u32[]{:S(2)}, u32[]{:S(2)}) collective-permute-start(bf16[3,2,128,128]{2,3,1,0:T(8,128)(2,1)} %stack.693), channel_id=1, source_target_pairs={{0,64},{8,72},{16,80},{24,88},{32,96},{40,104},{48,112},{56,120},{... | collective-permute-start | bytes 589832 | tf_op jit(solution)/shard_map/ppermute | solution.py:104
  26.4 438.4 %collective-permute-start.14 = (bf16[2,128,128]{1,2,0:T(8,128)(2,1)S(1)}, bf16[2,128,128]{1,2,0:T(8,128)(2,1)}, u32[]{:S(2)}, u32[]{:S(2)}) collective-permute-start(bf16[2,128,128]{1,2,0:T(8,128)(2,1)S(1)} %get-tuple-element.160), channel_id=1, source_target_pairs={{120,8},{121,9},{122,10},{123,11},{124,12},{125,13},{126,14},{127,... | collective-permute-start | bytes 196616 | tf_op jit(solution)/shard_map/ppermute | solution.py:101
  99.1 22.3 %collective-permute-start.10 = (bf16[3,2,128,128]{2,3,1,0:T(8,128)(2,1)S(1)}, bf16[3,2,128,128]{2,3,1,0:T(8,128)(2,1)S(1)}, u32[]{:S(2)}, u32[]{:S(2)}) collective-permute-start(bf16[3,2,128,128]{2,3,1,0:T(8,128)(2,1)S(1)} %stack.711), channel_id=1, source_target_pairs={{0,64},{8,72},{16,80},{24,88},{32,96},{40,104},{48,112},{56,120},{... | collective-permute-start | bytes 589832 | tf_op jit(solution)/shard_map/ppermute | solution.py:104
  121.5 20.7 %collective-permute-start.18 = (bf16[3,2,128,128]{2,3,1,0:T(8,128)(2,1)S(1)}, bf16[3,2,128,128]{2,3,1,0:T(8,128)(2,1)S(1)}, u32[]{:S(2)}, u32[]{:S(2)}) collective-permute-start(bf16[3,2,128,128]{2,3,1,0:T(8,128)(2,1)S(1)} %stack.730), channel_id=1, source_target_pairs={{0,64},{8,72},{16,80},{24,88},{32,96},{40,104},{48,112},{56,120},{... | collective-permute-start | bytes 589832 | tf_op jit(solution)/shard_map/ppermute | solution.py:104
  142.2 21.8 %collective-permute-start.26 = (bf16[3,2,128,128]{2,3,1,0:T(8,128)(2,1)S(1)}, bf16[3,2,128,128]{2,3,1,0:T(8,128)(2,1)S(1)}, u32[]{:S(2)}, u32[]{:S(2)}) collective-permute-start(bf16[3,2,128,128]{2,3,1,0:T(8,128)(2,1)S(1)} %stack.749), channel_id=1, source_target_pairs={{0,64},{8,72},{16,80},{24,88},{32,96},{40,104},{48,112},{56,120},{... | collective-permute-start | bytes 589832 | tf_op jit(solution)/shard_map/ppermute | solution.py:104
  164.0 21.3 %collective-permute-start.34 = (bf16[3,2,128,128]{2,3,1,0:T(8,128)(2,1)S(1)}, bf16[3,2,128,128]{2,3,1,0:T(8,128)(2,1)S(1)}, u32[]{:S(2)}, u32[]{:S(2)}) collective-permute-start(bf16[3,2,128,128]{2,3,1,0:T(8,128)(2,1)S(1)} %stack.768), channel_id=1, source_target_pairs={{0,64},{8,72},{16,80},{24,88},{32,96},{40,104},{48,112},{56,120},{... | collective-permute-start | bytes 589832 | tf_op jit(solution)/shard_map/ppermute | solution.py:104
  186.2 21.0 %collective-permute-start.42 = (bf16[3,2,128,128]{2,3,1,0:T(8,128)(2,1)S(1)}, bf16[3,2,128,128]{2,3,1,0:T(8,128)(2,1)S(1)}, u32[]{:S(2)}, u32[]{:S(2)}) collective-permute-start(bf16[3,2,128,128]{2,3,1,0:T(8,128)(2,1)S(1)} %stack.787), channel_id=1, source_target_pairs={{0,64},{8,72},{16,80},{24,88},{32,96},{40,104},{48,112},{56,120},{... | collective-permute-start | bytes 589832 | tf_op jit(solution)/shard_map/ppermute | solution.py:104
  228.6 53.5 %collective-permute-start.3 = (bf16[3,2,128,128]{2,3,1,0:T(8,128)(2,1)S(1)}, bf16[3,2,128,128]{2,3,1,0:T(8,128)(2,1)S(1)}, u32[]{:S(2)}, u32[]{:S(2)}) collective-permute-start(bf16[3,2,128,128]{2,3,1,0:T(8,128)(2,1)S(1)} %pad_maximum_fusion.35), channel_id=1, source_target_pairs={{0,32},{32,0},{40,8},{48,16},{56,24},{64,96},{72,104},{80,112},{88... | collective-permute-start | bytes 589832 | tf_op jit(solution)/shard_map/ppermute | solution.py:104
  282.1 32.0 %collective-permute-start.11 = (bf16[3,2,128,128]{2,3,1,0:T(8,128)(2,1)S(1)}, bf16[3,2,128,128]{2,3,1,0:T(8,128)(2,1)S(1)}, u32[]{:S(2)}, u32[]{:S(2)}) collective-permute-start(bf16[3,2,128,128]{2,3,1,0:T(8,128)(2,1)S(1)} %pad_maximum_fusion.38), channel_id=1, source_target_pairs={{0,32},{32,0},{40,8},{48,16},{56,24},{64,96},{72,104},{80,112},{88... | collective-permute-start | bytes 589832 | tf_op jit(solution)/shard_map/ppermute | solution.py:104
  445.1 29.5 %collective-permute-start.9 = (bf16[2,128,128]{1,2,0:T(8,128)(2,1)S(1)}, bf16[2,128,128]{1,2,0:T(8,128)(2,1)}, u32[]{:S(2)}, u32[]{:S(2)}) collective-permute-start(bf16[2,128,128]{1,2,0:T(8,128)(2,1)S(1)} %get-tuple-element.160), channel_id=1, source_target_pairs={{0,120},{8,0},{16,8},{24,16},{32,24},{40,32},{48,40},{56,48},{64,5... | collective-permute-start | bytes 196616 | tf_op jit(solution)/shard_map/ppermute | solution.py:19
  453.6 25.1 %collective-permute-start.8 = (bf16[2,128,128]{1,2,0:T(8,128)(2,1)S(1)}, bf16[2,128,128]{1,2,0:T(8,128)(2,1)}, u32[]{:S(2)}, u32[]{:S(2)}) collective-permute-start(bf16[2,128,128]{1,2,0:T(8,128)(2,1)S(1)} %get-tuple-element.160), channel_id=1, source_target_pairs={{0,8},{8,16},{16,24},{24,32},{32,40},{40,48},{48,56},{56,64},{64,7... | collective-permute-start | bytes 196616 | tf_op jit(solution)/shard_map/ppermute | solution.py:19
  455.6 24.7 %collective-permute-start.22 = (bf16[2,128,128]{1,2,0:T(8,128)(2,1)S(1)}, bf16[2,128,128]{1,2,0:T(8,128)(2,1)}, u32[]{:S(2)}, u32[]{:S(2)}) collective-permute-start(bf16[2,128,128]{1,2,0:T(8,128)(2,1)S(1)} %get-tuple-element.161), channel_id=1, source_target_pairs={{120,8},{121,9},{122,10},{123,11},{124,12},{125,13},{126,14},{127,... | collective-permute-start | bytes 196616 | tf_op jit(solution)/shard_map/ppermute | solution.py:101
  464.8 24.0 %collective-permute-start.17 = (bf16[2,128,128]{1,2,0:T(8,128)(2,1)S(1)}, bf16[2,128,128]{1,2,0:T(8,128)(2,1)S(1)}, u32[]{:S(2)}, u32[]{:S(2)}) collective-permute-start(bf16[2,128,128]{1,2,0:T(8,128)(2,1)S(1)} %get-tuple-element.161), channel_id=1, source_target_pairs={{0,120},{8,0},{16,8},{24,16},{32,24},{40,32},{48,40},{56,48},{64,5... | collective-permute-start | bytes 196616 | tf_op jit(solution)/shard_map/ppermute | solution.py:19
  480.3 22.9 %collective-permute-start.25 = (bf16[2,128,128]{1,2,0:T(8,128)(2,1)S(1)}, bf16[2,128,128]{1,2,0:T(8,128)(2,1)S(1)}, u32[]{:S(2)}, u32[]{:S(2)}) collective-permute-start(bf16[2,128,128]{1,2,0:T(8,128)(2,1)S(1)} %get-tuple-element.162), channel_id=1, source_target_pairs={{0,120},{8,0},{16,8},{24,16},{32,24},{40,32},{48,40},{56,48},{64,5... | collective-permute-start | bytes 196616 | tf_op jit(solution)/shard_map/ppermute | solution.py:19
  494.4 22.7 %collective-permute-start.33 = (bf16[2,128,128]{1,2,0:T(8,128)(2,1)S(1)}, bf16[2,128,128]{1,2,0:T(8,128)(2,1)S(1)}, u32[]{:S(2)}, u32[]{:S(2)}) collective-permute-start(bf16[2,128,128]{1,2,0:T(8,128)(2,1)S(1)} %get-tuple-element.163), channel_id=1, source_target_pairs={{0,120},{8,0},{16,8},{24,16},{32,24},{40,32},{48,40},{56,48},{64,5... | collective-permute-start | bytes 196616 | tf_op jit(solution)/shard_map/ppermute | solution.py:19
  508.4 24.6 %collective-permute-start.41 = (bf16[2,128,128]{1,2,0:T(8,128)(2,1)}, bf16[2,128,128]{1,2,0:T(8,128)(2,1)}, u32[]{:S(2)}, u32[]{:S(2)}) collective-permute-start(bf16[2,128,128]{1,2,0:T(8,128)(2,1)} %fusion.283), channel_id=1, source_target_pairs={{0,120},{8,0},{16,8},{24,16},{32,24},{40,32},{48,40},{56,48},{64,5... | collective-permute-start | bytes 196616 | tf_op jit(solution)/shard_map/ppermute | solution.py:19
  514.3 21.5 %collective-permute-start.40 = (bf16[2,128,128]{1,2,0:T(8,128)(2,1)}, bf16[2,128,128]{1,2,0:T(8,128)(2,1)}, u32[]{:S(2)}, u32[]{:S(2)}) collective-permute-start(bf16[2,128,128]{1,2,0:T(8,128)(2,1)} %fusion.283), channel_id=1, source_target_pairs={{0,8},{8,16},{16,24},{24,32},{32,40},{40,48},{48,56},{56,64},{64,7... | collective-permute-start | bytes 196616 | tf_op jit(solution)/shard_map/ppermute | solution.py:19
  517.0 28.2 %collective-permute-start.54 = (bf16[2,128,128]{1,2,0:T(8,128)(2,1)}, bf16[2,128,128]{1,2,0:T(8,128)(2,1)}, u32[]{:S(2)}, u32[]{:S(2)}) collective-permute-start(bf16[2,128,128]{1,2,0:T(8,128)(2,1)} %get-tuple-element.158), channel_id=1, source_target_pairs={{120,8},{121,9},{122,10},{123,11},{124,12},{125,13},{126,14},{127,... | collective-permute-start | bytes 196616 | tf_op jit(solution)/shard_map/ppermute | solution.py:101
  524.7 22.3 %collective-permute-start.49 = (bf16[2,128,128]{1,2,0:T(8,128)(2,1)}, bf16[2,128,128]{1,2,0:T(8,128)(2,1)}, u32[]{:S(2)}, u32[]{:S(2)}) collective-permute-start(bf16[2,128,128]{1,2,0:T(8,128)(2,1)} %get-tuple-element.158), channel_id=1, source_target_pairs={{0,120},{8,0},{16,8},{24,16},{32,24},{40,32},{48,40},{56,48},{64,5... | collective-permute-start | bytes 196616 | tf_op jit(solution)/shard_map/ppermute | solution.py:19
  535.7 45.9 %collective-permute-start.7 = (bf16[128,1024]{0,1:T(8,128)(2,1)}, bf16[128,1024]{0,1:T(8,128)(2,1)}, u32[]{:S(2)}, u32[]{:S(2)}) collective-permute-start(bf16[128,1024]{0,1:T(8,128)(2,1)} %fusion.52), channel_id=1, source_target_pairs={{128,0},{256,128},{384,256},{129,1},{257,129},{385,257},{130,2},{2... | collective-permute-start | bytes 786440 | tf_op jit(solution)/shard_map/ppermute | solution.py:14
  549.5 294.2 %collective-permute-start.57 = (f32[2,128,128]{1,2,0:T(8,128)S(1)}, f32[2,128,128]{1,2,0:T(8,128)}, u32[]{:S(2)}, u32[]{:S(2)}) collective-permute-start(f32[2,128,128]{1,2,0:T(8,128)S(1)} %bitcast.1828), channel_id=1, source_target_pairs={{8,120},{9,121},{10,122},{11,123},{12,124},{13,125},{14,126},{15,1... | collective-permute-start | bytes 393224 | tf_op jit(solution)/shard_map/ppermute | solution.py:121
  550.8 293.5 %collective-permute-start.56 = (f32[2,128,128]{1,2,0:T(8,128)}, f32[2,128,128]{1,2,0:T(8,128)}, u32[]{:S(2)}, u32[]{:S(2)}) collective-permute-start(f32[2,128,128]{1,2,0:T(8,128)} %get-tuple-element.66), channel_id=1, source_target_pairs={{0,8},{8,16},{16,24},{24,32},{32,40},{40,48},{48,56},{56,64},{64,7... | collective-permute-start | bytes 393224 | tf_op jit(solution)/shard_map/ppermute | solution.py:19
  557.3 292.4 %collective-permute-start.55 = (f32[2,128,128]{1,2,0:T(8,128)}, f32[2,128,128]{1,2,0:T(8,128)}, u32[]{:S(2)}, u32[]{:S(2)}) collective-permute-start(f32[2,128,128]{1,2,0:T(8,128)} %get-tuple-element.65), channel_id=1, source_target_pairs={{0,120},{8,0},{16,8},{24,16},{32,24},{40,32},{48,40},{56,48},{64,5... | collective-permute-start | bytes 393224 | tf_op jit(solution)/shard_map/ppermute | solution.py:19
  560.0 37.6 %collective-permute-start.58 = (f32[3,2,128,128]{2,3,1,0:T(8,128)}, f32[3,2,128,128]{2,3,1,0:T(8,128)}, u32[]{:S(2)}, u32[]{:S(2)}) collective-permute-start(f32[3,2,128,128]{2,3,1,0:T(8,128)} %pad_maximum_fusion), channel_id=1, source_target_pairs={{0,8},{8,0},{24,16},{40,32},{56,48},{72,64},{88,80},{104,96},{120,... | collective-permute-start | bytes 1179656 | tf_op jit(solution)/shard_map/ppermute | solution.py:131
  601.5 38.2 %collective-permute-start.59 = (f32[3,2,128,128]{2,3,1,0:T(8,128)}, f32[3,2,128,128]{2,3,1,0:T(8,128)}, u32[]{:S(2)}, u32[]{:S(2)}) collective-permute-start(f32[3,2,128,128]{2,3,1,0:T(8,128)} %pad_maximum_fusion.1), channel_id=1, source_target_pairs={{0,16},{8,24},{16,0},{48,32},{80,64},{112,96},{120,104},{1,17},{9,... | collective-permute-start | bytes 1179656 | tf_op jit(solution)/shard_map/ppermute | solution.py:131
  639.8 25.0 %collective-permute-start.66 = (f32[3,2,128,128]{2,3,1,0:T(8,128)}, f32[3,2,128,128]{2,3,1,0:T(8,128)}, u32[]{:S(2)}, u32[]{:S(2)}) collective-permute-start(f32[3,2,128,128]{2,3,1,0:T(8,128)} %pad_maximum_fusion.5), channel_id=1, source_target_pairs={{0,16},{8,24},{16,0},{48,32},{80,64},{112,96},{120,104},{1,17},{9,... | collective-permute-start | bytes 1179656 | tf_op jit(solution)/shard_map/ppermute | solution.py:131
  653.9 30.1 %collective-permute-start.60 = (f32[3,2,128,128]{2,3,1,0:T(8,128)}, f32[3,2,128,128]{2,3,1,0:T(8,128)}, u32[]{:S(2)}, u32[]{:S(2)}) collective-permute-start(f32[3,2,128,128]{2,3,1,0:T(8,128)} %pad_maximum_fusion.2), channel_id=1, source_target_pairs={{0,32},{8,40},{16,48},{24,56},{32,0},{96,64},{104,72},{112,80},{12... | collective-permute-start | bytes 1179656 | tf_op jit(solution)/shard_map/ppermute | solution.py:131
  680.4 23.2 %collective-permute-start.73 = (f32[3,2,128,128]{2,3,1,0:T(8,128)}, f32[3,2,128,128]{2,3,1,0:T(8,128)}, u32[]{:S(2)}, u32[]{:S(2)}) collective-permute-start(f32[3,2,128,128]{2,3,1,0:T(8,128)} %pad_maximum_fusion.9), channel_id=1, source_target_pairs={{0,16},{8,24},{16,0},{48,32},{80,64},{112,96},{120,104},{1,17},{9,... | collective-permute-start | bytes 1179656 | tf_op jit(solution)/shard_map/ppermute | solution.py:131
  692.2 31.0 %collective-permute-start.67 = (f32[3,2,128,128]{2,3,1,0:T(8,128)}, f32[3,2,128,128]{2,3,1,0:T(8,128)}, u32[]{:S(2)}, u32[]{:S(2)}) collective-permute-start(f32[3,2,128,128]{2,3,1,0:T(8,128)} %pad_maximum_fusion.6), channel_id=1, source_target_pairs={{0,32},{8,40},{16,48},{24,56},{32,0},{96,64},{104,72},{112,80},{12... | collective-permute-start | bytes 1179656 | tf_op jit(solution)/shard_map/ppermute | solution.py:131
  703.5 34.5 %collective-permute-start.86 = (f32[3,2,128,128]{2,3,1,0:T(8,128)S(1)}, f32[3,2,128,128]{2,3,1,0:T(8,128)S(1)}, u32[]{:S(2)}, u32[]{:S(2)}) collective-permute-start(f32[3,2,128,128]{2,3,1,0:T(8,128)S(1)} %copy-done.235), channel_id=1, source_target_pairs={{0,8},{8,0},{24,16},{40,32},{56,48},{72,64},{88,80},{104,96},{120,... | collective-permute-start | bytes 1179656 | tf_op jit(solution)/shard_map/ppermute | solution.py:131
  723.2 128.6 %collective-permute-start.61 = (f32[3,2,128,128]{2,3,1,0:T(8,128)}, f32[3,2,128,128]{2,3,1,0:T(8,128)}, u32[]{:S(2)}, u32[]{:S(2)}) collective-permute-start(f32[3,2,128,128]{2,3,1,0:T(8,128)} %pad_maximum_fusion.3), channel_id=1, source_target_pairs={{0,64},{8,72},{16,80},{24,88},{32,96},{40,104},{48,112},{56,120},{... | collective-permute-start | bytes 1179656 | tf_op jit(solution)/shard_map/ppermute | solution.py:131
  746.4 110.2 %collective-permute-start.80 = (f32[3,2,128,128]{2,3,1,0:T(8,128)}, f32[3,2,128,128]{2,3,1,0:T(8,128)}, u32[]{:S(2)}, u32[]{:S(2)}) collective-permute-start(f32[3,2,128,128]{2,3,1,0:T(8,128)} %pad_maximum_fusion.13), channel_id=1, source_target_pairs={{0,16},{8,24},{16,0},{48,32},{80,64},{112,96},{120,104},{1,17},{9,... | collective-permute-start | bytes 1179656 | tf_op jit(solution)/shard_map/ppermute | solution.py:131
  843.7 99.2 %collective-permute-start.64 = (f32[2,128,128]{1,2,0:T(8,128)}, f32[2,128,128]{1,2,0:T(8,128)S(1)}, u32[]{:S(2)}, u32[]{:S(2)}) collective-permute-start(f32[2,128,128]{1,2,0:T(8,128)} %bitcast.324), channel_id=1, source_target_pairs={{8,120},{9,121},{10,122},{11,123},{12,124},{13,125},{14,126},{15,1... | collective-permute-start | bytes 393224 | tf_op jit(solution)/shard_map/ppermute | solution.py:121
  844.4 99.2 %collective-permute-start.63 = (f32[2,128,128]{1,2,0:T(8,128)}, f32[2,128,128]{1,2,0:T(8,128)S(1)}, u32[]{:S(2)}, u32[]{:S(2)}) collective-permute-start(f32[2,128,128]{1,2,0:T(8,128)} %get-tuple-element.64), channel_id=1, source_target_pairs={{0,8},{8,16},{16,24},{24,32},{32,40},{40,48},{48,56},{56,64},{64,7... | collective-permute-start | bytes 393224 | tf_op jit(solution)/shard_map/ppermute | solution.py:19
  849.7 99.5 %collective-permute-start.62 = (f32[2,128,128]{1,2,0:T(8,128)}, f32[2,128,128]{1,2,0:T(8,128)S(1)}, u32[]{:S(2)}, u32[]{:S(2)}) collective-permute-start(f32[2,128,128]{1,2,0:T(8,128)} %get-tuple-element.63), channel_id=1, source_target_pairs={{0,120},{8,0},{16,8},{24,16},{32,24},{40,32},{48,40},{56,48},{64,5... | collective-permute-start | bytes 393224 | tf_op jit(solution)/shard_map/ppermute | solution.py:19
  856.6 41.1 %collective-permute-start.93 = (f32[3,2,128,128]{2,3,1,0:T(8,128)S(1)}, f32[3,2,128,128]{2,3,1,0:T(8,128)S(1)}, u32[]{:S(2)}, u32[]{:S(2)}) collective-permute-start(f32[3,2,128,128]{2,3,1,0:T(8,128)S(1)} %copy-done.233), channel_id=1, source_target_pairs={{0,8},{8,0},{24,16},{40,32},{56,48},{72,64},{88,80},{104,96},{120,... | collective-permute-start | bytes 1179656 | tf_op jit(solution)/shard_map/ppermute | solution.py:131
  868.3 82.9 %collective-permute-start.68 = (f32[3,2,128,128]{2,3,1,0:T(8,128)S(1)}, f32[3,2,128,128]{2,3,1,0:T(8,128)S(1)}, u32[]{:S(2)}, u32[]{:S(2)}) collective-permute-start(f32[3,2,128,128]{2,3,1,0:T(8,128)S(1)} %copy-done.232), channel_id=1, source_target_pairs={{0,64},{8,72},{16,80},{24,88},{32,96},{40,104},{48,112},{56,120},{... | collective-permute-start | bytes 1179656 | tf_op jit(solution)/shard_map/ppermute | solution.py:131
  897.8 33.6 %collective-permute-start.87 = (f32[3,2,128,128]{2,3,1,0:T(8,128)S(1)}, f32[3,2,128,128]{2,3,1,0:T(8,128)S(1)}, u32[]{:S(2)}, u32[]{:S(2)}) collective-permute-start(f32[3,2,128,128]{2,3,1,0:T(8,128)S(1)} %copy-done.234), channel_id=1, source_target_pairs={{0,16},{8,24},{16,0},{48,32},{80,64},{112,96},{120,104},{1,17},{9,... | collective-permute-start | bytes 1179656 | tf_op jit(solution)/shard_map/ppermute | solution.py:131
  931.3 24.7 %collective-permute-start.100 = (f32[3,2,128,128]{2,3,1,0:T(8,128)S(1)}, f32[3,2,128,128]{2,3,1,0:T(8,128)S(1)}, u32[]{:S(2)}, u32[]{:S(2)}) collective-permute-start(f32[3,2,128,128]{2,3,1,0:T(8,128)S(1)} %pad_maximum_fusion.24), channel_id=1, source_target_pairs={{0,8},{8,0},{24,16},{40,32},{56,48},{72,64},{88,80},{104,96},{120,... | collective-permute-start | bytes 1179656 | tf_op jit(solution)/shard_map/ppermute | solution.py:131
  942.9 54.1 %collective-permute-start.71 = (f32[2,128,128]{1,2,0:T(8,128)S(1)}, f32[2,128,128]{1,2,0:T(8,128)S(1)}, u32[]{:S(2)}, u32[]{:S(2)}) collective-permute-start(f32[2,128,128]{1,2,0:T(8,128)S(1)} %bitcast.1883), channel_id=1, source_target_pairs={{8,120},{9,121},{10,122},{11,123},{12,124},{13,125},{14,126},{15,1... | collective-permute-start | bytes 393224 | tf_op jit(solution)/shard_map/ppermute | solution.py:121
  943.6 54.1 %collective-permute-start.70 = (f32[2,128,128]{1,2,0:T(8,128)S(1)}, f32[2,128,128]{1,2,0:T(8,128)S(1)}, u32[]{:S(2)}, u32[]{:S(2)}) collective-permute-start(f32[2,128,128]{1,2,0:T(8,128)S(1)} %copy-done.251), channel_id=1, source_target_pairs={{0,8},{8,16},{16,24},{24,32},{32,40},{40,48},{48,56},{56,64},{64,7... | collective-permute-start | bytes 393224 | tf_op jit(solution)/shard_map/ppermute | solution.py:19
  949.2 96.9 %collective-permute-start.69 = (f32[2,128,128]{1,2,0:T(8,128)S(1)}, f32[2,128,128]{1,2,0:T(8,128)S(1)}, u32[]{:S(2)}, u32[]{:S(2)}) collective-permute-start(f32[2,128,128]{1,2,0:T(8,128)S(1)} %copy-done.250), channel_id=1, source_target_pairs={{0,120},{8,0},{16,8},{24,16},{32,24},{40,32},{48,40},{56,48},{64,5... | collective-permute-start | bytes 393224 | tf_op jit(solution)/shard_map/ppermute | solution.py:19
  956.0 39.1 %collective-permute-start.94 = (f32[3,2,128,128]{2,3,1,0:T(8,128)S(1)}, f32[3,2,128,128]{2,3,1,0:T(8,128)S(1)}, u32[]{:S(2)}, u32[]{:S(2)}) collective-permute-start(f32[3,2,128,128]{2,3,1,0:T(8,128)S(1)} %pad_maximum_fusion.21), channel_id=1, source_target_pairs={{0,16},{8,24},{16,0},{48,32},{80,64},{112,96},{120,104},{1,17},{9,... | collective-permute-start | bytes 1179656 | tf_op jit(solution)/shard_map/ppermute | solution.py:131
  967.3 80.8 %collective-permute-start.75 = (f32[3,2,128,128]{2,3,1,0:T(8,128)S(1)}, f32[3,2,128,128]{2,3,1,0:T(8,128)S(1)}, u32[]{:S(2)}, u32[]{:S(2)}) collective-permute-start(f32[3,2,128,128]{2,3,1,0:T(8,128)S(1)} %pad_maximum_fusion.11), channel_id=1, source_target_pairs={{0,64},{8,72},{16,80},{24,88},{32,96},{40,104},{48,112},{56,120},{... | collective-permute-start | bytes 1179656 | tf_op jit(solution)/shard_map/ppermute | solution.py:131
  995.1 58.0 %collective-permute-start.88 = (f32[3,2,128,128]{2,3,1,0:T(8,128)S(1)}, f32[3,2,128,128]{2,3,1,0:T(8,128)S(1)}, u32[]{:S(2)}, u32[]{:S(2)}) collective-permute-start(f32[3,2,128,128]{2,3,1,0:T(8,128)S(1)} %pad_maximum_fusion.18), channel_id=1, source_target_pairs={{0,32},{8,40},{16,48},{24,56},{32,0},{96,64},{104,72},{112,80},{12... | collective-permute-start | bytes 1179656 | tf_op jit(solution)/shard_map/ppermute | solution.py:131
  997.1 87.3 %collective-permute-start.78 = (f32[2,128,128]{1,2,0:T(8,128)S(1)}, f32[2,128,128]{1,2,0:T(8,128)S(1)}, u32[]{:S(2)}, u32[]{:S(2)}) collective-permute-start(f32[2,128,128]{1,2,0:T(8,128)S(1)} %bitcast.1881), channel_id=1, source_target_pairs={{8,120},{9,121},{10,122},{11,123},{12,124},{13,125},{14,126},{15,1... | collective-permute-start | bytes 393224 | tf_op jit(solution)/shard_map/ppermute | solution.py:121
  997.8 87.3 %collective-permute-start.77 = (f32[2,128,128]{1,2,0:T(8,128)S(1)}, f32[2,128,128]{1,2,0:T(8,128)S(1)}, u32[]{:S(2)}, u32[]{:S(2)}) collective-permute-start(f32[2,128,128]{1,2,0:T(8,128)S(1)} %copy-done.247), channel_id=1, source_target_pairs={{0,8},{8,16},{16,24},{24,32},{32,40},{40,48},{48,56},{56,64},{64,7... | collective-permute-start | bytes 393224 | tf_op jit(solution)/shard_map/ppermute | solution.py:19
  1046.2 67.5 %collective-permute-start.76 = (f32[2,128,128]{1,2,0:T(8,128)S(1)}, f32[2,128,128]{1,2,0:T(8,128)S(1)}, u32[]{:S(2)}, u32[]{:S(2)}) collective-permute-start(f32[2,128,128]{1,2,0:T(8,128)S(1)} %copy-done.246), channel_id=1, source_target_pairs={{0,120},{8,0},{16,8},{24,16},{32,24},{40,32},{48,40},{56,48},{64,5... | collective-permute-start | bytes 393224 | tf_op jit(solution)/shard_map/ppermute | solution.py:19
  1048.1 34.3 %collective-permute-start.101 = (f32[3,2,128,128]{2,3,1,0:T(8,128)S(1)}, f32[3,2,128,128]{2,3,1,0:T(8,128)S(1)}, u32[]{:S(2)}, u32[]{:S(2)}) collective-permute-start(f32[3,2,128,128]{2,3,1,0:T(8,128)S(1)} %pad_maximum_fusion.25), channel_id=1, source_target_pairs={{0,16},{8,24},{16,0},{48,32},{80,64},{112,96},{120,104},{1,17},{9,... | collective-permute-start | bytes 1179656 | tf_op jit(solution)/shard_map/ppermute | solution.py:131
  1053.1 62.5 %collective-permute-start.82 = (f32[3,2,128,128]{2,3,1,0:T(8,128)S(1)}, f32[3,2,128,128]{2,3,1,0:T(8,128)S(1)}, u32[]{:S(2)}, u32[]{:S(2)}) collective-permute-start(f32[3,2,128,128]{2,3,1,0:T(8,128)S(1)} %pad_maximum_fusion.15), channel_id=1, source_target_pairs={{0,64},{8,72},{16,80},{24,88},{32,96},{40,104},{48,112},{56,120},{... | collective-permute-start | bytes 1179656 | tf_op jit(solution)/shard_map/ppermute | solution.py:131
  1082.4 41.3 %collective-permute-start.95 = (f32[3,2,128,128]{2,3,1,0:T(8,128)S(1)}, f32[3,2,128,128]{2,3,1,0:T(8,128)S(1)}, u32[]{:S(2)}, u32[]{:S(2)}) collective-permute-start(f32[3,2,128,128]{2,3,1,0:T(8,128)S(1)} %pad_maximum_fusion.22), channel_id=1, source_target_pairs={{0,32},{8,40},{16,48},{24,56},{32,0},{96,64},{104,72},{112,80},{12... | collective-permute-start | bytes 1179656 | tf_op jit(solution)/shard_map/ppermute | solution.py:131
  1084.4 163.6 %collective-permute-start.85 = (f32[2,128,128]{1,2,0:T(8,128)S(1)}, f32[2,128,128]{1,2,0:T(8,128)S(1)}, u32[]{:S(2)}, u32[]{:S(2)}) collective-permute-start(f32[2,128,128]{1,2,0:T(8,128)S(1)} %bitcast.1882), channel_id=1, source_target_pairs={{8,120},{9,121},{10,122},{11,123},{12,124},{13,125},{14,126},{15,1... | collective-permute-start | bytes 393224 | tf_op jit(solution)/shard_map/ppermute | solution.py:121
  1085.1 163.6 %collective-permute-start.84 = (f32[2,128,128]{1,2,0:T(8,128)S(1)}, f32[2,128,128]{1,2,0:T(8,128)S(1)}, u32[]{:S(2)}, u32[]{:S(2)}) collective-permute-start(f32[2,128,128]{1,2,0:T(8,128)S(1)} %copy-done.249), channel_id=1, source_target_pairs={{0,8},{8,16},{16,24},{24,32},{32,40},{40,48},{48,56},{56,64},{64,7... | collective-permute-start | bytes 393224 | tf_op jit(solution)/shard_map/ppermute | solution.py:19
  1113.6 137.1 %collective-permute-start.83 = (f32[2,128,128]{1,2,0:T(8,128)S(1)}, f32[2,128,128]{1,2,0:T(8,128)S(1)}, u32[]{:S(2)}, u32[]{:S(2)}) collective-permute-start(f32[2,128,128]{1,2,0:T(8,128)S(1)} %copy-done.248), channel_id=1, source_target_pairs={{0,120},{8,0},{16,8},{24,16},{32,24},{40,32},{48,40},{56,48},{64,5... | collective-permute-start | bytes 393224 | tf_op jit(solution)/shard_map/ppermute | solution.py:19
  1115.6 88.2 %collective-permute-start.102 = (f32[3,2,128,128]{2,3,1,0:T(8,128)S(1)}, f32[3,2,128,128]{2,3,1,0:T(8,128)S(1)}, u32[]{:S(2)}, u32[]{:S(2)}) collective-permute-start(f32[3,2,128,128]{2,3,1,0:T(8,128)S(1)} %pad_maximum_fusion.26), channel_id=1, source_target_pairs={{0,32},{8,40},{16,48},{24,56},{32,0},{96,64},{104,72},{112,80},{12... | collective-permute-start | bytes 1179656 | tf_op jit(solution)/shard_map/ppermute | solution.py:131
  1123.7 132.3 %collective-permute-start.89 = (f32[3,2,128,128]{2,3,1,0:T(8,128)S(1)}, f32[3,2,128,128]{2,3,1,0:T(8,128)S(1)}, u32[]{:S(2)}, u32[]{:S(2)}) collective-permute-start(f32[3,2,128,128]{2,3,1,0:T(8,128)S(1)} %pad_maximum_fusion.19), channel_id=1, source_target_pairs={{0,64},{8,72},{16,80},{24,88},{32,96},{40,104},{48,112},{56,120},{... | collective-permute-start | bytes 1179656 | tf_op jit(solution)/shard_map/ppermute | solution.py:131
  1203.8 88.7 %collective-permute-start.96 = (f32[3,2,128,128]{2,3,1,0:T(8,128)S(1)}, f32[3,2,128,128]{2,3,1,0:T(8,128)S(1)}, u32[]{:S(2)}, u32[]{:S(2)}) collective-permute-start(f32[3,2,128,128]{2,3,1,0:T(8,128)S(1)} %pad_maximum_fusion.23), channel_id=1, source_target_pairs={{0,64},{8,72},{16,80},{24,88},{32,96},{40,104},{48,112},{56,120},{... | collective-permute-start | bytes 1179656 | tf_op jit(solution)/shard_map/ppermute | solution.py:131
  1250.7 35.9 %collective-permute-start.90 = (f32[2,128,128]{1,2,0:T(8,128)S(1)}, f32[2,128,128]{1,2,0:T(8,128)S(1)}, u32[]{:S(2)}, u32[]{:S(2)}) collective-permute-start(f32[2,128,128]{1,2,0:T(8,128)S(1)} %copy-done.252), channel_id=1, source_target_pairs={{0,120},{8,0},{16,8},{24,16},{32,24},{40,32},{48,40},{56,48},{64,5... | collective-permute-start | bytes 393224 | tf_op jit(solution)/shard_map/ppermute | solution.py:19
  1256.0 44.9 %collective-permute-start.103 = (f32[3,2,128,128]{2,3,1,0:T(8,128)S(1)}, f32[3,2,128,128]{2,3,1,0:T(8,128)S(1)}, u32[]{:S(2)}, u32[]{:S(2)}) collective-permute-start(f32[3,2,128,128]{2,3,1,0:T(8,128)S(1)} %pad_maximum_fusion.27), channel_id=1, source_target_pairs={{0,64},{8,72},{16,80},{24,88},{32,96},{40,104},{48,112},{56,120},{... | collective-permute-start | bytes 1179656 | tf_op jit(solution)/shard_map/ppermute | solution.py:131
  1258.2 34.5 %collective-permute-start.99 = (f32[2,128,128]{1,2,0:T(8,128)S(1)}, f32[2,128,128]{1,2,0:T(8,128)S(1)}, u32[]{:S(2)}, u32[]{:S(2)}) collective-permute-start(f32[2,128,128]{1,2,0:T(8,128)S(1)} %bitcast.1885), channel_id=1, source_target_pairs={{8,120},{9,121},{10,122},{11,123},{12,124},{13,125},{14,126},{15,1... | collective-permute-start | bytes 393224 | tf_op jit(solution)/shard_map/ppermute | solution.py:121
  1267.9 24.8 %collective-permute-start.98 = (f32[2,128,128]{1,2,0:T(8,128)S(1)}, f32[2,128,128]{1,2,0:T(8,128)S(1)}, u32[]{:S(2)}, u32[]{:S(2)}) collective-permute-start(f32[2,128,128]{1,2,0:T(8,128)S(1)} %copy-done.255), channel_id=1, source_target_pairs={{0,8},{8,16},{16,24},{24,32},{32,40},{40,48},{48,56},{56,64},{64,7... | collective-permute-start | bytes 393224 | tf_op jit(solution)/shard_map/ppermute | solution.py:19
  (324 other events, 7312.3 us)

commit v3 on v0

--- a/solution.py
+++ b/solution.py
@@ -135,8 +135,7 @@
         safe_index = jnp.clip(unit, 0, unit_count - 1)
         target = jnp.where(active, safe_index, unit_count)
         from_top = lax.dynamic_slice_in_dim(head_top, safe_index * turn_rows, turn_rows, 0)
-        arrived = lax.all_to_all(incoming, "ctx", split_axis=1, concat_axis=0, tiled=True)
-        head_grad = jnp.where(on_top, from_top, arrived)
+        head_grad = jnp.where(on_top, from_top, incoming)
         query_grad, key_part, value_part, gain_part = lax.cond(
             active, attend, spare, safe_index, head_grad
         )
@@ -148,11 +147,10 @@
         key_slots = lax.dynamic_update_slice_in_dim(key_slots, key_part, target * per_turn, 0)
         value_slots = lax.dynamic_update_slice_in_dim(value_slots, value_part, target * per_turn, 0)
         gain_acc = gain_acc + gain_part
-        outgoing = lax.all_to_all(handed, "ctx", split_axis=0, concat_axis=1, tiled=True)
-        incoming = passed_along(outgoing, "section", -1)
+        incoming = passed_along(handed, "section", -1)
         return (incoming, result_heads, key_slots, value_slots, gain_acc)
 
-    first_incoming = jnp.zeros((token_rows, feature_count), jnp.bfloat16)
+    first_incoming = jnp.zeros((turn_rows, local_width), jnp.bfloat16)
     slot_zeros = jnp.zeros(
         ((unit_count + 1) * per_turn, listed * block_rows, slot_width), jnp.float32
     )

time: 882 us -> 485 us (0.55)
  waiting for transfers between devices: 548 us -> 259 us
  starting transfers between devices: 172 us -> 74.9 us
    all_to_all x22 -> x0, waiting for transfers between devices: 292 us -> none  [the longest x11 147 us: turn_step(): lax.all_to_all(incoming, 'ctx', split_axis=1, concat_axis=0, tiled=True)]
    all_to_all x22 -> x0, starting transfers between devices: 94.6 us -> none  [the longest x11 49.3 us: turn_step(): lax.all_to_all(incoming, 'ctx', split_axis=1, concat_axis=0, tiled=True)]
  transfers between devices with their start and end apart: 40 -> 18, of which waited for: 40 -> 18; matrix products, arithmetic and copies ran while one was open for 5% -> 8% of each run, Pallas kernels for 0% -> 0%
where the time goes in v3:
time: 485 us; the launch traced here: 483 us
  waiting for transfers between devices  259 us (53%)
  starting transfers between devices  74.9 us (15%)
  local copies, waits for them, and re-layouts  72.1 us (15%)
  other arithmetic  51.8 us (11%)
  matrix products  12.1 us (2%)
  blocking collectives  10.9 us (2%)
    ppermute x11, waiting for transfers between devices, passed_along(): return lax.ppermute(block, axis, route)  66 us
    all_to_all x1, waiting for transfers between devices, shards(): lax.all_to_all(layer_input, 'ctx', split_axis=1, concat_axis=0, tiled=True)  48.5 us
    all_to_all x1, waiting for transfers between devices, shards(): lax.all_to_all(top_grad[0], 'ctx', split_axis=1, concat_axis=0, tiled=True)  47.5 us
    all_to_all x1, waiting for transfers between devices, shards(): lax.all_to_all(sent_values, 'ctx', split_axis=1, concat_axis=0, tiled=True)  27.6 us
    all_to_all x1, waiting for transfers between devices, shards(): lax.all_to_all(sent_keys, 'ctx', split_axis=1, concat_axis=0, tiled=True)  26.5 us
    all_to_all x1, waiting for transfers between devices, shards(): lax.all_to_all(result_heads[:total_rows], 'ctx', split_axis=0, concat_axi...  19.3 us
    all_to_all x1, waiting for transfers between devices, shards(): lax.all_to_all(value_acc.reshape(total_rows, slot_width).astype(jnp.bfloa...  18.4 us
    all_to_all x1, starting transfers between devices, shards(): lax.all_to_all(sent_keys, 'ctx', split_axis=1, concat_axis=0, tiled=True)  15.2 us
  transfers between devices with their start and end apart: 18, of which 18 were waited for; matrix products, arithmetic and copies ran while one was open for 8% of the time, Pallas kernels for 0%

profile of v3, /device:TPU:6, one launch (start us, length us, event | category | flops | bytes accessed | tf_op | source)
XLA Modules:
  0.0 482.9 jit_solution(11112941961113360390)
XLA Ops:
  2.6 1.4 gather_fusion.2
  4.0 15.2 %all-to-all-start.1 = ((bf16[128,16,128]{2,0,1:T(8,128)(2,1)}), bf16[128,16,128]{2,0,1:T(8,128)(2,1)S(1)}, u32[]{:S(2)}, u32[]{:S(2)}) async-start(bf16[128,16,128]{2,0,1:T(8,128)(2,1)} %bitcast.29), calls=%async_computation.1 | async-start | bytes 1048576 | tf_op jit(solution)/shard_map/all_to_all | solution.py:52
  20.4 1.4 gather_fusion.3
  21.8 26.5 %all-to-all-done.1 = bf16[128,16,128]{2,0,1:T(8,128)(2,1)S(1)} async-done(((bf16[128,16,128]{2,0,1:T(8,128)(2,1)}), bf16[128,16,128]{2,0,1:T(8,128)(2,1)S(1)}, u32[]{:S(2)}, u32[]{:S(2)}) %all-to-all-start.1) | async-done | bytes 524320 | tf_op jit(solution)/shard_map/all_to_all | solution.py:52
  48.3 6.3 %all-to-all-start.3 = ((bf16[128,16,128]{2,0,1:T(8,128)(2,1)}), bf16[128,16,128]{2,0,1:T(8,128)(2,1)}, u32[]{:S(2)}, u32[]{:S(2)}) async-start(bf16[128,16,128]{2,0,1:T(8,128)(2,1)} %bitcast.36), calls=%async_computation.3 | async-start | bytes 1048576 | tf_op jit(solution)/shard_map/all_to_all | solution.py:53
  54.9 1.3 copy.135
  56.2 27.6 %all-to-all-done.3 = bf16[128,16,128]{2,0,1:T(8,128)(2,1)} async-done(((bf16[128,16,128]{2,0,1:T(8,128)(2,1)}), bf16[128,16,128]{2,0,1:T(8,128)(2,1)}, u32[]{:S(2)}, u32[]{:S(2)}) %all-to-all-start.3) | async-done | bytes 524320 | tf_op jit(solution)/shard_map/all_to_all | solution.py:53
  83.8 6.3 %all-to-all-start.2 = ((bf16[128,16,256]{2,0,1:T(8,128)(2,1)}), bf16[128,16,256]{2,0,1:T(8,128)(2,1)}, u32[]{:S(2)}, u32[]{:S(2)}) async-start(bf16[128,16,256]{2,0,1:T(8,128)(2,1)} %copy.135), calls=%async_computation.2 | async-start | bytes 2097152 | tf_op jit(solution)/shard_map/all_to_all | solution.py:51
  90.4 1.3 copy.132
  91.7 48.5 %all-to-all-done.2 = bf16[128,16,256]{2,0,1:T(8,128)(2,1)} async-done(((bf16[128,16,256]{2,0,1:T(8,128)(2,1)}), bf16[128,16,256]{2,0,1:T(8,128)(2,1)}, u32[]{:S(2)}, u32[]{:S(2)}) %all-to-all-start.2) | async-done | bytes 1048608 | tf_op jit(solution)/shard_map/all_to_all | solution.py:51
  140.2 7.9 %all-to-all-start = ((bf16[128,16,256]{2,0,1:T(8,128)(2,1)}), bf16[128,16,256]{2,0,1:T(8,128)(2,1)}, u32[]{:S(2)}, u32[]{:S(2)}) async-start(bf16[128,16,256]{2,0,1:T(8,128)(2,1)} %copy.132), calls=%async_computation | async-start | bytes 2097152 | tf_op jit(solution)/shard_map/all_to_all | solution.py:54
  148.4 2.4 multiply_convert_fusion.2
  150.8 47.5 %all-to-all-done = bf16[128,16,256]{2,0,1:T(8,128)(2,1)} async-done(((bf16[128,16,256]{2,0,1:T(8,128)(2,1)}), bf16[128,16,256]{2,0,1:T(8,128)(2,1)}, u32[]{:S(2)}, u32[]{:S(2)}) %all-to-all-start) | async-done | bytes 1048608 | tf_op jit(solution)/shard_map/all_to_all | solution.py:54
  198.3 2.6 broadcast_in_dim.34.clone
  200.9 2.7 broadcast_in_dim.34.clone2
  204.7 165.9 %while.24 = (s32[]{:T(128)}, bf16[256,256]{1,0:T(8,128)(2,1)S(1)}, bf16[2304,256]{1,0:T(8,128)(2,1)}, f32[18,512,128]{2,1,0:T(8,128)}, f32[18,512,128]{2,1,0:T(8...) while((s32[]{:T(128)}, bf16[256,256]{1,0:T(8,128)(2,1)S(1)}, ...), condition=%wide.region_7.8_spmd.clone, body=%wide.region_0.7_spmd.clone.sunk | while | flops 340590400 | bytes 19562376 | solution.py:164
  206.5 1.3 collective-permute-start
  209.1 4.2 collective-permute-done
  215.2 1.3 collective-permute-start
  217.8 4.2 collective-permute-done
  223.8 1.3 collective-permute-start
  226.4 21.4 %collective-permute-done = bf16[256,256]{1,0:T(8,128)(2,1)S(1)} collective-permute-done((bf16[256,256]{1,0:T(8,128)(2,1)S(1)}, bf16[256,256]{1,0:T(8,128)(2,1)S(1)}, u32[]{:S(2)}, u32[]{:S(2)}) %collective-permute-start) | collective-permute-done | bytes 131104 | tf_op jit(solution)/shard_map/while/body/eval_jaxpr/ppermute | solution.py:15
  248.7 6.6 %conditional.3 = (f32[256,256]{1,0:T(8,128)S(1)}, f32[2,512,128]{1,2,0:T(8,128)S(1)}, f32[2,512,128]{2,1,0:T(8,128)S(1)}, f32[256]{0:T(256)S(1)}) conditional(s32[]{:T(128)} %convert_element_type.154, () %tuple.81, (s32[]{:T(128)}, s32[16,4]{1,0:T(8,128)S(1)}, bf16[16,128,1,128]{3,1,0,2:T(8,128)(2,1)S(1)}, bf16[2048,256]{1,0:T(8,128)(2,1)}, ...), branch_computations={%region_1.1_spmd, %region_2.6_spmd} | conditional | flops 340131104 | bytes 14839144 | solution.py:139
  251.4 1.6 gather_fusion.1
  256.0 1.3 collective-permute-start
  258.6 4.3 collective-permute-done
  263.9 6.6 %conditional.3 = (f32[256,256]{1,0:T(8,128)S(1)}, f32[2,512,128]{1,2,0:T(8,128)S(1)}, f32[2,512,128]{2,1,0:T(8,128)S(1)}, f32[256]{0:T(256)S(1)}) conditional(s32[]{:T(128)} %convert_element_type.154, () %tuple.81, (s32[]{:T(128)}, s32[16,4]{1,0:T(8,128)S(1)}, bf16[16,128,1,128]{3,1,0,2:T(8,128)(2,1)S(1)}, bf16[2048,256]{1,0:T(8,128)(2,1)}, ...), branch_computations={%region_1.1_spmd, %region_2.6_spmd} | conditional | flops 340131104 | bytes 14839144 | solution.py:139
  266.5 1.6 gather_fusion.1
  271.2 1.3 collective-permute-start
  273.8 4.3 collective-permute-done
  279.0 6.6 %conditional.3 = (f32[256,256]{1,0:T(8,128)S(1)}, f32[2,512,128]{1,2,0:T(8,128)S(1)}, f32[2,512,128]{2,1,0:T(8,128)S(1)}, f32[256]{0:T(256)S(1)}) conditional(s32[]{:T(128)} %convert_element_type.154, () %tuple.81, (s32[]{:T(128)}, s32[16,4]{1,0:T(8,128)S(1)}, bf16[16,128,1,128]{3,1,0,2:T(8,128)(2,1)S(1)}, bf16[2048,256]{1,0:T(8,128)(2,1)}, ...), branch_computations={%region_1.1_spmd, %region_2.6_spmd} | conditional | flops 340131104 | bytes 14839144 | solution.py:139
  281.6 1.6 gather_fusion.1
  286.3 1.3 collective-permute-start
  288.8 4.3 collective-permute-done
  294.0 6.6 %conditional.3 = (f32[256,256]{1,0:T(8,128)S(1)}, f32[2,512,128]{1,2,0:T(8,128)S(1)}, f32[2,512,128]{2,1,0:T(8,128)S(1)}, f32[256]{0:T(256)S(1)}) conditional(s32[]{:T(128)} %convert_element_type.154, () %tuple.81, (s32[]{:T(128)}, s32[16,4]{1,0:T(8,128)S(1)}, bf16[16,128,1,128]{3,1,0,2:T(8,128)(2,1)S(1)}, bf16[2048,256]{1,0:T(8,128)(2,1)}, ...), branch_computations={%region_1.1_spmd, %region_2.6_spmd} | conditional | flops 340131104 | bytes 14839144 | solution.py:139
  296.7 1.6 gather_fusion.1
  301.3 1.3 collective-permute-start
  304.0 4.2 collective-permute-done
  309.1 6.6 %conditional.3 = (f32[256,256]{1,0:T(8,128)S(1)}, f32[2,512,128]{1,2,0:T(8,128)S(1)}, f32[2,512,128]{2,1,0:T(8,128)S(1)}, f32[256]{0:T(256)S(1)}) conditional(s32[]{:T(128)} %convert_element_type.154, () %tuple.81, (s32[]{:T(128)}, s32[16,4]{1,0:T(8,128)S(1)}, bf16[16,128,1,128]{3,1,0,2:T(8,128)(2,1)S(1)}, bf16[2048,256]{1,0:T(8,128)(2,1)}, ...), branch_computations={%region_1.1_spmd, %region_2.6_spmd} | conditional | flops 340131104 | bytes 14839144 | solution.py:139
  311.8 1.6 gather_fusion.1
  316.5 1.3 collective-permute-start
  319.1 5.0 %collective-permute-done = bf16[256,256]{1,0:T(8,128)(2,1)S(1)} collective-permute-done((bf16[256,256]{1,0:T(8,128)(2,1)S(1)}, bf16[256,256]{1,0:T(8,128)(2,1)S(1)}, u32[]{:S(2)}, u32[]{:S(2)}) %collective-permute-start) | collective-permute-done | bytes 131104 | tf_op jit(solution)/shard_map/while/body/eval_jaxpr/ppermute | solution.py:15
  325.0 6.6 %conditional.3 = (f32[256,256]{1,0:T(8,128)S(1)}, f32[2,512,128]{1,2,0:T(8,128)S(1)}, f32[2,512,128]{2,1,0:T(8,128)S(1)}, f32[256]{0:T(256)S(1)}) conditional(s32[]{:T(128)} %convert_element_type.154, () %tuple.81, (s32[]{:T(128)}, s32[16,4]{1,0:T(8,128)S(1)}, bf16[16,128,1,128]{3,1,0,2:T(8,128)(2,1)S(1)}, bf16[2048,256]{1,0:T(8,128)(2,1)}, ...), branch_computations={%region_1.1_spmd, %region_2.6_spmd} | conditional | flops 340131104 | bytes 14839144 | solution.py:139
  327.7 1.6 gather_fusion.1
  332.3 1.3 collective-permute-start
  334.9 5.5 %collective-permute-done = bf16[256,256]{1,0:T(8,128)(2,1)S(1)} collective-permute-done((bf16[256,256]{1,0:T(8,128)(2,1)S(1)}, bf16[256,256]{1,0:T(8,128)(2,1)S(1)}, u32[]{:S(2)}, u32[]{:S(2)}) %collective-permute-start) | collective-permute-done | bytes 131104 | tf_op jit(solution)/shard_map/while/body/eval_jaxpr/ppermute | solution.py:15
  341.3 6.6 %conditional.3 = (f32[256,256]{1,0:T(8,128)S(1)}, f32[2,512,128]{1,2,0:T(8,128)S(1)}, f32[2,512,128]{2,1,0:T(8,128)S(1)}, f32[256]{0:T(256)S(1)}) conditional(s32[]{:T(128)} %convert_element_type.154, () %tuple.81, (s32[]{:T(128)}, s32[16,4]{1,0:T(8,128)S(1)}, bf16[16,128,1,128]{3,1,0,2:T(8,128)(2,1)S(1)}, bf16[2048,256]{1,0:T(8,128)(2,1)}, ...), branch_computations={%region_1.1_spmd, %region_2.6_spmd} | conditional | flops 340131104 | bytes 14839144 | solution.py:139
  344.0 1.6 gather_fusion.1
  351.2 4.3 collective-permute-done
  356.5 6.6 %conditional.3 = (f32[256,256]{1,0:T(8,128)S(1)}, f32[2,512,128]{1,2,0:T(8,128)S(1)}, f32[2,512,128]{2,1,0:T(8,128)S(1)}, f32[256]{0:T(256)S(1)}) conditional(s32[]{:T(128)} %convert_element_type.154, () %tuple.81, (s32[]{:T(128)}, s32[16,4]{1,0:T(8,128)S(1)}, bf16[16,128,1,128]{3,1,0,2:T(8,128)(2,1)S(1)}, bf16[2048,256]{1,0:T(8,128)(2,1)}, ...), branch_computations={%region_1.1_spmd, %region_2.6_spmd} | conditional | flops 340131104 | bytes 14839144 | solution.py:139
  359.2 1.6 gather_fusion.1
  366.4 4.3 collective-permute-done
  370.6 4.7 slice.10
  375.4 8.8 %scatter_fusion = f32[16,128,128]{2,1,0:T(8,128)S(1)} fusion(f32[16,128,128]{2,1,0:T(8,128)S(1)} %broadcast.75.clone, s32[64]{0:T(128)S(1)} %fusion.12, f32[64,128,128]{2,1,0:T(8,128)} %bitcast.112), kind=kCustom, calls=%fused_computation.4 | custom fusion | flops 1048576 | bytes 12583168 | tf_op jit(solution)/shard_map/scatter-add | solution.py:175
  385.1 7.5 %all-to-all-start.5 = ((bf16[16,128,128]{2,1,0:T(8,128)(2,1)}), bf16[16,128,128]{2,1,0:T(8,128)(2,1)S(1)}, u32[]{:S(2)}, u32[]{:S(2)}) async-start(bf16[16,128,128]{2,1,0:T(8,128)(2,1)} %convert_element_type.116), calls=%async_computation.5 | async-start | bytes 1048576 | tf_op jit(solution)/shard_map/all_to_all | solution.py:183
  392.6 4.5 slice.11
  397.3 8.8 %scatter_fusion.1 = f32[16,128,128]{2,1,0:T(8,128)S(1)} fusion(f32[16,128,128]{2,1,0:T(8,128)S(1)} %broadcast.75.clone.1, s32[64]{0:T(128)S(1)} %fusion.12, f32[64,128,128]{2,1,0:T(8,128)} %bitcast.111), kind=kCustom, calls=%fused_computation.5 | custom fusion | flops 1048576 | bytes 12583168 | tf_op jit(solution)/shard_map/scatter-add | solution.py:180
  406.9 5.0 %all-to-all-done.5 = bf16[16,128,128]{2,1,0:T(8,128)(2,1)S(1)} async-done(((bf16[16,128,128]{2,1,0:T(8,128)(2,1)}), bf16[16,128,128]{2,1,0:T(8,128)(2,1)S(1)}, u32[]{:S(2)}, u32[]{:S(2)}) %all-to-all-start.5) | async-done | bytes 524320 | tf_op jit(solution)/shard_map/all_to_all | solution.py:183
  411.9 7.0 %all-to-all-start.6 = ((bf16[16,128,128]{2,1,0:T(8,128)(2,1)}), bf16[16,128,128]{2,1,0:T(8,128)(2,1)S(1)}, u32[]{:S(2)}, u32[]{:S(2)}) async-start(bf16[16,128,128]{2,1,0:T(8,128)(2,1)} %convert_element_type.122), calls=%async_computation.6 | async-start | bytes 1048576 | tf_op jit(solution)/shard_map/all_to_all | solution.py:190
  420.0 18.4 %all-to-all-done.6 = bf16[16,128,128]{2,1,0:T(8,128)(2,1)S(1)} async-done(((bf16[16,128,128]{2,1,0:T(8,128)(2,1)}), bf16[16,128,128]{2,1,0:T(8,128)(2,1)S(1)}, u32[]{:S(2)}, u32[]{:S(2)}) %all-to-all-start.6) | async-done | bytes 524320 | tf_op jit(solution)/shard_map/all_to_all | solution.py:190
  438.4 10.4 %all-to-all-start.4 = ((bf16[16,128,256]{2,1,0:T(8,128)(2,1)}), bf16[16,128,256]{2,1,0:T(8,128)(2,1)S(1)}, u32[]{:S(2)}, u32[]{:S(2)}) async-start(bf16[16,128,256]{2,1,0:T(8,128)(2,1)} %bitcast.39), calls=%async_computation.4 | async-start | bytes 2097152 | tf_op jit(solution)/shard_map/all_to_all | solution.py:166
  448.8 10.9 %psum.7 = f32[1,256]{1,0:T(1,128)} all-reduce(f32[1,256]{1,0:T(1,128)S(1)} %bitcast.127), channel_id=1, replica_groups=mesh['section'=4,'ctx'=16,'dp'=8] {'dp'}, use_global_device_ids=true, to_apply=%region_12.13 | all-reduce | flops 256 | bytes 2048 | tf_op jit(solution)/shard_map/psum | solution.py:210
  461.7 19.3 %all-to-all-done.4 = bf16[16,128,256]{2,1,0:T(8,128)(2,1)S(1)} async-done(((bf16[16,128,256]{2,1,0:T(8,128)(2,1)}), bf16[16,128,256]{2,1,0:T(8,128)(2,1)S(1)}, u32[]{:S(2)}, u32[]{:S(2)}) %all-to-all-start.4) | async-done | bytes 1048608 | tf_op jit(solution)/shard_map/all_to_all | solution.py:166
  481.6 1.3 copy.145
  (243 shorter events, 84.7 us)
Async XLA Ops:
  0.6 54.0 %copy-start.1 = (bf16[1,1,128,4096]{3,2,1,0:T(8,128)(2,1)S(1)}, bf16[1,1,128,4096]{3,2,1,0:T(8,128)(2,1)}, u32[]{:S(2)}) copy-start(bf16[1,1,128,4096]{3,2,1,0:T(8,128)(2,1)} %param.13) | copy-start | bytes 3145732
  4.0 44.3 %all-to-all-start.1 = ((bf16[128,16,128]{2,0,1:T(8,128)(2,1)}), bf16[128,16,128]{2,0,1:T(8,128)(2,1)S(1)}, u32[]{:S(2)}, u32[]{:S(2)}) async-start(bf16[128,16,128]{2,0,1:T(8,128)(2,1)} %bitcast.29), calls=%async_computation.1 | async-start | bytes 1048576 | tf_op jit(solution)/shard_map/all_to_all | solution.py:52
  20.3 69.8 %copy-start.2 = (bf16[1,128,4096]{2,1,0:T(8,128)(2,1)S(1)}, bf16[1,128,4096]{2,1,0:T(8,128)(2,1)}, u32[]{:S(2)}) copy-start(bf16[1,128,4096]{2,1,0:T(8,128)(2,1)} %param.17) | copy-start | bytes 3145732
  48.3 35.5 %all-to-all-start.3 = ((bf16[128,16,128]{2,0,1:T(8,128)(2,1)}), bf16[128,16,128]{2,0,1:T(8,128)(2,1)}, u32[]{:S(2)}, u32[]{:S(2)}) async-start(bf16[128,16,128]{2,0,1:T(8,128)(2,1)} %bitcast.36), calls=%async_computation.3 | async-start | bytes 1048576 | tf_op jit(solution)/shard_map/all_to_all | solution.py:53
  56.2 92.0 %copy-start.4 = (s32[16,4]{0,1:T(4,128)S(1)}, s32[16,4]{0,1:T(4,128)}, u32[]{:S(2)}) copy-start(s32[16,4]{0,1:T(4,128)} %param.18) | copy-start | bytes 772
  56.2 92.2 %copy-start.3 = (f32[1,256]{1,0:T(1,128)S(1)}, f32[1,256]{1,0:T(1,128)}, u32[]{:S(2)}) copy-start(f32[1,256]{1,0:T(1,128)} %param.16) | copy-start | bytes 3076
  83.8 56.4 %all-to-all-start.2 = ((bf16[128,16,256]{2,0,1:T(8,128)(2,1)}), bf16[128,16,256]{2,0,1:T(8,128)(2,1)}, u32[]{:S(2)}, u32[]{:S(2)}) async-start(bf16[128,16,256]{2,0,1:T(8,128)(2,1)} %copy.135), calls=%async_computation.2 | async-start | bytes 2097152 | tf_op jit(solution)/shard_map/all_to_all | solution.py:51
  140.2 58.1 %all-to-all-start = ((bf16[128,16,256]{2,0,1:T(8,128)(2,1)}), bf16[128,16,256]{2,0,1:T(8,128)(2,1)}, u32[]{:S(2)}, u32[]{:S(2)}) async-start(bf16[128,16,256]{2,0,1:T(8,128)(2,1)} %copy.132), calls=%async_computation | async-start | bytes 2097152 | tf_op jit(solution)/shard_map/all_to_all | solution.py:54
  206.5 6.8 %collective-permute-start = (bf16[256,256]{1,0:T(8,128)(2,1)S(1)}, bf16[256,256]{1,0:T(8,128)(2,1)S(1)}, u32[]{:S(2)}, u32[]{:S(2)}) collective-permute-start(bf16[256,256]{1,0:T(8,128)(2,1)S(1)} %get-tuple-element.711), channel_id=1, source_target_pairs={{128,0},{256,128},{384,256},{129,1},{257,129},{385,257},{130,2},{2... | collective-permute-start | bytes 393224 | tf_op jit(solution)/shard_map/while/body/eval_jaxpr/ppermute | solution.py:15
  215.2 6.8 %collective-permute-start = (bf16[256,256]{1,0:T(8,128)(2,1)S(1)}, bf16[256,256]{1,0:T(8,128)(2,1)S(1)}, u32[]{:S(2)}, u32[]{:S(2)}) collective-permute-start(bf16[256,256]{1,0:T(8,128)(2,1)S(1)} %get-tuple-element.711), channel_id=1, source_target_pairs={{128,0},{256,128},{384,256},{129,1},{257,129},{385,257},{130,2},{2... | collective-permute-start | bytes 393224 | tf_op jit(solution)/shard_map/while/body/eval_jaxpr/ppermute | solution.py:15
  223.8 24.0 %collective-permute-start = (bf16[256,256]{1,0:T(8,128)(2,1)S(1)}, bf16[256,256]{1,0:T(8,128)(2,1)S(1)}, u32[]{:S(2)}, u32[]{:S(2)}) collective-permute-start(bf16[256,256]{1,0:T(8,128)(2,1)S(1)} %get-tuple-element.711), channel_id=1, source_target_pairs={{128,0},{256,128},{384,256},{129,1},{257,129},{385,257},{130,2},{2... | collective-permute-start | bytes 393224 | tf_op jit(solution)/shard_map/while/body/eval_jaxpr/ppermute | solution.py:15
  256.0 6.9 %collective-permute-start = (bf16[256,256]{1,0:T(8,128)(2,1)S(1)}, bf16[256,256]{1,0:T(8,128)(2,1)S(1)}, u32[]{:S(2)}, u32[]{:S(2)}) collective-permute-start(bf16[256,256]{1,0:T(8,128)(2,1)S(1)} %get-tuple-element.711), channel_id=1, source_target_pairs={{128,0},{256,128},{384,256},{129,1},{257,129},{385,257},{130,2},{2... | collective-permute-start | bytes 393224 | tf_op jit(solution)/shard_map/while/body/eval_jaxpr/ppermute | solution.py:15
  271.2 6.8 %collective-permute-start = (bf16[256,256]{1,0:T(8,128)(2,1)S(1)}, bf16[256,256]{1,0:T(8,128)(2,1)S(1)}, u32[]{:S(2)}, u32[]{:S(2)}) collective-permute-start(bf16[256,256]{1,0:T(8,128)(2,1)S(1)} %get-tuple-element.711), channel_id=1, source_target_pairs={{128,0},{256,128},{384,256},{129,1},{257,129},{385,257},{130,2},{2... | collective-permute-start | bytes 393224 | tf_op jit(solution)/shard_map/while/body/eval_jaxpr/ppermute | solution.py:15
  286.3 6.8 %collective-permute-start = (bf16[256,256]{1,0:T(8,128)(2,1)S(1)}, bf16[256,256]{1,0:T(8,128)(2,1)S(1)}, u32[]{:S(2)}, u32[]{:S(2)}) collective-permute-start(bf16[256,256]{1,0:T(8,128)(2,1)S(1)} %get-tuple-element.711), channel_id=1, source_target_pairs={{128,0},{256,128},{384,256},{129,1},{257,129},{385,257},{130,2},{2... | collective-permute-start | bytes 393224 | tf_op jit(solution)/shard_map/while/body/eval_jaxpr/ppermute | solution.py:15
  301.3 6.8 %collective-permute-start = (bf16[256,256]{1,0:T(8,128)(2,1)S(1)}, bf16[256,256]{1,0:T(8,128)(2,1)S(1)}, u32[]{:S(2)}, u32[]{:S(2)}) collective-permute-start(bf16[256,256]{1,0:T(8,128)(2,1)S(1)} %get-tuple-element.711), channel_id=1, source_target_pairs={{128,0},{256,128},{384,256},{129,1},{257,129},{385,257},{130,2},{2... | collective-permute-start | bytes 393224 | tf_op jit(solution)/shard_map/while/body/eval_jaxpr/ppermute | solution.py:15
  316.5 7.6 %collective-permute-start = (bf16[256,256]{1,0:T(8,128)(2,1)S(1)}, bf16[256,256]{1,0:T(8,128)(2,1)S(1)}, u32[]{:S(2)}, u32[]{:S(2)}) collective-permute-start(bf16[256,256]{1,0:T(8,128)(2,1)S(1)} %get-tuple-element.711), channel_id=1, source_target_pairs={{128,0},{256,128},{384,256},{129,1},{257,129},{385,257},{130,2},{2... | collective-permute-start | bytes 393224 | tf_op jit(solution)/shard_map/while/body/eval_jaxpr/ppermute | solution.py:15
  332.3 8.1 %collective-permute-start = (bf16[256,256]{1,0:T(8,128)(2,1)S(1)}, bf16[256,256]{1,0:T(8,128)(2,1)S(1)}, u32[]{:S(2)}, u32[]{:S(2)}) collective-permute-start(bf16[256,256]{1,0:T(8,128)(2,1)S(1)} %get-tuple-element.711), channel_id=1, source_target_pairs={{128,0},{256,128},{384,256},{129,1},{257,129},{385,257},{130,2},{2... | collective-permute-start | bytes 393224 | tf_op jit(solution)/shard_map/while/body/eval_jaxpr/ppermute | solution.py:15
  348.6 6.9 %collective-permute-start = (bf16[256,256]{1,0:T(8,128)(2,1)S(1)}, bf16[256,256]{1,0:T(8,128)(2,1)S(1)}, u32[]{:S(2)}, u32[]{:S(2)}) collective-permute-start(bf16[256,256]{1,0:T(8,128)(2,1)S(1)} %get-tuple-element.711), channel_id=1, source_target_pairs={{128,0},{256,128},{384,256},{129,1},{257,129},{385,257},{130,2},{2... | collective-permute-start | bytes 393224 | tf_op jit(solution)/shard_map/while/body/eval_jaxpr/ppermute | solution.py:15
  363.8 6.8 %collective-permute-start = (bf16[256,256]{1,0:T(8,128)(2,1)S(1)}, bf16[256,256]{1,0:T(8,128)(2,1)S(1)}, u32[]{:S(2)}, u32[]{:S(2)}) collective-permute-start(bf16[256,256]{1,0:T(8,128)(2,1)S(1)} %get-tuple-element.711), channel_id=1, source_target_pairs={{128,0},{256,128},{384,256},{129,1},{257,129},{385,257},{130,2},{2... | collective-permute-start | bytes 393224 | tf_op jit(solution)/shard_map/while/body/eval_jaxpr/ppermute | solution.py:15
  385.1 26.9 %all-to-all-start.5 = ((bf16[16,128,128]{2,1,0:T(8,128)(2,1)}), bf16[16,128,128]{2,1,0:T(8,128)(2,1)S(1)}, u32[]{:S(2)}, u32[]{:S(2)}) async-start(bf16[16,128,128]{2,1,0:T(8,128)(2,1)} %convert_element_type.116), calls=%async_computation.5 | async-start | bytes 1048576 | tf_op jit(solution)/shard_map/all_to_all | solution.py:183
  397.2 21.7 %copy-start = (bf16[2304,256]{1,0:T(8,128)(2,1)S(1)}, bf16[2304,256]{1,0:T(8,128)(2,1)}, u32[]{:S(2)}) copy-start(bf16[2304,256]{1,0:T(8,128)(2,1)} %get-tuple-element.370) | copy-start | bytes 3538948
  411.9 26.5 %all-to-all-start.6 = ((bf16[16,128,128]{2,1,0:T(8,128)(2,1)}), bf16[16,128,128]{2,1,0:T(8,128)(2,1)S(1)}, u32[]{:S(2)}, u32[]{:S(2)}) async-start(bf16[16,128,128]{2,1,0:T(8,128)(2,1)} %convert_element_type.122), calls=%async_computation.6 | async-start | bytes 1048576 | tf_op jit(solution)/shard_map/all_to_all | solution.py:190
  438.4 42.5 %all-to-all-start.4 = ((bf16[16,128,256]{2,1,0:T(8,128)(2,1)}), bf16[16,128,256]{2,1,0:T(8,128)(2,1)S(1)}, u32[]{:S(2)}, u32[]{:S(2)}) async-start(bf16[16,128,256]{2,1,0:T(8,128)(2,1)} %bitcast.39), calls=%async_computation.4 | async-start | bytes 2097152 | tf_op jit(solution)/shard_map/all_to_all | solution.py:166

commit v4 on v3

--- a/solution.py
+++ b/solution.py
@@ -47,11 +47,20 @@
         .reshape(tok_local, kv_heads, HEAD_FEATURES)[:, slot_heads]
         .reshape(tok_local, ctx_count * slot_width)
     )
-    head_input, head_keys, head_values, head_top = (
-        lax.all_to_all(layer_input, "ctx", split_axis=1, concat_axis=0, tiled=True),
-        lax.all_to_all(sent_keys, "ctx", split_axis=1, concat_axis=0, tiled=True),
-        lax.all_to_all(sent_values, "ctx", split_axis=1, concat_axis=0, tiled=True),
-        lax.all_to_all(top_grad[0], "ctx", split_axis=1, concat_axis=0, tiled=True),
+    sent_widths = (local_width, local_width, slot_width, slot_width)
+    packed = jnp.concatenate(
+        [
+            piece.reshape(tok_local, ctx_count, width)
+            for piece, width in zip(
+                (layer_input, top_grad[0], sent_keys, sent_values), sent_widths
+            )
+        ],
+        axis=2,
+    ).reshape(tok_local, ctx_count * sum(sent_widths))
+    moved = lax.all_to_all(packed, "ctx", split_axis=1, concat_axis=0, tiled=True)
+    edges = np.cumsum((0,) + sent_widths)
+    head_input, head_top, head_keys, head_values = (
+        moved[:, edges[i] : edges[i + 1]] for i in range(len(sent_widths))
     )
     gain_row = query_gain[0]
     query_rows = (head_input.astype(jnp.float32) * gain_row).astype(jnp.bfloat16)
@@ -133,7 +142,6 @@
         unit = turn - (section_count - 1 - section_pos)
         active = (unit >= 0) & (unit < unit_count)
         safe_index = jnp.clip(unit, 0, unit_count - 1)
-        target = jnp.where(active, safe_index, unit_count)
         from_top = lax.dynamic_slice_in_dim(head_top, safe_index * turn_rows, turn_rows, 0)
         head_grad = jnp.where(on_top, from_top, incoming)
         query_grad, key_part, value_part, gain_part = lax.cond(
@@ -143,32 +151,32 @@
         handed = (head_grad.astype(jnp.float32) + moved_grad.astype(jnp.float32)).astype(
             jnp.bfloat16
         )
-        result_heads = lax.dynamic_update_slice_in_dim(result_heads, handed, target * turn_rows, 0)
-        key_slots = lax.dynamic_update_slice_in_dim(key_slots, key_part, target * per_turn, 0)
-        value_slots = lax.dynamic_update_slice_in_dim(value_slots, value_part, target * per_turn, 0)
+        def kept(array, part, size):
+            start = safe_index * size
+            old = lax.dynamic_slice_in_dim(array, start, size, 0)
+            return lax.dynamic_update_slice_in_dim(array, jnp.where(active, part, old), start, 0)
+
+        result_heads = kept(result_heads, handed, turn_rows)
+        key_slots = kept(key_slots, key_part, per_turn)
+        value_slots = kept(value_slots, value_part, per_turn)
         gain_acc = gain_acc + gain_part
         incoming = passed_along(handed, "section", -1)
         return (incoming, result_heads, key_slots, value_slots, gain_acc)
 
     first_incoming = jnp.zeros((turn_rows, local_width), jnp.bfloat16)
-    slot_zeros = jnp.zeros(
-        ((unit_count + 1) * per_turn, listed * block_rows, slot_width), jnp.float32
-    )
+    slot_zeros = jnp.zeros((unit_count * per_turn, listed * block_rows, slot_width), jnp.float32)
     start_carry = (
         first_incoming,
-        jnp.zeros(((unit_count + 1) * turn_rows, local_width), jnp.bfloat16),
+        jnp.zeros((unit_count * turn_rows, local_width), jnp.bfloat16),
         slot_zeros,
         slot_zeros,
         jnp.zeros((local_width,), jnp.float32),
     )
     final_carry = lax.fori_loop(0, turn_count, turn_step, start_carry)
     incoming, result_heads, key_slots, value_slots, gain_acc = final_carry
-    result_rows = lax.all_to_all(
-        result_heads[:total_rows], "ctx", split_axis=0, concat_axis=1, tiled=True
-    )
     target_labels = block_lists.reshape(-1)
-    key_pieces = key_slots[:block_count].reshape(block_count * listed, block_rows, slot_width)
-    value_pieces = value_slots[:block_count].reshape(block_count * listed, block_rows, slot_width)
+    key_pieces = key_slots.reshape(block_count * listed, block_rows, slot_width)
+    value_pieces = value_slots.reshape(block_count * listed, block_rows, slot_width)
     key_acc = (
         jnp.zeros((block_count, block_rows, slot_width), jnp.float32)
         .at[target_labels]
@@ -179,30 +187,33 @@
         .at[target_labels]
         .add(value_pieces)
     )
-    key_back, value_back = (
-        lax.all_to_all(
+    back_widths = (local_width, slot_width, slot_width)
+    sent_back = jnp.concatenate(
+        [
+            result_heads,
             key_acc.reshape(total_rows, slot_width).astype(jnp.bfloat16),
-            "ctx",
-            split_axis=0,
-            concat_axis=1,
-            tiled=True,
-        ).astype(jnp.float32),
-        lax.all_to_all(
             value_acc.reshape(total_rows, slot_width).astype(jnp.bfloat16),
-            "ctx",
-            split_axis=0,
-            concat_axis=1,
-            tiled=True,
-        ).astype(jnp.float32),
+        ],
+        axis=1,
+    )
+    came_back = lax.all_to_all(
+        sent_back, "ctx", split_axis=0, concat_axis=1, tiled=True
+    ).reshape(tok_local, ctx_count, sum(back_widths))
+    back_edges = np.cumsum((0,) + back_widths)
+    result_rows, key_back, value_back = (
+        came_back[:, :, back_edges[i] : back_edges[i + 1]].reshape(tok_local, -1)
+        for i in range(len(back_widths))
     )
     key_out = (
-        key_back.reshape(tok_local, kv_heads, repeats, HEAD_FEATURES)
+        key_back.astype(jnp.float32)
+        .reshape(tok_local, kv_heads, repeats, HEAD_FEATURES)
         .sum(axis=2)
         .reshape(tok_local, kv_width)
         .astype(jnp.bfloat16)
     )
     value_out = (
-        value_back.reshape(tok_local, kv_heads, repeats, HEAD_FEATURES)
+        value_back.astype(jnp.float32)
+        .reshape(tok_local, kv_heads, repeats, HEAD_FEATURES)
         .sum(axis=2)
         .reshape(tok_local, kv_width)
         .astype(jnp.bfloat16)

time: 485 us -> 512 us (1.056)
  other arithmetic: 51.8 us -> 115 us
  starting transfers between devices: 74.9 us -> 38.7 us
  local copies, waits for them, and re-layouts: 72.1 us -> 64.7 us
  matrix products: 12.1 us -> 19.3 us
    all_to_all x7 -> x2, starting transfers between devices: 60.8 us -> 24.7 us  [the longest x1 15.3 us: shards(): lax.all_to_all(packed, 'ctx', split_axis=1, concat_axis=0, tiled=True)]
    dynamic_update_slice x11 -> x22, other arithmetic: 7.49 us -> 43.6 us  [kept(): lax.dynamic_update_slice_in_dim(array, jnp.where(active, part, old), star...]
    ppermute x11, waiting for transfers between devices: 66 us -> 47 us  [passed_along(): return lax.ppermute(block, axis, route)]
    all_to_all x7 -> x2, waiting for transfers between devices: 193 us -> 210 us  [the longest x1 139 us: shards(): lax.all_to_all(packed, 'ctx', split_axis=1, concat_axis=0, tiled=True)]
    dynamic_update_slice x22 -> x0, local copies, waits for them, and re-layouts: 14 us -> none  [the longest x11 11.9 us: turn_step(): lax.dynamic_update_slice_in_dim(value_slots, value_part, target * per_tur...]
    add x11, other arithmetic: 0.13 us -> 13.8 us  [turn_step(): gain_acc = gain_acc + gain_part]
    reduce_sum x8, other arithmetic: 7.76 us -> 17.6 us  [attend(): gain_part = jnp.sum(input_now.astype(jnp.float32) * query_grad, axis=0)]
    gather x8, local copies, waits for them, and re-layouts: 4.77 us -> 13.1 us  [attend(): blocked_keys[lists_now]]
  transfers between devices with their start and end apart: 18 -> 13, of which waited for: 18 -> 13; matrix products, arithmetic and copies ran while one was open for 8% -> 8% of each run, Pallas kernels for 0% -> 0%
where the time goes in v4:
time: 512 us; the launch traced here: 508 us
  waiting for transfers between devices  257 us (50%)
  other arithmetic  115 us (22%)
  local copies, waits for them, and re-layouts  64.7 us (13%)
  starting transfers between devices  38.7 us (8%)
  matrix products  19.3 us (4%)
  blocking collectives  10.6 us (2%)
    all_to_all x1, waiting for transfers between devices, shards(): lax.all_to_all(packed, 'ctx', split_axis=1, concat_axis=0, tiled=True)  139 us
    all_to_all x1, waiting for transfers between devices, shards(): lax.all_to_all(sent_back, 'ctx', split_axis=0, concat_axis=1, tiled=True)  71.6 us
    ppermute x11, waiting for transfers between devices, passed_along(): return lax.ppermute(block, axis, route)  47 us
    dynamic_update_slice x22, other arithmetic, kept(): lax.dynamic_update_slice_in_dim(array, jnp.where(active, part, old), star...  43.6 us
    reduce_sum x8, other arithmetic, attend(): gain_part = jnp.sum(input_now.astype(jnp.float32) * query_grad, axis=0)  17.6 us
    all_to_all x1, starting transfers between devices, shards(): lax.all_to_all(packed, 'ctx', split_axis=1, concat_axis=0, tiled=True)  15.3 us
    ppermute x11, starting transfers between devices, passed_along(): return lax.ppermute(block, axis, route)  14.1 us
    add x11, other arithmetic, turn_step(): gain_acc = gain_acc + gain_part  13.8 us
  transfers between devices with their start and end apart: 13, of which 13 were waited for; matrix products, arithmetic and copies ran while one was open for 8% of the time, Pallas kernels for 0%

profile of v4, /device:TPU:6, one launch (start us, length us, event | category | flops | bytes accessed | tf_op | source)
XLA Modules:
  0.0 508.2 jit_solution(8373442158065680581)
XLA Ops:
  7.5 1.8 pad_maximum_fusion
  9.3 15.3 %all-to-all-start = ((bf16[128,16,768]{2,0,1:T(8,128)(2,1)}), bf16[128,16,768]{2,0,1:T(8,128)(2,1)S(1)}, u32[]{:S(2)}, u32[]{:S(2)}) async-start(bf16[128,16,768]{2,0,1:T(8,128)(2,1)} %pad_maximum_fusion), calls=%async_computation | async-start | bytes 6291456 | tf_op jit(solution)/shard_map/all_to_all | solution.py:60
  25.4 138.7 %all-to-all-done = bf16[128,16,768]{2,0,1:T(8,128)(2,1)S(1)} async-done(((bf16[128,16,768]{2,0,1:T(8,128)(2,1)}), bf16[128,16,768]{2,0,1:T(8,128)(2,1)S(1)}, u32[]{:S(2)}, u32[]{:S(2)}) %all-to-all-start) | async-done | bytes 3145760 | tf_op jit(solution)/shard_map/all_to_all | solution.py:60
  166.6 1.9 multiply_convert_fusion.2
  168.5 2.4 broadcast_in_dim.31
  170.8 2.4 broadcast_in_dim.31.clone
  175.0 214.1 %while.24 = (s32[]{:T(128)}, bf16[256,256]{1,0:T(8,128)(2,1)}, bf16[2048,256]{1,0:T(8,128)(2,1)}, f32[16,512,128]{2,1,0:T(8,128)}, f32[16,512,128]{2,1,0:T(8,128...) while((s32[]{:T(128)}, bf16[256,256]{1,0:T(8,128)(2,1)}, ...), condition=%wide.region_7.8_spmd.clone, body=%wide.region_0.7_spmd.clone.sunk | while | flops 340918048 | bytes 21266268 | solution.py:175
  177.3 1.7 select_dynamic-update-slice_fusion.5
  180.3 2.3 select_dynamic-update-slice_fusion.6
  183.8 2.2 collective-permute-done
  188.4 1.7 select_dynamic-update-slice_fusion.5
  191.4 2.3 select_dynamic-update-slice_fusion.6
  194.9 2.1 collective-permute-done
  199.4 1.7 select_dynamic-update-slice_fusion.5
  202.4 2.3 select_dynamic-update-slice_fusion.6
  206.0 25.7 %collective-permute-done = bf16[256,256]{1,0:T(8,128)(2,1)} collective-permute-done((bf16[256,256]{1,0:T(8,128)(2,1)S(1)}, bf16[256,256]{1,0:T(8,128)(2,1)}, u32[]{:S(2)}, u32[]{:S(2)}) %collective-permute-start) | collective-permute-done | bytes 131104 | tf_op jit(solution)/shard_map/while/body/eval_jaxpr/ppermute | solution.py:15
  232.7 10.0 %conditional.3 = (f32[256,256]{1,0:T(8,128)}, f32[2,512,128]{2,1,0:T(8,128)S(1)}, f32[256]{0:T(256)}, f32[2,512,128]{2,1,0:T(8,128)S(1)}) conditional(s32[]{:T(128)} %convert_element_type.152, () %tuple.83, (s32[]{:T(128)}, s32[16,4]{1,0:T(8,128)S(1)}, bf16[16,128,1,128]{3,1,0,2:T(8,128)(2,1)}, bf16[2048,256]{1,0:T(8,128)(2,1)}, ...), branch_computations={%region_1.1_spmd, %region_2.6_spmd} | conditional | flops 340131104 | bytes 16412036 | solution.py:147
  236.0 1.6 gather_fusion.1
  240.5 2.2 multiply_reduce_fusion.1
  242.7 1.7 select_dynamic-update-slice_fusion.5
  245.7 2.3 select_dynamic-update-slice_fusion.6
  249.2 2.1 collective-permute-done
  252.3 10.0 %conditional.3 = (f32[256,256]{1,0:T(8,128)}, f32[2,512,128]{2,1,0:T(8,128)S(1)}, f32[256]{0:T(256)}, f32[2,512,128]{2,1,0:T(8,128)S(1)}) conditional(s32[]{:T(128)} %convert_element_type.152, () %tuple.83, (s32[]{:T(128)}, s32[16,4]{1,0:T(8,128)S(1)}, bf16[16,128,1,128]{3,1,0,2:T(8,128)(2,1)}, bf16[2048,256]{1,0:T(8,128)(2,1)}, ...), branch_computations={%region_1.1_spmd, %region_2.6_spmd} | conditional | flops 340131104 | bytes 16412036 | solution.py:147
  260.2 2.2 multiply_reduce_fusion.1
  262.4 1.7 select_dynamic-update-slice_fusion.5
  265.4 2.3 select_dynamic-update-slice_fusion.6
  268.9 2.1 collective-permute-done
  272.0 10.0 %conditional.3 = (f32[256,256]{1,0:T(8,128)}, f32[2,512,128]{2,1,0:T(8,128)S(1)}, f32[256]{0:T(256)}, f32[2,512,128]{2,1,0:T(8,128)S(1)}) conditional(s32[]{:T(128)} %convert_element_type.152, () %tuple.83, (s32[]{:T(128)}, s32[16,4]{1,0:T(8,128)S(1)}, bf16[16,128,1,128]{3,1,0,2:T(8,128)(2,1)}, bf16[2048,256]{1,0:T(8,128)(2,1)}, ...), branch_computations={%region_1.1_spmd, %region_2.6_spmd} | conditional | flops 340131104 | bytes 16412036 | solution.py:147
  279.8 2.2 multiply_reduce_fusion.1
  282.0 1.7 select_dynamic-update-slice_fusion.5
  285.0 2.3 select_dynamic-update-slice_fusion.6
  288.6 2.1 collective-permute-done
  291.7 10.0 %conditional.3 = (f32[256,256]{1,0:T(8,128)}, f32[2,512,128]{2,1,0:T(8,128)S(1)}, f32[256]{0:T(256)}, f32[2,512,128]{2,1,0:T(8,128)S(1)}) conditional(s32[]{:T(128)} %convert_element_type.152, () %tuple.83, (s32[]{:T(128)}, s32[16,4]{1,0:T(8,128)S(1)}, bf16[16,128,1,128]{3,1,0,2:T(8,128)(2,1)}, bf16[2048,256]{1,0:T(8,128)(2,1)}, ...), branch_computations={%region_1.1_spmd, %region_2.6_spmd} | conditional | flops 340131104 | bytes 16412036 | solution.py:147
  299.5 2.2 multiply_reduce_fusion.1
  301.7 1.7 select_dynamic-update-slice_fusion.5
  304.7 2.3 select_dynamic-update-slice_fusion.6
  308.2 2.1 collective-permute-done
  311.4 10.0 %conditional.3 = (f32[256,256]{1,0:T(8,128)}, f32[2,512,128]{2,1,0:T(8,128)S(1)}, f32[256]{0:T(256)}, f32[2,512,128]{2,1,0:T(8,128)S(1)}) conditional(s32[]{:T(128)} %convert_element_type.152, () %tuple.83, (s32[]{:T(128)}, s32[16,4]{1,0:T(8,128)S(1)}, bf16[16,128,1,128]{3,1,0,2:T(8,128)(2,1)}, bf16[2048,256]{1,0:T(8,128)(2,1)}, ...), branch_computations={%region_1.1_spmd, %region_2.6_spmd} | conditional | flops 340131104 | bytes 16412036 | solution.py:147
  319.2 2.2 multiply_reduce_fusion.1
  321.4 1.7 select_dynamic-update-slice_fusion.5
  324.4 2.3 select_dynamic-update-slice_fusion.6
  327.9 2.1 collective-permute-done
  331.0 10.0 %conditional.3 = (f32[256,256]{1,0:T(8,128)}, f32[2,512,128]{2,1,0:T(8,128)S(1)}, f32[256]{0:T(256)}, f32[2,512,128]{2,1,0:T(8,128)S(1)}) conditional(s32[]{:T(128)} %convert_element_type.152, () %tuple.83, (s32[]{:T(128)}, s32[16,4]{1,0:T(8,128)S(1)}, bf16[16,128,1,128]{3,1,0,2:T(8,128)(2,1)}, bf16[2048,256]{1,0:T(8,128)(2,1)}, ...), branch_computations={%region_1.1_spmd, %region_2.6_spmd} | conditional | flops 340131104 | bytes 16412036 | solution.py:147
  338.8 2.2 multiply_reduce_fusion.1
  341.0 1.7 select_dynamic-update-slice_fusion.5
  344.0 2.3 select_dynamic-update-slice_fusion.6
  347.6 2.1 collective-permute-done
  350.7 10.0 %conditional.3 = (f32[256,256]{1,0:T(8,128)}, f32[2,512,128]{2,1,0:T(8,128)S(1)}, f32[256]{0:T(256)}, f32[2,512,128]{2,1,0:T(8,128)S(1)}) conditional(s32[]{:T(128)} %convert_element_type.152, () %tuple.83, (s32[]{:T(128)}, s32[16,4]{1,0:T(8,128)S(1)}, bf16[16,128,1,128]{3,1,0,2:T(8,128)(2,1)}, bf16[2048,256]{1,0:T(8,128)(2,1)}, ...), branch_computations={%region_1.1_spmd, %region_2.6_spmd} | conditional | flops 340131104 | bytes 16412036 | solution.py:147
  358.5 2.2 multiply_reduce_fusion.1
  360.7 1.7 select_dynamic-update-slice_fusion.5
  363.7 2.3 select_dynamic-update-slice_fusion.6
  367.2 2.1 collective-permute-done
  370.4 10.0 %conditional.3 = (f32[256,256]{1,0:T(8,128)}, f32[2,512,128]{2,1,0:T(8,128)S(1)}, f32[256]{0:T(256)}, f32[2,512,128]{2,1,0:T(8,128)S(1)}) conditional(s32[]{:T(128)} %convert_element_type.152, () %tuple.83, (s32[]{:T(128)}, s32[16,4]{1,0:T(8,128)S(1)}, bf16[16,128,1,128]{3,1,0,2:T(8,128)(2,1)}, bf16[2048,256]{1,0:T(8,128)(2,1)}, ...), branch_computations={%region_1.1_spmd, %region_2.6_spmd} | conditional | flops 340131104 | bytes 16412036 | solution.py:147
  373.7 1.6 gather_fusion.1
  378.2 2.2 multiply_reduce_fusion.1
  380.4 1.7 select_dynamic-update-slice_fusion.5
  383.4 2.3 select_dynamic-update-slice_fusion.6
  386.9 2.1 collective-permute-done
  389.2 9.0 %scatter_fusion = f32[16,128,128]{2,1,0:T(8,128)S(1)} fusion(f32[16,128,128]{2,1,0:T(8,128)S(1)} %broadcast.75.clone.1, s32[64]{0:T(128)} %fusion.12, f32[64,128,128]{2,1,0:T(8,128)} %bitcast.99), kind=kCustom, calls=%fused_computation.4 | custom fusion | flops 1048576 | bytes 12583168 | tf_op jit(solution)/shard_map/scatter-add | solution.py:183
  398.4 8.8 %scatter_fusion.1 = f32[16,128,128]{2,1,0:T(8,128)S(1)} fusion(f32[16,128,128]{2,1,0:T(8,128)S(1)} %broadcast.75.clone, s32[64]{0:T(128)S(1)} %copy-done.4, f32[64,128,128]{2,1,0:T(8,128)} %bitcast.100), kind=kCustom, calls=%fused_computation.5 | custom fusion | flops 1048576 | bytes 12583168 | tf_op jit(solution)/shard_map/scatter-add | solution.py:188
  408.9 9.3 %all-to-all-start.1 = ((bf16[16,128,512]{2,1,0:T(8,128)(2,1)}), bf16[16,128,512]{2,1,0:T(8,128)(2,1)S(1)}, u32[]{:S(2)}, u32[]{:S(2)}) async-start(bf16[16,128,512]{2,1,0:T(8,128)(2,1)} %bitcast.105), calls=%async_computation.1 | async-start | bytes 4194304 | tf_op jit(solution)/shard_map/all_to_all | solution.py:199
  418.2 10.6 %psum.7 = f32[1,256]{1,0:T(1,128)} all-reduce(f32[1,256]{1,0:T(1,128)S(1)} %bitcast.122), channel_id=1, replica_groups=mesh['section'=4,'ctx'=16,'dp'=8] {'dp'}, use_global_device_ids=true, to_apply=%region_12.13 | all-reduce | flops 256 | bytes 2048 | tf_op jit(solution)/shard_map/psum | solution.py:221
  428.8 71.6 %all-to-all-done.1 = bf16[16,128,512]{2,1,0:T(8,128)(2,1)S(1)} async-done(((bf16[16,128,512]{2,1,0:T(8,128)(2,1)}), bf16[16,128,512]{2,1,0:T(8,128)(2,1)S(1)}, u32[]{:S(2)}, u32[]{:S(2)}) %all-to-all-start.1) | async-done | bytes 2097184 | tf_op jit(solution)/shard_map/all_to_all | solution.py:199
  500.4 2.4 copy.116
  (245 shorter events, 124.5 us)
Async XLA Ops:
  0.6 6.2 %copy-start.2 = (bf16[1,128,4096]{2,1,0:T(8,128)(2,1)S(1)}, bf16[1,128,4096]{2,1,0:T(8,128)(2,1)}, u32[]{:S(2)}) copy-start(bf16[1,128,4096]{2,1,0:T(8,128)(2,1)} %param.17) | copy-start | bytes 3145732
  9.3 15.4 %copy-start.5 = (s32[16,4]{0,1:T(4,128)S(1)}, s32[16,4]{0,1:T(4,128)}, u32[]{:S(2)}) copy-start(s32[16,4]{0,1:T(4,128)} %param.18) | copy-start | bytes 772
  9.3 154.7 %all-to-all-start = ((bf16[128,16,768]{2,0,1:T(8,128)(2,1)}), bf16[128,16,768]{2,0,1:T(8,128)(2,1)S(1)}, u32[]{:S(2)}, u32[]{:S(2)}) async-start(bf16[128,16,768]{2,0,1:T(8,128)(2,1)} %pad_maximum_fusion), calls=%async_computation | async-start | bytes 6291456 | tf_op jit(solution)/shard_map/all_to_all | solution.py:60
  179.0 7.0 %collective-permute-start = (bf16[256,256]{1,0:T(8,128)(2,1)S(1)}, bf16[256,256]{1,0:T(8,128)(2,1)}, u32[]{:S(2)}, u32[]{:S(2)}) collective-permute-start(bf16[256,256]{1,0:T(8,128)(2,1)S(1)} %get-tuple-element.695), channel_id=1, source_target_pairs={{128,0},{256,128},{384,256},{129,1},{257,129},{385,257},{130,2},{2... | collective-permute-start | bytes 393224 | tf_op jit(solution)/shard_map/while/body/eval_jaxpr/ppermute | solution.py:15
  190.1 7.0 %collective-permute-start = (bf16[256,256]{1,0:T(8,128)(2,1)S(1)}, bf16[256,256]{1,0:T(8,128)(2,1)}, u32[]{:S(2)}, u32[]{:S(2)}) collective-permute-start(bf16[256,256]{1,0:T(8,128)(2,1)S(1)} %get-tuple-element.695), channel_id=1, source_target_pairs={{128,0},{256,128},{384,256},{129,1},{257,129},{385,257},{130,2},{2... | collective-permute-start | bytes 393224 | tf_op jit(solution)/shard_map/while/body/eval_jaxpr/ppermute | solution.py:15
  201.1 30.5 %collective-permute-start = (bf16[256,256]{1,0:T(8,128)(2,1)S(1)}, bf16[256,256]{1,0:T(8,128)(2,1)}, u32[]{:S(2)}, u32[]{:S(2)}) collective-permute-start(bf16[256,256]{1,0:T(8,128)(2,1)S(1)} %get-tuple-element.695), channel_id=1, source_target_pairs={{128,0},{256,128},{384,256},{129,1},{257,129},{385,257},{130,2},{2... | collective-permute-start | bytes 393224 | tf_op jit(solution)/shard_map/while/body/eval_jaxpr/ppermute | solution.py:15
  237.7 0.9 copy-start.1
  244.4 7.0 %collective-permute-start = (bf16[256,256]{1,0:T(8,128)(2,1)S(1)}, bf16[256,256]{1,0:T(8,128)(2,1)}, u32[]{:S(2)}, u32[]{:S(2)}) collective-permute-start(bf16[256,256]{1,0:T(8,128)(2,1)S(1)} %get-tuple-element.695), channel_id=1, source_target_pairs={{128,0},{256,128},{384,256},{129,1},{257,129},{385,257},{130,2},{2... | collective-permute-start | bytes 393224 | tf_op jit(solution)/shard_map/while/body/eval_jaxpr/ppermute | solution.py:15
  257.4 0.9 copy-start.1
  264.1 7.0 %collective-permute-start = (bf16[256,256]{1,0:T(8,128)(2,1)S(1)}, bf16[256,256]{1,0:T(8,128)(2,1)}, u32[]{:S(2)}, u32[]{:S(2)}) collective-permute-start(bf16[256,256]{1,0:T(8,128)(2,1)S(1)} %get-tuple-element.695), channel_id=1, source_target_pairs={{128,0},{256,128},{384,256},{129,1},{257,129},{385,257},{130,2},{2... | collective-permute-start | bytes 393224 | tf_op jit(solution)/shard_map/while/body/eval_jaxpr/ppermute | solution.py:15
  277.1 0.9 copy-start.1
  283.7 7.0 %collective-permute-start = (bf16[256,256]{1,0:T(8,128)(2,1)S(1)}, bf16[256,256]{1,0:T(8,128)(2,1)}, u32[]{:S(2)}, u32[]{:S(2)}) collective-permute-start(bf16[256,256]{1,0:T(8,128)(2,1)S(1)} %get-tuple-element.695), channel_id=1, source_target_pairs={{128,0},{256,128},{384,256},{129,1},{257,129},{385,257},{130,2},{2... | collective-permute-start | bytes 393224 | tf_op jit(solution)/shard_map/while/body/eval_jaxpr/ppermute | solution.py:15
  296.7 0.9 copy-start.1
  303.4 7.0 %collective-permute-start = (bf16[256,256]{1,0:T(8,128)(2,1)S(1)}, bf16[256,256]{1,0:T(8,128)(2,1)}, u32[]{:S(2)}, u32[]{:S(2)}) collective-permute-start(bf16[256,256]{1,0:T(8,128)(2,1)S(1)} %get-tuple-element.695), channel_id=1, source_target_pairs={{128,0},{256,128},{384,256},{129,1},{257,129},{385,257},{130,2},{2... | collective-permute-start | bytes 393224 | tf_op jit(solution)/shard_map/while/body/eval_jaxpr/ppermute | solution.py:15
  316.4 0.9 copy-start.1
  323.1 7.0 %collective-permute-start = (bf16[256,256]{1,0:T(8,128)(2,1)S(1)}, bf16[256,256]{1,0:T(8,128)(2,1)}, u32[]{:S(2)}, u32[]{:S(2)}) collective-permute-start(bf16[256,256]{1,0:T(8,128)(2,1)S(1)} %get-tuple-element.695), channel_id=1, source_target_pairs={{128,0},{256,128},{384,256},{129,1},{257,129},{385,257},{130,2},{2... | collective-permute-start | bytes 393224 | tf_op jit(solution)/shard_map/while/body/eval_jaxpr/ppermute | solution.py:15
  336.1 0.9 copy-start.1
  342.7 7.0 %collective-permute-start = (bf16[256,256]{1,0:T(8,128)(2,1)S(1)}, bf16[256,256]{1,0:T(8,128)(2,1)}, u32[]{:S(2)}, u32[]{:S(2)}) collective-permute-start(bf16[256,256]{1,0:T(8,128)(2,1)S(1)} %get-tuple-element.695), channel_id=1, source_target_pairs={{128,0},{256,128},{384,256},{129,1},{257,129},{385,257},{130,2},{2... | collective-permute-start | bytes 393224 | tf_op jit(solution)/shard_map/while/body/eval_jaxpr/ppermute | solution.py:15
  355.7 0.9 copy-start.1
  362.4 7.0 %collective-permute-start = (bf16[256,256]{1,0:T(8,128)(2,1)S(1)}, bf16[256,256]{1,0:T(8,128)(2,1)}, u32[]{:S(2)}, u32[]{:S(2)}) collective-permute-start(bf16[256,256]{1,0:T(8,128)(2,1)S(1)} %get-tuple-element.695), channel_id=1, source_target_pairs={{128,0},{256,128},{384,256},{129,1},{257,129},{385,257},{130,2},{2... | collective-permute-start | bytes 393224 | tf_op jit(solution)/shard_map/while/body/eval_jaxpr/ppermute | solution.py:15
  375.4 0.9 copy-start.1
  382.1 7.0 %collective-permute-start = (bf16[256,256]{1,0:T(8,128)(2,1)S(1)}, bf16[256,256]{1,0:T(8,128)(2,1)}, u32[]{:S(2)}, u32[]{:S(2)}) collective-permute-start(bf16[256,256]{1,0:T(8,128)(2,1)S(1)} %get-tuple-element.695), channel_id=1, source_target_pairs={{128,0},{256,128},{384,256},{129,1},{257,129},{385,257},{130,2},{2... | collective-permute-start | bytes 393224 | tf_op jit(solution)/shard_map/while/body/eval_jaxpr/ppermute | solution.py:15
  389.1 9.3 %copy-start.4 = (s32[64]{0:T(128)S(1)}, s32[64]{0:T(128)}, u32[]{:S(2)}) copy-start(s32[64]{0:T(128)} %fusion.12) | copy-start | bytes 772
  398.4 8.9 %copy-start = (bf16[2048,256]{1,0:T(8,128)(2,1)S(1)}, bf16[2048,256]{1,0:T(8,128)(2,1)}, u32[]{:S(2)}) copy-start(bf16[2048,256]{1,0:T(8,128)(2,1)} %get-tuple-element.370) | copy-start | bytes 3145732
  407.3 10.9 %copy-start.3 = (f32[256]{0:T(256)S(1)}, f32[256]{0:T(256)}, u32[]{:S(2)}) copy-start(f32[256]{0:T(256)} %get-tuple-element.373) | copy-start | bytes 3076
  408.9 91.5 %all-to-all-start.1 = ((bf16[16,128,512]{2,1,0:T(8,128)(2,1)}), bf16[16,128,512]{2,1,0:T(8,128)(2,1)S(1)}, u32[]{:S(2)}, u32[]{:S(2)}) async-start(bf16[16,128,512]{2,1,0:T(8,128)(2,1)} %bitcast.105), calls=%async_computation.1 | async-start | bytes 4194304 | tf_op jit(solution)/shard_map/all_to_all | solution.py:199

commit v5 on v3

--- a/solution.py
+++ b/solution.py
@@ -47,11 +47,20 @@
         .reshape(tok_local, kv_heads, HEAD_FEATURES)[:, slot_heads]
         .reshape(tok_local, ctx_count * slot_width)
     )
-    head_input, head_keys, head_values, head_top = (
-        lax.all_to_all(layer_input, "ctx", split_axis=1, concat_axis=0, tiled=True),
-        lax.all_to_all(sent_keys, "ctx", split_axis=1, concat_axis=0, tiled=True),
-        lax.all_to_all(sent_values, "ctx", split_axis=1, concat_axis=0, tiled=True),
-        lax.all_to_all(top_grad[0], "ctx", split_axis=1, concat_axis=0, tiled=True),
+    sent_widths = (local_width, local_width, slot_width, slot_width)
+    packed = jnp.concatenate(
+        [
+            piece.reshape(tok_local, ctx_count, width)
+            for piece, width in zip(
+                (layer_input, top_grad[0], sent_keys, sent_values), sent_widths
+            )
+        ],
+        axis=2,
+    ).reshape(tok_local, ctx_count * sum(sent_widths))
+    moved = lax.all_to_all(packed, "ctx", split_axis=1, concat_axis=0, tiled=True)
+    edges = np.cumsum((0,) + sent_widths)
+    head_input, head_top, head_keys, head_values = lax.optimization_barrier(
+        tuple(moved[:, edges[i] : edges[i + 1]] for i in range(len(sent_widths)))
     )
     gain_row = query_gain[0]
     query_rows = (head_input.astype(jnp.float32) * gain_row).astype(jnp.bfloat16)

time: 485 us -> 457 us (0.942)
  starting transfers between devices: 74.9 us -> 53.3 us
  waiting for transfers between devices: 259 us -> 249 us
    all_to_all x4 -> x1, starting transfers between devices: 35.8 us -> 15.3 us  [shards(): lax.all_to_all(packed, 'ctx', split_axis=1, concat_axis=0, tiled=True)]
    all_to_all x4 -> x1, waiting for transfers between devices: 150 us -> 139 us  [shards(): lax.all_to_all(packed, 'ctx', split_axis=1, concat_axis=0, tiled=True)]
    gather x8, local copies, waits for them, and re-layouts: 4.77 us -> 13.1 us  [attend(): blocked_keys[lists_now]]
    gather x8, local copies, waits for them, and re-layouts: 13.1 us -> 4.78 us  [attend(): blocked_values[lists_now]]
  transfers between devices with their start and end apart: 18 -> 15, of which waited for: 18 -> 15; matrix products, arithmetic and copies ran while one was open for 8% -> 7% of each run, Pallas kernels for 0% -> 0%
where the time goes in v5:
time: 457 us; the launch traced here: 452 us
  waiting for transfers between devices  249 us (54%)
  local copies, waits for them, and re-layouts  72.2 us (16%)
  starting transfers between devices  53.3 us (12%)
  other arithmetic  52.5 us (11%)
  matrix products  12.1 us (3%)
  blocking collectives  10.9 us (2%)
    all_to_all x1, waiting for transfers between devices, shards(): lax.all_to_all(packed, 'ctx', split_axis=1, concat_axis=0, tiled=True)  139 us
    ppermute x11, waiting for transfers between devices, passed_along(): return lax.ppermute(block, axis, route)  65 us
    all_to_all x1, waiting for transfers between devices, shards(): lax.all_to_all(result_heads[:total_rows], 'ctx', split_axis=0, concat_axi...  24 us
    all_to_all x1, waiting for transfers between devices, shards(): lax.all_to_all(value_acc.reshape(total_rows, slot_width).astype(jnp.bfloa...  16.8 us
    all_to_all x1, starting transfers between devices, shards(): lax.all_to_all(packed, 'ctx', split_axis=1, concat_axis=0, tiled=True)  15.3 us
    ppermute x11, starting transfers between devices, passed_along(): return lax.ppermute(block, axis, route)  14.1 us
    gather x8, local copies, waits for them, and re-layouts, attend(): blocked_keys[lists_now]  13.1 us
    dynamic_update_slice x11, local copies, waits for them, and re-layouts, turn_step(): lax.dynamic_update_slice_in_dim(value_slots, value_part, target * per_tur...  12 us
  transfers between devices with their start and end apart: 15, of which 15 were waited for; matrix products, arithmetic and copies ran while one was open for 7% of the time, Pallas kernels for 0%

profile of v5, /device:TPU:6, one launch (start us, length us, event | category | flops | bytes accessed | tf_op | source)
XLA Modules:
  0.0 452.3 jit_solution(15123260246855516666)
XLA Ops:
  5.0 1.5 copy.160
  7.5 1.8 pad_maximum_fusion
  9.3 15.3 %all-to-all-start = ((bf16[128,16,768]{2,0,1:T(8,128)(2,1)}), bf16[128,16,768]{2,0,1:T(8,128)(2,1)S(1)}, u32[]{:S(2)}, u32[]{:S(2)}) async-start(bf16[128,16,768]{2,0,1:T(8,128)(2,1)} %pad_maximum_fusion), calls=%async_computation | async-start | bytes 6291456 | tf_op jit(solution)/shard_map/all_to_all | solution.py:60
  24.9 139.2 %all-to-all-done = bf16[128,16,768]{2,0,1:T(8,128)(2,1)S(1)} async-done(((bf16[128,16,768]{2,0,1:T(8,128)(2,1)}), bf16[128,16,768]{2,0,1:T(8,128)(2,1)S(1)}, u32[]{:S(2)}, u32[]{:S(2)}) %all-to-all-start) | async-done | bytes 3145760 | tf_op jit(solution)/shard_map/all_to_all | solution.py:60
  164.1 1.1 fusion.15
  166.2 1.2 multiply_convert_fusion.2
  167.5 2.6 broadcast_in_dim.34.clone
  170.1 2.7 broadcast_in_dim.34.clone2
  172.8 1.1 broadcast_in_dim.33
  173.9 165.1 %while.24 = (s32[]{:T(128)}, bf16[256,256]{1,0:T(8,128)(2,1)S(1)}, bf16[2304,256]{1,0:T(8,128)(2,1)}, f32[18,512,128]{2,1,0:T(8,128)}, f32[18,512,128]{2,1,0:T(8...) while((s32[]{:T(128)}, bf16[256,256]{1,0:T(8,128)(2,1)S(1)}, ...), condition=%wide.region_7.8_spmd.clone, body=%wide.region_0.7_spmd.clone.sunk | while | flops 340590400 | bytes 19562376 | solution.py:173
  175.7 1.3 collective-permute-start
  177.3 1.1 constant_dynamic-update-slice_fusion.6
  178.4 4.2 collective-permute-done
  184.4 1.3 collective-permute-start
  185.9 1.1 constant_dynamic-update-slice_fusion.6
  187.0 4.2 collective-permute-done
  193.0 1.3 collective-permute-start
  194.5 1.1 constant_dynamic-update-slice_fusion.6
  195.6 21.4 %collective-permute-done = bf16[256,256]{1,0:T(8,128)(2,1)S(1)} collective-permute-done((bf16[256,256]{1,0:T(8,128)(2,1)S(1)}, bf16[256,256]{1,0:T(8,128)(2,1)S(1)}, u32[]{:S(2)}, u32[]{:S(2)}) %collective-permute-start) | collective-permute-done | bytes 131104 | tf_op jit(solution)/shard_map/while/body/eval_jaxpr/ppermute | solution.py:15
  218.0 6.6 %conditional.3 = (f32[256,256]{1,0:T(8,128)S(1)}, f32[2,512,128]{1,2,0:T(8,128)S(1)}, f32[2,512,128]{2,1,0:T(8,128)S(1)}, f32[256]{0:T(256)S(1)}) conditional(s32[]{:T(128)} %convert_element_type.154, () %tuple.85, (s32[]{:T(128)}, s32[16,4]{1,0:T(8,128)S(1)}, bf16[16,128,1,128]{3,1,0,2:T(8,128)(2,1)}, bf16[2048,256]{1,0:T(8,128)(2,1)}, ...), branch_computations={%region_1.1_spmd, %region_2.6_spmd} | conditional | flops 340131104 | bytes 14839144 | solution.py:148
  219.2 1.6 gather_fusion
  225.3 1.3 collective-permute-start
  227.9 4.3 collective-permute-done
  233.1 6.6 %conditional.3 = (f32[256,256]{1,0:T(8,128)S(1)}, f32[2,512,128]{1,2,0:T(8,128)S(1)}, f32[2,512,128]{2,1,0:T(8,128)S(1)}, f32[256]{0:T(256)S(1)}) conditional(s32[]{:T(128)} %convert_element_type.154, () %tuple.85, (s32[]{:T(128)}, s32[16,4]{1,0:T(8,128)S(1)}, bf16[16,128,1,128]{3,1,0,2:T(8,128)(2,1)}, bf16[2048,256]{1,0:T(8,128)(2,1)}, ...), branch_computations={%region_1.1_spmd, %region_2.6_spmd} | conditional | flops 340131104 | bytes 14839144 | solution.py:148
  234.3 1.6 gather_fusion
  240.4 1.3 collective-permute-start
  243.0 4.2 collective-permute-done
  248.2 6.6 %conditional.3 = (f32[256,256]{1,0:T(8,128)S(1)}, f32[2,512,128]{1,2,0:T(8,128)S(1)}, f32[2,512,128]{2,1,0:T(8,128)S(1)}, f32[256]{0:T(256)S(1)}) conditional(s32[]{:T(128)} %convert_element_type.154, () %tuple.85, (s32[]{:T(128)}, s32[16,4]{1,0:T(8,128)S(1)}, bf16[16,128,1,128]{3,1,0,2:T(8,128)(2,1)}, bf16[2048,256]{1,0:T(8,128)(2,1)}, ...), branch_computations={%region_1.1_spmd, %region_2.6_spmd} | conditional | flops 340131104 | bytes 14839144 | solution.py:148
  249.4 1.6 gather_fusion
  255.5 1.3 collective-permute-start
  258.1 4.2 collective-permute-done
  263.3 6.6 %conditional.3 = (f32[256,256]{1,0:T(8,128)S(1)}, f32[2,512,128]{1,2,0:T(8,128)S(1)}, f32[2,512,128]{2,1,0:T(8,128)S(1)}, f32[256]{0:T(256)S(1)}) conditional(s32[]{:T(128)} %convert_element_type.154, () %tuple.85, (s32[]{:T(128)}, s32[16,4]{1,0:T(8,128)S(1)}, bf16[16,128,1,128]{3,1,0,2:T(8,128)(2,1)}, bf16[2048,256]{1,0:T(8,128)(2,1)}, ...), branch_computations={%region_1.1_spmd, %region_2.6_spmd} | conditional | flops 340131104 | bytes 14839144 | solution.py:148
  264.5 1.6 gather_fusion
  270.6 1.3 collective-permute-start
  272.1 1.1 constant_dynamic-update-slice_fusion.6
  273.2 4.2 collective-permute-done
  278.4 6.6 %conditional.3 = (f32[256,256]{1,0:T(8,128)S(1)}, f32[2,512,128]{1,2,0:T(8,128)S(1)}, f32[2,512,128]{2,1,0:T(8,128)S(1)}, f32[256]{0:T(256)S(1)}) conditional(s32[]{:T(128)} %convert_element_type.154, () %tuple.85, (s32[]{:T(128)}, s32[16,4]{1,0:T(8,128)S(1)}, bf16[16,128,1,128]{3,1,0,2:T(8,128)(2,1)}, bf16[2048,256]{1,0:T(8,128)(2,1)}, ...), branch_computations={%region_1.1_spmd, %region_2.6_spmd} | conditional | flops 340131104 | bytes 14839144 | solution.py:148
  279.6 1.6 gather_fusion
  285.7 1.3 collective-permute-start
  288.3 4.3 collective-permute-done
  293.5 6.6 %conditional.3 = (f32[256,256]{1,0:T(8,128)S(1)}, f32[2,512,128]{1,2,0:T(8,128)S(1)}, f32[2,512,128]{2,1,0:T(8,128)S(1)}, f32[256]{0:T(256)S(1)}) conditional(s32[]{:T(128)} %convert_element_type.154, () %tuple.85, (s32[]{:T(128)}, s32[16,4]{1,0:T(8,128)S(1)}, bf16[16,128,1,128]{3,1,0,2:T(8,128)(2,1)}, bf16[2048,256]{1,0:T(8,128)(2,1)}, ...), branch_computations={%region_1.1_spmd, %region_2.6_spmd} | conditional | flops 340131104 | bytes 14839144 | solution.py:148
  294.7 1.6 gather_fusion
  300.8 1.3 collective-permute-start
  303.4 4.2 collective-permute-done
  308.6 6.6 %conditional.3 = (f32[256,256]{1,0:T(8,128)S(1)}, f32[2,512,128]{1,2,0:T(8,128)S(1)}, f32[2,512,128]{2,1,0:T(8,128)S(1)}, f32[256]{0:T(256)S(1)}) conditional(s32[]{:T(128)} %convert_element_type.154, () %tuple.85, (s32[]{:T(128)}, s32[16,4]{1,0:T(8,128)S(1)}, bf16[16,128,1,128]{3,1,0,2:T(8,128)(2,1)}, bf16[2048,256]{1,0:T(8,128)(2,1)}, ...), branch_computations={%region_1.1_spmd, %region_2.6_spmd} | conditional | flops 340131104 | bytes 14839144 | solution.py:148
  309.8 1.6 gather_fusion
  315.9 1.3 collective-permute-start
  318.5 5.4 %collective-permute-done = bf16[256,256]{1,0:T(8,128)(2,1)S(1)} collective-permute-done((bf16[256,256]{1,0:T(8,128)(2,1)S(1)}, bf16[256,256]{1,0:T(8,128)(2,1)S(1)}, u32[]{:S(2)}, u32[]{:S(2)}) %collective-permute-start) | collective-permute-done | bytes 131104 | tf_op jit(solution)/shard_map/while/body/eval_jaxpr/ppermute | solution.py:15
  324.9 6.6 %conditional.3 = (f32[256,256]{1,0:T(8,128)S(1)}, f32[2,512,128]{1,2,0:T(8,128)S(1)}, f32[2,512,128]{2,1,0:T(8,128)S(1)}, f32[256]{0:T(256)S(1)}) conditional(s32[]{:T(128)} %convert_element_type.154, () %tuple.85, (s32[]{:T(128)}, s32[16,4]{1,0:T(8,128)S(1)}, bf16[16,128,1,128]{3,1,0,2:T(8,128)(2,1)}, bf16[2048,256]{1,0:T(8,128)(2,1)}, ...), branch_computations={%region_1.1_spmd, %region_2.6_spmd} | conditional | flops 340131104 | bytes 14839144 | solution.py:148
  326.1 1.6 gather_fusion
  332.2 1.3 collective-permute-start
  334.8 4.3 collective-permute-done
  339.0 4.7 %slice.26 = f32[16,512,128]{2,1,0:T(8,128)} slice(f32[18,512,128]{2,1,0:T(8,128)} %get-tuple-element.379), slice={[0:16], [0:512], [0:128]} | slice | bytes 8388608 | tf_op jit(solution)/shard_map/slice | solution.py:179
  343.8 8.8 %scatter_fusion = f32[16,128,128]{2,1,0:T(8,128)S(1)} fusion(f32[16,128,128]{2,1,0:T(8,128)S(1)} %broadcast.75.clone, s32[64]{0:T(128)S(1)} %fusion.12, f32[64,128,128]{2,1,0:T(8,128)} %bitcast.104), kind=kCustom, calls=%fused_computation.4 | custom fusion | flops 1048576 | bytes 12583168 | tf_op jit(solution)/shard_map/scatter-add | solution.py:184
  353.5 8.1 %all-to-all-start.2 = ((bf16[16,128,128]{2,1,0:T(8,128)(2,1)}), bf16[16,128,128]{2,1,0:T(8,128)(2,1)S(1)}, u32[]{:S(2)}, u32[]{:S(2)}) async-start(bf16[16,128,128]{2,1,0:T(8,128)(2,1)} %convert_element_type.116), calls=%async_computation.2 | async-start | bytes 1048576 | tf_op jit(solution)/shard_map/all_to_all | solution.py:192
  361.6 4.5 slice.27
  366.2 8.8 %scatter_fusion.1 = f32[16,128,128]{2,1,0:T(8,128)S(1)} fusion(f32[16,128,128]{2,1,0:T(8,128)S(1)} %broadcast.75.clone.1, s32[64]{0:T(128)S(1)} %fusion.12, f32[64,128,128]{2,1,0:T(8,128)} %bitcast.103), kind=kCustom, calls=%fused_computation.5 | custom fusion | flops 1048576 | bytes 12583168 | tf_op jit(solution)/shard_map/scatter-add | solution.py:189
  375.9 4.0 all-to-all-done.2
  379.8 8.1 %all-to-all-start.3 = ((bf16[16,128,128]{2,1,0:T(8,128)(2,1)}), bf16[16,128,128]{2,1,0:T(8,128)(2,1)S(1)}, u32[]{:S(2)}, u32[]{:S(2)}) async-start(bf16[16,128,128]{2,1,0:T(8,128)(2,1)} %convert_element_type.122), calls=%async_computation.3 | async-start | bytes 1048576 | tf_op jit(solution)/shard_map/all_to_all | solution.py:199
  389.0 16.8 %all-to-all-done.3 = bf16[16,128,128]{2,1,0:T(8,128)(2,1)S(1)} async-done(((bf16[16,128,128]{2,1,0:T(8,128)(2,1)}), bf16[16,128,128]{2,1,0:T(8,128)(2,1)S(1)}, u32[]{:S(2)}, u32[]{:S(2)}) %all-to-all-start.3) | async-done | bytes 524320 | tf_op jit(solution)/shard_map/all_to_all | solution.py:199
  405.8 7.7 %all-to-all-start.1 = ((bf16[16,128,256]{2,1,0:T(8,128)(2,1)}), bf16[16,128,256]{2,1,0:T(8,128)(2,1)S(1)}, u32[]{:S(2)}, u32[]{:S(2)}) async-start(bf16[16,128,256]{2,1,0:T(8,128)(2,1)} %bitcast.36), calls=%async_computation.1 | async-start | bytes 2097152 | tf_op jit(solution)/shard_map/all_to_all | solution.py:175
  413.5 10.9 %psum.7 = f32[1,256]{1,0:T(1,128)} all-reduce(f32[1,256]{1,0:T(1,128)S(1)} %bitcast.123), channel_id=1, replica_groups=mesh['section'=4,'ctx'=16,'dp'=8] {'dp'}, use_global_device_ids=true, to_apply=%region_12.13 | all-reduce | flops 256 | bytes 2048 | tf_op jit(solution)/shard_map/psum | solution.py:219
  426.3 24.0 %all-to-all-done.1 = bf16[16,128,256]{2,1,0:T(8,128)(2,1)S(1)} async-done(((bf16[16,128,256]{2,1,0:T(8,128)(2,1)}), bf16[16,128,256]{2,1,0:T(8,128)(2,1)S(1)}, u32[]{:S(2)}, u32[]{:S(2)}) %all-to-all-start.1) | async-done | bytes 1048608 | tf_op jit(solution)/shard_map/all_to_all | solution.py:175
  451.0 1.3 copy.145
  (242 shorter events, 79.6 us)
Async XLA Ops:
  0.6 6.2 %copy-start.3 = (bf16[1,128,4096]{2,1,0:T(8,128)(2,1)S(1)}, bf16[1,128,4096]{2,1,0:T(8,128)(2,1)}, u32[]{:S(2)}) copy-start(bf16[1,128,4096]{2,1,0:T(8,128)(2,1)} %param.17) | copy-start | bytes 3145732
  9.3 15.4 %copy-start.5 = (s32[16,4]{0,1:T(4,128)S(1)}, s32[16,4]{0,1:T(4,128)}, u32[]{:S(2)}) copy-start(s32[16,4]{0,1:T(4,128)} %param.18) | copy-start | bytes 772
  9.3 154.7 %all-to-all-start = ((bf16[128,16,768]{2,0,1:T(8,128)(2,1)}), bf16[128,16,768]{2,0,1:T(8,128)(2,1)S(1)}, u32[]{:S(2)}, u32[]{:S(2)}) async-start(bf16[128,16,768]{2,0,1:T(8,128)(2,1)} %pad_maximum_fusion), calls=%async_computation | async-start | bytes 6291456 | tf_op jit(solution)/shard_map/all_to_all | solution.py:60
  24.7 141.6 %copy-start.4 = (f32[1,256]{1,0:T(1,128)S(1)}, f32[1,256]{1,0:T(1,128)}, u32[]{:S(2)}) copy-start(f32[1,256]{1,0:T(1,128)} %param.16) | copy-start | bytes 3076
  165.2 4.9 %copy-start = (bf16[2048,256]{1,0:T(8,128)(2,1)}, bf16[2048,256]{1,0:T(8,128)(2,1)S(1)}, u32[]{:S(2)}) copy-start(bf16[2048,256]{1,0:T(8,128)(2,1)S(1)} %get-tuple-element.752) | copy-start | bytes 3145732
  170.1 3.8 copy-start.1
  175.7 6.8 %collective-permute-start = (bf16[256,256]{1,0:T(8,128)(2,1)S(1)}, bf16[256,256]{1,0:T(8,128)(2,1)S(1)}, u32[]{:S(2)}, u32[]{:S(2)}) collective-permute-start(bf16[256,256]{1,0:T(8,128)(2,1)S(1)} %get-tuple-element.723), channel_id=1, source_target_pairs={{128,0},{256,128},{384,256},{129,1},{257,129},{385,257},{130,2},{2... | collective-permute-start | bytes 393224 | tf_op jit(solution)/shard_map/while/body/eval_jaxpr/ppermute | solution.py:15
  184.4 6.8 %collective-permute-start = (bf16[256,256]{1,0:T(8,128)(2,1)S(1)}, bf16[256,256]{1,0:T(8,128)(2,1)S(1)}, u32[]{:S(2)}, u32[]{:S(2)}) collective-permute-start(bf16[256,256]{1,0:T(8,128)(2,1)S(1)} %get-tuple-element.723), channel_id=1, source_target_pairs={{128,0},{256,128},{384,256},{129,1},{257,129},{385,257},{130,2},{2... | collective-permute-start | bytes 393224 | tf_op jit(solution)/shard_map/while/body/eval_jaxpr/ppermute | solution.py:15
  193.0 24.0 %collective-permute-start = (bf16[256,256]{1,0:T(8,128)(2,1)S(1)}, bf16[256,256]{1,0:T(8,128)(2,1)S(1)}, u32[]{:S(2)}, u32[]{:S(2)}) collective-permute-start(bf16[256,256]{1,0:T(8,128)(2,1)S(1)} %get-tuple-element.723), channel_id=1, source_target_pairs={{128,0},{256,128},{384,256},{129,1},{257,129},{385,257},{130,2},{2... | collective-permute-start | bytes 393224 | tf_op jit(solution)/shard_map/while/body/eval_jaxpr/ppermute | solution.py:15
  225.3 6.9 %collective-permute-start = (bf16[256,256]{1,0:T(8,128)(2,1)S(1)}, bf16[256,256]{1,0:T(8,128)(2,1)S(1)}, u32[]{:S(2)}, u32[]{:S(2)}) collective-permute-start(bf16[256,256]{1,0:T(8,128)(2,1)S(1)} %get-tuple-element.723), channel_id=1, source_target_pairs={{128,0},{256,128},{384,256},{129,1},{257,129},{385,257},{130,2},{2... | collective-permute-start | bytes 393224 | tf_op jit(solution)/shard_map/while/body/eval_jaxpr/ppermute | solution.py:15
  240.4 6.8 %collective-permute-start = (bf16[256,256]{1,0:T(8,128)(2,1)S(1)}, bf16[256,256]{1,0:T(8,128)(2,1)S(1)}, u32[]{:S(2)}, u32[]{:S(2)}) collective-permute-start(bf16[256,256]{1,0:T(8,128)(2,1)S(1)} %get-tuple-element.723), channel_id=1, source_target_pairs={{128,0},{256,128},{384,256},{129,1},{257,129},{385,257},{130,2},{2... | collective-permute-start | bytes 393224 | tf_op jit(solution)/shard_map/while/body/eval_jaxpr/ppermute | solution.py:15
  255.5 6.8 %collective-permute-start = (bf16[256,256]{1,0:T(8,128)(2,1)S(1)}, bf16[256,256]{1,0:T(8,128)(2,1)S(1)}, u32[]{:S(2)}, u32[]{:S(2)}) collective-permute-start(bf16[256,256]{1,0:T(8,128)(2,1)S(1)} %get-tuple-element.723), channel_id=1, source_target_pairs={{128,0},{256,128},{384,256},{129,1},{257,129},{385,257},{130,2},{2... | collective-permute-start | bytes 393224 | tf_op jit(solution)/shard_map/while/body/eval_jaxpr/ppermute | solution.py:15
  270.6 6.8 %collective-permute-start = (bf16[256,256]{1,0:T(8,128)(2,1)S(1)}, bf16[256,256]{1,0:T(8,128)(2,1)S(1)}, u32[]{:S(2)}, u32[]{:S(2)}) collective-permute-start(bf16[256,256]{1,0:T(8,128)(2,1)S(1)} %get-tuple-element.723), channel_id=1, source_target_pairs={{128,0},{256,128},{384,256},{129,1},{257,129},{385,257},{130,2},{2... | collective-permute-start | bytes 393224 | tf_op jit(solution)/shard_map/while/body/eval_jaxpr/ppermute | solution.py:15
  285.7 6.8 %collective-permute-start = (bf16[256,256]{1,0:T(8,128)(2,1)S(1)}, bf16[256,256]{1,0:T(8,128)(2,1)S(1)}, u32[]{:S(2)}, u32[]{:S(2)}) collective-permute-start(bf16[256,256]{1,0:T(8,128)(2,1)S(1)} %get-tuple-element.723), channel_id=1, source_target_pairs={{128,0},{256,128},{384,256},{129,1},{257,129},{385,257},{130,2},{2... | collective-permute-start | bytes 393224 | tf_op jit(solution)/shard_map/while/body/eval_jaxpr/ppermute | solution.py:15
  300.8 6.8 %collective-permute-start = (bf16[256,256]{1,0:T(8,128)(2,1)S(1)}, bf16[256,256]{1,0:T(8,128)(2,1)S(1)}, u32[]{:S(2)}, u32[]{:S(2)}) collective-permute-start(bf16[256,256]{1,0:T(8,128)(2,1)S(1)} %get-tuple-element.723), channel_id=1, source_target_pairs={{128,0},{256,128},{384,256},{129,1},{257,129},{385,257},{130,2},{2... | collective-permute-start | bytes 393224 | tf_op jit(solution)/shard_map/while/body/eval_jaxpr/ppermute | solution.py:15
  315.9 8.1 %collective-permute-start = (bf16[256,256]{1,0:T(8,128)(2,1)S(1)}, bf16[256,256]{1,0:T(8,128)(2,1)S(1)}, u32[]{:S(2)}, u32[]{:S(2)}) collective-permute-start(bf16[256,256]{1,0:T(8,128)(2,1)S(1)} %get-tuple-element.723), channel_id=1, source_target_pairs={{128,0},{256,128},{384,256},{129,1},{257,129},{385,257},{130,2},{2... | collective-permute-start | bytes 393224 | tf_op jit(solution)/shard_map/while/body/eval_jaxpr/ppermute | solution.py:15
  332.2 6.8 %collective-permute-start = (bf16[256,256]{1,0:T(8,128)(2,1)S(1)}, bf16[256,256]{1,0:T(8,128)(2,1)S(1)}, u32[]{:S(2)}, u32[]{:S(2)}) collective-permute-start(bf16[256,256]{1,0:T(8,128)(2,1)S(1)} %get-tuple-element.723), channel_id=1, source_target_pairs={{128,0},{256,128},{384,256},{129,1},{257,129},{385,257},{130,2},{2... | collective-permute-start | bytes 393224 | tf_op jit(solution)/shard_map/while/body/eval_jaxpr/ppermute | solution.py:15
  353.5 26.4 %all-to-all-start.2 = ((bf16[16,128,128]{2,1,0:T(8,128)(2,1)}), bf16[16,128,128]{2,1,0:T(8,128)(2,1)S(1)}, u32[]{:S(2)}, u32[]{:S(2)}) async-start(bf16[16,128,128]{2,1,0:T(8,128)(2,1)} %convert_element_type.116), calls=%async_computation.2 | async-start | bytes 1048576 | tf_op jit(solution)/shard_map/all_to_all | solution.py:192
  366.2 21.7 %copy-start.2 = (bf16[2304,256]{1,0:T(8,128)(2,1)S(1)}, bf16[2304,256]{1,0:T(8,128)(2,1)}, u32[]{:S(2)}) copy-start(bf16[2304,256]{1,0:T(8,128)(2,1)} %get-tuple-element.378) | copy-start | bytes 3538948
  379.8 25.9 %all-to-all-start.3 = ((bf16[16,128,128]{2,1,0:T(8,128)(2,1)}), bf16[16,128,128]{2,1,0:T(8,128)(2,1)S(1)}, u32[]{:S(2)}, u32[]{:S(2)}) async-start(bf16[16,128,128]{2,1,0:T(8,128)(2,1)} %convert_element_type.122), calls=%async_computation.3 | async-start | bytes 1048576 | tf_op jit(solution)/shard_map/all_to_all | solution.py:199
  405.8 44.5 %all-to-all-start.1 = ((bf16[16,128,256]{2,1,0:T(8,128)(2,1)}), bf16[16,128,256]{2,1,0:T(8,128)(2,1)S(1)}, u32[]{:S(2)}, u32[]{:S(2)}) async-start(bf16[16,128,256]{2,1,0:T(8,128)(2,1)} %bitcast.36), calls=%async_computation.1 | async-start | bytes 2097152 | tf_op jit(solution)/shard_map/all_to_all | solution.py:175

commit v6 on v5

--- a/solution.py
+++ b/solution.py
@@ -66,7 +66,7 @@
     query_rows = (head_input.astype(jnp.float32) * gain_row).astype(jnp.bfloat16)
     blocked_keys = head_keys.reshape(block_count, block_rows, local_kv, HEAD_FEATURES)
     blocked_values = head_values.reshape(block_count, block_rows, local_kv, HEAD_FEATURES)
-    per_turn = 2
+    per_turn = 4
     unit_count = block_count // per_turn
     turn_rows = per_turn * block_rows
     token_rows = turn_rows // ctx_count
@@ -160,9 +160,8 @@
         return (incoming, result_heads, key_slots, value_slots, gain_acc)
 
     first_incoming = jnp.zeros((turn_rows, local_width), jnp.bfloat16)
-    slot_zeros = jnp.zeros(
-        ((unit_count + 1) * per_turn, listed * block_rows, slot_width), jnp.float32
-    )
+    slot_count = (unit_count + 1) * per_turn
+    slot_zeros = jnp.zeros((slot_count, listed * block_rows, slot_width), jnp.float32)
     start_carry = (
         first_incoming,
         jnp.zeros(((unit_count + 1) * turn_rows, local_width), jnp.bfloat16),
@@ -175,19 +174,19 @@
     result_rows = lax.all_to_all(
         result_heads[:total_rows], "ctx", split_axis=0, concat_axis=1, tiled=True
     )
-    target_labels = block_lists.reshape(-1)
-    key_pieces = key_slots[:block_count].reshape(block_count * listed, block_rows, slot_width)
-    value_pieces = value_slots[:block_count].reshape(block_count * listed, block_rows, slot_width)
-    key_acc = (
-        jnp.zeros((block_count, block_rows, slot_width), jnp.float32)
-        .at[target_labels]
-        .add(key_pieces)
-    )
-    value_acc = (
-        jnp.zeros((block_count, block_rows, slot_width), jnp.float32)
-        .at[target_labels]
-        .add(value_pieces)
-    )
+    spare_labels = jnp.full(((slot_count - block_count) * listed,), -1, block_lists.dtype)
+    target_labels = jnp.concatenate([block_lists.reshape(-1), spare_labels])
+    pick = (target_labels[None, :] == jnp.arange(block_count)[:, None]).astype(jnp.float32)
+
+    def gathered(slots):
+        return jnp.dot(
+            pick,
+            slots.reshape(slot_count * listed, block_rows * slot_width),
+            precision=lax.Precision.HIGHEST,
+        )
+
+    key_acc = gathered(key_slots)
+    value_acc = gathered(value_slots)
     key_back, value_back = (
         lax.all_to_all(
             key_acc.reshape(total_rows, slot_width).astype(jnp.bfloat16),

time: 457 us -> 465 us (1.018)
  waiting for transfers between devices: 249 us -> 279 us
  other arithmetic: 52.5 us -> 25.8 us
  matrix products: 12.1 us -> 21.4 us
    all_to_all x1, waiting for transfers between devices: 3.96 us -> 24.7 us  [shards(): lax.all_to_all(key_acc.reshape(total_rows, slot_width).astype(jnp.bfloat1...]
    scatter-add x2 -> x0, other arithmetic: 17.6 us -> none  [the longest x1 8.78 us: shards(): key_acc = jnp.zeros((block_count, block_rows, slot_width), jnp.float32).a...]
    reshape x1 -> x3, local copies, waits for them, and re-layouts: 0.09 us -> 13.7 us  [the longest x2 13.6 us: gathered(): slots.reshape(slot_count * listed, block_rows * slot_width)]
    all_to_all x1, waiting for transfers between devices: 24 us -> 35.6 us  [shards(): lax.all_to_all(result_heads[:total_rows], 'ctx', split_axis=0, concat_axi...]
    slice x2 -> x0, local copies, waits for them, and re-layouts: 9.18 us -> none  [the longest x1 4.66 us: shards(): key_slots[:block_count]]
    dot_general x0 -> x2, matrix products: none -> 8.57 us  [gathered(): jnp.dot(pick, slots.reshape(slot_count * listed, block_rows * slot_width)...]
    all_to_all x1, waiting for transfers between devices: 16.8 us -> 10.2 us  [shards(): lax.all_to_all(value_acc.reshape(total_rows, slot_width).astype(jnp.bfloa...]
    gather x8 -> x4, local copies, waits for them, and re-layouts: 13.1 us -> 6.76 us  [attend(): blocked_keys[lists_now]]
  transfers between devices with their start and end apart: 15 -> 11, of which waited for: 15 -> 11; matrix products, arithmetic and copies ran while one was open for 7% -> 6% of each run, Pallas kernels for 0% -> 0%
where the time goes in v6:
time: 465 us; the launch traced here: 463 us
  waiting for transfers between devices  279 us (60%)
  local copies, waits for them, and re-layouts  73.4 us (16%)
  starting transfers between devices  51.1 us (11%)
  other arithmetic  25.8 us (6%)
  matrix products  21.4 us (5%)
  blocking collectives  10.6 us (2%)
    all_to_all x1, waiting for transfers between devices, shards(): lax.all_to_all(packed, 'ctx', split_axis=1, concat_axis=0, tiled=True)  139 us
    ppermute x7, waiting for transfers between devices, passed_along(): return lax.ppermute(block, axis, route)  68.9 us
    all_to_all x1, waiting for transfers between devices, shards(): lax.all_to_all(result_heads[:total_rows], 'ctx', split_axis=0, concat_axi...  35.6 us
    all_to_all x1, waiting for transfers between devices, shards(): lax.all_to_all(key_acc.reshape(total_rows, slot_width).astype(jnp.bfloat1...  24.7 us
    all_to_all x1, starting transfers between devices, shards(): lax.all_to_all(packed, 'ctx', split_axis=1, concat_axis=0, tiled=True)  15.3 us
    reshape x2, local copies, waits for them, and re-layouts, gathered(): slots.reshape(slot_count * listed, block_rows * slot_width)  13.6 us
    all_to_all x1, starting transfers between devices, shards(): lax.all_to_all(value_acc.reshape(total_rows, slot_width).astype(jnp.bfloa...  13.2 us
    dynamic_update_slice x7, local copies, waits for them, and re-layouts, turn_step(): lax.dynamic_update_slice_in_dim(value_slots, value_part, target * per_tur...  10.6 us
  transfers between devices with their start and end apart: 11, of which 11 were waited for; matrix products, arithmetic and copies ran while one was open for 6% of the time, Pallas kernels for 0%

profile of v6, /device:TPU:6, one launch (start us, length us, event | category | flops | bytes accessed | tf_op | source)
XLA Modules:
  0.0 462.7 jit_solution(3493454228505531025)
XLA Ops:
  6.9 1.8 pad_maximum_fusion
  8.7 15.3 %all-to-all-start = ((bf16[128,16,768]{2,0,1:T(8,128)(2,1)}), bf16[128,16,768]{2,0,1:T(8,128)(2,1)S(1)}, u32[]{:S(2)}, u32[]{:S(2)}) async-start(bf16[128,16,768]{2,0,1:T(8,128)(2,1)} %pad_maximum_fusion), calls=%async_computation | async-start | bytes 6291456 | tf_op jit(solution)/shard_map/all_to_all | solution.py:60
  24.2 139.2 %all-to-all-done = bf16[128,16,768]{2,0,1:T(8,128)(2,1)S(1)} async-done(((bf16[128,16,768]{2,0,1:T(8,128)(2,1)}), bf16[128,16,768]{2,0,1:T(8,128)(2,1)S(1)}, u32[]{:S(2)}, u32[]{:S(2)}) %all-to-all-start) | async-done | bytes 3145760 | tf_op jit(solution)/shard_map/all_to_all | solution.py:60
  163.4 1.1 fusion.34
  164.5 1.1 fusion.35
  165.6 1.3 multiply_convert_fusion.1
  167.7 1.1 broadcast_in_dim.33
  168.8 2.9 broadcast_in_dim.34.clone2
  171.7 2.9 broadcast_in_dim.34.clone
  174.6 151.1 %while.24 = (s32[]{:T(128)}, bf16[512,256]{1,0:T(8,128)(2,1)}, bf16[2560,256]{1,0:T(8,128)(2,1)}, f32[20,512,128]{2,1,0:T(8,128)}, f32[20,512,128]{2,1,0:T(8,128...) while((s32[]{:T(128)}, bf16[512,256]{1,0:T(8,128)(2,1)}, ...), condition=%wide.region_7.8_spmd.clone, body=%wide.region_0.7_spmd.clone.sunk | while | flops 683276608 | bytes 39114844 | solution.py:172
  176.8 1.3 collective-permute-start
  178.4 1.5 constant_dynamic-update-slice_fusion.6
  179.9 5.4 %collective-permute-done = bf16[512,256]{1,0:T(8,128)(2,1)} collective-permute-done((bf16[512,256]{1,0:T(8,128)(2,1)}, bf16[512,256]{1,0:T(8,128)(2,1)}, u32[]{:S(2)}, u32[]{:S(2)}) %collective-permute-start) | collective-permute-done | bytes 262176 | tf_op jit(solution)/shard_map/while/body/eval_jaxpr/ppermute | solution.py:15
  185.4 1.1 dynamic-slice_select_fusion.2
  187.6 1.3 collective-permute-start
  189.2 1.5 constant_dynamic-update-slice_fusion.6
  190.7 5.4 %collective-permute-done = bf16[512,256]{1,0:T(8,128)(2,1)} collective-permute-done((bf16[512,256]{1,0:T(8,128)(2,1)}, bf16[512,256]{1,0:T(8,128)(2,1)}, u32[]{:S(2)}, u32[]{:S(2)}) %collective-permute-start) | collective-permute-done | bytes 262176 | tf_op jit(solution)/shard_map/while/body/eval_jaxpr/ppermute | solution.py:15
  198.4 1.3 collective-permute-start
  200.1 1.5 constant_dynamic-update-slice_fusion.6
  201.5 36.4 %collective-permute-done = bf16[512,256]{1,0:T(8,128)(2,1)} collective-permute-done((bf16[512,256]{1,0:T(8,128)(2,1)}, bf16[512,256]{1,0:T(8,128)(2,1)}, u32[]{:S(2)}, u32[]{:S(2)}) %collective-permute-start) | collective-permute-done | bytes 262176 | tf_op jit(solution)/shard_map/while/body/eval_jaxpr/ppermute | solution.py:15
  239.1 11.4 %conditional.3 = (f32[512,256]{1,0:T(8,128)S(1)}, f32[4,512,128]{1,2,0:T(8,128)S(1)}, f32[4,512,128]{2,1,0:T(8,128)S(1)}, f32[256]{0:T(256)S(1)}) conditional(s32[]{:T(128)} %convert_element_type.157, () %tuple.85, (s32[]{:T(128)}, s32[16,4]{1,0:T(8,128)S(1)}, bf16[16,128,1,128]{3,1,0,2:T(8,128)(2,1)}, bf16[2048,256]{1,0:T(8,128)(2,1)}, ...), branch_computations={%region_1.1_spmd, %region_2.6_spmd} | conditional | flops 682358592 | bytes 29673032 | solution.py:148
  239.2 1.7 gather_fusion.1
  240.9 1.7 gather_fusion
  246.5 1.1 fusion.8
  248.1 1.3 copy.144
  251.3 1.3 collective-permute-start
  252.9 1.5 constant_dynamic-update-slice_fusion.6
  254.5 5.4 %collective-permute-done = bf16[512,256]{1,0:T(8,128)(2,1)} collective-permute-done((bf16[512,256]{1,0:T(8,128)(2,1)}, bf16[512,256]{1,0:T(8,128)(2,1)}, u32[]{:S(2)}, u32[]{:S(2)}) %collective-permute-start) | collective-permute-done | bytes 262176 | tf_op jit(solution)/shard_map/while/body/eval_jaxpr/ppermute | solution.py:15
  261.0 11.4 %conditional.3 = (f32[512,256]{1,0:T(8,128)S(1)}, f32[4,512,128]{1,2,0:T(8,128)S(1)}, f32[4,512,128]{2,1,0:T(8,128)S(1)}, f32[256]{0:T(256)S(1)}) conditional(s32[]{:T(128)} %convert_element_type.157, () %tuple.85, (s32[]{:T(128)}, s32[16,4]{1,0:T(8,128)S(1)}, bf16[16,128,1,128]{3,1,0,2:T(8,128)(2,1)}, bf16[2048,256]{1,0:T(8,128)(2,1)}, ...), branch_computations={%region_1.1_spmd, %region_2.6_spmd} | conditional | flops 682358592 | bytes 29673032 | solution.py:148
  261.1 1.7 gather_fusion.1
  262.8 1.7 gather_fusion
  268.4 1.1 fusion.8
  270.0 1.3 copy.144
  273.2 1.3 collective-permute-start
  274.8 1.5 constant_dynamic-update-slice_fusion.6
  276.4 5.4 %collective-permute-done = bf16[512,256]{1,0:T(8,128)(2,1)} collective-permute-done((bf16[512,256]{1,0:T(8,128)(2,1)}, bf16[512,256]{1,0:T(8,128)(2,1)}, u32[]{:S(2)}, u32[]{:S(2)}) %collective-permute-start) | collective-permute-done | bytes 262176 | tf_op jit(solution)/shard_map/while/body/eval_jaxpr/ppermute | solution.py:15
  282.9 11.4 %conditional.3 = (f32[512,256]{1,0:T(8,128)S(1)}, f32[4,512,128]{1,2,0:T(8,128)S(1)}, f32[4,512,128]{2,1,0:T(8,128)S(1)}, f32[256]{0:T(256)S(1)}) conditional(s32[]{:T(128)} %convert_element_type.157, () %tuple.85, (s32[]{:T(128)}, s32[16,4]{1,0:T(8,128)S(1)}, bf16[16,128,1,128]{3,1,0,2:T(8,128)(2,1)}, bf16[2048,256]{1,0:T(8,128)(2,1)}, ...), branch_computations={%region_1.1_spmd, %region_2.6_spmd} | conditional | flops 682358592 | bytes 29673032 | solution.py:148
  283.0 1.7 gather_fusion.1
  284.7 1.7 gather_fusion
  290.3 1.1 fusion.8
  291.9 1.3 copy.144
  295.1 1.3 collective-permute-start
  296.7 1.5 constant_dynamic-update-slice_fusion.6
  298.3 5.5 %collective-permute-done = bf16[512,256]{1,0:T(8,128)(2,1)} collective-permute-done((bf16[512,256]{1,0:T(8,128)(2,1)}, bf16[512,256]{1,0:T(8,128)(2,1)}, u32[]{:S(2)}, u32[]{:S(2)}) %collective-permute-start) | collective-permute-done | bytes 262176 | tf_op jit(solution)/shard_map/while/body/eval_jaxpr/ppermute | solution.py:15
  304.8 11.4 %conditional.3 = (f32[512,256]{1,0:T(8,128)S(1)}, f32[4,512,128]{1,2,0:T(8,128)S(1)}, f32[4,512,128]{2,1,0:T(8,128)S(1)}, f32[256]{0:T(256)S(1)}) conditional(s32[]{:T(128)} %convert_element_type.157, () %tuple.85, (s32[]{:T(128)}, s32[16,4]{1,0:T(8,128)S(1)}, bf16[16,128,1,128]{3,1,0,2:T(8,128)(2,1)}, bf16[2048,256]{1,0:T(8,128)(2,1)}, ...), branch_computations={%region_1.1_spmd, %region_2.6_spmd} | conditional | flops 682358592 | bytes 29673032 | solution.py:148
  305.0 1.7 gather_fusion.1
  306.7 1.7 gather_fusion
  312.2 1.1 fusion.8
  313.8 1.3 copy.144
  317.1 1.3 collective-permute-start
  318.7 1.6 constant_dynamic-update-slice_fusion.6
  320.3 5.4 %collective-permute-done = bf16[512,256]{1,0:T(8,128)(2,1)} collective-permute-done((bf16[512,256]{1,0:T(8,128)(2,1)}, bf16[512,256]{1,0:T(8,128)(2,1)}, u32[]{:S(2)}, u32[]{:S(2)}) %collective-permute-start) | collective-permute-done | bytes 262176 | tf_op jit(solution)/shard_map/while/body/eval_jaxpr/ppermute | solution.py:15
  325.6 6.8 %reshape.147 = f32[80,16384]{1,0:T(8,128)} reshape(f32[20,512,128]{2,1,0:T(8,128)} %get-tuple-element.380) | data formatting | bytes 10485760 | tf_op jit(solution)/shard_map/reshape | solution.py:184
  332.5 4.3 fusion.26
  337.7 13.2 %all-to-all-start.3 = ((bf16[16,128,128]{2,1,0:T(8,128)(2,1)}), bf16[16,128,128]{2,1,0:T(8,128)(2,1)S(1)}, u32[]{:S(2)}, u32[]{:S(2)}) async-start(bf16[16,128,128]{2,1,0:T(8,128)(2,1)} %copy.163), calls=%async_computation.3 | async-start | bytes 1048576 | tf_op jit(solution)/shard_map/all_to_all | solution.py:198
  350.9 6.8 %reshape.146 = f32[80,16384]{1,0:T(8,128)} reshape(f32[20,512,128]{2,1,0:T(8,128)} %get-tuple-element.379) | data formatting | bytes 10485760 | tf_op jit(solution)/shard_map/reshape | solution.py:184
  357.7 4.3 fusion.23
  362.9 10.2 %all-to-all-done.3 = bf16[16,128,128]{2,1,0:T(8,128)(2,1)S(1)} async-done(((bf16[16,128,128]{2,1,0:T(8,128)(2,1)}), bf16[16,128,128]{2,1,0:T(8,128)(2,1)S(1)}, u32[]{:S(2)}, u32[]{:S(2)}) %all-to-all-start.3) | async-done | bytes 524320 | tf_op jit(solution)/shard_map/all_to_all | solution.py:198
  373.2 7.2 %all-to-all-start.2 = ((bf16[16,128,128]{2,1,0:T(8,128)(2,1)}), bf16[16,128,128]{2,1,0:T(8,128)(2,1)S(1)}, u32[]{:S(2)}, u32[]{:S(2)}) async-start(bf16[16,128,128]{2,1,0:T(8,128)(2,1)} %copy.160), calls=%async_computation.2 | async-start | bytes 1048576 | tf_op jit(solution)/shard_map/all_to_all | solution.py:191
  381.4 24.7 %all-to-all-done.2 = bf16[16,128,128]{2,1,0:T(8,128)(2,1)S(1)} async-done(((bf16[16,128,128]{2,1,0:T(8,128)(2,1)}), bf16[16,128,128]{2,1,0:T(8,128)(2,1)S(1)}, u32[]{:S(2)}, u32[]{:S(2)}) %all-to-all-start.2) | async-done | bytes 524320 | tf_op jit(solution)/shard_map/all_to_all | solution.py:191
  406.1 6.5 %all-to-all-start.1 = ((bf16[16,128,256]{2,1,0:T(8,128)(2,1)}), bf16[16,128,256]{2,1,0:T(8,128)(2,1)S(1)}, u32[]{:S(2)}, u32[]{:S(2)}) async-start(bf16[16,128,256]{2,1,0:T(8,128)(2,1)} %bitcast.36), calls=%async_computation.1 | async-start | bytes 2097152 | tf_op jit(solution)/shard_map/all_to_all | solution.py:174
  412.6 10.6 %psum.7 = f32[1,256]{1,0:T(1,128)} all-reduce(f32[1,256]{1,0:T(1,128)S(1)} %bitcast.160), channel_id=1, replica_groups=mesh['section'=4,'ctx'=16,'dp'=8] {'dp'}, use_global_device_ids=true, to_apply=%region_10.11 | all-reduce | flops 256 | bytes 2048 | tf_op jit(solution)/shard_map/psum | solution.py:218
  425.1 35.6 %all-to-all-done.1 = bf16[16,128,256]{2,1,0:T(8,128)(2,1)S(1)} async-done(((bf16[16,128,256]{2,1,0:T(8,128)(2,1)}), bf16[16,128,256]{2,1,0:T(8,128)(2,1)S(1)}, u32[]{:S(2)}, u32[]{:S(2)}) %all-to-all-start.1) | async-done | bytes 1048608 | tf_op jit(solution)/shard_map/all_to_all | solution.py:174
  461.4 1.3 copy.165
  (136 shorter events, 50.8 us)
Async XLA Ops:
  0.6 4.4 copy-start.2
  5.1 1.2 copy-start.3
  8.7 15.4 %copy-start.5 = (s32[16,4]{0,1:T(4,128)S(1)}, s32[16,4]{0,1:T(4,128)}, u32[]{:S(2)}) copy-start(s32[16,4]{0,1:T(4,128)} %param.18) | copy-start | bytes 772
  8.7 154.7 %all-to-all-start = ((bf16[128,16,768]{2,0,1:T(8,128)(2,1)}), bf16[128,16,768]{2,0,1:T(8,128)(2,1)S(1)}, u32[]{:S(2)}, u32[]{:S(2)}) async-start(bf16[128,16,768]{2,0,1:T(8,128)(2,1)} %pad_maximum_fusion), calls=%async_computation | async-start | bytes 6291456 | tf_op jit(solution)/shard_map/all_to_all | solution.py:60
  164.5 1.1 copy-start.4
  165.6 6.1 %copy-start = (bf16[2048,256]{1,0:T(8,128)(2,1)}, bf16[2048,256]{1,0:T(8,128)(2,1)S(1)}, u32[]{:S(2)}) copy-start(bf16[2048,256]{1,0:T(8,128)(2,1)S(1)} %get-tuple-element.752) | copy-start | bytes 3145732
  176.8 8.6 %collective-permute-start = (bf16[512,256]{1,0:T(8,128)(2,1)}, bf16[512,256]{1,0:T(8,128)(2,1)}, u32[]{:S(2)}, u32[]{:S(2)}) collective-permute-start(bf16[512,256]{1,0:T(8,128)(2,1)} %get-tuple-element.723), channel_id=1, source_target_pairs={{128,0},{256,128},{384,256},{129,1},{257,129},{385,257},{130,2},{2... | collective-permute-start | bytes 786440 | tf_op jit(solution)/shard_map/while/body/eval_jaxpr/ppermute | solution.py:15
  187.6 8.6 %collective-permute-start = (bf16[512,256]{1,0:T(8,128)(2,1)}, bf16[512,256]{1,0:T(8,128)(2,1)}, u32[]{:S(2)}, u32[]{:S(2)}) collective-permute-start(bf16[512,256]{1,0:T(8,128)(2,1)} %get-tuple-element.723), channel_id=1, source_target_pairs={{128,0},{256,128},{384,256},{129,1},{257,129},{385,257},{130,2},{2... | collective-permute-start | bytes 786440 | tf_op jit(solution)/shard_map/while/body/eval_jaxpr/ppermute | solution.py:15
  198.4 39.6 %collective-permute-start = (bf16[512,256]{1,0:T(8,128)(2,1)}, bf16[512,256]{1,0:T(8,128)(2,1)}, u32[]{:S(2)}, u32[]{:S(2)}) collective-permute-start(bf16[512,256]{1,0:T(8,128)(2,1)} %get-tuple-element.723), channel_id=1, source_target_pairs={{128,0},{256,128},{384,256},{129,1},{257,129},{385,257},{130,2},{2... | collective-permute-start | bytes 786440 | tf_op jit(solution)/shard_map/while/body/eval_jaxpr/ppermute | solution.py:15
  251.3 8.6 %collective-permute-start = (bf16[512,256]{1,0:T(8,128)(2,1)}, bf16[512,256]{1,0:T(8,128)(2,1)}, u32[]{:S(2)}, u32[]{:S(2)}) collective-permute-start(bf16[512,256]{1,0:T(8,128)(2,1)} %get-tuple-element.723), channel_id=1, source_target_pairs={{128,0},{256,128},{384,256},{129,1},{257,129},{385,257},{130,2},{2... | collective-permute-start | bytes 786440 | tf_op jit(solution)/shard_map/while/body/eval_jaxpr/ppermute | solution.py:15
  273.2 8.6 %collective-permute-start = (bf16[512,256]{1,0:T(8,128)(2,1)}, bf16[512,256]{1,0:T(8,128)(2,1)}, u32[]{:S(2)}, u32[]{:S(2)}) collective-permute-start(bf16[512,256]{1,0:T(8,128)(2,1)} %get-tuple-element.723), channel_id=1, source_target_pairs={{128,0},{256,128},{384,256},{129,1},{257,129},{385,257},{130,2},{2... | collective-permute-start | bytes 786440 | tf_op jit(solution)/shard_map/while/body/eval_jaxpr/ppermute | solution.py:15
  295.1 8.6 %collective-permute-start = (bf16[512,256]{1,0:T(8,128)(2,1)}, bf16[512,256]{1,0:T(8,128)(2,1)}, u32[]{:S(2)}, u32[]{:S(2)}) collective-permute-start(bf16[512,256]{1,0:T(8,128)(2,1)} %get-tuple-element.723), channel_id=1, source_target_pairs={{128,0},{256,128},{384,256},{129,1},{257,129},{385,257},{130,2},{2... | collective-permute-start | bytes 786440 | tf_op jit(solution)/shard_map/while/body/eval_jaxpr/ppermute | solution.py:15
  317.1 8.6 %collective-permute-start = (bf16[512,256]{1,0:T(8,128)(2,1)}, bf16[512,256]{1,0:T(8,128)(2,1)}, u32[]{:S(2)}, u32[]{:S(2)}) collective-permute-start(bf16[512,256]{1,0:T(8,128)(2,1)} %get-tuple-element.723), channel_id=1, source_target_pairs={{128,0},{256,128},{384,256},{129,1},{257,129},{385,257},{130,2},{2... | collective-permute-start | bytes 786440 | tf_op jit(solution)/shard_map/while/body/eval_jaxpr/ppermute | solution.py:15
  337.7 35.5 %all-to-all-start.3 = ((bf16[16,128,128]{2,1,0:T(8,128)(2,1)}), bf16[16,128,128]{2,1,0:T(8,128)(2,1)S(1)}, u32[]{:S(2)}, u32[]{:S(2)}) async-start(bf16[16,128,128]{2,1,0:T(8,128)(2,1)} %copy.163), calls=%async_computation.3 | async-start | bytes 1048576 | tf_op jit(solution)/shard_map/all_to_all | solution.py:198
  362.0 18.4 %copy-start.1 = (bf16[2560,256]{1,0:T(8,128)(2,1)S(1)}, bf16[2560,256]{1,0:T(8,128)(2,1)}, u32[]{:S(2)}) copy-start(bf16[2560,256]{1,0:T(8,128)(2,1)} %get-tuple-element.378) | copy-start | bytes 3932164
  373.2 33.0 %all-to-all-start.2 = ((bf16[16,128,128]{2,1,0:T(8,128)(2,1)}), bf16[16,128,128]{2,1,0:T(8,128)(2,1)S(1)}, u32[]{:S(2)}, u32[]{:S(2)}) async-start(bf16[16,128,128]{2,1,0:T(8,128)(2,1)} %copy.160), calls=%async_computation.2 | async-start | bytes 1048576 | tf_op jit(solution)/shard_map/all_to_all | solution.py:191
  406.1 54.6 %all-to-all-start.1 = ((bf16[16,128,256]{2,1,0:T(8,128)(2,1)}), bf16[16,128,256]{2,1,0:T(8,128)(2,1)S(1)}, u32[]{:S(2)}, u32[]{:S(2)}) async-start(bf16[16,128,256]{2,1,0:T(8,128)(2,1)} %bitcast.36), calls=%async_computation.1 | async-start | bytes 2097152 | tf_op jit(solution)/shard_map/all_to_all | solution.py:174

commit v7 on v1

v7 whole, which is shorter than its diff:
```python
import math

import jax
import jax.numpy as jnp
from jax import lax
from jax.sharding import PartitionSpec as P

HEAD_FEATURES = 128


def passed_along(block, axis, distance):
    devices = range(lax.axis_size(axis))
    route = [(i - distance, i) for i in devices if i - distance in devices]
    return lax.ppermute(block, axis, route)


def cyclic_shift(block, axis, distance):
    count = lax.axis_size(axis)
    return lax.ppermute(block, axis, [(i, (i + distance) % count) for i in range(count)])


def shards(query_input, key_states, value_states, query_gain, top_grad, block_lists):
    ctx_count = lax.axis_size("ctx")
    section_count = lax.axis_size("section")
    section_pos = lax.axis_index("section")
    ctx_pos = lax.axis_index("ctx")
    layer_input = query_input[0, 0]
    tok_local, feature_count = layer_input.shape
    kv_width = key_states.shape[-1]
    kv_heads = kv_width // HEAD_FEATURES
    head_count = feature_count // HEAD_FEATURES
    group_width = head_count // kv_heads
    group_features = group_width * HEAD_FEATURES
    gain_width = query_gain.shape[-1]
    block_count, listed = block_lists.shape
    block_rows = tok_local
    assert block_count == ctx_count and listed == 4
    scale_factor = 1.0 / math.sqrt(HEAD_FEATURES)
    turn_count = kv_heads + section_count - 1
    last = ctx_count - 1

    first_row = block_lists[0]
    first_extra = jnp.sum(
        jnp.where((first_row != last) & (first_row != 0) & (first_row != 1), first_row, 0)
    )
    last_row = block_lists[last]
    last_extra = jnp.sum(
        jnp.where((last_row != last - 1) & (last_row != last) & (last_row != 0), last_row, 0)
    )
    is_first = ctx_pos == 0
    is_last = ctx_pos == last
    is_second = ctx_pos == 1
    uses_zero = ~(is_first | is_last | is_second)
    lane_sources = jnp.stack([ctx_pos == 0, ctx_pos == first_extra, ctx_pos == last_extra, is_last])
    lane_users = jnp.stack([uses_zero, is_first, is_last, is_second])

    gain_placed = jnp.zeros((feature_count,), jnp.float32)
    gain_placed = lax.dynamic_update_slice_in_dim(
        gain_placed, query_gain[0], ctx_pos * gain_width, 0
    )
    own_kv = jnp.stack([key_states[0, 0], value_states[0, 0]])
    lanes_out = jnp.where(lane_sources[:, None, None, None], own_kv[None], jnp.zeros_like(own_kv)[None])
    lanes_in = lax.psum(lanes_out, "ctx")
    gain_row = lax.psum(gain_placed, "ctx")
    extra_kv = jnp.sum(
        jnp.where(lane_users[:, None, None, None], lanes_in, jnp.zeros_like(lanes_in)), axis=0
    )
    prev_kv = cyclic_shift(own_kv, "ctx", 1)
    next_kv = cyclic_shift(own_kv, "ctx", -1)
    pool_kv = jnp.stack([prev_kv, own_kv, next_kv, extra_kv], axis=1)

    query_rows = (layer_input.astype(jnp.float32) * gain_row).astype(jnp.bfloat16)
    own_top = top_grad[0]
    on_top = section_pos == section_count - 1
    lag = section_count - 1 - section_pos

    def group_cols(array, group, width):
        return lax.dynamic_slice_in_dim(array, group * width, width, array.ndim - 1)

    def attend(group, head_grad):
        pool = group_cols(pool_kv, group, HEAD_FEATURES)
        neighbor_keys = pool[0].reshape(listed * block_rows, HEAD_FEATURES)
        neighbor_values = pool[1].reshape(listed * block_rows, HEAD_FEATURES)
        query_now = group_cols(query_rows, group, group_features).reshape(
            tok_local, group_width, HEAD_FEATURES
        )
        input_now = group_cols(layer_input, group, group_features)
        gain_now = lax.dynamic_slice_in_dim(gain_row, group * group_features, group_features, 0)
        grad_now = head_grad.reshape(tok_local, group_width, HEAD_FEATURES)
        scores = (
            jnp.einsum("bhd,jd->hbj", query_now, neighbor_keys, preferred_element_type=jnp.float32)
            * scale_factor
        )
        row_max = jnp.max(scores, axis=-1, keepdims=True)
        weights = jnp.exp(scores - row_max)
        probs = weights / jnp.sum(weights, axis=-1, keepdims=True)
        probs_low = probs.astype(jnp.bfloat16)
        prob_grad = jnp.einsum(
            "bhd,jd->hbj", grad_now, neighbor_values, preferred_element_type=jnp.float32
        )
        row_dot = jnp.sum(probs * prob_grad, axis=-1, keepdims=True)
        score_grad = (probs * (prob_grad - row_dot)).astype(jnp.bfloat16)
        query_grad = (
            jnp.einsum("hbj,jd->bhd", score_grad, neighbor_keys, preferred_element_type=jnp.float32)
            * scale_factor
        ).reshape(tok_local, group_features)
        key_part = (
            jnp.einsum("hbj,bhd->jd", score_grad, query_now, preferred_element_type=jnp.float32)
            * scale_factor
        )
        value_part = jnp.einsum(
            "hbj,bhd->jd", probs_low, grad_now, preferred_element_type=jnp.float32
        )
        moved_grad = (gain_now * query_grad).astype(jnp.bfloat16)
        handed = (head_grad.astype(jnp.float32) + moved_grad.astype(jnp.float32)).astype(
            jnp.bfloat16
        )
        gain_part = jnp.sum(input_now.astype(jnp.float32) * query_grad, axis=0)
        parts = jnp.stack([key_part, value_part]).reshape(2, listed, block_rows, HEAD_FEATURES)
        return handed, parts, gain_part

    incoming = jnp.zeros((tok_local, group_features), jnp.bfloat16)
    handed_turns, part_turns, gain_turns = [], [], []
    for turn in range(turn_count):
        group = jnp.clip(turn - lag, 0, kv_heads - 1)
        from_top = group_cols(own_top, group, group_features)
        head_grad = jnp.where(on_top, from_top, incoming)
        handed, parts, gain_part = attend(group, head_grad)
        handed_turns.append(handed)
        part_turns.append(parts)
        gain_turns.append(gain_part)
        if turn + 1 < turn_count:
            incoming = passed_along(handed, "section", -1)

    def own_turns(pieces):
        stacked = jnp.stack(pieces)
        return lax.dynamic_slice_in_dim(stacked, lag, kv_heads, 0)

    stream_out = own_turns(handed_turns).transpose(1, 0, 2).reshape(tok_local, feature_count)
    all_parts = own_turns(part_turns).transpose(1, 2, 3, 0, 4).reshape(
        2, listed, block_rows, kv_width
    )
    from_next = cyclic_shift(all_parts[:, 0], "ctx", -1)
    from_prev = cyclic_shift(all_parts[:, 2], "ctx", 1)
    extra_part = all_parts[:, 3]
    lanes_back = jnp.where(
        lane_users[:, None, None, None], extra_part[None], jnp.zeros_like(extra_part)[None]
    )
    gain_full = own_turns(gain_turns).reshape(feature_count)
    summed = lax.psum(jnp.concatenate([lanes_back.reshape(-1), gain_full]), "ctx")
    lanes_sum = summed[: lanes_back.size].reshape(lanes_back.shape)
    extra_back = jnp.sum(
        jnp.where(lane_sources[:, None, None, None], lanes_sum, jnp.zeros_like(lanes_sum)), axis=0
    )
    kv_total = all_parts[:, 1] + from_next + from_prev + extra_back
    kv_out = kv_total.astype(jnp.bfloat16)
    gain_ctx = lax.dynamic_slice_in_dim(summed[lanes_back.size :], ctx_pos * gain_width, gain_width, 0)
    gain_total = lax.psum(gain_ctx, "dp")
    return (stream_out[None, None], kv_out[0][None, None], kv_out[1][None, None], gain_total[None])


def solution(mesh):
    placed = (
        P("section", "dp", "ctx", None),
        P("section", "dp", "ctx", None),
        P("section", "dp", "ctx", None),
        P("section", "ctx"),
        P("dp", "ctx", None),
        P(),
    )
    return jax.shard_map(
        shards,
        mesh=mesh,
        in_specs=placed,
        out_specs=(
            P("section", "dp", "ctx", None),
            P("section", "dp", "ctx", None),
            P("section", "dp", "ctx", None),
            P("section", "ctx"),
        ),
        check_vma=False,
    )
```

time: 1450 us -> 461 us (0.32)
  waiting for transfers between devices: 698 us -> 210 us
  blocking collectives: 539 us -> 65.1 us
  starting transfers between devices: 8.64 us -> 28.6 us
  other arithmetic: 73 us -> 54.1 us
  matrix products: 42.1 us -> 25.9 us
    reduce_scatter x14 -> x0, waiting for transfers between devices: 690 us -> none  [the longest x7 495 us: attend(): lax.psum_scatter(value_blocks.reshape(block_count * block_rows, HEAD_FEAT...]
    all_gather x15 -> x0, blocking collectives: 475 us -> none  [the longest x7 226 us: attend(): lax.all_gather(group_cols(own_keys, group, HEAD_FEATURES), 'ctx', tiled=T...]
    psum x0 -> x2, waiting for transfers between devices: none -> 188 us  [the longest x1 130 us: shards(): lax.psum(jnp.concatenate([lanes_back.reshape(-1), gain_full]), 'ctx')]
    psum x1 -> x2, blocking collectives: 10.5 us -> 65.1 us  [the longest x1 54.6 us: shards(): gain_row = lax.psum(gain_placed, 'ctx')]
    unnamed x1 -> x0, blocking collectives: 53.1 us -> none
    scatter-add x14 -> x0, other arithmetic: 28.7 us -> none  [the longest x7 15.6 us: attend(): value_blocks = jnp.zeros((block_count, block_rows, HEAD_FEATURES), jnp.fl...]
    ppermute x0 -> x4, starting transfers between devices: none -> 19.8 us  [cyclic_shift(): lax.ppermute(block, axis, [(i, (i + distance) % count) for i in range(cou...]
    gather x14 -> x0, local copies, waits for them, and re-layouts: 19.5 us -> none  [the longest x7 13.3 us: attend(): values_now.reshape(block_count, block_rows, HEAD_FEATURES)[own_list]]
  transfers between devices with their start and end apart: 20 -> 12, of which waited for: 13 -> 7; matrix products, arithmetic and copies ran while one was open for 10% -> 17% of each run, Pallas kernels for 0% -> 0%
where the time goes in v7:
time: 461 us; the launch traced here: 456 us
  waiting for transfers between devices  210 us (46%)
  blocking collectives  65.1 us (14%)
  local copies, waits for them, and re-layouts  55.6 us (12%)
  other arithmetic  54.1 us (12%)
  starting transfers between devices  28.6 us (6%)
  matrix products  25.9 us (6%)
  between operations  16.8 us (4%)
    psum x1, waiting for transfers between devices, shards(): lax.psum(jnp.concatenate([lanes_back.reshape(-1), gain_full]), 'ctx')  130 us
    psum x1, waiting for transfers between devices, shards(): lanes_in = lax.psum(lanes_out, 'ctx')  57.9 us
    psum x1, blocking collectives, shards(): gain_row = lax.psum(gain_placed, 'ctx')  54.6 us
    ppermute x6, waiting for transfers between devices, passed_along(): return lax.ppermute(block, axis, route)  22.2 us
    ppermute x4, starting transfers between devices, cyclic_shift(): lax.ppermute(block, axis, [(i, (i + distance) % count) for i in range(cou...  19.8 us
    unnamed x12, other arithmetic  16.8 us
    unnamed x219, local copies, waits for them, and re-layouts  11.3 us
    dynamic_slice x8, local copies, waits for them, and re-layouts, group_cols(): return lax.dynamic_slice_in_dim(array, group * width, width, array.ndim - 1)  11.3 us
  transfers between devices with their start and end apart: 12, of which 7 were waited for; matrix products, arithmetic and copies ran while one was open for 17% of the time, Pallas kernels for 0%

profile of v7, /device:TPU:6, one launch (start us, length us, event | category | flops | bytes accessed | tf_op | source)
XLA Modules:
  0.0 456.0 jit_solution(11499054971535403620)
XLA Ops:
  7.2 1.9 fusion.75
  9.1 3.8 collective-permute-start
  12.9 9.5 %collective-permute-start.1 = (bf16[2,128,512]{2,1,0:T(8,128)(2,1)}, bf16[2,128,512]{2,1,0:T(8,128)(2,1)}, u32[]{:S(2)}, u32[]{:S(2)}) collective-permute-start(bf16[2,128,512]{2,1,0:T(8,128)(2,1)} %get-tuple-element.56), channel_id=1, source_target_pairs={{0,120},{8,0},{16,8},{24,16},{32,24},{40,32},{48,40},{56,48},{64,5... | collective-permute-start | bytes 786440 | tf_op jit(solution)/shard_map/ppermute | solution.py:19
  26.0 2.1 broadcast_select_fusion.1
  28.5 54.6 %psum.28 = f32[4096]{0:T(1024)S(1)} all-reduce(f32[4096]{0:T(1024)S(1)} %dynamic_update_slice.3), channel_id=1, replica_groups=mesh['section'=4,'ctx'=16,'dp'=8] {'ctx'}, use_global_device_ids=true, to_apply=%region_0.1 | all-reduce | flops 4096 | bytes 32768 | tf_op jit(solution)/shard_map/psum | solution.py:64
  83.7 1.6 dynamic-slice_convert_fusion
  85.5 1.2 constant_dynamic-slice_fusion.10
  86.7 1.1 copy.250
  89.5 1.8 copy.144
  92.3 1.9 copy.149
  94.2 2.0 copy.195
  96.2 1.8 copy.154
  99.0 1.8 copy.159
  101.8 1.8 copy.164
  107.5 57.9 %all-reduce.3.cloned.1.call-done = bf16[4,2,128,512]{3,2,1,0:T(8,128)(2,1)} async-done(((bf16[4,2,128,512]{3,2,1,0:T(8,128)(2,1)}), bf16[4,2,128,512]{3,2,1,0:T(8,128)(2,1)}) %all-reduce.3.cloned.1.call-update) | async-done | bytes 1048592 | tf_op jit(solution)/shard_map/psum | solution.py:63
  165.4 1.5 select_reduce_fusion.1
  167.0 1.2 pad_maximum_fusion.1
  168.1 1.2 constant_dynamic-slice_fusion.9
  171.7 1.1 fusion.49
  174.8 1.5 collective-permute-start.2
  176.3 1.8 copy.175
  183.2 1.4 divide_convert_fusion
  184.6 1.4 divide_convert_fusion.1
  186.1 1.4 divide_convert_fusion.2
  187.5 1.4 divide_convert_fusion.3
  188.9 1.4 divide_convert_fusion.5
  191.9 1.4 divide_convert_fusion.4
  197.7 1.2 fusion.48
  201.0 1.5 collective-permute-start.3
  202.5 1.8 copy.177
  204.8 2.1 maximum_dynamic-update-slice_fusion.5
  206.9 3.6 collective-permute-done.3
  213.0 1.2 fusion.47
  216.2 1.3 collective-permute-start.4
  217.5 1.8 copy.179
  219.8 2.0 maximum_dynamic-update-slice_fusion.4
  221.9 4.5 collective-permute-done.4
  228.9 1.1 fusion.46
  232.1 1.4 collective-permute-start.5
  233.6 1.8 copy.181
  235.8 2.0 maximum_dynamic-update-slice_fusion.3
  237.9 5.8 %collective-permute-done.5 = bf16[128,1024]{0,1:T(8,128)(2,1)} collective-permute-done((bf16[128,1024]{0,1:T(8,128)(2,1)}, bf16[128,1024]{0,1:T(8,128)(2,1)}, u32[]{:S(2)}, u32[]{:S(2)}) %collective-permute-start.5) | collective-permute-done | bytes 262176 | tf_op jit(solution)/shard_map/ppermute | solution.py:14
  246.3 1.1 fusion.45
  249.5 1.4 collective-permute-start.6
  250.9 1.8 copy.183
  253.2 2.0 maximum_dynamic-update-slice_fusion.2
  255.2 5.4 %collective-permute-done.6 = bf16[128,1024]{0,1:T(8,128)(2,1)} collective-permute-done((bf16[128,1024]{0,1:T(8,128)(2,1)}, bf16[128,1024]{0,1:T(8,128)(2,1)}, u32[]{:S(2)}, u32[]{:S(2)}) %collective-permute-start.6) | collective-permute-done | bytes 262176 | tf_op jit(solution)/shard_map/ppermute | solution.py:14
  266.4 1.7 collective-permute-start.7
  268.0 1.8 copy.185
  270.3 1.8 maximum_dynamic-update-slice_fusion.1
  272.1 2.9 collective-permute-done.7
  280.1 1.7 dynamic-slice_bitcast_fusion
  282.1 1.2 fusion.76
  284.9 1.8 fusion.64
  287.5 1.5 pad_maximum_fusion
  290.2 4.6 %collective-permute-start.8 = (f32[2,128,512]{2,1,0:T(8,128)S(1)}, f32[2,128,512]{2,1,0:T(8,128)}, u32[]{:S(2)}, u32[]{:S(2)}) collective-permute-start(f32[2,128,512]{2,1,0:T(8,128)S(1)} %bitcast.642), channel_id=1, source_target_pairs={{0,120},{8,0},{16,8},{24,16},{32,24},{40,32},{48,40},{56,48},{64,5... | collective-permute-start | bytes 1572872 | tf_op jit(solution)/shard_map/ppermute | solution.py:19
  295.8 1.9 collective-permute-start.9
  298.9 1.3 constant_dynamic-slice_fusion.7
  300.2 1.3 copy.200
  301.5 129.8 %all-reduce.5.cloned.1.call-done = f32[528384]{0:T(1024)} async-done(((f32[528384]{0:T(1024)}), f32[528384]{0:T(1024)}) %all-reduce.5.cloned.1.call-update) | async-done | bytes 2113552 | tf_op jit(solution)/shard_map/psum | solution.py:150
  431.3 3.1 slice.100
  434.3 1.7 reshape.315
  436.4 1.4 fusion.63
  438.6 10.5 %psum.31 = f32[1,256]{1,0:T(1,128)} all-reduce(f32[1,256]{1,0:T(1,128)S(1)} %bitcast.674), channel_id=1, replica_groups=mesh['section'=4,'ctx'=16,'dp'=8] {'dp'}, use_global_device_ids=true, to_apply=%region_35.36 | all-reduce | flops 256 | bytes 2048 | tf_op jit(solution)/shard_map/psum | solution.py:158
  (313 shorter events, 62.8 us)
Async XLA Ops:
  7.2 21.0 %copy-start.104 = (f32[1,256]{1,0:T(1,128)S(1)}, f32[1,256]{1,0:T(1,128)}, u32[]{:S(2)}) copy-start(f32[1,256]{1,0:T(1,128)} %param.9) | copy-start | bytes 3076
  7.2 75.9 %copy-start.10 = (bf16[1,1,128,4096]{3,2,1,0:T(8,128)(2,1)S(1)}, bf16[1,1,128,4096]{3,2,1,0:T(8,128)(2,1)}, u32[]{:S(2)}) copy-start(bf16[1,1,128,4096]{3,2,1,0:T(8,128)(2,1)} %param.6) | copy-start | bytes 3145732
  7.2 158.3 %all-reduce.3.cloned.1.call-start = ((), (), s32[]{:S(2)}) async-start(), calls=%async_computation | async-start | bytes 2097152 | tf_op jit(solution)/shard_map/psum | solution.py:63
  9.1 157.8 %collective-permute-start = (bf16[2,128,512]{2,1,0:T(8,128)(2,1)}, bf16[2,128,512]{2,1,0:T(8,128)(2,1)}, u32[]{:S(2)}, u32[]{:S(2)}) collective-permute-start(bf16[2,128,512]{2,1,0:T(8,128)(2,1)} %get-tuple-element.56), channel_id=1, source_target_pairs={{0,8},{8,16},{16,24},{24,32},{32,40},{40,48},{48,56},{56,64},{64,7... | collective-permute-start | bytes 786440 | tf_op jit(solution)/shard_map/ppermute | solution.py:19
  12.9 154.0 %collective-permute-start.1 = (bf16[2,128,512]{2,1,0:T(8,128)(2,1)}, bf16[2,128,512]{2,1,0:T(8,128)(2,1)}, u32[]{:S(2)}, u32[]{:S(2)}) collective-permute-start(bf16[2,128,512]{2,1,0:T(8,128)(2,1)} %get-tuple-element.56), channel_id=1, source_target_pairs={{0,120},{8,0},{16,8},{24,16},{32,24},{40,32},{48,40},{56,48},{64,5... | collective-permute-start | bytes 786440 | tf_op jit(solution)/shard_map/ppermute | solution.py:19
  28.1 403.2 %all-reduce.5.cloned.1.call-start = ((), (), s32[]{:S(2)}) async-start(), calls=%async_computation.1 | async-start | bytes 4227072 | tf_op jit(solution)/shard_map/psum | solution.py:150
  85.5 5.8 %copy-start.40 = (f32[1,1,128,1024]{3,2,1,0:T(8,128)S(1)}, f32[1,1,128,1024]{3,2,1,0:T(8,128)}, u32[]{:S(2)}) copy-start(f32[1,1,128,1024]{3,2,1,0:T(8,128)} %get-tuple-element.22) | copy-start | bytes 1572868
  88.9 9.1 %copy-start.39 = (f32[1,1,128,1024]{3,2,1,0:T(8,128)S(1)}, f32[1,1,128,1024]{3,2,1,0:T(8,128)}, u32[]{:S(2)}) copy-start(f32[1,1,128,1024]{3,2,1,0:T(8,128)} %get-tuple-element.20) | copy-start | bytes 1572868
  89.5 84.5 %copy-start.76 = (f32[1024]{0:T(1024)}, f32[1024]{0:T(1024)S(1)}, u32[]{:S(2)}) copy-start(f32[1024]{0:T(1024)S(1)} %get-tuple-element.63) | copy-start | bytes 12292
  92.3 8.5 %copy-start.38 = (f32[1,1,128,1024]{3,2,1,0:T(8,128)S(1)}, f32[1,1,128,1024]{3,2,1,0:T(8,128)}, u32[]{:S(2)}) copy-start(f32[1,1,128,1024]{3,2,1,0:T(8,128)} %get-tuple-element.19) | copy-start | bytes 1572868
  99.0 5.6 %copy-start.65 = (bf16[1,128,1024]{2,1,0:T(8,128)(2,1)S(1)}, bf16[1,128,1024]{2,1,0:T(8,128)(2,1)}, u32[]{:S(2)}) copy-start(bf16[1,128,1024]{2,1,0:T(8,128)(2,1)} %get-tuple-element.32) | copy-start | bytes 786436
  107.2 59.8 %copy-start.64 = (bf16[2,1,128,512]{3,2,0,1:T(8,128)(2,1)S(1)}, bf16[2,1,128,512]{3,2,0,1:T(8,128)(2,1)}, u32[]{:S(2)}) copy-start(bf16[2,1,128,512]{3,2,0,1:T(8,128)(2,1)} %get-tuple-element.55) | copy-start | bytes 786436
  107.3 70.8 %copy-start.28 = (bf16[128,1024]{0,1:T(8,128)(2,1)}, bf16[128,1024]{0,1:T(8,128)(2,1)S(1)}, u32[]{:S(2)}) copy-start(bf16[128,1024]{0,1:T(8,128)(2,1)S(1)} %get-tuple-element.30) | copy-start | bytes 786436
  107.3 71.6 %copy-start.26 = (bf16[128,1024]{0,1:T(8,128)(2,1)}, bf16[128,1024]{0,1:T(8,128)(2,1)S(1)}, u32[]{:S(2)}) copy-start(bf16[128,1024]{0,1:T(8,128)(2,1)S(1)} %get-tuple-element.29) | copy-start | bytes 786436
  107.3 72.5 %copy-start.24 = (bf16[128,1024]{0,1:T(8,128)(2,1)}, bf16[128,1024]{0,1:T(8,128)(2,1)S(1)}, u32[]{:S(2)}) copy-start(bf16[128,1024]{0,1:T(8,128)(2,1)S(1)} %get-tuple-element.28) | copy-start | bytes 786436
  107.4 73.4 %copy-start.22 = (bf16[128,1024]{0,1:T(8,128)(2,1)}, bf16[128,1024]{0,1:T(8,128)(2,1)S(1)}, u32[]{:S(2)}) copy-start(bf16[128,1024]{0,1:T(8,128)(2,1)S(1)} %get-tuple-element.27) | copy-start | bytes 786436
  107.4 74.2 %copy-start.20 = (bf16[128,1024]{0,1:T(8,128)(2,1)}, bf16[128,1024]{0,1:T(8,128)(2,1)S(1)}, u32[]{:S(2)}) copy-start(bf16[128,1024]{0,1:T(8,128)(2,1)S(1)} %get-tuple-element.26) | copy-start | bytes 786436
  107.4 75.0 %copy-start.18 = (bf16[128,1024]{0,1:T(8,128)(2,1)}, bf16[128,1024]{0,1:T(8,128)(2,1)S(1)}, u32[]{:S(2)}) copy-start(bf16[128,1024]{0,1:T(8,128)(2,1)S(1)} %get-tuple-element.25) | copy-start | bytes 786436
  107.4 62.7 %copy-start.55 = (bf16[1,128,1024]{1,2,0:T(8,128)(2,1)}, bf16[1,128,1024]{1,2,0:T(8,128)(2,1)S(1)}, u32[]{:S(2)}) copy-start(bf16[1,128,1024]{1,2,0:T(8,128)(2,1)S(1)} %broadcast_select_fusion.2) | copy-start | bytes 786436
  107.5 61.8 %copy-start.102 = (pred[4]{0:T(512)(128)(4,1)}, pred[4]{0:T(512)(128)(4,1)S(1)}, u32[]{:S(2)}) copy-start(pred[4]{0:T(512)(128)(4,1)S(1)} %pad_add_fusion) | copy-start | bytes 16
  169.3 11.4 %copy-start.47 = (bf16[1,4,128,128]{3,2,0,1:T(8,128)(2,1)}, bf16[1,4,128,128]{3,2,0,1:T(8,128)(2,1)S(1)}, u32[]{:S(2)}) copy-start(bf16[1,4,128,128]{3,2,0,1:T(8,128)(2,1)S(1)} %get-tuple-element.42) | copy-start | bytes 393220
  169.3 12.2 %copy-start.45 = (bf16[1,4,128,128]{3,2,0,1:T(8,128)(2,1)}, bf16[1,4,128,128]{3,2,0,1:T(8,128)(2,1)S(1)}, u32[]{:S(2)}) copy-start(bf16[1,4,128,128]{3,2,0,1:T(8,128)(2,1)S(1)} %get-tuple-element.41) | copy-start | bytes 393220
  172.8 5.3 %copy-start.53 = (bf16[1,4,128,128]{3,2,0,1:T(8,128)(2,1)S(1)}, bf16[1,4,128,128]{3,2,0,1:T(8,128)(2,1)}, u32[]{:S(2)}) copy-start(bf16[1,4,128,128]{3,2,0,1:T(8,128)(2,1)} %get-tuple-element.45) | copy-start | bytes 393220
  174.8 20.3 %collective-permute-start.2 = (bf16[128,1024]{0,1:T(8,128)(2,1)}, bf16[128,1024]{0,1:T(8,128)(2,1)}, u32[]{:S(2)}, u32[]{:S(2)}) collective-permute-start(bf16[128,1024]{0,1:T(8,128)(2,1)} %fusion.52), channel_id=1, source_target_pairs={{128,0},{256,128},{384,256},{129,1},{257,129},{385,257},{130,2},{2... | collective-permute-start | bytes 786440 | tf_op jit(solution)/shard_map/ppermute | solution.py:14
  179.4 12.5 %copy-start.6 = (f32[512,128,8]{1,0,2:T(8,128)}, f32[512,128,8]{1,0,2:T(8,128)S(1)}, u32[]{:S(2)}) copy-start(f32[512,128,8]{1,0,2:T(8,128)S(1)} %get-tuple-element.75) | copy-start | bytes 6291460
  179.5 12.5 %copy-start.72 = (f32[8,128]{1,0:T(8,128)}, f32[8,128]{1,0:T(8,128)S(1)}, u32[]{:S(2)}) copy-start(f32[8,128]{1,0:T(8,128)S(1)} %get-tuple-element.74) | copy-start | bytes 12292
  179.8 12.1 %copy-start.86 = (f32[8,128]{1,0:T(8,128)}, f32[8,128]{1,0:T(8,128)S(1)}, u32[]{:S(2)}) copy-start(f32[8,128]{1,0:T(8,128)S(1)} %fusion.34) | copy-start | bytes 12292
  180.3 7.1 %copy-start.4 = (f32[512,128,8]{1,0,2:T(8,128)}, f32[512,128,8]{1,0,2:T(8,128)S(1)}, u32[]{:S(2)}) copy-start(f32[512,128,8]{1,0,2:T(8,128)S(1)} %get-tuple-element.81) | copy-start | bytes 6291460
  180.7 6.8 %copy-start.84 = (f32[8,128]{1,0:T(8,128)}, f32[8,128]{1,0:T(8,128)S(1)}, u32[]{:S(2)}) copy-start(f32[8,128]{1,0:T(8,128)S(1)} %fusion.36) | copy-start | bytes 12292
  198.8 5.5 %copy-start.16 = (bf16[512,128,8]{1,0,2:T(8,128)(2,1)S(1)}, bf16[512,128,8]{1,0,2:T(8,128)(2,1)}, u32[]{:S(2)}) copy-start(bf16[512,128,8]{1,0,2:T(8,128)(2,1)} %divide_convert_fusion.5) | copy-start | bytes 3145732
  201.0 9.5 %collective-permute-start.3 = (bf16[128,1024]{0,1:T(8,128)(2,1)}, bf16[128,1024]{0,1:T(8,128)(2,1)}, u32[]{:S(2)}, u32[]{:S(2)}) collective-permute-start(bf16[128,1024]{0,1:T(8,128)(2,1)} %get-tuple-element.73), channel_id=1, source_target_pairs={{128,0},{256,128},{384,256},{129,1},{257,129},{385,257},{130,2},{2... | collective-permute-start | bytes 786440 | tf_op jit(solution)/shard_map/ppermute | solution.py:14
  204.3 6.2 %copy-start.61 = (bf16[1,128,1024]{1,2,0:T(8,128)(2,1)S(1)}, bf16[1,128,1024]{1,2,0:T(8,128)(2,1)}, u32[]{:S(2)}) copy-start(bf16[1,128,1024]{1,2,0:T(8,128)(2,1)} %copy.149) | copy-start | bytes 786436
  204.3 7.2 %copy-start.7 = (f32[512,128,8]{1,0,2:T(8,128)S(1)}, f32[512,128,8]{1,0,2:T(8,128)}, u32[]{:S(2)}) copy-start(f32[512,128,8]{1,0,2:T(8,128)} %copy-done.6) | copy-start | bytes 6291460
  204.3 7.2 %copy-start.70 = (bf16[1,4,128,128]{3,2,0,1:T(8,128)(2,1)S(1)}, bf16[1,4,128,128]{3,2,0,1:T(8,128)(2,1)}, u32[]{:S(2)}) copy-start(bf16[1,4,128,128]{3,2,0,1:T(8,128)(2,1)} %get-tuple-element.50) | copy-start | bytes 393220
  204.3 7.2 %copy-start.73 = (f32[8,128]{1,0:T(8,128)S(1)}, f32[8,128]{1,0:T(8,128)}, u32[]{:S(2)}) copy-start(f32[8,128]{1,0:T(8,128)} %copy-done.72) | copy-start | bytes 12292
  204.3 7.2 %copy-start.87 = (f32[8,128]{1,0:T(8,128)S(1)}, f32[8,128]{1,0:T(8,128)}, u32[]{:S(2)}) copy-start(f32[8,128]{1,0:T(8,128)} %copy-done.86) | copy-start | bytes 12292
  216.2 10.1 %collective-permute-start.4 = (bf16[128,1024]{0,1:T(8,128)(2,1)}, bf16[128,1024]{0,1:T(8,128)(2,1)}, u32[]{:S(2)}, u32[]{:S(2)}) collective-permute-start(bf16[128,1024]{0,1:T(8,128)(2,1)} %get-tuple-element.79), channel_id=1, source_target_pairs={{128,0},{256,128},{384,256},{129,1},{257,129},{385,257},{130,2},{2... | collective-permute-start | bytes 786440 | tf_op jit(solution)/shard_map/ppermute | solution.py:14
  219.3 7.0 %copy-start.60 = (bf16[1,128,1024]{1,2,0:T(8,128)(2,1)S(1)}, bf16[1,128,1024]{1,2,0:T(8,128)(2,1)}, u32[]{:S(2)}) copy-start(bf16[1,128,1024]{1,2,0:T(8,128)(2,1)} %copy.154) | copy-start | bytes 786436
  219.3 8.0 %copy-start.5 = (f32[512,128,8]{1,0,2:T(8,128)S(1)}, f32[512,128,8]{1,0,2:T(8,128)}, u32[]{:S(2)}) copy-start(f32[512,128,8]{1,0,2:T(8,128)} %copy-done.4) | copy-start | bytes 6291460
  219.3 8.0 %copy-start.69 = (bf16[1,4,128,128]{3,2,0,1:T(8,128)(2,1)S(1)}, bf16[1,4,128,128]{3,2,0,1:T(8,128)(2,1)}, u32[]{:S(2)}) copy-start(bf16[1,4,128,128]{3,2,0,1:T(8,128)(2,1)} %get-tuple-element.49) | copy-start | bytes 393220
  219.3 8.0 %copy-start.85 = (f32[8,128]{1,0:T(8,128)S(1)}, f32[8,128]{1,0:T(8,128)}, u32[]{:S(2)}) copy-start(f32[8,128]{1,0:T(8,128)} %copy-done.84) | copy-start | bytes 12292
  230.1 5.3 %copy-start.14 = (bf16[512,128,8]{1,0,2:T(8,128)(2,1)S(1)}, bf16[512,128,8]{1,0,2:T(8,128)(2,1)}, u32[]{:S(2)}) copy-start(bf16[512,128,8]{1,0,2:T(8,128)(2,1)} %divide_convert_fusion.3) | copy-start | bytes 3145732
  232.1 12.6 %copy-start.83 = (f32[8,128]{1,0:T(8,128)S(1)}, f32[8,128]{1,0:T(8,128)}, u32[]{:S(2)}) copy-start(f32[8,128]{1,0:T(8,128)} %copy-done.82) | copy-start | bytes 12292
  232.1 11.6 %collective-permute-start.5 = (bf16[128,1024]{0,1:T(8,128)(2,1)}, bf16[128,1024]{0,1:T(8,128)(2,1)}, u32[]{:S(2)}, u32[]{:S(2)}) collective-permute-start(bf16[128,1024]{0,1:T(8,128)(2,1)} %get-tuple-element.85), channel_id=1, source_target_pairs={{128,0},{256,128},{384,256},{129,1},{257,129},{385,257},{130,2},{2... | collective-permute-start | bytes 786440 | tf_op jit(solution)/shard_map/ppermute | solution.py:14
  235.3 8.4 %copy-start.59 = (bf16[1,128,1024]{1,2,0:T(8,128)(2,1)S(1)}, bf16[1,128,1024]{1,2,0:T(8,128)(2,1)}, u32[]{:S(2)}) copy-start(bf16[1,128,1024]{1,2,0:T(8,128)(2,1)} %copy.159) | copy-start | bytes 786436
  235.3 9.4 %copy-start.3 = (f32[512,128,8]{1,0,2:T(8,128)S(1)}, f32[512,128,8]{1,0,2:T(8,128)}, u32[]{:S(2)}) copy-start(f32[512,128,8]{1,0,2:T(8,128)} %copy-done.2) | copy-start | bytes 6291460
  235.3 9.4 %copy-start.68 = (bf16[1,4,128,128]{3,2,0,1:T(8,128)(2,1)S(1)}, bf16[1,4,128,128]{3,2,0,1:T(8,128)(2,1)}, u32[]{:S(2)}) copy-start(bf16[1,4,128,128]{3,2,0,1:T(8,128)(2,1)} %get-tuple-element.48) | copy-start | bytes 393220
  247.4 5.3 %copy-start.13 = (bf16[512,128,8]{1,0,2:T(8,128)(2,1)S(1)}, bf16[512,128,8]{1,0,2:T(8,128)(2,1)}, u32[]{:S(2)}) copy-start(bf16[512,128,8]{1,0,2:T(8,128)(2,1)} %divide_convert_fusion.2) | copy-start | bytes 3145732
  249.5 12.1 %copy-start.81 = (f32[8,128]{1,0:T(8,128)S(1)}, f32[8,128]{1,0:T(8,128)}, u32[]{:S(2)}) copy-start(f32[8,128]{1,0:T(8,128)} %copy-done.80) | copy-start | bytes 12292
  249.5 11.1 %collective-permute-start.6 = (bf16[128,1024]{0,1:T(8,128)(2,1)}, bf16[128,1024]{0,1:T(8,128)(2,1)}, u32[]{:S(2)}, u32[]{:S(2)}) collective-permute-start(bf16[128,1024]{0,1:T(8,128)(2,1)} %get-tuple-element.91), channel_id=1, source_target_pairs={{128,0},{256,128},{384,256},{129,1},{257,129},{385,257},{130,2},{2... | collective-permute-start | bytes 786440 | tf_op jit(solution)/shard_map/ppermute | solution.py:14
  252.7 7.9 %copy-start.58 = (bf16[1,128,1024]{1,2,0:T(8,128)(2,1)S(1)}, bf16[1,128,1024]{1,2,0:T(8,128)(2,1)}, u32[]{:S(2)}) copy-start(bf16[1,128,1024]{1,2,0:T(8,128)(2,1)} %copy.164) | copy-start | bytes 786436
  252.7 8.9 %copy-start.1 = (f32[512,128,8]{1,0,2:T(8,128)S(1)}, f32[512,128,8]{1,0,2:T(8,128)}, u32[]{:S(2)}) copy-start(f32[512,128,8]{1,0,2:T(8,128)} %copy-done) | copy-start | bytes 6291460
  252.7 8.9 %copy-start.67 = (bf16[1,4,128,128]{3,2,0,1:T(8,128)(2,1)S(1)}, bf16[1,4,128,128]{3,2,0,1:T(8,128)(2,1)}, u32[]{:S(2)}) copy-start(bf16[1,4,128,128]{3,2,0,1:T(8,128)(2,1)} %get-tuple-element.47) | copy-start | bytes 393220
  264.3 5.6 %copy-start.12 = (bf16[512,128,8]{1,0,2:T(8,128)(2,1)S(1)}, bf16[512,128,8]{1,0,2:T(8,128)(2,1)}, u32[]{:S(2)}) copy-start(bf16[512,128,8]{1,0,2:T(8,128)(2,1)} %divide_convert_fusion.1) | copy-start | bytes 3145732
  266.4 9.7 %copy-start.79 = (f32[8,128]{1,0:T(8,128)S(1)}, f32[8,128]{1,0:T(8,128)}, u32[]{:S(2)}) copy-start(f32[8,128]{1,0:T(8,128)} %copy-done.78) | copy-start | bytes 12292
  266.4 8.7 %collective-permute-start.7 = (bf16[128,1024]{0,1:T(8,128)(2,1)}, bf16[128,1024]{0,1:T(8,128)(2,1)}, u32[]{:S(2)}, u32[]{:S(2)}) collective-permute-start(bf16[128,1024]{0,1:T(8,128)(2,1)} %get-tuple-element.97), channel_id=1, source_target_pairs={{128,0},{256,128},{384,256},{129,1},{257,129},{385,257},{130,2},{2... | collective-permute-start | bytes 786440 | tf_op jit(solution)/shard_map/ppermute | solution.py:14
  269.8 5.2 %copy-start.57 = (bf16[1,128,1024]{1,2,0:T(8,128)(2,1)S(1)}, bf16[1,128,1024]{1,2,0:T(8,128)(2,1)}, u32[]{:S(2)}) copy-start(bf16[1,128,1024]{1,2,0:T(8,128)(2,1)} %copy.169) | copy-start | bytes 786436
  269.8 6.2 %copy-start.66 = (bf16[1,4,128,128]{3,2,0,1:T(8,128)(2,1)S(1)}, bf16[1,4,128,128]{3,2,0,1:T(8,128)(2,1)}, u32[]{:S(2)}) copy-start(bf16[1,4,128,128]{3,2,0,1:T(8,128)(2,1)} %get-tuple-element.39) | copy-start | bytes 393220
  289.0 5.8 %copy-start.43 = (f32[2,1,128,512]{2,3,1,0:T(8,128)S(1)}, f32[2,1,128,512]{2,3,1,0:T(8,128)}, u32[]{:S(2)}) copy-start(f32[2,1,128,512]{2,3,1,0:T(8,128)} %get-tuple-element.17) | copy-start | bytes 1572868
  289.0 8.8 %copy-start.42 = (f32[2,1,128,512]{2,3,1,0:T(8,128)S(1)}, f32[2,1,128,512]{2,3,1,0:T(8,128)}, u32[]{:S(2)}) copy-start(f32[2,1,128,512]{2,3,1,0:T(8,128)} %get-tuple-element.14) | copy-start | bytes 1572868
  289.0 9.0 %copy-start.37 = (f32[128,8,128]{2,0,1:T(8,128)S(1)}, f32[128,8,128]{2,0,1:T(8,128)}, u32[]{:S(2)}) copy-start(f32[128,8,128]{2,0,1:T(8,128)} %get-tuple-element.115) | copy-start | bytes 1572868
  289.0 9.0 %copy-start.90 = (f32[1024]{0:T(1024)S(1)}, f32[1024]{0:T(1024)}, u32[]{:S(2)}) copy-start(f32[1024]{0:T(1024)} %get-tuple-element.57) | copy-start | bytes 12292
  290.2 146.2 %collective-permute-start.8 = (f32[2,128,512]{2,1,0:T(8,128)S(1)}, f32[2,128,512]{2,1,0:T(8,128)}, u32[]{:S(2)}, u32[]{:S(2)}) collective-permute-start(f32[2,128,512]{2,1,0:T(8,128)S(1)} %bitcast.642), channel_id=1, source_target_pairs={{0,120},{8,0},{16,8},{24,16},{32,24},{40,32},{48,40},{56,48},{64,5... | collective-permute-start | bytes 1572872 | tf_op jit(solution)/shard_map/ppermute | solution.py:19
  295.8 140.6 %collective-permute-start.9 = (f32[2,128,512]{2,1,0:T(8,128)}, f32[2,128,512]{2,1,0:T(8,128)}, u32[]{:S(2)}, u32[]{:S(2)}) collective-permute-start(f32[2,128,512]{2,1,0:T(8,128)} %bitcast.174), channel_id=1, source_target_pairs={{0,8},{8,16},{16,24},{24,32},{32,40},{40,48},{48,56},{56,64},{64,7... | collective-permute-start | bytes 1572872 | tf_op jit(solution)/shard_map/ppermute | solution.py:19
  (54 other events, 106.5 us)
Sparse Core Ops, SparseCore 0:
  28.2 137.2 all-reduce.2
  289.1 142.1 all-reduce.4

commit v8 on v7

--- a/solution.py
+++ b/solution.py
@@ -54,14 +54,23 @@
     lane_sources = jnp.stack([ctx_pos == 0, ctx_pos == first_extra, ctx_pos == last_extra, is_last])
     lane_users = jnp.stack([uses_zero, is_first, is_last, is_second])
 
-    gain_placed = jnp.zeros((feature_count,), jnp.float32)
+    gain_own = query_gain[0]
+    gain_high = gain_own.astype(jnp.bfloat16)
+    gain_rest = gain_own - gain_high.astype(jnp.float32)
+    gain_mid = gain_rest.astype(jnp.bfloat16)
+    gain_low = (gain_rest - gain_mid.astype(jnp.float32)).astype(jnp.bfloat16)
     gain_placed = lax.dynamic_update_slice_in_dim(
-        gain_placed, query_gain[0], ctx_pos * gain_width, 0
+        jnp.zeros((3, feature_count), jnp.bfloat16),
+        jnp.stack([gain_high, gain_mid, gain_low]),
+        ctx_pos * gain_width,
+        1,
     )
     own_kv = jnp.stack([key_states[0, 0], value_states[0, 0]])
     lanes_out = jnp.where(lane_sources[:, None, None, None], own_kv[None], jnp.zeros_like(own_kv)[None])
-    lanes_in = lax.psum(lanes_out, "ctx")
-    gain_row = lax.psum(gain_placed, "ctx")
+    came_in = lax.psum(jnp.concatenate([lanes_out.reshape(-1), gain_placed.reshape(-1)]), "ctx")
+    lanes_in = came_in[: lanes_out.size].reshape(lanes_out.shape)
+    gain_pieces = came_in[lanes_out.size :].reshape(3, feature_count).astype(jnp.float32)
+    gain_row = (gain_pieces[0] + gain_pieces[1]) + gain_pieces[2]
     extra_kv = jnp.sum(
         jnp.where(lane_users[:, None, None, None], lanes_in, jnp.zeros_like(lanes_in)), axis=0
     )
@@ -147,14 +156,16 @@
         lane_users[:, None, None, None], extra_part[None], jnp.zeros_like(extra_part)[None]
     )
     gain_full = own_turns(gain_turns).reshape(feature_count)
-    summed = lax.psum(jnp.concatenate([lanes_back.reshape(-1), gain_full]), "ctx")
-    lanes_sum = summed[: lanes_back.size].reshape(lanes_back.shape)
+    zero_size = lanes_back[0].size
+    summed = lax.psum(jnp.concatenate([lanes_back[0].reshape(-1), gain_full]), "ctx")
+    single_sum = lax.psum(lanes_back[1:].astype(jnp.bfloat16), "ctx").astype(jnp.float32)
+    lanes_sum = jnp.concatenate([summed[:zero_size].reshape(lanes_back[:1].shape), single_sum])
     extra_back = jnp.sum(
         jnp.where(lane_sources[:, None, None, None], lanes_sum, jnp.zeros_like(lanes_sum)), axis=0
     )
     kv_total = all_parts[:, 1] + from_next + from_prev + extra_back
     kv_out = kv_total.astype(jnp.bfloat16)
-    gain_ctx = lax.dynamic_slice_in_dim(summed[lanes_back.size :], ctx_pos * gain_width, gain_width, 0)
+    gain_ctx = lax.dynamic_slice_in_dim(summed[zero_size:], ctx_pos * gain_width, gain_width, 0)
     gain_total = lax.psum(gain_ctx, "dp")
     return (stream_out[None, None], kv_out[0][None, None], kv_out[1][None, None], gain_total[None])
 

time: 461 us -> 561 us (1.22)
  waiting for transfers between devices: 210 us -> 372 us
  blocking collectives: 65.1 us -> 10.5 us
    psum x2 -> x3, waiting for transfers between devices: 188 us -> 351 us  [the longest x1 125 us: shards(): lax.psum(lanes_back[1:].astype(jnp.bfloat16), 'ctx').astype(jnp.float32)]
    psum x1 -> x0, blocking collectives: 54.6 us -> none  [shards(): gain_row = lax.psum(gain_placed, 'ctx')]
    unnamed x219 -> x220, local copies, waits for them, and re-layouts: 11.3 us -> 11.1 us
  transfers between devices with their start and end apart: 12 -> 13, of which waited for: 7 -> 8; matrix products, arithmetic and copies ran while one was open for 17% -> 13% of each run, Pallas kernels for 0% -> 0%
where the time goes in v8:
time: 561 us; the launch traced here: 559 us
  waiting for transfers between devices  372 us (66%)
  other arithmetic  55.8 us (10%)
  local copies, waits for them, and re-layouts  52.1 us (9%)
  starting transfers between devices  29.2 us (5%)
  matrix products  22.7 us (4%)
  between operations  16.5 us (3%)
  blocking collectives  10.5 us (2%)
    psum x1, waiting for transfers between devices, shards(): lax.psum(lanes_back[1:].astype(jnp.bfloat16), 'ctx').astype(jnp.float32)  125 us
    psum x1, waiting for transfers between devices, shards(): lax.psum(jnp.concatenate([lanes_back[0].reshape(-1), gain_full]), 'ctx')  118 us
    psum x1, waiting for transfers between devices, shards(): lax.psum(jnp.concatenate([lanes_out.reshape(-1), gain_placed.reshape(-1)]...  108 us
    ppermute x6, waiting for transfers between devices, passed_along(): return lax.ppermute(block, axis, route)  21.5 us
    ppermute x4, starting transfers between devices, cyclic_shift(): lax.ppermute(block, axis, [(i, (i + distance) % count) for i in range(cou...  20.4 us
    unnamed x12, other arithmetic  16.8 us
  transfers between devices with their start and end apart: 13, of which 8 were waited for; matrix products, arithmetic and copies ran while one was open for 13% of the time, Pallas kernels for 0%

profile of v8, /device:TPU:6, one launch (start us, length us, event | category | flops | bytes accessed | tf_op | source)
XLA Modules:
  0.0 559.3 jit_solution(5078420554884760606)
XLA Ops:
  11.0 1.8 fusion.77
  12.9 1.1 broadcast_select_fusion.1
  15.5 11.4 %collective-permute-start.1 = (bf16[2,128,512]{2,1,0:T(8,128)(2,1)}, bf16[2,128,512]{2,1,0:T(8,128)(2,1)}, u32[]{:S(2)}, u32[]{:S(2)}) collective-permute-start(bf16[2,128,512]{2,1,0:T(8,128)(2,1)} %get-tuple-element.56), channel_id=1, source_target_pairs={{0,120},{8,0},{16,8},{24,16},{32,24},{40,32},{48,40},{56,48},{64,5... | collective-permute-start | bytes 786440 | tf_op jit(solution)/shard_map/ppermute | solution.py:19
  27.0 1.9 collective-permute-start
  29.6 1.9 dynamic-slice_convert_fusion
  31.5 2.0 copy.193
  33.6 1.3 constant_dynamic-slice_fusion.10
  34.8 1.2 copy.250
  36.0 2.0 copy.194
  38.0 1.8 copy.144
  42.8 1.9 copy.154
  45.7 1.8 copy.159
  52.0 107.9 %all-reduce.4.cloned.1.call-done = bf16[536576]{0:T(1024)(128)(2,1)} async-done(((bf16[536576]{0:T(1024)(128)(2,1)}), bf16[536576]{0:T(1024)(128)(2,1)}) %all-reduce.4.cloned.1.call-update) | async-done | bytes 1073168 | tf_op jit(solution)/shard_map/psum | solution.py:70
  159.8 1.2 slice-done
  164.5 1.2 pad_maximum_fusion.1
  165.6 1.1 constant_dynamic-slice_fusion.9
  171.6 1.5 collective-permute-start.2
  180.9 1.4 divide_convert_fusion.5
  182.3 1.4 divide_convert_fusion.4
  183.7 1.4 divide_convert_fusion.3
  185.2 1.4 divide_convert_fusion.2
  186.6 1.4 divide_convert_fusion.1
  188.0 1.4 divide_convert_fusion
  193.7 1.1 fusion.49
  194.9 1.1 fusion.70
  197.0 1.5 collective-permute-start.3
  198.5 1.8 copy.177
  200.8 2.1 maximum_dynamic-update-slice_fusion.5
  202.9 3.4 collective-permute-done.3
  208.8 1.1 fusion.48
  210.0 1.1 fusion.69
  212.0 1.3 collective-permute-start.4
  213.3 1.8 copy.179
  215.6 2.1 maximum_dynamic-update-slice_fusion.4
  217.7 4.2 collective-permute-done.4
  224.5 1.2 fusion.47
  225.6 1.1 fusion.68
  227.7 1.4 collective-permute-start.5
  229.1 1.8 copy.181
  231.4 2.0 maximum_dynamic-update-slice_fusion.3
  233.5 6.0 %collective-permute-done.5 = bf16[128,1024]{0,1:T(8,128)(2,1)} collective-permute-done((bf16[128,1024]{0,1:T(8,128)(2,1)}, bf16[128,1024]{0,1:T(8,128)(2,1)}, u32[]{:S(2)}, u32[]{:S(2)}) %collective-permute-start.5) | collective-permute-done | bytes 262176 | tf_op jit(solution)/shard_map/ppermute | solution.py:14
  242.0 1.1 fusion.46
  244.7 1.4 collective-permute-start.6
  246.1 1.8 copy.183
  248.4 2.0 maximum_dynamic-update-slice_fusion.2
  250.4 4.9 collective-permute-done.6
  257.9 1.1 fusion.45
  260.5 1.7 collective-permute-start.7
  262.2 1.8 copy.185
  264.5 1.8 maximum_dynamic-update-slice_fusion.1
  266.3 3.0 collective-permute-done.7
  274.3 1.7 dynamic-slice_bitcast_fusion
  276.3 1.2 fusion.78
  280.4 2.0 copy.253
  282.5 3.2 collective-permute-start.9
  286.6 3.9 collective-permute-start.8
  291.4 1.4 constant_dynamic-slice_fusion.7
  292.8 1.3 copy.200
  294.3 118.4 %all-reduce.6.cloned.1.call-done = f32[135168]{0:T(1024)} async-done(((f32[135168]{0:T(1024)}), f32[135168]{0:T(1024)}) %all-reduce.6.cloned.1.call-update) | async-done | bytes 540688 | tf_op jit(solution)/shard_map/psum | solution.py:160
  412.7 1.1 slice.146
  414.0 10.5 %psum.31 = f32[1,256]{1,0:T(1,128)} all-reduce(f32[1,256]{1,0:T(1,128)S(1)} %bitcast.676), channel_id=1, replica_groups=mesh['section'=4,'ctx'=16,'dp'=8] {'dp'}, use_global_device_ids=true, to_apply=%region_35.36 | all-reduce | flops 256 | bytes 2048 | tf_op jit(solution)/shard_map/psum | solution.py:169
  424.5 124.6 %all-reduce.8.cloned.1.call-done = bf16[3,2,128,512]{3,2,1,0:T(8,128)(2,1)} async-done(((bf16[3,2,128,512]{3,2,1,0:T(8,128)(2,1)}), bf16[3,2,128,512]{3,2,1,0:T(8,128)(2,1)}) %all-reduce.8.cloned.1.call-update) | async-done | bytes 786448 | tf_op jit(solution)/shard_map/psum | solution.py:161
  549.1 1.3 convert_element_type.325
  550.8 1.2 fusion.64
  (327 shorter events, 62.9 us)
Async XLA Ops:
  7.2 152.7 %all-reduce.4.cloned.1.call-start = ((), (), s32[]{:S(2)}) async-start(), calls=%async_computation | async-start | bytes 2146304 | tf_op jit(solution)/shard_map/psum | solution.py:70
  14.4 14.5 %copy-start.10 = (bf16[1,1,128,4096]{3,2,1,0:T(8,128)(2,1)S(1)}, bf16[1,1,128,4096]{3,2,1,0:T(8,128)(2,1)}, u32[]{:S(2)}) copy-start(bf16[1,1,128,4096]{3,2,1,0:T(8,128)(2,1)} %param.6) | copy-start | bytes 3145732
  15.5 397.2 %all-reduce.6.cloned.1.call-start = ((), (), s32[]{:S(2)}) async-start(), calls=%async_computation.1 | async-start | bytes 1081344 | tf_op jit(solution)/shard_map/psum | solution.py:160
  15.5 148.9 %collective-permute-start.1 = (bf16[2,128,512]{2,1,0:T(8,128)(2,1)}, bf16[2,128,512]{2,1,0:T(8,128)(2,1)}, u32[]{:S(2)}, u32[]{:S(2)}) collective-permute-start(bf16[2,128,512]{2,1,0:T(8,128)(2,1)} %get-tuple-element.56), channel_id=1, source_target_pairs={{0,120},{8,0},{16,8},{24,16},{32,24},{40,32},{48,40},{56,48},{64,5... | collective-permute-start | bytes 786440 | tf_op jit(solution)/shard_map/ppermute | solution.py:19
  27.0 137.5 %collective-permute-start = (bf16[2,128,512]{2,1,0:T(8,128)(2,1)}, bf16[2,128,512]{2,1,0:T(8,128)(2,1)}, u32[]{:S(2)}, u32[]{:S(2)}) collective-permute-start(bf16[2,128,512]{2,1,0:T(8,128)(2,1)} %get-tuple-element.56), channel_id=1, source_target_pairs={{0,8},{8,16},{16,24},{24,32},{32,40},{40,48},{48,56},{56,64},{64,7... | collective-permute-start | bytes 786440 | tf_op jit(solution)/shard_map/ppermute | solution.py:19
  33.6 6.3 %copy-start.41 = (f32[1,1,128,1024]{3,2,1,0:T(8,128)S(1)}, f32[1,1,128,1024]{3,2,1,0:T(8,128)}, u32[]{:S(2)}) copy-start(f32[1,1,128,1024]{3,2,1,0:T(8,128)} %get-tuple-element.21) | copy-start | bytes 1572868
  34.8 7.0 %copy-start.40 = (f32[1,1,128,1024]{3,2,1,0:T(8,128)S(1)}, f32[1,1,128,1024]{3,2,1,0:T(8,128)}, u32[]{:S(2)}) copy-start(f32[1,1,128,1024]{3,2,1,0:T(8,128)} %get-tuple-element.20) | copy-start | bytes 1572868
  38.0 6.6 %copy-start.39 = (f32[1,1,128,1024]{3,2,1,0:T(8,128)S(1)}, f32[1,1,128,1024]{3,2,1,0:T(8,128)}, u32[]{:S(2)}) copy-start(f32[1,1,128,1024]{3,2,1,0:T(8,128)} %get-tuple-element.19) | copy-start | bytes 1572868
  40.9 6.6 %copy-start.38 = (f32[1,1,128,1024]{3,2,1,0:T(8,128)S(1)}, f32[1,1,128,1024]{3,2,1,0:T(8,128)}, u32[]{:S(2)}) copy-start(f32[1,1,128,1024]{3,2,1,0:T(8,128)} %get-tuple-element.24) | copy-start | bytes 1572868
  41.8 6.7 %copy-start.65 = (bf16[1,128,1024]{2,1,0:T(8,128)(2,1)S(1)}, bf16[1,128,1024]{2,1,0:T(8,128)(2,1)}, u32[]{:S(2)}) copy-start(bf16[1,128,1024]{2,1,0:T(8,128)(2,1)} %get-tuple-element.38) | copy-start | bytes 786436
  42.8 6.5 %copy-start.64 = (bf16[1,128,1024]{2,1,0:T(8,128)(2,1)S(1)}, bf16[1,128,1024]{2,1,0:T(8,128)(2,1)}, u32[]{:S(2)}) copy-start(bf16[1,128,1024]{2,1,0:T(8,128)(2,1)} %get-tuple-element.32) | copy-start | bytes 786436
  42.8 7.4 %copy-start.37 = (f32[1,1,128,1024]{3,2,1,0:T(8,128)S(1)}, f32[1,1,128,1024]{3,2,1,0:T(8,128)}, u32[]{:S(2)}) copy-start(f32[1,1,128,1024]{3,2,1,0:T(8,128)} %get-tuple-element.18) | copy-start | bytes 1572868
  51.2 112.9 %copy-start.103 = (pred[4]{0:T(512)(128)(4,1)}, pred[4]{0:T(512)(128)(4,1)S(1)}, u32[]{:S(2)}) copy-start(pred[4]{0:T(512)(128)(4,1)S(1)} %pad_add_fusion.1) | copy-start | bytes 16
  163.3 10.6 %copy-start.28 = (bf16[128,1024]{0,1:T(8,128)(2,1)}, bf16[128,1024]{0,1:T(8,128)(2,1)S(1)}, u32[]{:S(2)}) copy-start(bf16[128,1024]{0,1:T(8,128)(2,1)S(1)} %get-tuple-element.30) | copy-start | bytes 786436
  163.4 11.4 %copy-start.26 = (bf16[128,1024]{0,1:T(8,128)(2,1)}, bf16[128,1024]{0,1:T(8,128)(2,1)S(1)}, u32[]{:S(2)}) copy-start(bf16[128,1024]{0,1:T(8,128)(2,1)S(1)} %get-tuple-element.29) | copy-start | bytes 786436
  163.4 12.2 %copy-start.24 = (bf16[128,1024]{0,1:T(8,128)(2,1)}, bf16[128,1024]{0,1:T(8,128)(2,1)S(1)}, u32[]{:S(2)}) copy-start(bf16[128,1024]{0,1:T(8,128)(2,1)S(1)} %get-tuple-element.28) | copy-start | bytes 786436
  163.4 13.1 %copy-start.22 = (bf16[128,1024]{0,1:T(8,128)(2,1)}, bf16[128,1024]{0,1:T(8,128)(2,1)S(1)}, u32[]{:S(2)}) copy-start(bf16[128,1024]{0,1:T(8,128)(2,1)S(1)} %get-tuple-element.27) | copy-start | bytes 786436
  163.4 13.9 %copy-start.20 = (bf16[128,1024]{0,1:T(8,128)(2,1)}, bf16[128,1024]{0,1:T(8,128)(2,1)S(1)}, u32[]{:S(2)}) copy-start(bf16[128,1024]{0,1:T(8,128)(2,1)S(1)} %get-tuple-element.26) | copy-start | bytes 786436
  163.4 14.7 %copy-start.18 = (bf16[128,1024]{0,1:T(8,128)(2,1)}, bf16[128,1024]{0,1:T(8,128)(2,1)S(1)}, u32[]{:S(2)}) copy-start(bf16[128,1024]{0,1:T(8,128)(2,1)S(1)} %get-tuple-element.25) | copy-start | bytes 786436
  164.2 6.5 %copy-start.77 = (f32[1024]{0:T(1024)}, f32[1024]{0:T(1024)S(1)}, u32[]{:S(2)}) copy-start(f32[1024]{0:T(1024)S(1)} %get-tuple-element.63) | copy-start | bytes 12292
  166.8 7.2 %copy-start.52 = (bf16[1,4,128,128]{3,2,0,1:T(8,128)(2,1)}, bf16[1,4,128,128]{3,2,0,1:T(8,128)(2,1)S(1)}, u32[]{:S(2)}) copy-start(bf16[1,4,128,128]{3,2,0,1:T(8,128)(2,1)S(1)} %get-tuple-element.45) | copy-start | bytes 393220
  166.8 8.0 %copy-start.50 = (bf16[1,4,128,128]{3,2,0,1:T(8,128)(2,1)}, bf16[1,4,128,128]{3,2,0,1:T(8,128)(2,1)S(1)}, u32[]{:S(2)}) copy-start(bf16[1,4,128,128]{3,2,0,1:T(8,128)(2,1)S(1)} %get-tuple-element.44) | copy-start | bytes 393220
  166.8 8.8 %copy-start.48 = (bf16[1,4,128,128]{3,2,0,1:T(8,128)(2,1)}, bf16[1,4,128,128]{3,2,0,1:T(8,128)(2,1)S(1)}, u32[]{:S(2)}) copy-start(bf16[1,4,128,128]{3,2,0,1:T(8,128)(2,1)S(1)} %get-tuple-element.43) | copy-start | bytes 393220
  166.8 9.7 %copy-start.46 = (bf16[1,4,128,128]{3,2,0,1:T(8,128)(2,1)}, bf16[1,4,128,128]{3,2,0,1:T(8,128)(2,1)S(1)}, u32[]{:S(2)}) copy-start(bf16[1,4,128,128]{3,2,0,1:T(8,128)(2,1)S(1)} %get-tuple-element.42) | copy-start | bytes 393220
  166.8 10.5 %copy-start.44 = (bf16[1,4,128,128]{3,2,0,1:T(8,128)(2,1)}, bf16[1,4,128,128]{3,2,0,1:T(8,128)(2,1)S(1)}, u32[]{:S(2)}) copy-start(bf16[1,4,128,128]{3,2,0,1:T(8,128)(2,1)S(1)} %get-tuple-element.41) | copy-start | bytes 393220
  171.6 19.6 %collective-permute-start.2 = (bf16[128,1024]{0,1:T(8,128)(2,1)}, bf16[128,1024]{0,1:T(8,128)(2,1)}, u32[]{:S(2)}, u32[]{:S(2)}) collective-permute-start(bf16[128,1024]{0,1:T(8,128)(2,1)} %fusion.53), channel_id=1, source_target_pairs={{128,0},{256,128},{384,256},{129,1},{257,129},{385,257},{130,2},{2... | collective-permute-start | bytes 786440 | tf_op jit(solution)/shard_map/ppermute | solution.py:14
  175.2 7.1 %copy-start.6 = (f32[512,128,8]{1,0,2:T(8,128)}, f32[512,128,8]{1,0,2:T(8,128)S(1)}, u32[]{:S(2)}) copy-start(f32[512,128,8]{1,0,2:T(8,128)S(1)} %get-tuple-element.78) | copy-start | bytes 6291460
  175.2 7.1 %copy-start.73 = (f32[8,128]{1,0:T(8,128)}, f32[8,128]{1,0:T(8,128)S(1)}, u32[]{:S(2)}) copy-start(f32[8,128]{1,0:T(8,128)S(1)} %get-tuple-element.77) | copy-start | bytes 12292
  175.6 6.7 %copy-start.87 = (f32[8,128]{1,0:T(8,128)}, f32[8,128]{1,0:T(8,128)S(1)}, u32[]{:S(2)}) copy-start(f32[8,128]{1,0:T(8,128)S(1)} %fusion.35) | copy-start | bytes 12292
  176.0 7.7 %copy-start.4 = (f32[512,128,8]{1,0,2:T(8,128)}, f32[512,128,8]{1,0,2:T(8,128)S(1)}, u32[]{:S(2)}) copy-start(f32[512,128,8]{1,0,2:T(8,128)S(1)} %get-tuple-element.84) | copy-start | bytes 6291460
  176.4 7.3 %copy-start.85 = (f32[8,128]{1,0:T(8,128)}, f32[8,128]{1,0:T(8,128)S(1)}, u32[]{:S(2)}) copy-start(f32[8,128]{1,0:T(8,128)S(1)} %fusion.37) | copy-start | bytes 12292
  176.9 8.3 %copy-start.2 = (f32[512,128,8]{1,0,2:T(8,128)}, f32[512,128,8]{1,0,2:T(8,128)S(1)}, u32[]{:S(2)}) copy-start(f32[512,128,8]{1,0,2:T(8,128)S(1)} %get-tuple-element.90) | copy-start | bytes 6291460
  177.2 7.9 %copy-start.83 = (f32[8,128]{1,0:T(8,128)}, f32[8,128]{1,0:T(8,128)S(1)}, u32[]{:S(2)}) copy-start(f32[8,128]{1,0:T(8,128)S(1)} %fusion.39) | copy-start | bytes 12292
  177.7 8.9 %copy-start = (f32[512,128,8]{1,0,2:T(8,128)}, f32[512,128,8]{1,0,2:T(8,128)S(1)}, u32[]{:S(2)}) copy-start(f32[512,128,8]{1,0,2:T(8,128)S(1)} %get-tuple-element.96) | copy-start | bytes 6291460
  178.1 8.5 %copy-start.81 = (f32[8,128]{1,0:T(8,128)}, f32[8,128]{1,0:T(8,128)S(1)}, u32[]{:S(2)}) copy-start(f32[8,128]{1,0:T(8,128)S(1)} %fusion.41) | copy-start | bytes 12292
  178.9 9.1 %copy-start.79 = (f32[8,128]{1,0:T(8,128)}, f32[8,128]{1,0:T(8,128)S(1)}, u32[]{:S(2)}) copy-start(f32[8,128]{1,0:T(8,128)S(1)} %fusion.43) | copy-start | bytes 12292
  197.0 9.3 %collective-permute-start.3 = (bf16[128,1024]{0,1:T(8,128)(2,1)}, bf16[128,1024]{0,1:T(8,128)(2,1)}, u32[]{:S(2)}, u32[]{:S(2)}) collective-permute-start(bf16[128,1024]{0,1:T(8,128)(2,1)} %get-tuple-element.76), channel_id=1, source_target_pairs={{128,0},{256,128},{384,256},{129,1},{257,129},{385,257},{130,2},{2... | collective-permute-start | bytes 786440 | tf_op jit(solution)/shard_map/ppermute | solution.py:14
  200.3 6.9 %copy-start.7 = (f32[512,128,8]{1,0,2:T(8,128)S(1)}, f32[512,128,8]{1,0,2:T(8,128)}, u32[]{:S(2)}) copy-start(f32[512,128,8]{1,0,2:T(8,128)} %copy-done.6) | copy-start | bytes 6291460
  200.3 6.9 %copy-start.71 = (bf16[1,4,128,128]{3,2,0,1:T(8,128)(2,1)S(1)}, bf16[1,4,128,128]{3,2,0,1:T(8,128)(2,1)}, u32[]{:S(2)}) copy-start(bf16[1,4,128,128]{3,2,0,1:T(8,128)(2,1)} %get-tuple-element.50) | copy-start | bytes 393220
  200.3 6.9 %copy-start.74 = (f32[8,128]{1,0:T(8,128)S(1)}, f32[8,128]{1,0:T(8,128)}, u32[]{:S(2)}) copy-start(f32[8,128]{1,0:T(8,128)} %copy-done.73) | copy-start | bytes 12292
  200.3 6.9 %copy-start.88 = (f32[8,128]{1,0:T(8,128)S(1)}, f32[8,128]{1,0:T(8,128)}, u32[]{:S(2)}) copy-start(f32[8,128]{1,0:T(8,128)} %copy-done.87) | copy-start | bytes 12292
  212.0 9.9 %collective-permute-start.4 = (bf16[128,1024]{0,1:T(8,128)(2,1)}, bf16[128,1024]{0,1:T(8,128)(2,1)}, u32[]{:S(2)}, u32[]{:S(2)}) collective-permute-start(bf16[128,1024]{0,1:T(8,128)(2,1)} %get-tuple-element.82), channel_id=1, source_target_pairs={{128,0},{256,128},{384,256},{129,1},{257,129},{385,257},{130,2},{2... | collective-permute-start | bytes 786440 | tf_op jit(solution)/shard_map/ppermute | solution.py:14
  215.1 6.8 %copy-start.59 = (bf16[1,128,1024]{1,2,0:T(8,128)(2,1)S(1)}, bf16[1,128,1024]{1,2,0:T(8,128)(2,1)}, u32[]{:S(2)}) copy-start(bf16[1,128,1024]{1,2,0:T(8,128)(2,1)} %copy.154) | copy-start | bytes 786436
  215.1 7.8 %copy-start.5 = (f32[512,128,8]{1,0,2:T(8,128)S(1)}, f32[512,128,8]{1,0,2:T(8,128)}, u32[]{:S(2)}) copy-start(f32[512,128,8]{1,0,2:T(8,128)} %copy-done.4) | copy-start | bytes 6291460
  215.1 7.8 %copy-start.70 = (bf16[1,4,128,128]{3,2,0,1:T(8,128)(2,1)S(1)}, bf16[1,4,128,128]{3,2,0,1:T(8,128)(2,1)}, u32[]{:S(2)}) copy-start(bf16[1,4,128,128]{3,2,0,1:T(8,128)(2,1)} %get-tuple-element.49) | copy-start | bytes 393220
  215.1 7.8 %copy-start.86 = (f32[8,128]{1,0:T(8,128)S(1)}, f32[8,128]{1,0:T(8,128)}, u32[]{:S(2)}) copy-start(f32[8,128]{1,0:T(8,128)} %copy-done.85) | copy-start | bytes 12292
  227.7 12.8 %copy-start.84 = (f32[8,128]{1,0:T(8,128)S(1)}, f32[8,128]{1,0:T(8,128)}, u32[]{:S(2)}) copy-start(f32[8,128]{1,0:T(8,128)} %copy-done.83) | copy-start | bytes 12292
  227.7 11.8 %collective-permute-start.5 = (bf16[128,1024]{0,1:T(8,128)(2,1)}, bf16[128,1024]{0,1:T(8,128)(2,1)}, u32[]{:S(2)}, u32[]{:S(2)}) collective-permute-start(bf16[128,1024]{0,1:T(8,128)(2,1)} %get-tuple-element.88), channel_id=1, source_target_pairs={{128,0},{256,128},{384,256},{129,1},{257,129},{385,257},{130,2},{2... | collective-permute-start | bytes 786440 | tf_op jit(solution)/shard_map/ppermute | solution.py:14
  230.9 8.6 %copy-start.58 = (bf16[1,128,1024]{1,2,0:T(8,128)(2,1)S(1)}, bf16[1,128,1024]{1,2,0:T(8,128)(2,1)}, u32[]{:S(2)}) copy-start(bf16[1,128,1024]{1,2,0:T(8,128)(2,1)} %copy.159) | copy-start | bytes 786436
  230.9 9.5 %copy-start.3 = (f32[512,128,8]{1,0,2:T(8,128)S(1)}, f32[512,128,8]{1,0,2:T(8,128)}, u32[]{:S(2)}) copy-start(f32[512,128,8]{1,0,2:T(8,128)} %copy-done.2) | copy-start | bytes 6291460
  230.9 9.6 %copy-start.69 = (bf16[1,4,128,128]{3,2,0,1:T(8,128)(2,1)S(1)}, bf16[1,4,128,128]{3,2,0,1:T(8,128)(2,1)}, u32[]{:S(2)}) copy-start(bf16[1,4,128,128]{3,2,0,1:T(8,128)(2,1)} %get-tuple-element.48) | copy-start | bytes 393220
  244.7 11.6 %copy-start.82 = (f32[8,128]{1,0:T(8,128)S(1)}, f32[8,128]{1,0:T(8,128)}, u32[]{:S(2)}) copy-start(f32[8,128]{1,0:T(8,128)} %copy-done.81) | copy-start | bytes 12292
  244.7 10.6 %collective-permute-start.6 = (bf16[128,1024]{0,1:T(8,128)(2,1)}, bf16[128,1024]{0,1:T(8,128)(2,1)}, u32[]{:S(2)}, u32[]{:S(2)}) collective-permute-start(bf16[128,1024]{0,1:T(8,128)(2,1)} %get-tuple-element.94), channel_id=1, source_target_pairs={{128,0},{256,128},{384,256},{129,1},{257,129},{385,257},{130,2},{2... | collective-permute-start | bytes 786440 | tf_op jit(solution)/shard_map/ppermute | solution.py:14
  247.9 7.4 %copy-start.57 = (bf16[1,128,1024]{1,2,0:T(8,128)(2,1)S(1)}, bf16[1,128,1024]{1,2,0:T(8,128)(2,1)}, u32[]{:S(2)}) copy-start(bf16[1,128,1024]{1,2,0:T(8,128)(2,1)} %copy.164) | copy-start | bytes 786436
  247.9 8.4 %copy-start.1 = (f32[512,128,8]{1,0,2:T(8,128)S(1)}, f32[512,128,8]{1,0,2:T(8,128)}, u32[]{:S(2)}) copy-start(f32[512,128,8]{1,0,2:T(8,128)} %copy-done) | copy-start | bytes 6291460
  247.9 8.4 %copy-start.68 = (bf16[1,4,128,128]{3,2,0,1:T(8,128)(2,1)S(1)}, bf16[1,4,128,128]{3,2,0,1:T(8,128)(2,1)}, u32[]{:S(2)}) copy-start(bf16[1,4,128,128]{3,2,0,1:T(8,128)(2,1)} %get-tuple-element.47) | copy-start | bytes 393220
  260.5 9.7 %copy-start.80 = (f32[8,128]{1,0:T(8,128)S(1)}, f32[8,128]{1,0:T(8,128)}, u32[]{:S(2)}) copy-start(f32[8,128]{1,0:T(8,128)} %copy-done.79) | copy-start | bytes 12292
  260.5 8.7 %collective-permute-start.7 = (bf16[128,1024]{0,1:T(8,128)(2,1)}, bf16[128,1024]{0,1:T(8,128)(2,1)}, u32[]{:S(2)}, u32[]{:S(2)}) collective-permute-start(bf16[128,1024]{0,1:T(8,128)(2,1)} %get-tuple-element.100), channel_id=1, source_target_pairs={{128,0},{256,128},{384,256},{129,1},{257,129},{385,257},{130,2},{2... | collective-permute-start | bytes 786440 | tf_op jit(solution)/shard_map/ppermute | solution.py:14
  279.3 6.3 %copy-start.43 = (f32[2,1,128,512]{2,3,1,0:T(8,128)S(1)}, f32[2,1,128,512]{2,3,1,0:T(8,128)}, u32[]{:S(2)}) copy-start(f32[2,1,128,512]{2,3,1,0:T(8,128)} %get-tuple-element.15) | copy-start | bytes 1572868
  279.3 11.2 %copy-start.91 = (f32[1024]{0:T(1024)S(1)}, f32[1024]{0:T(1024)}, u32[]{:S(2)}) copy-start(f32[1024]{0:T(1024)} %get-tuple-element.57) | copy-start | bytes 12292
  279.4 269.7 %all-reduce.8.cloned.1.call-start = ((), (), s32[]{:S(2)}) async-start(), calls=%async_computation.2 | async-start | bytes 1572864 | tf_op jit(solution)/shard_map/psum | solution.py:161
  282.5 268.3 %collective-permute-start.9 = (f32[2,128,512]{2,1,0:T(8,128)}, f32[2,128,512]{2,1,0:T(8,128)}, u32[]{:S(2)}, u32[]{:S(2)}) collective-permute-start(f32[2,128,512]{2,1,0:T(8,128)} %bitcast.173), channel_id=1, source_target_pairs={{0,8},{8,16},{16,24},{24,32},{32,40},{40,48},{48,56},{56,64},{64,7... | collective-permute-start | bytes 1572872 | tf_op jit(solution)/shard_map/ppermute | solution.py:19
  286.6 264.2 %collective-permute-start.8 = (f32[2,128,512]{2,1,0:T(8,128)}, f32[2,128,512]{2,1,0:T(8,128)S(1)}, u32[]{:S(2)}, u32[]{:S(2)}) collective-permute-start(f32[2,128,512]{2,1,0:T(8,128)} %bitcast.172), channel_id=1, source_target_pairs={{0,120},{8,0},{16,8},{24,16},{32,24},{40,32},{48,40},{56,48},{64,5... | collective-permute-start | bytes 1572872 | tf_op jit(solution)/shard_map/ppermute | solution.py:19
  294.3 256.1 %copy-start.102 = (pred[4]{0:T(512)(128)(4,1)S(1)}, pred[4]{0:T(512)(128)(4,1)}, u32[]{:S(2)}) copy-start(pred[4]{0:T(512)(128)(4,1)} %copy-done.101) | copy-start | bytes 16
  (56 other events, 126.5 us)
Sparse Core Ops, SparseCore 0:
  15.6 144.1 all-reduce.3
  279.5 133.2 all-reduce.5
  415.2 133.8 all-reduce.7

commit v9 on v5

--- a/solution.py
+++ b/solution.py
@@ -66,7 +66,7 @@
     query_rows = (head_input.astype(jnp.float32) * gain_row).astype(jnp.bfloat16)
     blocked_keys = head_keys.reshape(block_count, block_rows, local_kv, HEAD_FEATURES)
     blocked_values = head_values.reshape(block_count, block_rows, local_kv, HEAD_FEATURES)
-    per_turn = 2
+    per_turn = 4
     unit_count = block_count // per_turn
     turn_rows = per_turn * block_rows
     token_rows = turn_rows // ctx_count

time: 457 us -> 512 us (1.12)
  local copies, waits for them, and re-layouts: 72.2 us -> 98.5 us
  waiting for transfers between devices: 249 us -> 266 us
  matrix products: 12.1 us -> 24.9 us
    all_to_all x1, waiting for transfers between devices: 24 us -> 35.7 us  [shards(): lax.all_to_all(result_heads[:total_rows], 'ctx', split_axis=0, concat_axi...]
    dynamic_update_slice x11 -> x7, local copies, waits for them, and re-layouts: 2.08 us -> 10.8 us  [turn_step(): lax.dynamic_update_slice_in_dim(key_slots, key_part, target * per_turn, 0)]
    another operation x38 -> x26, local copies, waits for them, and re-layouts: 2.12 us -> 10.6 us
    all_to_all x1, waiting for transfers between devices: 16.8 us -> 24.7 us  [shards(): lax.all_to_all(value_acc.reshape(total_rows, slot_width).astype(jnp.bfloa...]
    dot_general x8 -> x4, matrix products: 2.44 us -> 9.84 us  [attend(): jnp.einsum('pkgbj,pbkgd->pjkd', score_grad, query_now, preferred_element_...]
    dynamic_update_slice x11 -> x7, local copies, waits for them, and re-layouts: 12 us -> 19.2 us  [turn_step(): lax.dynamic_update_slice_in_dim(value_slots, value_part, target * per_tur...]
    mul x8 -> x4, local copies, waits for them, and re-layouts: 1.29 us -> 8.23 us  [attend(): jnp.einsum('pkgbj,pjkd->pbkgd', score_grad, neighbor_keys, preferred_elem...]
    ppermute x11 -> x7, waiting for transfers between devices: 65 us -> 58.4 us  [passed_along(): return lax.ppermute(block, axis, route)]
  transfers between devices with their start and end apart: 15 -> 11, of which waited for: 15 -> 11; matrix products, arithmetic and copies ran while one was open for 7% -> 9% of each run, Pallas kernels for 0% -> 0%
where the time goes in v9:
time: 512 us; the launch traced here: 509 us
  waiting for transfers between devices  266 us (52%)
  local copies, waits for them, and re-layouts  98.5 us (19%)
  other arithmetic  55.9 us (11%)
  starting transfers between devices  51.1 us (10%)
  matrix products  24.9 us (5%)
  blocking collectives  10.6 us (2%)
    all_to_all x1, waiting for transfers between devices, shards(): lax.all_to_all(packed, 'ctx', split_axis=1, concat_axis=0, tiled=True)  139 us
    ppermute x7, waiting for transfers between devices, passed_along(): return lax.ppermute(block, axis, route)  58.4 us
    all_to_all x1, waiting for transfers between devices, shards(): lax.all_to_all(result_heads[:total_rows], 'ctx', split_axis=0, concat_axi...  35.7 us
    all_to_all x1, waiting for transfers between devices, shards(): lax.all_to_all(value_acc.reshape(total_rows, slot_width).astype(jnp.bfloa...  24.7 us
    dynamic_update_slice x7, local copies, waits for them, and re-layouts, turn_step(): lax.dynamic_update_slice_in_dim(value_slots, value_part, target * per_tur...  19.2 us
    all_to_all x1, starting transfers between devices, shards(): lax.all_to_all(packed, 'ctx', split_axis=1, concat_axis=0, tiled=True)  15.3 us
    all_to_all x1, starting transfers between devices, shards(): lax.all_to_all(key_acc.reshape(total_rows, slot_width).astype(jnp.bfloat1...  13.2 us
    dynamic_update_slice x7, other arithmetic, turn_step(): lax.dynamic_update_slice_in_dim(result_heads, handed, target * turn_rows, 0)  12.7 us
  transfers between devices with their start and end apart: 11, of which 11 were waited for; matrix products, arithmetic and copies ran while one was open for 9% of the time, Pallas kernels for 0%

profile of v9, /device:TPU:6, one launch (start us, length us, event | category | flops | bytes accessed | tf_op | source)
XLA Modules:
  0.0 508.6 jit_solution(9695312200063948824)
XLA Ops:
  6.9 1.8 pad_maximum_fusion
  8.7 15.3 %all-to-all-start = ((bf16[128,16,768]{2,0,1:T(8,128)(2,1)}), bf16[128,16,768]{2,0,1:T(8,128)(2,1)S(1)}, u32[]{:S(2)}, u32[]{:S(2)}) async-start(bf16[128,16,768]{2,0,1:T(8,128)(2,1)} %pad_maximum_fusion), calls=%async_computation | async-start | bytes 6291456 | tf_op jit(solution)/shard_map/all_to_all | solution.py:60
  24.3 139.2 %all-to-all-done = bf16[128,16,768]{2,0,1:T(8,128)(2,1)S(1)} async-done(((bf16[128,16,768]{2,0,1:T(8,128)(2,1)}), bf16[128,16,768]{2,0,1:T(8,128)(2,1)S(1)}, u32[]{:S(2)}, u32[]{:S(2)}) %all-to-all-start) | async-done | bytes 3145760 | tf_op jit(solution)/shard_map/all_to_all | solution.py:60
  168.8 2.9 broadcast_in_dim.34.clone
  171.6 2.9 broadcast_in_dim.34.clone2
  174.5 194.6 %while.24 = (s32[]{:T(128)}, bf16[512,256]{1,0:T(8,128)(2,1)}, bf16[2560,256]{1,0:T(8,128)(2,1)}, f32[20,512,128]{2,1,0:T(8,128)}, f32[20,512,128]{2,1,0:T(8,128...) while((s32[]{:T(128)}, bf16[512,256]{1,0:T(8,128)(2,1)}, ...), condition=%wide.region_7.8_spmd.clone, body=%wide.region_0.7_spmd.clone.sunk | while | flops 683276608 | bytes 46455016 | solution.py:173
  175.6 3.1 conditional.3
  178.7 1.8 constant_dynamic-update-slice_fusion.5
  183.3 2.7 constant_dynamic-update-slice_fusion.6
  186.1 2.8 collective-permute-done
  189.9 3.1 conditional.3
  193.0 1.8 constant_dynamic-update-slice_fusion.5
  197.7 2.7 constant_dynamic-update-slice_fusion.6
  200.4 2.8 collective-permute-done
  204.3 3.1 conditional.3
  207.3 1.8 constant_dynamic-update-slice_fusion.5
  212.0 2.7 constant_dynamic-update-slice_fusion.6
  214.7 41.9 %collective-permute-done = bf16[512,256]{1,0:T(8,128)(2,1)} collective-permute-done((bf16[512,256]{1,0:T(8,128)(2,1)S(1)}, bf16[512,256]{1,0:T(8,128)(2,1)}, u32[]{:S(2)}, u32[]{:S(2)}) %collective-permute-start) | collective-permute-done | bytes 262176 | tf_op jit(solution)/shard_map/while/body/eval_jaxpr/ppermute | solution.py:15
  257.7 16.9 %conditional.3 = (f32[512,256]{1,0:T(8,128)}, f32[4,512,128]{1,2,0:T(8,128)}, f32[4,512,128]{2,1,0:T(8,128)}, f32[256]{0:T(256)S(1)}) conditional(s32[]{:T(128)} %convert_element_type.154, () %tuple.85, (s32[]{:T(128)}, s32[16,4]{1,0:T(8,128)S(1)}, bf16[16,128,1,128]{3,1,0,2:T(8,128)(2,1)}, bf16[2048,256]{1,0:T(8,128)(2,1)}, ...), branch_computations={%region_1.1_spmd, %region_2.6_spmd} | conditional | flops 682358592 | bytes 37013204 | solution.py:148
  257.8 1.7 gather_fusion
  261.8 1.7 gather_fusion.1
  266.5 2.1 copy.128
  268.5 2.0 multiply_reduce_fusion
  270.5 2.5 fusion.7
  274.5 1.8 constant_dynamic-update-slice_fusion.5
  279.2 2.8 constant_dynamic-update-slice_fusion.6
  282.0 2.7 collective-permute-done
  285.8 16.9 %conditional.3 = (f32[512,256]{1,0:T(8,128)}, f32[4,512,128]{1,2,0:T(8,128)}, f32[4,512,128]{2,1,0:T(8,128)}, f32[256]{0:T(256)S(1)}) conditional(s32[]{:T(128)} %convert_element_type.154, () %tuple.85, (s32[]{:T(128)}, s32[16,4]{1,0:T(8,128)S(1)}, bf16[16,128,1,128]{3,1,0,2:T(8,128)(2,1)}, bf16[2048,256]{1,0:T(8,128)(2,1)}, ...), branch_computations={%region_1.1_spmd, %region_2.6_spmd} | conditional | flops 682358592 | bytes 37013204 | solution.py:148
  285.9 1.7 gather_fusion
  289.9 1.7 gather_fusion.1
  294.6 2.1 copy.128
  296.7 2.0 multiply_reduce_fusion
  298.7 2.5 fusion.7
  302.7 1.8 constant_dynamic-update-slice_fusion.5
  307.3 2.7 constant_dynamic-update-slice_fusion.6
  310.1 2.8 collective-permute-done
  313.9 16.9 %conditional.3 = (f32[512,256]{1,0:T(8,128)}, f32[4,512,128]{1,2,0:T(8,128)}, f32[4,512,128]{2,1,0:T(8,128)}, f32[256]{0:T(256)S(1)}) conditional(s32[]{:T(128)} %convert_element_type.154, () %tuple.85, (s32[]{:T(128)}, s32[16,4]{1,0:T(8,128)S(1)}, bf16[16,128,1,128]{3,1,0,2:T(8,128)(2,1)}, bf16[2048,256]{1,0:T(8,128)(2,1)}, ...), branch_computations={%region_1.1_spmd, %region_2.6_spmd} | conditional | flops 682358592 | bytes 37013204 | solution.py:148
  314.1 1.7 gather_fusion
  318.0 1.7 gather_fusion.1
  322.7 2.1 copy.128
  324.8 2.0 multiply_reduce_fusion
  326.8 2.5 fusion.7
  330.8 1.8 constant_dynamic-update-slice_fusion.5
  335.4 2.7 constant_dynamic-update-slice_fusion.6
  338.2 2.8 collective-permute-done
  342.1 16.9 %conditional.3 = (f32[512,256]{1,0:T(8,128)}, f32[4,512,128]{1,2,0:T(8,128)}, f32[4,512,128]{2,1,0:T(8,128)}, f32[256]{0:T(256)S(1)}) conditional(s32[]{:T(128)} %convert_element_type.154, () %tuple.85, (s32[]{:T(128)}, s32[16,4]{1,0:T(8,128)S(1)}, bf16[16,128,1,128]{3,1,0,2:T(8,128)(2,1)}, bf16[2048,256]{1,0:T(8,128)(2,1)}, ...), branch_computations={%region_1.1_spmd, %region_2.6_spmd} | conditional | flops 682358592 | bytes 37013204 | solution.py:148
  342.2 1.7 gather_fusion
  350.8 2.1 copy.128
  352.9 2.0 multiply_reduce_fusion
  354.9 2.5 fusion.7
  358.9 1.8 constant_dynamic-update-slice_fusion.5
  363.6 2.8 constant_dynamic-update-slice_fusion.6
  366.4 2.7 collective-permute-done
  369.1 4.7 slice.26
  373.8 8.8 %scatter_fusion = f32[16,128,128]{2,1,0:T(8,128)S(1)} fusion(f32[16,128,128]{2,1,0:T(8,128)S(1)} %broadcast.75.clone, s32[64]{0:T(128)S(1)} %fusion.17, f32[64,128,128]{2,1,0:T(8,128)} %bitcast.129), kind=kCustom, calls=%fused_computation.4 | custom fusion | flops 1048576 | bytes 12583168 | tf_op jit(solution)/shard_map/scatter-add | solution.py:184
  383.5 13.2 %all-to-all-start.2 = ((bf16[16,128,128]{2,1,0:T(8,128)(2,1)}), bf16[16,128,128]{2,1,0:T(8,128)(2,1)S(1)}, u32[]{:S(2)}, u32[]{:S(2)}) async-start(bf16[16,128,128]{2,1,0:T(8,128)(2,1)} %convert_element_type.116), calls=%async_computation.2 | async-start | bytes 1048576 | tf_op jit(solution)/shard_map/all_to_all | solution.py:192
  396.7 4.5 slice.27
  401.3 8.8 %scatter_fusion.1 = f32[16,128,128]{2,1,0:T(8,128)S(1)} fusion(f32[16,128,128]{2,1,0:T(8,128)S(1)} %broadcast.75.clone.1, s32[64]{0:T(128)S(1)} %fusion.17, f32[64,128,128]{2,1,0:T(8,128)} %bitcast.128), kind=kCustom, calls=%fused_computation.5 | custom fusion | flops 1048576 | bytes 12583168 | tf_op jit(solution)/shard_map/scatter-add | solution.py:189
  411.0 7.9 %all-to-all-done.2 = bf16[16,128,128]{2,1,0:T(8,128)(2,1)S(1)} async-done(((bf16[16,128,128]{2,1,0:T(8,128)(2,1)}), bf16[16,128,128]{2,1,0:T(8,128)(2,1)S(1)}, u32[]{:S(2)}, u32[]{:S(2)}) %all-to-all-start.2) | async-done | bytes 524320 | tf_op jit(solution)/shard_map/all_to_all | solution.py:192
  419.0 7.2 %all-to-all-start.3 = ((bf16[16,128,128]{2,1,0:T(8,128)(2,1)}), bf16[16,128,128]{2,1,0:T(8,128)(2,1)S(1)}, u32[]{:S(2)}, u32[]{:S(2)}) async-start(bf16[16,128,128]{2,1,0:T(8,128)(2,1)} %convert_element_type.122), calls=%async_computation.3 | async-start | bytes 1048576 | tf_op jit(solution)/shard_map/all_to_all | solution.py:199
  427.2 24.7 %all-to-all-done.3 = bf16[16,128,128]{2,1,0:T(8,128)(2,1)S(1)} async-done(((bf16[16,128,128]{2,1,0:T(8,128)(2,1)}), bf16[16,128,128]{2,1,0:T(8,128)(2,1)S(1)}, u32[]{:S(2)}, u32[]{:S(2)}) %all-to-all-start.3) | async-done | bytes 524320 | tf_op jit(solution)/shard_map/all_to_all | solution.py:199
  451.9 6.5 %all-to-all-start.1 = ((bf16[16,128,256]{2,1,0:T(8,128)(2,1)}), bf16[16,128,256]{2,1,0:T(8,128)(2,1)S(1)}, u32[]{:S(2)}, u32[]{:S(2)}) async-start(bf16[16,128,256]{2,1,0:T(8,128)(2,1)} %bitcast.36), calls=%async_computation.1 | async-start | bytes 2097152 | tf_op jit(solution)/shard_map/all_to_all | solution.py:175
  458.4 10.6 %psum.7 = f32[1,256]{1,0:T(1,128)} all-reduce(f32[1,256]{1,0:T(1,128)S(1)} %bitcast.144), channel_id=1, replica_groups=mesh['section'=4,'ctx'=16,'dp'=8] {'dp'}, use_global_device_ids=true, to_apply=%region_12.13 | all-reduce | flops 256 | bytes 2048 | tf_op jit(solution)/shard_map/psum | solution.py:219
  471.0 35.7 %all-to-all-done.1 = bf16[16,128,256]{2,1,0:T(8,128)(2,1)S(1)} async-done(((bf16[16,128,256]{2,1,0:T(8,128)(2,1)}), bf16[16,128,256]{2,1,0:T(8,128)(2,1)S(1)}, u32[]{:S(2)}, u32[]{:S(2)}) %all-to-all-start.1) | async-done | bytes 1048608 | tf_op jit(solution)/shard_map/all_to_all | solution.py:175
  (178 shorter events, 84.2 us)
Async XLA Ops:
  0.6 4.4 copy-start.7
  5.1 1.2 copy-start.8
  8.7 15.4 %copy-start.10 = (s32[16,4]{0,1:T(4,128)S(1)}, s32[16,4]{0,1:T(4,128)}, u32[]{:S(2)}) copy-start(s32[16,4]{0,1:T(4,128)} %param.18) | copy-start | bytes 772
  8.7 154.7 %all-to-all-start = ((bf16[128,16,768]{2,0,1:T(8,128)(2,1)}), bf16[128,16,768]{2,0,1:T(8,128)(2,1)S(1)}, u32[]{:S(2)}, u32[]{:S(2)}) async-start(bf16[128,16,768]{2,0,1:T(8,128)(2,1)} %pad_maximum_fusion), calls=%async_computation | async-start | bytes 6291456 | tf_op jit(solution)/shard_map/all_to_all | solution.py:60
  164.5 2.3 copy-start.3
  164.5 1.1 copy-start.9
  180.5 8.4 %collective-permute-start = (bf16[512,256]{1,0:T(8,128)(2,1)S(1)}, bf16[512,256]{1,0:T(8,128)(2,1)}, u32[]{:S(2)}, u32[]{:S(2)}) collective-permute-start(bf16[512,256]{1,0:T(8,128)(2,1)S(1)} %get-tuple-element.723), channel_id=1, source_target_pairs={{128,0},{256,128},{384,256},{129,1},{257,129},{385,257},{130,2},{2... | collective-permute-start | bytes 786440 | tf_op jit(solution)/shard_map/while/body/eval_jaxpr/ppermute | solution.py:15
  194.8 8.4 %collective-permute-start = (bf16[512,256]{1,0:T(8,128)(2,1)S(1)}, bf16[512,256]{1,0:T(8,128)(2,1)}, u32[]{:S(2)}, u32[]{:S(2)}) collective-permute-start(bf16[512,256]{1,0:T(8,128)(2,1)S(1)} %get-tuple-element.723), channel_id=1, source_target_pairs={{128,0},{256,128},{384,256},{129,1},{257,129},{385,257},{130,2},{2... | collective-permute-start | bytes 786440 | tf_op jit(solution)/shard_map/while/body/eval_jaxpr/ppermute | solution.py:15
  209.1 47.4 %collective-permute-start = (bf16[512,256]{1,0:T(8,128)(2,1)S(1)}, bf16[512,256]{1,0:T(8,128)(2,1)}, u32[]{:S(2)}, u32[]{:S(2)}) collective-permute-start(bf16[512,256]{1,0:T(8,128)(2,1)S(1)} %get-tuple-element.723), channel_id=1, source_target_pairs={{128,0},{256,128},{384,256},{129,1},{257,129},{385,257},{130,2},{2... | collective-permute-start | bytes 786440 | tf_op jit(solution)/shard_map/while/body/eval_jaxpr/ppermute | solution.py:15
  259.5 1.9 copy-start
  260.9 0.8 copy-start.2
  263.5 0.7 copy-start.4
  264.2 1.0 copy-start.1
  268.5 4.5 copy-start.5
  276.3 8.4 %collective-permute-start = (bf16[512,256]{1,0:T(8,128)(2,1)S(1)}, bf16[512,256]{1,0:T(8,128)(2,1)}, u32[]{:S(2)}, u32[]{:S(2)}) collective-permute-start(bf16[512,256]{1,0:T(8,128)(2,1)S(1)} %get-tuple-element.723), channel_id=1, source_target_pairs={{128,0},{256,128},{384,256},{129,1},{257,129},{385,257},{130,2},{2... | collective-permute-start | bytes 786440 | tf_op jit(solution)/shard_map/while/body/eval_jaxpr/ppermute | solution.py:15
  287.6 1.9 copy-start
  289.1 0.8 copy-start.2
  291.7 0.7 copy-start.4
  292.4 1.0 copy-start.1
  296.7 4.5 copy-start.5
  304.5 8.4 %collective-permute-start = (bf16[512,256]{1,0:T(8,128)(2,1)S(1)}, bf16[512,256]{1,0:T(8,128)(2,1)}, u32[]{:S(2)}, u32[]{:S(2)}) collective-permute-start(bf16[512,256]{1,0:T(8,128)(2,1)S(1)} %get-tuple-element.723), channel_id=1, source_target_pairs={{128,0},{256,128},{384,256},{129,1},{257,129},{385,257},{130,2},{2... | collective-permute-start | bytes 786440 | tf_op jit(solution)/shard_map/while/body/eval_jaxpr/ppermute | solution.py:15
  315.8 1.9 copy-start
  317.2 0.8 copy-start.2
  319.8 0.7 copy-start.4
  320.5 1.0 copy-start.1
  324.8 4.5 copy-start.5
  332.6 8.4 %collective-permute-start = (bf16[512,256]{1,0:T(8,128)(2,1)S(1)}, bf16[512,256]{1,0:T(8,128)(2,1)}, u32[]{:S(2)}, u32[]{:S(2)}) collective-permute-start(bf16[512,256]{1,0:T(8,128)(2,1)S(1)} %get-tuple-element.723), channel_id=1, source_target_pairs={{128,0},{256,128},{384,256},{129,1},{257,129},{385,257},{130,2},{2... | collective-permute-start | bytes 786440 | tf_op jit(solution)/shard_map/while/body/eval_jaxpr/ppermute | solution.py:15
  343.9 1.9 copy-start
  345.3 0.8 copy-start.2
  347.9 0.7 copy-start.4
  348.6 1.0 copy-start.1
  352.9 4.5 copy-start.5
  360.7 8.4 %collective-permute-start = (bf16[512,256]{1,0:T(8,128)(2,1)S(1)}, bf16[512,256]{1,0:T(8,128)(2,1)}, u32[]{:S(2)}, u32[]{:S(2)}) collective-permute-start(bf16[512,256]{1,0:T(8,128)(2,1)S(1)} %get-tuple-element.723), channel_id=1, source_target_pairs={{128,0},{256,128},{384,256},{129,1},{257,129},{385,257},{130,2},{2... | collective-permute-start | bytes 786440 | tf_op jit(solution)/shard_map/while/body/eval_jaxpr/ppermute | solution.py:15
  383.5 35.4 %all-to-all-start.2 = ((bf16[16,128,128]{2,1,0:T(8,128)(2,1)}), bf16[16,128,128]{2,1,0:T(8,128)(2,1)S(1)}, u32[]{:S(2)}, u32[]{:S(2)}) async-start(bf16[16,128,128]{2,1,0:T(8,128)(2,1)} %convert_element_type.116), calls=%async_computation.2 | async-start | bytes 1048576 | tf_op jit(solution)/shard_map/all_to_all | solution.py:192
  410.1 16.0 %copy-start.6 = (bf16[2560,256]{1,0:T(8,128)(2,1)S(1)}, bf16[2560,256]{1,0:T(8,128)(2,1)}, u32[]{:S(2)}) copy-start(bf16[2560,256]{1,0:T(8,128)(2,1)} %get-tuple-element.378) | copy-start | bytes 3932164
  419.0 33.0 %all-to-all-start.3 = ((bf16[16,128,128]{2,1,0:T(8,128)(2,1)}), bf16[16,128,128]{2,1,0:T(8,128)(2,1)S(1)}, u32[]{:S(2)}, u32[]{:S(2)}) async-start(bf16[16,128,128]{2,1,0:T(8,128)(2,1)} %convert_element_type.122), calls=%async_computation.3 | async-start | bytes 1048576 | tf_op jit(solution)/shard_map/all_to_all | solution.py:199
  451.9 54.7 %all-to-all-start.1 = ((bf16[16,128,256]{2,1,0:T(8,128)(2,1)}), bf16[16,128,256]{2,1,0:T(8,128)(2,1)S(1)}, u32[]{:S(2)}, u32[]{:S(2)}) async-start(bf16[16,128,256]{2,1,0:T(8,128)(2,1)} %bitcast.36), calls=%async_computation.1 | async-start | bytes 2097152 | tf_op jit(solution)/shard_map/all_to_all | solution.py:175

commit v10 on v5

--- a/solution.py
+++ b/solution.py
@@ -47,21 +47,35 @@
         .reshape(tok_local, kv_heads, HEAD_FEATURES)[:, slot_heads]
         .reshape(tok_local, ctx_count * slot_width)
     )
-    sent_widths = (local_width, local_width, slot_width, slot_width)
+    quarter = tok_local // section_count
+    top_width = local_width * quarter // tok_local
+    top_rows = lax.dynamic_slice_in_dim(top_grad[0], section_pos * quarter, quarter, 0)
+    top_piece = (
+        top_rows.reshape(quarter, ctx_count, local_width)
+        .transpose(1, 0, 2)
+        .reshape(ctx_count, tok_local, top_width)
+        .transpose(1, 0, 2)
+    )
+    sent_widths = (local_width, top_width, slot_width, slot_width)
     packed = jnp.concatenate(
-        [
-            piece.reshape(tok_local, ctx_count, width)
-            for piece, width in zip(
-                (layer_input, top_grad[0], sent_keys, sent_values), sent_widths
-            )
+        [layer_input.reshape(tok_local, ctx_count, local_width), top_piece]
+        + [
+            piece.reshape(tok_local, ctx_count, slot_width)
+            for piece in (sent_keys, sent_values)
         ],
         axis=2,
     ).reshape(tok_local, ctx_count * sum(sent_widths))
     moved = lax.all_to_all(packed, "ctx", split_axis=1, concat_axis=0, tiled=True)
     edges = np.cumsum((0,) + sent_widths)
-    head_input, head_top, head_keys, head_values = lax.optimization_barrier(
+    head_input, top_part, head_keys, head_values = lax.optimization_barrier(
         tuple(moved[:, edges[i] : edges[i + 1]] for i in range(len(sent_widths)))
     )
+    top_part = top_part.reshape(ctx_count, quarter, local_width)
+    top_quarters = [
+        lax.ppermute(top_part, "section", [(q, section_count - 1)])
+        for q in range(section_count - 1)
+    ]
+    head_top = jnp.stack(top_quarters + [top_part], axis=1).reshape(total_rows, local_width)
     gain_row = query_gain[0]
     query_rows = (head_input.astype(jnp.float32) * gain_row).astype(jnp.bfloat16)
     blocked_keys = head_keys.reshape(block_count, block_rows, local_kv, HEAD_FEATURES)

time: 457 us -> 475 us (1.039)
  waiting for transfers between devices: 249 us -> 213 us
  local copies, waits for them, and re-layouts: 72.2 us -> 92.6 us
  other arithmetic: 52.5 us -> 68.8 us
  starting transfers between devices: 53.3 us -> 64.7 us
  matrix products: 12.1 us -> 19.4 us
    all_to_all x1, waiting for transfers between devices: 139 us -> 106 us  [shards(): lax.all_to_all(packed, 'ctx', split_axis=1, concat_axis=0, tiled=True)]
    gather x8, local copies, waits for them, and re-layouts: 4.78 us -> 13.1 us  [attend(): blocked_values[lists_now]]
    all_to_all x1, waiting for transfers between devices: 24 us -> 16.3 us  [shards(): lax.all_to_all(result_heads[:total_rows], 'ctx', split_axis=0, concat_axi...]
    add x11, other arithmetic: 0.13 us -> 7.6 us  [turn_step(): gain_acc = gain_acc + gain_part]
    dot_general x8, matrix products: 2.44 us -> 9.71 us  [attend(): jnp.einsum('pkgbj,pbkgd->pjkd', score_grad, query_now, preferred_element_...]
    ppermute x0 -> x3, starting transfers between devices: none -> 6.29 us  [shards(): lax.ppermute(top_part, 'section', [(q, section_count - 1)])]
  transfers between devices with their start and end apart: 15 -> 18, of which waited for: 15 -> 16; matrix products, arithmetic and copies ran while one was open for 7% -> 9% of each run, Pallas kernels for 0% -> 0%
where the time goes in v10:
time: 475 us; the launch traced here: 472 us
  waiting for transfers between devices  213 us (45%)
  local copies, waits for them, and re-layouts  92.6 us (19%)
  other arithmetic  68.8 us (14%)
  starting transfers between devices  64.7 us (14%)
  matrix products  19.4 us (4%)
  blocking collectives  10.9 us (2%)
    all_to_all x1, waiting for transfers between devices, shards(): lax.all_to_all(packed, 'ctx', split_axis=1, concat_axis=0, tiled=True)  106 us
    ppermute x11, waiting for transfers between devices, passed_along(): return lax.ppermute(block, axis, route)  64.5 us
    all_to_all x1, waiting for transfers between devices, shards(): lax.all_to_all(value_acc.reshape(total_rows, slot_width).astype(jnp.bfloa...  18.1 us
    all_to_all x1, waiting for transfers between devices, shards(): lax.all_to_all(result_heads[:total_rows], 'ctx', split_axis=0, concat_axi...  16.3 us
    all_to_all x1, starting transfers between devices, shards(): lax.all_to_all(packed, 'ctx', split_axis=1, concat_axis=0, tiled=True)  15.2 us
    ppermute x11, starting transfers between devices, passed_along(): return lax.ppermute(block, axis, route)  14.1 us
    gather x8, local copies, waits for them, and re-layouts, attend(): blocked_values[lists_now]  13.1 us
    gather x8, local copies, waits for them, and re-layouts, attend(): blocked_keys[lists_now]  13.1 us
  transfers between devices with their start and end apart: 18, of which 16 were waited for; matrix products, arithmetic and copies ran while one was open for 9% of the time, Pallas kernels for 0%

profile of v10, /device:TPU:6, one launch (start us, length us, event | category | flops | bytes accessed | tf_op | source)
XLA Modules:
  0.0 471.8 jit_solution(12560396173400996463)
XLA Ops:
  6.5 1.6 copy.148
  8.1 1.6 pad_maximum_fusion
  9.7 15.2 %all-to-all-start = ((bf16[128,16,576]{0,2,1:T(8,128)(2,1)}), bf16[128,16,576]{0,2,1:T(8,128)(2,1)S(1)}, u32[]{:S(2)}, u32[]{:S(2)}) async-start(bf16[128,16,576]{0,2,1:T(8,128)(2,1)} %pad_maximum_fusion), calls=%async_computation | async-start | bytes 4718592 | tf_op jit(solution)/shard_map/all_to_all | solution.py:68
  25.7 106.0 %all-to-all-done = bf16[128,16,576]{0,2,1:T(8,128)(2,1)S(1)} async-done(((bf16[128,16,576]{0,2,1:T(8,128)(2,1)}), bf16[128,16,576]{0,2,1:T(8,128)(2,1)S(1)}, u32[]{:S(2)}, u32[]{:S(2)}) %all-to-all-start) | async-done | bytes 2359328 | tf_op jit(solution)/shard_map/all_to_all | solution.py:68
  131.7 2.5 copy.157
  134.2 2.9 fusion.14
  137.2 2.3 slice.36
  140.8 4.9 %collective-permute-start.1 = (bf16[16,32,256]{2,1,0:T(8,128)(2,1)S(1)}, bf16[16,32,256]{2,1,0:T(8,128)(2,1)S(1)}, u32[]{:S(2)}, u32[]{:S(2)}) collective-permute-start(bf16[16,32,256]{2,1,0:T(8,128)(2,1)S(1)} %reshape.182), channel_id=1, source_target_pairs={{0,384},{1,385},{2,386},{3,387},{4,388},{5,389},{6,390},{7,391},{8... | collective-permute-start | bytes 786440 | tf_op jit(solution)/shard_map/ppermute | solution.py:75
  147.5 2.4 multiply_convert_fusion.2
  149.9 3.1 collective-permute-done.1
  154.2 2.6 broadcast_in_dim.34.clone
  156.8 2.7 broadcast_in_dim.34.clone2
  161.3 194.6 %while.24 = (s32[]{:T(128)}, bf16[256,256]{1,0:T(8,128)(2,1)}, bf16[2304,256]{1,0:T(8,128)(2,1)}, f32[18,512,128]{2,1,0:T(8,128)}, f32[18,512,128]{2,1,0:T(8,128...) while((s32[]{:T(128)}, bf16[256,256]{1,0:T(8,128)(2,1)}, ...), condition=%wide.region_7.8_spmd.clone, body=%wide.region_0.7_spmd.clone.sunk | while | flops 340590400 | bytes 20086688 | solution.py:187
  167.0 3.7 collective-permute-done
  176.3 3.7 collective-permute-done
  185.7 27.4 %collective-permute-done = bf16[256,256]{1,0:T(8,128)(2,1)} collective-permute-done((bf16[256,256]{1,0:T(8,128)(2,1)S(1)}, bf16[256,256]{1,0:T(8,128)(2,1)}, u32[]{:S(2)}, u32[]{:S(2)}) %collective-permute-start) | collective-permute-done | bytes 131104 | tf_op jit(solution)/shard_map/while/body/eval_jaxpr/ppermute | solution.py:15
  214.1 9.2 %conditional.3 = (f32[256,256]{1,0:T(8,128)S(1)}, f32[2,512,128]{1,2,0:T(8,128)S(1)}, f32[2,512,128]{2,1,0:T(8,128)S(1)}, f32[256]{0:T(256)}) conditional(s32[]{:T(128)} %convert_element_type.154, () %tuple.84, (s32[]{:T(128)}, s32[16,4]{1,0:T(8,128)S(1)}, bf16[16,128,1,128]{3,1,0,2:T(8,128)(2,1)}, bf16[2048,256]{1,0:T(8,128)(2,1)}, ...), branch_computations={%region_1.1_spmd, %region_2.6_spmd} | conditional | flops 340131104 | bytes 15363460 | solution.py:162
  215.3 1.6 gather_fusion
  217.8 1.6 gather_fusion.1
  221.7 1.5 multiply_reduce_fusion.1
  227.2 3.7 collective-permute-done
  231.9 9.2 %conditional.3 = (f32[256,256]{1,0:T(8,128)S(1)}, f32[2,512,128]{1,2,0:T(8,128)S(1)}, f32[2,512,128]{2,1,0:T(8,128)S(1)}, f32[256]{0:T(256)}) conditional(s32[]{:T(128)} %convert_element_type.154, () %tuple.84, (s32[]{:T(128)}, s32[16,4]{1,0:T(8,128)S(1)}, bf16[16,128,1,128]{3,1,0,2:T(8,128)(2,1)}, bf16[2048,256]{1,0:T(8,128)(2,1)}, ...), branch_computations={%region_1.1_spmd, %region_2.6_spmd} | conditional | flops 340131104 | bytes 15363460 | solution.py:162
  233.2 1.6 gather_fusion
  235.6 1.6 gather_fusion.1
  239.5 1.5 multiply_reduce_fusion.1
  245.0 3.7 collective-permute-done
  249.7 9.2 %conditional.3 = (f32[256,256]{1,0:T(8,128)S(1)}, f32[2,512,128]{1,2,0:T(8,128)S(1)}, f32[2,512,128]{2,1,0:T(8,128)S(1)}, f32[256]{0:T(256)}) conditional(s32[]{:T(128)} %convert_element_type.154, () %tuple.84, (s32[]{:T(128)}, s32[16,4]{1,0:T(8,128)S(1)}, bf16[16,128,1,128]{3,1,0,2:T(8,128)(2,1)}, bf16[2048,256]{1,0:T(8,128)(2,1)}, ...), branch_computations={%region_1.1_spmd, %region_2.6_spmd} | conditional | flops 340131104 | bytes 15363460 | solution.py:162
  251.0 1.6 gather_fusion
  253.5 1.6 gather_fusion.1
  257.4 1.5 multiply_reduce_fusion.1
  262.8 3.7 collective-permute-done
  267.5 9.2 %conditional.3 = (f32[256,256]{1,0:T(8,128)S(1)}, f32[2,512,128]{1,2,0:T(8,128)S(1)}, f32[2,512,128]{2,1,0:T(8,128)S(1)}, f32[256]{0:T(256)}) conditional(s32[]{:T(128)} %convert_element_type.154, () %tuple.84, (s32[]{:T(128)}, s32[16,4]{1,0:T(8,128)S(1)}, bf16[16,128,1,128]{3,1,0,2:T(8,128)(2,1)}, bf16[2048,256]{1,0:T(8,128)(2,1)}, ...), branch_computations={%region_1.1_spmd, %region_2.6_spmd} | conditional | flops 340131104 | bytes 15363460 | solution.py:162
  268.8 1.6 gather_fusion
  271.3 1.6 gather_fusion.1
  275.2 1.5 multiply_reduce_fusion.1
  280.6 3.7 collective-permute-done
  285.3 9.2 %conditional.3 = (f32[256,256]{1,0:T(8,128)S(1)}, f32[2,512,128]{1,2,0:T(8,128)S(1)}, f32[2,512,128]{2,1,0:T(8,128)S(1)}, f32[256]{0:T(256)}) conditional(s32[]{:T(128)} %convert_element_type.154, () %tuple.84, (s32[]{:T(128)}, s32[16,4]{1,0:T(8,128)S(1)}, bf16[16,128,1,128]{3,1,0,2:T(8,128)(2,1)}, bf16[2048,256]{1,0:T(8,128)(2,1)}, ...), branch_computations={%region_1.1_spmd, %region_2.6_spmd} | conditional | flops 340131104 | bytes 15363460 | solution.py:162
  286.6 1.6 gather_fusion
  289.1 1.6 gather_fusion.1
  293.0 1.5 multiply_reduce_fusion.1
  298.5 3.7 collective-permute-done
  303.2 9.2 %conditional.3 = (f32[256,256]{1,0:T(8,128)S(1)}, f32[2,512,128]{1,2,0:T(8,128)S(1)}, f32[2,512,128]{2,1,0:T(8,128)S(1)}, f32[256]{0:T(256)}) conditional(s32[]{:T(128)} %convert_element_type.154, () %tuple.84, (s32[]{:T(128)}, s32[16,4]{1,0:T(8,128)S(1)}, bf16[16,128,1,128]{3,1,0,2:T(8,128)(2,1)}, bf16[2048,256]{1,0:T(8,128)(2,1)}, ...), branch_computations={%region_1.1_spmd, %region_2.6_spmd} | conditional | flops 340131104 | bytes 15363460 | solution.py:162
  304.4 1.6 gather_fusion
  306.9 1.6 gather_fusion.1
  316.3 3.7 collective-permute-done
  321.0 9.2 %conditional.3 = (f32[256,256]{1,0:T(8,128)S(1)}, f32[2,512,128]{1,2,0:T(8,128)S(1)}, f32[2,512,128]{2,1,0:T(8,128)S(1)}, f32[256]{0:T(256)}) conditional(s32[]{:T(128)} %convert_element_type.154, () %tuple.84, (s32[]{:T(128)}, s32[16,4]{1,0:T(8,128)S(1)}, bf16[16,128,1,128]{3,1,0,2:T(8,128)(2,1)}, bf16[2048,256]{1,0:T(8,128)(2,1)}, ...), branch_computations={%region_1.1_spmd, %region_2.6_spmd} | conditional | flops 340131104 | bytes 15363460 | solution.py:162
  322.2 1.6 gather_fusion
  324.7 1.6 gather_fusion.1
  334.1 3.9 collective-permute-done
  339.1 9.2 %conditional.3 = (f32[256,256]{1,0:T(8,128)S(1)}, f32[2,512,128]{1,2,0:T(8,128)S(1)}, f32[2,512,128]{2,1,0:T(8,128)S(1)}, f32[256]{0:T(256)}) conditional(s32[]{:T(128)} %convert_element_type.154, () %tuple.84, (s32[]{:T(128)}, s32[16,4]{1,0:T(8,128)S(1)}, bf16[16,128,1,128]{3,1,0,2:T(8,128)(2,1)}, bf16[2048,256]{1,0:T(8,128)(2,1)}, ...), branch_computations={%region_1.1_spmd, %region_2.6_spmd} | conditional | flops 340131104 | bytes 15363460 | solution.py:162
  340.3 1.6 gather_fusion
  342.8 1.6 gather_fusion.1
  352.2 3.7 collective-permute-done
  355.9 4.6 slice.26
  360.6 8.8 %scatter_fusion = f32[16,128,128]{2,1,0:T(8,128)S(1)} fusion(f32[16,128,128]{2,1,0:T(8,128)S(1)} %broadcast.75.clone, s32[64]{0:T(128)S(1)} %copy-done.6, f32[64,128,128]{2,1,0:T(8,128)} %bitcast.107), kind=kCustom, calls=%fused_computation.4 | custom fusion | flops 1048576 | bytes 12583168 | tf_op jit(solution)/shard_map/scatter-add | solution.py:198
  370.3 11.2 %all-to-all-start.2 = ((bf16[16,128,128]{2,1,0:T(8,128)(2,1)}), bf16[16,128,128]{2,1,0:T(8,128)(2,1)}, u32[]{:S(2)}, u32[]{:S(2)}) async-start(bf16[16,128,128]{2,1,0:T(8,128)(2,1)} %convert_element_type.116), calls=%async_computation.2 | async-start | bytes 1048576 | tf_op jit(solution)/shard_map/all_to_all | solution.py:206
  381.5 4.5 slice.27
  386.2 8.8 %scatter_fusion.1 = f32[16,128,128]{2,1,0:T(8,128)S(1)} fusion(f32[16,128,128]{2,1,0:T(8,128)S(1)} %broadcast.75.clone.1, s32[64]{0:T(128)S(1)} %copy-done.6, f32[64,128,128]{2,1,0:T(8,128)} %bitcast.106), kind=kCustom, calls=%fused_computation.5 | custom fusion | flops 1048576 | bytes 12583168 | tf_op jit(solution)/shard_map/scatter-add | solution.py:203
  395.8 4.9 %all-to-all-done.2 = bf16[16,128,128]{2,1,0:T(8,128)(2,1)} async-done(((bf16[16,128,128]{2,1,0:T(8,128)(2,1)}), bf16[16,128,128]{2,1,0:T(8,128)(2,1)}, u32[]{:S(2)}, u32[]{:S(2)}) %all-to-all-start.2) | async-done | bytes 524320 | tf_op jit(solution)/shard_map/all_to_all | solution.py:206
  400.7 7.1 %all-to-all-start.3 = ((bf16[16,128,128]{2,1,0:T(8,128)(2,1)}), bf16[16,128,128]{2,1,0:T(8,128)(2,1)S(1)}, u32[]{:S(2)}, u32[]{:S(2)}) async-start(bf16[16,128,128]{2,1,0:T(8,128)(2,1)} %convert_element_type.122), calls=%async_computation.3 | async-start | bytes 1048576 | tf_op jit(solution)/shard_map/all_to_all | solution.py:213
  408.9 18.1 %all-to-all-done.3 = bf16[16,128,128]{2,1,0:T(8,128)(2,1)S(1)} async-done(((bf16[16,128,128]{2,1,0:T(8,128)(2,1)}), bf16[16,128,128]{2,1,0:T(8,128)(2,1)S(1)}, u32[]{:S(2)}, u32[]{:S(2)}) %all-to-all-start.3) | async-done | bytes 524320 | tf_op jit(solution)/shard_map/all_to_all | solution.py:213
  427.7 10.9 %all-to-all-start.1 = ((bf16[16,128,256]{2,1,0:T(8,128)(2,1)}), bf16[16,128,256]{2,1,0:T(8,128)(2,1)S(1)}, u32[]{:S(2)}, u32[]{:S(2)}) async-start(bf16[16,128,256]{2,1,0:T(8,128)(2,1)} %bitcast.42), calls=%async_computation.1 | async-start | bytes 2097152 | tf_op jit(solution)/shard_map/all_to_all | solution.py:189
  438.6 10.9 %psum.7 = f32[1,256]{1,0:T(1,128)} all-reduce(f32[1,256]{1,0:T(1,128)S(1)} %bitcast.131), channel_id=1, replica_groups=mesh['section'=4,'ctx'=16,'dp'=8] {'dp'}, use_global_device_ids=true, to_apply=%region_12.13 | all-reduce | flops 256 | bytes 2048 | tf_op jit(solution)/shard_map/psum | solution.py:233
  453.5 16.3 %all-to-all-done.1 = bf16[16,128,256]{2,1,0:T(8,128)(2,1)S(1)} async-done(((bf16[16,128,256]{2,1,0:T(8,128)(2,1)}), bf16[16,128,256]{2,1,0:T(8,128)(2,1)S(1)}, u32[]{:S(2)}, u32[]{:S(2)}) %all-to-all-start.1) | async-done | bytes 1048608 | tf_op jit(solution)/shard_map/all_to_all | solution.py:189
  (276 shorter events, 119.1 us)
Async XLA Ops:
  0.6 1.2 copy-start
  0.6 4.6 copy-start.4
  8.1 16.8 %copy-start.7 = (s32[16,4]{0,1:T(4,128)S(1)}, s32[16,4]{0,1:T(4,128)}, u32[]{:S(2)}) copy-start(s32[16,4]{0,1:T(4,128)} %param.18) | copy-start | bytes 772
  9.7 122.0 %all-to-all-start = ((bf16[128,16,576]{0,2,1:T(8,128)(2,1)}), bf16[128,16,576]{0,2,1:T(8,128)(2,1)S(1)}, u32[]{:S(2)}, u32[]{:S(2)}) async-start(bf16[128,16,576]{0,2,1:T(8,128)(2,1)} %pad_maximum_fusion), calls=%async_computation | async-start | bytes 4718592 | tf_op jit(solution)/shard_map/all_to_all | solution.py:68
  134.2 13.3 %copy-start.5 = (f32[1,256]{1,0:T(1,128)S(1)}, f32[1,256]{1,0:T(1,128)}, u32[]{:S(2)}) copy-start(f32[1,256]{1,0:T(1,128)} %param.16) | copy-start | bytes 3076
  140.8 12.1 %collective-permute-start.1 = (bf16[16,32,256]{2,1,0:T(8,128)(2,1)S(1)}, bf16[16,32,256]{2,1,0:T(8,128)(2,1)S(1)}, u32[]{:S(2)}, u32[]{:S(2)}) collective-permute-start(bf16[16,32,256]{2,1,0:T(8,128)(2,1)S(1)} %reshape.182), channel_id=1, source_target_pairs={{0,384},{1,385},{2,386},{3,387},{4,388},{5,389},{6,390},{7,391},{8... | collective-permute-start | bytes 786440 | tf_op jit(solution)/shard_map/ppermute | solution.py:75
  145.8 7.2 %collective-permute-start.2 = (bf16[16,32,256]{2,1,0:T(8,128)(2,1)S(1)}, bf16[16,32,256]{2,1,0:T(8,128)(2,1)S(1)}, u32[]{:S(2)}, u32[]{:S(2)}) collective-permute-start(bf16[16,32,256]{2,1,0:T(8,128)(2,1)S(1)} %reshape.182), channel_id=1, source_target_pairs={{128,384},{129,385},{130,386},{131,387},{132,388},{133,389},{134,3... | collective-permute-start | bytes 786440 | tf_op jit(solution)/shard_map/ppermute | solution.py:75
  146.5 6.5 %collective-permute-start.3 = (bf16[16,32,256]{2,1,0:T(8,128)(2,1)S(1)}, bf16[16,32,256]{2,1,0:T(8,128)(2,1)S(1)}, u32[]{:S(2)}, u32[]{:S(2)}) collective-permute-start(bf16[16,32,256]{2,1,0:T(8,128)(2,1)S(1)} %reshape.182), channel_id=1, source_target_pairs={{256,384},{257,385},{258,386},{259,387},{260,388},{261,389},{262,3... | collective-permute-start | bytes 786440 | tf_op jit(solution)/shard_map/ppermute | solution.py:75
  163.7 7.0 %collective-permute-start = (bf16[256,256]{1,0:T(8,128)(2,1)S(1)}, bf16[256,256]{1,0:T(8,128)(2,1)}, u32[]{:S(2)}, u32[]{:S(2)}) collective-permute-start(bf16[256,256]{1,0:T(8,128)(2,1)S(1)} %get-tuple-element.721), channel_id=1, source_target_pairs={{128,0},{256,128},{384,256},{129,1},{257,129},{385,257},{130,2},{2... | collective-permute-start | bytes 393224 | tf_op jit(solution)/shard_map/while/body/eval_jaxpr/ppermute | solution.py:15
  173.0 7.0 %collective-permute-start = (bf16[256,256]{1,0:T(8,128)(2,1)S(1)}, bf16[256,256]{1,0:T(8,128)(2,1)}, u32[]{:S(2)}, u32[]{:S(2)}) collective-permute-start(bf16[256,256]{1,0:T(8,128)(2,1)S(1)} %get-tuple-element.721), channel_id=1, source_target_pairs={{128,0},{256,128},{384,256},{129,1},{257,129},{385,257},{130,2},{2... | collective-permute-start | bytes 393224 | tf_op jit(solution)/shard_map/while/body/eval_jaxpr/ppermute | solution.py:15
  182.4 30.7 %collective-permute-start = (bf16[256,256]{1,0:T(8,128)(2,1)S(1)}, bf16[256,256]{1,0:T(8,128)(2,1)}, u32[]{:S(2)}, u32[]{:S(2)}) collective-permute-start(bf16[256,256]{1,0:T(8,128)(2,1)S(1)} %get-tuple-element.721), channel_id=1, source_target_pairs={{128,0},{256,128},{384,256},{129,1},{257,129},{385,257},{130,2},{2... | collective-permute-start | bytes 393224 | tf_op jit(solution)/shard_map/while/body/eval_jaxpr/ppermute | solution.py:15
  215.2 2.2 copy-start.1
  223.9 7.0 %collective-permute-start = (bf16[256,256]{1,0:T(8,128)(2,1)S(1)}, bf16[256,256]{1,0:T(8,128)(2,1)}, u32[]{:S(2)}, u32[]{:S(2)}) collective-permute-start(bf16[256,256]{1,0:T(8,128)(2,1)S(1)} %get-tuple-element.721), channel_id=1, source_target_pairs={{128,0},{256,128},{384,256},{129,1},{257,129},{385,257},{130,2},{2... | collective-permute-start | bytes 393224 | tf_op jit(solution)/shard_map/while/body/eval_jaxpr/ppermute | solution.py:15
  233.0 2.2 copy-start.1
  241.8 7.0 %collective-permute-start = (bf16[256,256]{1,0:T(8,128)(2,1)S(1)}, bf16[256,256]{1,0:T(8,128)(2,1)}, u32[]{:S(2)}, u32[]{:S(2)}) collective-permute-start(bf16[256,256]{1,0:T(8,128)(2,1)S(1)} %get-tuple-element.721), channel_id=1, source_target_pairs={{128,0},{256,128},{384,256},{129,1},{257,129},{385,257},{130,2},{2... | collective-permute-start | bytes 393224 | tf_op jit(solution)/shard_map/while/body/eval_jaxpr/ppermute | solution.py:15
  250.9 2.2 copy-start.1
  259.6 7.0 %collective-permute-start = (bf16[256,256]{1,0:T(8,128)(2,1)S(1)}, bf16[256,256]{1,0:T(8,128)(2,1)}, u32[]{:S(2)}, u32[]{:S(2)}) collective-permute-start(bf16[256,256]{1,0:T(8,128)(2,1)S(1)} %get-tuple-element.721), channel_id=1, source_target_pairs={{128,0},{256,128},{384,256},{129,1},{257,129},{385,257},{130,2},{2... | collective-permute-start | bytes 393224 | tf_op jit(solution)/shard_map/while/body/eval_jaxpr/ppermute | solution.py:15
  268.7 2.2 copy-start.1
  277.4 7.0 %collective-permute-start = (bf16[256,256]{1,0:T(8,128)(2,1)S(1)}, bf16[256,256]{1,0:T(8,128)(2,1)}, u32[]{:S(2)}, u32[]{:S(2)}) collective-permute-start(bf16[256,256]{1,0:T(8,128)(2,1)S(1)} %get-tuple-element.721), channel_id=1, source_target_pairs={{128,0},{256,128},{384,256},{129,1},{257,129},{385,257},{130,2},{2... | collective-permute-start | bytes 393224 | tf_op jit(solution)/shard_map/while/body/eval_jaxpr/ppermute | solution.py:15
  286.5 2.2 copy-start.1
  295.2 7.0 %collective-permute-start = (bf16[256,256]{1,0:T(8,128)(2,1)S(1)}, bf16[256,256]{1,0:T(8,128)(2,1)}, u32[]{:S(2)}, u32[]{:S(2)}) collective-permute-start(bf16[256,256]{1,0:T(8,128)(2,1)S(1)} %get-tuple-element.721), channel_id=1, source_target_pairs={{128,0},{256,128},{384,256},{129,1},{257,129},{385,257},{130,2},{2... | collective-permute-start | bytes 393224 | tf_op jit(solution)/shard_map/while/body/eval_jaxpr/ppermute | solution.py:15
  304.3 2.2 copy-start.1
  313.0 7.0 %collective-permute-start = (bf16[256,256]{1,0:T(8,128)(2,1)S(1)}, bf16[256,256]{1,0:T(8,128)(2,1)}, u32[]{:S(2)}, u32[]{:S(2)}) collective-permute-start(bf16[256,256]{1,0:T(8,128)(2,1)S(1)} %get-tuple-element.721), channel_id=1, source_target_pairs={{128,0},{256,128},{384,256},{129,1},{257,129},{385,257},{130,2},{2... | collective-permute-start | bytes 393224 | tf_op jit(solution)/shard_map/while/body/eval_jaxpr/ppermute | solution.py:15
  322.1 2.2 copy-start.1
  330.8 7.2 %collective-permute-start = (bf16[256,256]{1,0:T(8,128)(2,1)S(1)}, bf16[256,256]{1,0:T(8,128)(2,1)}, u32[]{:S(2)}, u32[]{:S(2)}) collective-permute-start(bf16[256,256]{1,0:T(8,128)(2,1)S(1)} %get-tuple-element.721), channel_id=1, source_target_pairs={{128,0},{256,128},{384,256},{129,1},{257,129},{385,257},{130,2},{2... | collective-permute-start | bytes 393224 | tf_op jit(solution)/shard_map/while/body/eval_jaxpr/ppermute | solution.py:15
  340.2 2.2 copy-start.1
  348.9 7.0 %collective-permute-start = (bf16[256,256]{1,0:T(8,128)(2,1)S(1)}, bf16[256,256]{1,0:T(8,128)(2,1)}, u32[]{:S(2)}, u32[]{:S(2)}) collective-permute-start(bf16[256,256]{1,0:T(8,128)(2,1)S(1)} %get-tuple-element.721), channel_id=1, source_target_pairs={{128,0},{256,128},{384,256},{129,1},{257,129},{385,257},{130,2},{2... | collective-permute-start | bytes 393224 | tf_op jit(solution)/shard_map/while/body/eval_jaxpr/ppermute | solution.py:15
  355.9 4.8 %copy-start.6 = (s32[64]{0:T(128)S(1)}, s32[64]{0:T(128)}, u32[]{:S(2)}) copy-start(s32[64]{0:T(128)} %fusion.12) | copy-start | bytes 772
  370.3 30.4 %all-to-all-start.2 = ((bf16[16,128,128]{2,1,0:T(8,128)(2,1)}), bf16[16,128,128]{2,1,0:T(8,128)(2,1)}, u32[]{:S(2)}, u32[]{:S(2)}) async-start(bf16[16,128,128]{2,1,0:T(8,128)(2,1)} %convert_element_type.116), calls=%async_computation.2 | async-start | bytes 1048576 | tf_op jit(solution)/shard_map/all_to_all | solution.py:206
  386.1 21.7 %copy-start.2 = (bf16[2304,256]{1,0:T(8,128)(2,1)S(1)}, bf16[2304,256]{1,0:T(8,128)(2,1)}, u32[]{:S(2)}) copy-start(bf16[2304,256]{1,0:T(8,128)(2,1)} %get-tuple-element.378) | copy-start | bytes 3538948
  400.7 26.2 %all-to-all-start.3 = ((bf16[16,128,128]{2,1,0:T(8,128)(2,1)}), bf16[16,128,128]{2,1,0:T(8,128)(2,1)S(1)}, u32[]{:S(2)}, u32[]{:S(2)}) async-start(bf16[16,128,128]{2,1,0:T(8,128)(2,1)} %convert_element_type.122), calls=%async_computation.3 | async-start | bytes 1048576 | tf_op jit(solution)/shard_map/all_to_all | solution.py:213
  427.0 0.8 copy-start.3
  427.7 42.0 %all-to-all-start.1 = ((bf16[16,128,256]{2,1,0:T(8,128)(2,1)}), bf16[16,128,256]{2,1,0:T(8,128)(2,1)S(1)}, u32[]{:S(2)}, u32[]{:S(2)}) async-start(bf16[16,128,256]{2,1,0:T(8,128)(2,1)} %bitcast.42), calls=%async_computation.1 | async-start | bytes 2097152 | tf_op jit(solution)/shard_map/all_to_all | solution.py:189

commit v11 on v10

--- a/solution.py
+++ b/solution.py
@@ -67,8 +67,8 @@
     ).reshape(tok_local, ctx_count * sum(sent_widths))
     moved = lax.all_to_all(packed, "ctx", split_axis=1, concat_axis=0, tiled=True)
     edges = np.cumsum((0,) + sent_widths)
-    head_input, top_part, head_keys, head_values = lax.optimization_barrier(
-        tuple(moved[:, edges[i] : edges[i + 1]] for i in range(len(sent_widths)))
+    head_input, top_part, head_keys, head_values = (
+        moved[:, edges[i] : edges[i + 1]] for i in range(len(sent_widths))
     )
     top_part = top_part.reshape(ctx_count, quarter, local_width)
     top_quarters = [
@@ -76,6 +76,9 @@
         for q in range(section_count - 1)
     ]
     head_top = jnp.stack(top_quarters + [top_part], axis=1).reshape(total_rows, local_width)
+    head_input, head_top, head_keys, head_values = lax.optimization_barrier(
+        (head_input, head_top, head_keys, head_values)
+    )
     gain_row = query_gain[0]
     query_rows = (head_input.astype(jnp.float32) * gain_row).astype(jnp.bfloat16)
     blocked_keys = head_keys.reshape(block_count, block_rows, local_kv, HEAD_FEATURES)

time: 475 us -> 472 us (level)
  transfers between devices with their start and end apart: 18 -> 18, of which waited for: 16 -> 16; matrix products, arithmetic and copies ran while one was open for 9% -> 10% of each run, Pallas kernels for 0% -> 0%
where the time goes in v11:
time: 472 us; the launch traced here: 468 us
  waiting for transfers between devices  211 us (45%)
  local copies, waits for them, and re-layouts  92 us (19%)
  other arithmetic  67.6 us (14%)
  starting transfers between devices  64.7 us (14%)
  matrix products  19.4 us (4%)
  blocking collectives  10.9 us (2%)
    all_to_all x1, waiting for transfers between devices, shards(): lax.all_to_all(packed, 'ctx', split_axis=1, concat_axis=0, tiled=True)  106 us
    ppermute x11, waiting for transfers between devices, passed_along(): return lax.ppermute(block, axis, route)  64.5 us
    all_to_all x1, waiting for transfers between devices, shards(): lax.all_to_all(value_acc.reshape(total_rows, slot_width).astype(jnp.bfloa...  18.1 us
    all_to_all x1, waiting for transfers between devices, shards(): lax.all_to_all(result_heads[:total_rows], 'ctx', split_axis=0, concat_axi...  16.3 us
    all_to_all x1, starting transfers between devices, shards(): lax.all_to_all(packed, 'ctx', split_axis=1, concat_axis=0, tiled=True)  15.2 us
    ppermute x11, starting transfers between devices, passed_along(): return lax.ppermute(block, axis, route)  14.1 us
    gather x8, local copies, waits for them, and re-layouts, attend(): blocked_values[lists_now]  13.1 us
    gather x8, local copies, waits for them, and re-layouts, attend(): blocked_keys[lists_now]  13.1 us
  transfers between devices with their start and end apart: 18, of which 16 were waited for; matrix products, arithmetic and copies ran while one was open for 10% of the time, Pallas kernels for 0%

profile of v11, /device:TPU:6, one launch (start us, length us, event | category | flops | bytes accessed | tf_op | source)
XLA Modules:
  0.0 467.7 jit_solution(152311844203623174)
XLA Ops:
  6.5 1.6 copy.148
  8.1 1.6 pad_maximum_fusion
  9.7 15.2 %all-to-all-start = ((bf16[128,16,576]{0,2,1:T(8,128)(2,1)}), bf16[128,16,576]{0,2,1:T(8,128)(2,1)S(1)}, u32[]{:S(2)}, u32[]{:S(2)}) async-start(bf16[128,16,576]{0,2,1:T(8,128)(2,1)} %pad_maximum_fusion), calls=%async_computation | async-start | bytes 4718592 | tf_op jit(solution)/shard_map/all_to_all | solution.py:68
  25.7 106.0 %all-to-all-done = bf16[128,16,576]{0,2,1:T(8,128)(2,1)S(1)} async-done(((bf16[128,16,576]{0,2,1:T(8,128)(2,1)}), bf16[128,16,576]{0,2,1:T(8,128)(2,1)S(1)}, u32[]{:S(2)}, u32[]{:S(2)}) %all-to-all-start) | async-done | bytes 2359328 | tf_op jit(solution)/shard_map/all_to_all | solution.py:68
  131.7 2.5 copy.157
  135.7 4.9 %collective-permute-start.1 = (bf16[16,32,256]{2,1,0:T(8,128)(2,1)S(1)}, bf16[16,32,256]{2,1,0:T(8,128)(2,1)S(1)}, u32[]{:S(2)}, u32[]{:S(2)}) collective-permute-start(bf16[16,32,256]{2,1,0:T(8,128)(2,1)S(1)} %reshape.182), channel_id=1, source_target_pairs={{0,384},{1,385},{2,386},{3,387},{4,388},{5,389},{6,390},{7,391},{8... | collective-permute-start | bytes 786440 | tf_op jit(solution)/shard_map/ppermute | solution.py:75
  143.6 3.3 fusion.14
  150.2 2.6 broadcast_in_dim.34.clone
  152.9 2.7 broadcast_in_dim.34.clone2
  157.3 194.5 %while.24 = (s32[]{:T(128)}, bf16[256,256]{1,0:T(8,128)(2,1)}, bf16[2304,256]{1,0:T(8,128)(2,1)}, f32[18,512,128]{2,1,0:T(8,128)}, f32[18,512,128]{2,1,0:T(8,128...) while((s32[]{:T(128)}, bf16[256,256]{1,0:T(8,128)(2,1)}, ...), condition=%wide.region_7.8_spmd.clone, body=%wide.region_0.7_spmd.clone.sunk | while | flops 340590400 | bytes 20086688 | solution.py:190
  163.0 3.7 collective-permute-done
  172.4 3.7 collective-permute-done
  181.7 27.3 %collective-permute-done = bf16[256,256]{1,0:T(8,128)(2,1)} collective-permute-done((bf16[256,256]{1,0:T(8,128)(2,1)S(1)}, bf16[256,256]{1,0:T(8,128)(2,1)}, u32[]{:S(2)}, u32[]{:S(2)}) %collective-permute-start) | collective-permute-done | bytes 131104 | tf_op jit(solution)/shard_map/while/body/eval_jaxpr/ppermute | solution.py:15
  210.1 9.2 %conditional.3 = (f32[256,256]{1,0:T(8,128)S(1)}, f32[2,512,128]{1,2,0:T(8,128)S(1)}, f32[2,512,128]{2,1,0:T(8,128)S(1)}, f32[256]{0:T(256)}) conditional(s32[]{:T(128)} %convert_element_type.154, () %tuple.84, (s32[]{:T(128)}, s32[16,4]{1,0:T(8,128)S(1)}, bf16[16,128,1,128]{3,1,0,2:T(8,128)(2,1)}, bf16[2048,256]{1,0:T(8,128)(2,1)}, ...), branch_computations={%region_1.1_spmd, %region_2.6_spmd} | conditional | flops 340131104 | bytes 15363460 | solution.py:165
  211.3 1.6 gather_fusion
  213.8 1.6 gather_fusion.1
  217.7 1.5 multiply_reduce_fusion.1
  223.2 3.7 collective-permute-done
  227.9 9.2 %conditional.3 = (f32[256,256]{1,0:T(8,128)S(1)}, f32[2,512,128]{1,2,0:T(8,128)S(1)}, f32[2,512,128]{2,1,0:T(8,128)S(1)}, f32[256]{0:T(256)}) conditional(s32[]{:T(128)} %convert_element_type.154, () %tuple.84, (s32[]{:T(128)}, s32[16,4]{1,0:T(8,128)S(1)}, bf16[16,128,1,128]{3,1,0,2:T(8,128)(2,1)}, bf16[2048,256]{1,0:T(8,128)(2,1)}, ...), branch_computations={%region_1.1_spmd, %region_2.6_spmd} | conditional | flops 340131104 | bytes 15363460 | solution.py:165
  229.1 1.6 gather_fusion
  231.6 1.6 gather_fusion.1
  235.5 1.5 multiply_reduce_fusion.1
  241.0 3.7 collective-permute-done
  245.7 9.2 %conditional.3 = (f32[256,256]{1,0:T(8,128)S(1)}, f32[2,512,128]{1,2,0:T(8,128)S(1)}, f32[2,512,128]{2,1,0:T(8,128)S(1)}, f32[256]{0:T(256)}) conditional(s32[]{:T(128)} %convert_element_type.154, () %tuple.84, (s32[]{:T(128)}, s32[16,4]{1,0:T(8,128)S(1)}, bf16[16,128,1,128]{3,1,0,2:T(8,128)(2,1)}, bf16[2048,256]{1,0:T(8,128)(2,1)}, ...), branch_computations={%region_1.1_spmd, %region_2.6_spmd} | conditional | flops 340131104 | bytes 15363460 | solution.py:165
  246.9 1.6 gather_fusion
  249.4 1.6 gather_fusion.1
  253.3 1.5 multiply_reduce_fusion.1
  258.8 3.7 collective-permute-done
  263.5 9.2 %conditional.3 = (f32[256,256]{1,0:T(8,128)S(1)}, f32[2,512,128]{1,2,0:T(8,128)S(1)}, f32[2,512,128]{2,1,0:T(8,128)S(1)}, f32[256]{0:T(256)}) conditional(s32[]{:T(128)} %convert_element_type.154, () %tuple.84, (s32[]{:T(128)}, s32[16,4]{1,0:T(8,128)S(1)}, bf16[16,128,1,128]{3,1,0,2:T(8,128)(2,1)}, bf16[2048,256]{1,0:T(8,128)(2,1)}, ...), branch_computations={%region_1.1_spmd, %region_2.6_spmd} | conditional | flops 340131104 | bytes 15363460 | solution.py:165
  264.8 1.6 gather_fusion
  267.2 1.6 gather_fusion.1
  271.1 1.5 multiply_reduce_fusion.1
  276.6 3.7 collective-permute-done
  281.3 9.2 %conditional.3 = (f32[256,256]{1,0:T(8,128)S(1)}, f32[2,512,128]{1,2,0:T(8,128)S(1)}, f32[2,512,128]{2,1,0:T(8,128)S(1)}, f32[256]{0:T(256)}) conditional(s32[]{:T(128)} %convert_element_type.154, () %tuple.84, (s32[]{:T(128)}, s32[16,4]{1,0:T(8,128)S(1)}, bf16[16,128,1,128]{3,1,0,2:T(8,128)(2,1)}, bf16[2048,256]{1,0:T(8,128)(2,1)}, ...), branch_computations={%region_1.1_spmd, %region_2.6_spmd} | conditional | flops 340131104 | bytes 15363460 | solution.py:165
  282.6 1.6 gather_fusion
  285.0 1.6 gather_fusion.1
  288.9 1.5 multiply_reduce_fusion.1
  294.4 3.7 collective-permute-done
  299.1 9.2 %conditional.3 = (f32[256,256]{1,0:T(8,128)S(1)}, f32[2,512,128]{1,2,0:T(8,128)S(1)}, f32[2,512,128]{2,1,0:T(8,128)S(1)}, f32[256]{0:T(256)}) conditional(s32[]{:T(128)} %convert_element_type.154, () %tuple.84, (s32[]{:T(128)}, s32[16,4]{1,0:T(8,128)S(1)}, bf16[16,128,1,128]{3,1,0,2:T(8,128)(2,1)}, bf16[2048,256]{1,0:T(8,128)(2,1)}, ...), branch_computations={%region_1.1_spmd, %region_2.6_spmd} | conditional | flops 340131104 | bytes 15363460 | solution.py:165
  300.4 1.6 gather_fusion
  302.8 1.6 gather_fusion.1
  306.7 1.5 multiply_reduce_fusion.1
  312.2 3.7 collective-permute-done
  316.9 9.2 %conditional.3 = (f32[256,256]{1,0:T(8,128)S(1)}, f32[2,512,128]{1,2,0:T(8,128)S(1)}, f32[2,512,128]{2,1,0:T(8,128)S(1)}, f32[256]{0:T(256)}) conditional(s32[]{:T(128)} %convert_element_type.154, () %tuple.84, (s32[]{:T(128)}, s32[16,4]{1,0:T(8,128)S(1)}, bf16[16,128,1,128]{3,1,0,2:T(8,128)(2,1)}, bf16[2048,256]{1,0:T(8,128)(2,1)}, ...), branch_computations={%region_1.1_spmd, %region_2.6_spmd} | conditional | flops 340131104 | bytes 15363460 | solution.py:165
  318.2 1.6 gather_fusion
  320.6 1.6 gather_fusion.1
  324.5 1.5 multiply_reduce_fusion.1
  330.0 3.9 collective-permute-done
  335.0 9.2 %conditional.3 = (f32[256,256]{1,0:T(8,128)S(1)}, f32[2,512,128]{1,2,0:T(8,128)S(1)}, f32[2,512,128]{2,1,0:T(8,128)S(1)}, f32[256]{0:T(256)}) conditional(s32[]{:T(128)} %convert_element_type.154, () %tuple.84, (s32[]{:T(128)}, s32[16,4]{1,0:T(8,128)S(1)}, bf16[16,128,1,128]{3,1,0,2:T(8,128)(2,1)}, bf16[2048,256]{1,0:T(8,128)(2,1)}, ...), branch_computations={%region_1.1_spmd, %region_2.6_spmd} | conditional | flops 340131104 | bytes 15363460 | solution.py:165
  336.2 1.6 gather_fusion
  338.7 1.6 gather_fusion.1
  342.6 1.5 multiply_reduce_fusion.1
  348.1 3.7 collective-permute-done
  351.8 4.7 slice.26
  356.5 8.8 %scatter_fusion = f32[16,128,128]{2,1,0:T(8,128)S(1)} fusion(f32[16,128,128]{2,1,0:T(8,128)S(1)} %broadcast.75.clone, s32[64]{0:T(128)S(1)} %copy-done.7, f32[64,128,128]{2,1,0:T(8,128)} %bitcast.107), kind=kCustom, calls=%fused_computation.4 | custom fusion | flops 1048576 | bytes 12583168 | tf_op jit(solution)/shard_map/scatter-add | solution.py:201
  366.2 11.2 %all-to-all-start.2 = ((bf16[16,128,128]{2,1,0:T(8,128)(2,1)}), bf16[16,128,128]{2,1,0:T(8,128)(2,1)}, u32[]{:S(2)}, u32[]{:S(2)}) async-start(bf16[16,128,128]{2,1,0:T(8,128)(2,1)} %convert_element_type.116), calls=%async_computation.2 | async-start | bytes 1048576 | tf_op jit(solution)/shard_map/all_to_all | solution.py:209
  377.4 4.5 slice.27
  382.1 8.8 %scatter_fusion.1 = f32[16,128,128]{2,1,0:T(8,128)S(1)} fusion(f32[16,128,128]{2,1,0:T(8,128)S(1)} %broadcast.75.clone.1, s32[64]{0:T(128)S(1)} %copy-done.7, f32[64,128,128]{2,1,0:T(8,128)} %bitcast.106), kind=kCustom, calls=%fused_computation.5 | custom fusion | flops 1048576 | bytes 12583168 | tf_op jit(solution)/shard_map/scatter-add | solution.py:206
  391.8 4.9 %all-to-all-done.2 = bf16[16,128,128]{2,1,0:T(8,128)(2,1)} async-done(((bf16[16,128,128]{2,1,0:T(8,128)(2,1)}), bf16[16,128,128]{2,1,0:T(8,128)(2,1)}, u32[]{:S(2)}, u32[]{:S(2)}) %all-to-all-start.2) | async-done | bytes 524320 | tf_op jit(solution)/shard_map/all_to_all | solution.py:209
  396.7 7.1 %all-to-all-start.3 = ((bf16[16,128,128]{2,1,0:T(8,128)(2,1)}), bf16[16,128,128]{2,1,0:T(8,128)(2,1)S(1)}, u32[]{:S(2)}, u32[]{:S(2)}) async-start(bf16[16,128,128]{2,1,0:T(8,128)(2,1)} %convert_element_type.122), calls=%async_computation.3 | async-start | bytes 1048576 | tf_op jit(solution)/shard_map/all_to_all | solution.py:216
  404.8 18.1 %all-to-all-done.3 = bf16[16,128,128]{2,1,0:T(8,128)(2,1)S(1)} async-done(((bf16[16,128,128]{2,1,0:T(8,128)(2,1)}), bf16[16,128,128]{2,1,0:T(8,128)(2,1)S(1)}, u32[]{:S(2)}, u32[]{:S(2)}) %all-to-all-start.3) | async-done | bytes 524320 | tf_op jit(solution)/shard_map/all_to_all | solution.py:216
  423.7 10.8 %all-to-all-start.1 = ((bf16[16,128,256]{2,1,0:T(8,128)(2,1)}), bf16[16,128,256]{2,1,0:T(8,128)(2,1)S(1)}, u32[]{:S(2)}, u32[]{:S(2)}) async-start(bf16[16,128,256]{2,1,0:T(8,128)(2,1)} %bitcast.42), calls=%async_computation.1 | async-start | bytes 2097152 | tf_op jit(solution)/shard_map/all_to_all | solution.py:192
  434.5 10.9 %psum.7 = f32[1,256]{1,0:T(1,128)} all-reduce(f32[1,256]{1,0:T(1,128)S(1)} %bitcast.131), channel_id=1, replica_groups=mesh['section'=4,'ctx'=16,'dp'=8] {'dp'}, use_global_device_ids=true, to_apply=%region_12.13 | all-reduce | flops 256 | bytes 2048 | tf_op jit(solution)/shard_map/psum | solution.py:236
  449.4 16.3 %all-to-all-done.1 = bf16[16,128,256]{2,1,0:T(8,128)(2,1)S(1)} async-done(((bf16[16,128,256]{2,1,0:T(8,128)(2,1)}), bf16[16,128,256]{2,1,0:T(8,128)(2,1)S(1)}, u32[]{:S(2)}, u32[]{:S(2)}) %all-to-all-start.1) | async-done | bytes 1048608 | tf_op jit(solution)/shard_map/all_to_all | solution.py:192
  (278 shorter events, 117.9 us)
Async XLA Ops:
  0.6 1.2 copy-start
  0.6 4.6 copy-start.5
  8.1 16.8 %copy-start.8 = (s32[16,4]{0,1:T(4,128)S(1)}, s32[16,4]{0,1:T(4,128)}, u32[]{:S(2)}) copy-start(s32[16,4]{0,1:T(4,128)} %param.18) | copy-start | bytes 772
  9.7 122.0 %all-to-all-start = ((bf16[128,16,576]{0,2,1:T(8,128)(2,1)}), bf16[128,16,576]{0,2,1:T(8,128)(2,1)S(1)}, u32[]{:S(2)}, u32[]{:S(2)}) async-start(bf16[128,16,576]{0,2,1:T(8,128)(2,1)} %pad_maximum_fusion), calls=%async_computation | async-start | bytes 4718592 | tf_op jit(solution)/shard_map/all_to_all | solution.py:68
  135.7 12.1 %collective-permute-start.1 = (bf16[16,32,256]{2,1,0:T(8,128)(2,1)S(1)}, bf16[16,32,256]{2,1,0:T(8,128)(2,1)S(1)}, u32[]{:S(2)}, u32[]{:S(2)}) collective-permute-start(bf16[16,32,256]{2,1,0:T(8,128)(2,1)S(1)} %reshape.182), channel_id=1, source_target_pairs={{0,384},{1,385},{2,386},{3,387},{4,388},{5,389},{6,390},{7,391},{8... | collective-permute-start | bytes 786440 | tf_op jit(solution)/shard_map/ppermute | solution.py:75
  140.6 7.2 %collective-permute-start.2 = (bf16[16,32,256]{2,1,0:T(8,128)(2,1)S(1)}, bf16[16,32,256]{2,1,0:T(8,128)(2,1)S(1)}, u32[]{:S(2)}, u32[]{:S(2)}) collective-permute-start(bf16[16,32,256]{2,1,0:T(8,128)(2,1)S(1)} %reshape.182), channel_id=1, source_target_pairs={{128,384},{129,385},{130,386},{131,387},{132,388},{133,389},{134,3... | collective-permute-start | bytes 786440 | tf_op jit(solution)/shard_map/ppermute | solution.py:75
  141.3 6.5 %collective-permute-start.3 = (bf16[16,32,256]{2,1,0:T(8,128)(2,1)S(1)}, bf16[16,32,256]{2,1,0:T(8,128)(2,1)S(1)}, u32[]{:S(2)}, u32[]{:S(2)}) collective-permute-start(bf16[16,32,256]{2,1,0:T(8,128)(2,1)S(1)} %reshape.182), channel_id=1, source_target_pairs={{256,384},{257,385},{258,386},{259,387},{260,388},{261,389},{262,3... | collective-permute-start | bytes 786440 | tf_op jit(solution)/shard_map/ppermute | solution.py:75
  142.3 6.7 %copy-start.6 = (f32[1,256]{1,0:T(1,128)S(1)}, f32[1,256]{1,0:T(1,128)}, u32[]{:S(2)}) copy-start(f32[1,256]{1,0:T(1,128)} %param.16) | copy-start | bytes 3076
  143.6 6.6 %copy-start.2 = (bf16[2048,256]{1,0:T(8,128)(2,1)}, bf16[2048,256]{1,0:T(8,128)(2,1)S(1)}, u32[]{:S(2)}) copy-start(bf16[2048,256]{1,0:T(8,128)(2,1)S(1)} %slice.36) | copy-start | bytes 3145732
  159.7 7.0 %collective-permute-start = (bf16[256,256]{1,0:T(8,128)(2,1)S(1)}, bf16[256,256]{1,0:T(8,128)(2,1)}, u32[]{:S(2)}, u32[]{:S(2)}) collective-permute-start(bf16[256,256]{1,0:T(8,128)(2,1)S(1)} %get-tuple-element.721), channel_id=1, source_target_pairs={{128,0},{256,128},{384,256},{129,1},{257,129},{385,257},{130,2},{2... | collective-permute-start | bytes 393224 | tf_op jit(solution)/shard_map/while/body/eval_jaxpr/ppermute | solution.py:15
  169.1 7.0 %collective-permute-start = (bf16[256,256]{1,0:T(8,128)(2,1)S(1)}, bf16[256,256]{1,0:T(8,128)(2,1)}, u32[]{:S(2)}, u32[]{:S(2)}) collective-permute-start(bf16[256,256]{1,0:T(8,128)(2,1)S(1)} %get-tuple-element.721), channel_id=1, source_target_pairs={{128,0},{256,128},{384,256},{129,1},{257,129},{385,257},{130,2},{2... | collective-permute-start | bytes 393224 | tf_op jit(solution)/shard_map/while/body/eval_jaxpr/ppermute | solution.py:15
  178.5 30.6 %collective-permute-start = (bf16[256,256]{1,0:T(8,128)(2,1)S(1)}, bf16[256,256]{1,0:T(8,128)(2,1)}, u32[]{:S(2)}, u32[]{:S(2)}) collective-permute-start(bf16[256,256]{1,0:T(8,128)(2,1)S(1)} %get-tuple-element.721), channel_id=1, source_target_pairs={{128,0},{256,128},{384,256},{129,1},{257,129},{385,257},{130,2},{2... | collective-permute-start | bytes 393224 | tf_op jit(solution)/shard_map/while/body/eval_jaxpr/ppermute | solution.py:15
  211.2 2.2 copy-start.1
  219.9 7.0 %collective-permute-start = (bf16[256,256]{1,0:T(8,128)(2,1)S(1)}, bf16[256,256]{1,0:T(8,128)(2,1)}, u32[]{:S(2)}, u32[]{:S(2)}) collective-permute-start(bf16[256,256]{1,0:T(8,128)(2,1)S(1)} %get-tuple-element.721), channel_id=1, source_target_pairs={{128,0},{256,128},{384,256},{129,1},{257,129},{385,257},{130,2},{2... | collective-permute-start | bytes 393224 | tf_op jit(solution)/shard_map/while/body/eval_jaxpr/ppermute | solution.py:15
  229.0 2.2 copy-start.1
  237.7 7.0 %collective-permute-start = (bf16[256,256]{1,0:T(8,128)(2,1)S(1)}, bf16[256,256]{1,0:T(8,128)(2,1)}, u32[]{:S(2)}, u32[]{:S(2)}) collective-permute-start(bf16[256,256]{1,0:T(8,128)(2,1)S(1)} %get-tuple-element.721), channel_id=1, source_target_pairs={{128,0},{256,128},{384,256},{129,1},{257,129},{385,257},{130,2},{2... | collective-permute-start | bytes 393224 | tf_op jit(solution)/shard_map/while/body/eval_jaxpr/ppermute | solution.py:15
  246.8 2.2 copy-start.1
  255.5 7.0 %collective-permute-start = (bf16[256,256]{1,0:T(8,128)(2,1)S(1)}, bf16[256,256]{1,0:T(8,128)(2,1)}, u32[]{:S(2)}, u32[]{:S(2)}) collective-permute-start(bf16[256,256]{1,0:T(8,128)(2,1)S(1)} %get-tuple-element.721), channel_id=1, source_target_pairs={{128,0},{256,128},{384,256},{129,1},{257,129},{385,257},{130,2},{2... | collective-permute-start | bytes 393224 | tf_op jit(solution)/shard_map/while/body/eval_jaxpr/ppermute | solution.py:15
  264.6 2.2 copy-start.1
  273.4 7.0 %collective-permute-start = (bf16[256,256]{1,0:T(8,128)(2,1)S(1)}, bf16[256,256]{1,0:T(8,128)(2,1)}, u32[]{:S(2)}, u32[]{:S(2)}) collective-permute-start(bf16[256,256]{1,0:T(8,128)(2,1)S(1)} %get-tuple-element.721), channel_id=1, source_target_pairs={{128,0},{256,128},{384,256},{129,1},{257,129},{385,257},{130,2},{2... | collective-permute-start | bytes 393224 | tf_op jit(solution)/shard_map/while/body/eval_jaxpr/ppermute | solution.py:15
  282.4 2.2 copy-start.1
  291.2 7.0 %collective-permute-start = (bf16[256,256]{1,0:T(8,128)(2,1)S(1)}, bf16[256,256]{1,0:T(8,128)(2,1)}, u32[]{:S(2)}, u32[]{:S(2)}) collective-permute-start(bf16[256,256]{1,0:T(8,128)(2,1)S(1)} %get-tuple-element.721), channel_id=1, source_target_pairs={{128,0},{256,128},{384,256},{129,1},{257,129},{385,257},{130,2},{2... | collective-permute-start | bytes 393224 | tf_op jit(solution)/shard_map/while/body/eval_jaxpr/ppermute | solution.py:15
  300.2 2.2 copy-start.1
  309.0 7.0 %collective-permute-start = (bf16[256,256]{1,0:T(8,128)(2,1)S(1)}, bf16[256,256]{1,0:T(8,128)(2,1)}, u32[]{:S(2)}, u32[]{:S(2)}) collective-permute-start(bf16[256,256]{1,0:T(8,128)(2,1)S(1)} %get-tuple-element.721), channel_id=1, source_target_pairs={{128,0},{256,128},{384,256},{129,1},{257,129},{385,257},{130,2},{2... | collective-permute-start | bytes 393224 | tf_op jit(solution)/shard_map/while/body/eval_jaxpr/ppermute | solution.py:15
  318.1 2.2 copy-start.1
  326.8 7.2 %collective-permute-start = (bf16[256,256]{1,0:T(8,128)(2,1)S(1)}, bf16[256,256]{1,0:T(8,128)(2,1)}, u32[]{:S(2)}, u32[]{:S(2)}) collective-permute-start(bf16[256,256]{1,0:T(8,128)(2,1)S(1)} %get-tuple-element.721), channel_id=1, source_target_pairs={{128,0},{256,128},{384,256},{129,1},{257,129},{385,257},{130,2},{2... | collective-permute-start | bytes 393224 | tf_op jit(solution)/shard_map/while/body/eval_jaxpr/ppermute | solution.py:15
  336.1 2.2 copy-start.1
  344.8 7.0 %collective-permute-start = (bf16[256,256]{1,0:T(8,128)(2,1)S(1)}, bf16[256,256]{1,0:T(8,128)(2,1)}, u32[]{:S(2)}, u32[]{:S(2)}) collective-permute-start(bf16[256,256]{1,0:T(8,128)(2,1)S(1)} %get-tuple-element.721), channel_id=1, source_target_pairs={{128,0},{256,128},{384,256},{129,1},{257,129},{385,257},{130,2},{2... | collective-permute-start | bytes 393224 | tf_op jit(solution)/shard_map/while/body/eval_jaxpr/ppermute | solution.py:15
  351.8 4.8 %copy-start.7 = (s32[64]{0:T(128)S(1)}, s32[64]{0:T(128)}, u32[]{:S(2)}) copy-start(s32[64]{0:T(128)} %fusion.12) | copy-start | bytes 772
  366.2 30.5 %all-to-all-start.2 = ((bf16[16,128,128]{2,1,0:T(8,128)(2,1)}), bf16[16,128,128]{2,1,0:T(8,128)(2,1)}, u32[]{:S(2)}, u32[]{:S(2)}) async-start(bf16[16,128,128]{2,1,0:T(8,128)(2,1)} %convert_element_type.116), calls=%async_computation.2 | async-start | bytes 1048576 | tf_op jit(solution)/shard_map/all_to_all | solution.py:209
  382.1 21.7 %copy-start.3 = (bf16[2304,256]{1,0:T(8,128)(2,1)S(1)}, bf16[2304,256]{1,0:T(8,128)(2,1)}, u32[]{:S(2)}) copy-start(bf16[2304,256]{1,0:T(8,128)(2,1)} %get-tuple-element.378) | copy-start | bytes 3538948
  396.7 26.2 %all-to-all-start.3 = ((bf16[16,128,128]{2,1,0:T(8,128)(2,1)}), bf16[16,128,128]{2,1,0:T(8,128)(2,1)S(1)}, u32[]{:S(2)}, u32[]{:S(2)}) async-start(bf16[16,128,128]{2,1,0:T(8,128)(2,1)} %convert_element_type.122), calls=%async_computation.3 | async-start | bytes 1048576 | tf_op jit(solution)/shard_map/all_to_all | solution.py:216
  422.9 0.8 copy-start.4
  423.7 42.0 %all-to-all-start.1 = ((bf16[16,128,256]{2,1,0:T(8,128)(2,1)}), bf16[16,128,256]{2,1,0:T(8,128)(2,1)S(1)}, u32[]{:S(2)}, u32[]{:S(2)}) async-start(bf16[16,128,256]{2,1,0:T(8,128)(2,1)} %bitcast.42), calls=%async_computation.1 | async-start | bytes 2097152 | tf_op jit(solution)/shard_map/all_to_all | solution.py:192

commit v12 on v11

--- a/solution.py
+++ b/solution.py
@@ -56,18 +56,19 @@
         .reshape(ctx_count, tok_local, top_width)
         .transpose(1, 0, 2)
     )
-    sent_widths = (local_width, top_width, slot_width, slot_width)
+    sent_widths = (local_width, slot_width, slot_width, top_width)
     packed = jnp.concatenate(
-        [layer_input.reshape(tok_local, ctx_count, local_width), top_piece]
+        [layer_input.reshape(tok_local, ctx_count, local_width)]
         + [
             piece.reshape(tok_local, ctx_count, slot_width)
             for piece in (sent_keys, sent_values)
-        ],
+        ]
+        + [top_piece],
         axis=2,
     ).reshape(tok_local, ctx_count * sum(sent_widths))
     moved = lax.all_to_all(packed, "ctx", split_axis=1, concat_axis=0, tiled=True)
     edges = np.cumsum((0,) + sent_widths)
-    head_input, top_part, head_keys, head_values = (
+    head_input, head_keys, head_values, top_part = (
         moved[:, edges[i] : edges[i + 1]] for i in range(len(sent_widths))
     )
     top_part = top_part.reshape(ctx_count, quarter, local_width)

time: 472 us -> 472 us (level)
  no operation moved by 1% of the time
where the time goes in v12:
time: 472 us; the launch traced here: 468 us
  waiting for transfers between devices  211 us (45%)
  local copies, waits for them, and re-layouts  91.3 us (19%)
  other arithmetic  67.6 us (14%)
  starting transfers between devices  64.6 us (14%)
  matrix products  19.4 us (4%)
  blocking collectives  10.9 us (2%)
    all_to_all x1, waiting for transfers between devices, shards(): lax.all_to_all(packed, 'ctx', split_axis=1, concat_axis=0, tiled=True)  106 us
    ppermute x11, waiting for transfers between devices, passed_along(): return lax.ppermute(block, axis, route)  64.5 us
    all_to_all x1, waiting for transfers between devices, shards(): lax.all_to_all(value_acc.reshape(total_rows, slot_width).astype(jnp.bfloa...  18.1 us
    all_to_all x1, waiting for transfers between devices, shards(): lax.all_to_all(result_heads[:total_rows], 'ctx', split_axis=0, concat_axi...  16.3 us
    all_to_all x1, starting transfers between devices, shards(): lax.all_to_all(packed, 'ctx', split_axis=1, concat_axis=0, tiled=True)  15.2 us
    ppermute x11, starting transfers between devices, passed_along(): return lax.ppermute(block, axis, route)  14.1 us
    gather x8, local copies, waits for them, and re-layouts, attend(): blocked_values[lists_now]  13.1 us
    gather x8, local copies, waits for them, and re-layouts, attend(): blocked_keys[lists_now]  13.1 us
  transfers between devices with their start and end apart: 18, of which 16 were waited for; matrix products, arithmetic and copies ran while one was open for 10% of the time, Pallas kernels for 0%

profile of v12, /device:TPU:6, one launch (start us, length us, event | category | flops | bytes accessed | tf_op | source)
XLA Modules:
  0.0 467.6 jit_solution(4888657775875988774)
XLA Ops:
  6.5 1.6 copy.148
  8.1 1.5 pad_maximum_fusion
  9.7 15.2 %all-to-all-start = ((bf16[128,16,576]{0,2,1:T(8,128)(2,1)}), bf16[128,16,576]{0,2,1:T(8,128)(2,1)S(1)}, u32[]{:S(2)}, u32[]{:S(2)}) async-start(bf16[128,16,576]{0,2,1:T(8,128)(2,1)} %pad_maximum_fusion), calls=%async_computation | async-start | bytes 4718592 | tf_op jit(solution)/shard_map/all_to_all | solution.py:69
  25.6 106.0 %all-to-all-done = bf16[128,16,576]{0,2,1:T(8,128)(2,1)S(1)} async-done(((bf16[128,16,576]{0,2,1:T(8,128)(2,1)}), bf16[128,16,576]{0,2,1:T(8,128)(2,1)S(1)}, u32[]{:S(2)}, u32[]{:S(2)}) %all-to-all-start) | async-done | bytes 2359328 | tf_op jit(solution)/shard_map/all_to_all | solution.py:69
  131.6 2.5 copy.157
  135.6 4.9 %collective-permute-start.1 = (bf16[16,32,256]{2,1,0:T(8,128)(2,1)S(1)}, bf16[16,32,256]{2,1,0:T(8,128)(2,1)S(1)}, u32[]{:S(2)}, u32[]{:S(2)}) collective-permute-start(bf16[16,32,256]{2,1,0:T(8,128)(2,1)S(1)} %reshape.182), channel_id=1, source_target_pairs={{0,384},{1,385},{2,386},{3,387},{4,388},{5,389},{6,390},{7,391},{8... | collective-permute-start | bytes 786440 | tf_op jit(solution)/shard_map/ppermute | solution.py:76
  143.6 2.6 fusion.14
  150.1 2.6 broadcast_in_dim.34.clone
  152.8 2.7 broadcast_in_dim.34.clone2
  157.2 194.5 %while.24 = (s32[]{:T(128)}, bf16[256,256]{1,0:T(8,128)(2,1)}, bf16[2304,256]{1,0:T(8,128)(2,1)}, f32[18,512,128]{2,1,0:T(8,128)}, f32[18,512,128]{2,1,0:T(8,128...) while((s32[]{:T(128)}, bf16[256,256]{1,0:T(8,128)(2,1)}, ...), condition=%wide.region_7.8_spmd.clone, body=%wide.region_0.7_spmd.clone.sunk | while | flops 340590400 | bytes 20086688 | solution.py:191
  162.9 3.7 collective-permute-done
  172.3 3.7 collective-permute-done
  181.6 27.3 %collective-permute-done = bf16[256,256]{1,0:T(8,128)(2,1)} collective-permute-done((bf16[256,256]{1,0:T(8,128)(2,1)S(1)}, bf16[256,256]{1,0:T(8,128)(2,1)}, u32[]{:S(2)}, u32[]{:S(2)}) %collective-permute-start) | collective-permute-done | bytes 131104 | tf_op jit(solution)/shard_map/while/body/eval_jaxpr/ppermute | solution.py:15
  210.0 9.2 %conditional.3 = (f32[256,256]{1,0:T(8,128)S(1)}, f32[2,512,128]{1,2,0:T(8,128)S(1)}, f32[2,512,128]{2,1,0:T(8,128)S(1)}, f32[256]{0:T(256)}) conditional(s32[]{:T(128)} %convert_element_type.154, () %tuple.84, (s32[]{:T(128)}, s32[16,4]{1,0:T(8,128)S(1)}, bf16[16,128,1,128]{3,1,0,2:T(8,128)(2,1)}, bf16[2048,256]{1,0:T(8,128)(2,1)}, ...), branch_computations={%region_1.1_spmd, %region_2.6_spmd} | conditional | flops 340131104 | bytes 15363460 | solution.py:166
  211.2 1.6 gather_fusion
  213.7 1.6 gather_fusion.1
  217.6 1.5 multiply_reduce_fusion.1
  223.1 3.7 collective-permute-done
  227.8 9.2 %conditional.3 = (f32[256,256]{1,0:T(8,128)S(1)}, f32[2,512,128]{1,2,0:T(8,128)S(1)}, f32[2,512,128]{2,1,0:T(8,128)S(1)}, f32[256]{0:T(256)}) conditional(s32[]{:T(128)} %convert_element_type.154, () %tuple.84, (s32[]{:T(128)}, s32[16,4]{1,0:T(8,128)S(1)}, bf16[16,128,1,128]{3,1,0,2:T(8,128)(2,1)}, bf16[2048,256]{1,0:T(8,128)(2,1)}, ...), branch_computations={%region_1.1_spmd, %region_2.6_spmd} | conditional | flops 340131104 | bytes 15363460 | solution.py:166
  229.1 1.6 gather_fusion
  231.5 1.6 gather_fusion.1
  235.4 1.5 multiply_reduce_fusion.1
  240.9 3.7 collective-permute-done
  245.6 9.2 %conditional.3 = (f32[256,256]{1,0:T(8,128)S(1)}, f32[2,512,128]{1,2,0:T(8,128)S(1)}, f32[2,512,128]{2,1,0:T(8,128)S(1)}, f32[256]{0:T(256)}) conditional(s32[]{:T(128)} %convert_element_type.154, () %tuple.84, (s32[]{:T(128)}, s32[16,4]{1,0:T(8,128)S(1)}, bf16[16,128,1,128]{3,1,0,2:T(8,128)(2,1)}, bf16[2048,256]{1,0:T(8,128)(2,1)}, ...), branch_computations={%region_1.1_spmd, %region_2.6_spmd} | conditional | flops 340131104 | bytes 15363460 | solution.py:166
  246.9 1.6 gather_fusion
  249.3 1.6 gather_fusion.1
  253.2 1.5 multiply_reduce_fusion.1
  258.7 3.7 collective-permute-done
  263.4 9.2 %conditional.3 = (f32[256,256]{1,0:T(8,128)S(1)}, f32[2,512,128]{1,2,0:T(8,128)S(1)}, f32[2,512,128]{2,1,0:T(8,128)S(1)}, f32[256]{0:T(256)}) conditional(s32[]{:T(128)} %convert_element_type.154, () %tuple.84, (s32[]{:T(128)}, s32[16,4]{1,0:T(8,128)S(1)}, bf16[16,128,1,128]{3,1,0,2:T(8,128)(2,1)}, bf16[2048,256]{1,0:T(8,128)(2,1)}, ...), branch_computations={%region_1.1_spmd, %region_2.6_spmd} | conditional | flops 340131104 | bytes 15363460 | solution.py:166
  264.7 1.6 gather_fusion
  267.1 1.6 gather_fusion.1
  271.1 1.5 multiply_reduce_fusion.1
  276.5 3.7 collective-permute-done
  281.2 9.2 %conditional.3 = (f32[256,256]{1,0:T(8,128)S(1)}, f32[2,512,128]{1,2,0:T(8,128)S(1)}, f32[2,512,128]{2,1,0:T(8,128)S(1)}, f32[256]{0:T(256)}) conditional(s32[]{:T(128)} %convert_element_type.154, () %tuple.84, (s32[]{:T(128)}, s32[16,4]{1,0:T(8,128)S(1)}, bf16[16,128,1,128]{3,1,0,2:T(8,128)(2,1)}, bf16[2048,256]{1,0:T(8,128)(2,1)}, ...), branch_computations={%region_1.1_spmd, %region_2.6_spmd} | conditional | flops 340131104 | bytes 15363460 | solution.py:166
  282.5 1.6 gather_fusion
  285.0 1.6 gather_fusion.1
  288.9 1.5 multiply_reduce_fusion.1
  294.3 3.7 collective-permute-done
  299.0 9.2 %conditional.3 = (f32[256,256]{1,0:T(8,128)S(1)}, f32[2,512,128]{1,2,0:T(8,128)S(1)}, f32[2,512,128]{2,1,0:T(8,128)S(1)}, f32[256]{0:T(256)}) conditional(s32[]{:T(128)} %convert_element_type.154, () %tuple.84, (s32[]{:T(128)}, s32[16,4]{1,0:T(8,128)S(1)}, bf16[16,128,1,128]{3,1,0,2:T(8,128)(2,1)}, bf16[2048,256]{1,0:T(8,128)(2,1)}, ...), branch_computations={%region_1.1_spmd, %region_2.6_spmd} | conditional | flops 340131104 | bytes 15363460 | solution.py:166
  300.3 1.6 gather_fusion
  302.8 1.6 gather_fusion.1
  306.7 1.5 multiply_reduce_fusion.1
  312.1 3.7 collective-permute-done
  316.8 9.2 %conditional.3 = (f32[256,256]{1,0:T(8,128)S(1)}, f32[2,512,128]{1,2,0:T(8,128)S(1)}, f32[2,512,128]{2,1,0:T(8,128)S(1)}, f32[256]{0:T(256)}) conditional(s32[]{:T(128)} %convert_element_type.154, () %tuple.84, (s32[]{:T(128)}, s32[16,4]{1,0:T(8,128)S(1)}, bf16[16,128,1,128]{3,1,0,2:T(8,128)(2,1)}, bf16[2048,256]{1,0:T(8,128)(2,1)}, ...), branch_computations={%region_1.1_spmd, %region_2.6_spmd} | conditional | flops 340131104 | bytes 15363460 | solution.py:166
  318.1 1.6 gather_fusion
  320.6 1.6 gather_fusion.1
  324.5 1.5 multiply_reduce_fusion.1
  330.0 3.9 collective-permute-done
  334.9 9.2 %conditional.3 = (f32[256,256]{1,0:T(8,128)S(1)}, f32[2,512,128]{1,2,0:T(8,128)S(1)}, f32[2,512,128]{2,1,0:T(8,128)S(1)}, f32[256]{0:T(256)}) conditional(s32[]{:T(128)} %convert_element_type.154, () %tuple.84, (s32[]{:T(128)}, s32[16,4]{1,0:T(8,128)S(1)}, bf16[16,128,1,128]{3,1,0,2:T(8,128)(2,1)}, bf16[2048,256]{1,0:T(8,128)(2,1)}, ...), branch_computations={%region_1.1_spmd, %region_2.6_spmd} | conditional | flops 340131104 | bytes 15363460 | solution.py:166
  336.1 1.6 gather_fusion
  338.6 1.6 gather_fusion.1
  342.5 1.5 multiply_reduce_fusion.1
  348.0 3.7 collective-permute-done
  351.7 4.7 slice.26
  356.5 8.8 %scatter_fusion = f32[16,128,128]{2,1,0:T(8,128)S(1)} fusion(f32[16,128,128]{2,1,0:T(8,128)S(1)} %broadcast.75.clone, s32[64]{0:T(128)S(1)} %copy-done.7, f32[64,128,128]{2,1,0:T(8,128)} %bitcast.107), kind=kCustom, calls=%fused_computation.4 | custom fusion | flops 1048576 | bytes 12583168 | tf_op jit(solution)/shard_map/scatter-add | solution.py:202
  366.1 11.2 %all-to-all-start.2 = ((bf16[16,128,128]{2,1,0:T(8,128)(2,1)}), bf16[16,128,128]{2,1,0:T(8,128)(2,1)}, u32[]{:S(2)}, u32[]{:S(2)}) async-start(bf16[16,128,128]{2,1,0:T(8,128)(2,1)} %convert_element_type.116), calls=%async_computation.2 | async-start | bytes 1048576 | tf_op jit(solution)/shard_map/all_to_all | solution.py:210
  377.4 4.5 slice.27
  382.0 8.8 %scatter_fusion.1 = f32[16,128,128]{2,1,0:T(8,128)S(1)} fusion(f32[16,128,128]{2,1,0:T(8,128)S(1)} %broadcast.75.clone.1, s32[64]{0:T(128)S(1)} %copy-done.7, f32[64,128,128]{2,1,0:T(8,128)} %bitcast.106), kind=kCustom, calls=%fused_computation.5 | custom fusion | flops 1048576 | bytes 12583168 | tf_op jit(solution)/shard_map/scatter-add | solution.py:207
  391.7 4.9 %all-to-all-done.2 = bf16[16,128,128]{2,1,0:T(8,128)(2,1)} async-done(((bf16[16,128,128]{2,1,0:T(8,128)(2,1)}), bf16[16,128,128]{2,1,0:T(8,128)(2,1)}, u32[]{:S(2)}, u32[]{:S(2)}) %all-to-all-start.2) | async-done | bytes 524320 | tf_op jit(solution)/shard_map/all_to_all | solution.py:210
  396.6 7.1 %all-to-all-start.3 = ((bf16[16,128,128]{2,1,0:T(8,128)(2,1)}), bf16[16,128,128]{2,1,0:T(8,128)(2,1)S(1)}, u32[]{:S(2)}, u32[]{:S(2)}) async-start(bf16[16,128,128]{2,1,0:T(8,128)(2,1)} %convert_element_type.122), calls=%async_computation.3 | async-start | bytes 1048576 | tf_op jit(solution)/shard_map/all_to_all | solution.py:217
  404.7 18.1 %all-to-all-done.3 = bf16[16,128,128]{2,1,0:T(8,128)(2,1)S(1)} async-done(((bf16[16,128,128]{2,1,0:T(8,128)(2,1)}), bf16[16,128,128]{2,1,0:T(8,128)(2,1)S(1)}, u32[]{:S(2)}, u32[]{:S(2)}) %all-to-all-start.3) | async-done | bytes 524320 | tf_op jit(solution)/shard_map/all_to_all | solution.py:217
  423.6 10.8 %all-to-all-start.1 = ((bf16[16,128,256]{2,1,0:T(8,128)(2,1)}), bf16[16,128,256]{2,1,0:T(8,128)(2,1)S(1)}, u32[]{:S(2)}, u32[]{:S(2)}) async-start(bf16[16,128,256]{2,1,0:T(8,128)(2,1)} %bitcast.42), calls=%async_computation.1 | async-start | bytes 2097152 | tf_op jit(solution)/shard_map/all_to_all | solution.py:193
  434.4 10.9 %psum.7 = f32[1,256]{1,0:T(1,128)} all-reduce(f32[1,256]{1,0:T(1,128)S(1)} %bitcast.131), channel_id=1, replica_groups=mesh['section'=4,'ctx'=16,'dp'=8] {'dp'}, use_global_device_ids=true, to_apply=%region_12.13 | all-reduce | flops 256 | bytes 2048 | tf_op jit(solution)/shard_map/psum | solution.py:237
  449.3 16.3 %all-to-all-done.1 = bf16[16,128,256]{2,1,0:T(8,128)(2,1)S(1)} async-done(((bf16[16,128,256]{2,1,0:T(8,128)(2,1)}), bf16[16,128,256]{2,1,0:T(8,128)(2,1)S(1)}, u32[]{:S(2)}, u32[]{:S(2)}) %all-to-all-start.1) | async-done | bytes 1048608 | tf_op jit(solution)/shard_map/all_to_all | solution.py:193
  (278 shorter events, 118.5 us)
Async XLA Ops:
  0.6 1.2 copy-start
  0.6 4.6 copy-start.5
  8.1 16.8 %copy-start.8 = (s32[16,4]{0,1:T(4,128)S(1)}, s32[16,4]{0,1:T(4,128)}, u32[]{:S(2)}) copy-start(s32[16,4]{0,1:T(4,128)} %param.18) | copy-start | bytes 772
  9.7 122.0 %all-to-all-start = ((bf16[128,16,576]{0,2,1:T(8,128)(2,1)}), bf16[128,16,576]{0,2,1:T(8,128)(2,1)S(1)}, u32[]{:S(2)}, u32[]{:S(2)}) async-start(bf16[128,16,576]{0,2,1:T(8,128)(2,1)} %pad_maximum_fusion), calls=%async_computation | async-start | bytes 4718592 | tf_op jit(solution)/shard_map/all_to_all | solution.py:69
  135.6 12.1 %collective-permute-start.1 = (bf16[16,32,256]{2,1,0:T(8,128)(2,1)S(1)}, bf16[16,32,256]{2,1,0:T(8,128)(2,1)S(1)}, u32[]{:S(2)}, u32[]{:S(2)}) collective-permute-start(bf16[16,32,256]{2,1,0:T(8,128)(2,1)S(1)} %reshape.182), channel_id=1, source_target_pairs={{0,384},{1,385},{2,386},{3,387},{4,388},{5,389},{6,390},{7,391},{8... | collective-permute-start | bytes 786440 | tf_op jit(solution)/shard_map/ppermute | solution.py:76
  140.5 7.2 %collective-permute-start.2 = (bf16[16,32,256]{2,1,0:T(8,128)(2,1)S(1)}, bf16[16,32,256]{2,1,0:T(8,128)(2,1)S(1)}, u32[]{:S(2)}, u32[]{:S(2)}) collective-permute-start(bf16[16,32,256]{2,1,0:T(8,128)(2,1)S(1)} %reshape.182), channel_id=1, source_target_pairs={{128,384},{129,385},{130,386},{131,387},{132,388},{133,389},{134,3... | collective-permute-start | bytes 786440 | tf_op jit(solution)/shard_map/ppermute | solution.py:76
  141.2 6.5 %collective-permute-start.3 = (bf16[16,32,256]{2,1,0:T(8,128)(2,1)S(1)}, bf16[16,32,256]{2,1,0:T(8,128)(2,1)S(1)}, u32[]{:S(2)}, u32[]{:S(2)}) collective-permute-start(bf16[16,32,256]{2,1,0:T(8,128)(2,1)S(1)} %reshape.182), channel_id=1, source_target_pairs={{256,384},{257,385},{258,386},{259,387},{260,388},{261,389},{262,3... | collective-permute-start | bytes 786440 | tf_op jit(solution)/shard_map/ppermute | solution.py:76
  142.2 6.7 %copy-start.6 = (f32[1,256]{1,0:T(1,128)S(1)}, f32[1,256]{1,0:T(1,128)}, u32[]{:S(2)}) copy-start(f32[1,256]{1,0:T(1,128)} %param.16) | copy-start | bytes 3076
  143.5 6.6 %copy-start.2 = (bf16[2048,256]{1,0:T(8,128)(2,1)}, bf16[2048,256]{1,0:T(8,128)(2,1)S(1)}, u32[]{:S(2)}) copy-start(bf16[2048,256]{1,0:T(8,128)(2,1)S(1)} %slice.36) | copy-start | bytes 3145732
  159.6 7.0 %collective-permute-start = (bf16[256,256]{1,0:T(8,128)(2,1)S(1)}, bf16[256,256]{1,0:T(8,128)(2,1)}, u32[]{:S(2)}, u32[]{:S(2)}) collective-permute-start(bf16[256,256]{1,0:T(8,128)(2,1)S(1)} %get-tuple-element.721), channel_id=1, source_target_pairs={{128,0},{256,128},{384,256},{129,1},{257,129},{385,257},{130,2},{2... | collective-permute-start | bytes 393224 | tf_op jit(solution)/shard_map/while/body/eval_jaxpr/ppermute | solution.py:15
  169.0 7.0 %collective-permute-start = (bf16[256,256]{1,0:T(8,128)(2,1)S(1)}, bf16[256,256]{1,0:T(8,128)(2,1)}, u32[]{:S(2)}, u32[]{:S(2)}) collective-permute-start(bf16[256,256]{1,0:T(8,128)(2,1)S(1)} %get-tuple-element.721), channel_id=1, source_target_pairs={{128,0},{256,128},{384,256},{129,1},{257,129},{385,257},{130,2},{2... | collective-permute-start | bytes 393224 | tf_op jit(solution)/shard_map/while/body/eval_jaxpr/ppermute | solution.py:15
  178.4 30.6 %collective-permute-start = (bf16[256,256]{1,0:T(8,128)(2,1)S(1)}, bf16[256,256]{1,0:T(8,128)(2,1)}, u32[]{:S(2)}, u32[]{:S(2)}) collective-permute-start(bf16[256,256]{1,0:T(8,128)(2,1)S(1)} %get-tuple-element.721), channel_id=1, source_target_pairs={{128,0},{256,128},{384,256},{129,1},{257,129},{385,257},{130,2},{2... | collective-permute-start | bytes 393224 | tf_op jit(solution)/shard_map/while/body/eval_jaxpr/ppermute | solution.py:15
  211.1 2.2 copy-start.1
  219.8 7.0 %collective-permute-start = (bf16[256,256]{1,0:T(8,128)(2,1)S(1)}, bf16[256,256]{1,0:T(8,128)(2,1)}, u32[]{:S(2)}, u32[]{:S(2)}) collective-permute-start(bf16[256,256]{1,0:T(8,128)(2,1)S(1)} %get-tuple-element.721), channel_id=1, source_target_pairs={{128,0},{256,128},{384,256},{129,1},{257,129},{385,257},{130,2},{2... | collective-permute-start | bytes 393224 | tf_op jit(solution)/shard_map/while/body/eval_jaxpr/ppermute | solution.py:15
  228.9 2.2 copy-start.1
  237.6 7.0 %collective-permute-start = (bf16[256,256]{1,0:T(8,128)(2,1)S(1)}, bf16[256,256]{1,0:T(8,128)(2,1)}, u32[]{:S(2)}, u32[]{:S(2)}) collective-permute-start(bf16[256,256]{1,0:T(8,128)(2,1)S(1)} %get-tuple-element.721), channel_id=1, source_target_pairs={{128,0},{256,128},{384,256},{129,1},{257,129},{385,257},{130,2},{2... | collective-permute-start | bytes 393224 | tf_op jit(solution)/shard_map/while/body/eval_jaxpr/ppermute | solution.py:15
  246.7 2.2 copy-start.1
  255.4 7.0 %collective-permute-start = (bf16[256,256]{1,0:T(8,128)(2,1)S(1)}, bf16[256,256]{1,0:T(8,128)(2,1)}, u32[]{:S(2)}, u32[]{:S(2)}) collective-permute-start(bf16[256,256]{1,0:T(8,128)(2,1)S(1)} %get-tuple-element.721), channel_id=1, source_target_pairs={{128,0},{256,128},{384,256},{129,1},{257,129},{385,257},{130,2},{2... | collective-permute-start | bytes 393224 | tf_op jit(solution)/shard_map/while/body/eval_jaxpr/ppermute | solution.py:15
  264.5 2.2 copy-start.1
  273.3 7.0 %collective-permute-start = (bf16[256,256]{1,0:T(8,128)(2,1)S(1)}, bf16[256,256]{1,0:T(8,128)(2,1)}, u32[]{:S(2)}, u32[]{:S(2)}) collective-permute-start(bf16[256,256]{1,0:T(8,128)(2,1)S(1)} %get-tuple-element.721), channel_id=1, source_target_pairs={{128,0},{256,128},{384,256},{129,1},{257,129},{385,257},{130,2},{2... | collective-permute-start | bytes 393224 | tf_op jit(solution)/shard_map/while/body/eval_jaxpr/ppermute | solution.py:15
  282.4 2.2 copy-start.1
  291.1 7.0 %collective-permute-start = (bf16[256,256]{1,0:T(8,128)(2,1)S(1)}, bf16[256,256]{1,0:T(8,128)(2,1)}, u32[]{:S(2)}, u32[]{:S(2)}) collective-permute-start(bf16[256,256]{1,0:T(8,128)(2,1)S(1)} %get-tuple-element.721), channel_id=1, source_target_pairs={{128,0},{256,128},{384,256},{129,1},{257,129},{385,257},{130,2},{2... | collective-permute-start | bytes 393224 | tf_op jit(solution)/shard_map/while/body/eval_jaxpr/ppermute | solution.py:15
  300.2 2.2 copy-start.1
  308.9 7.0 %collective-permute-start = (bf16[256,256]{1,0:T(8,128)(2,1)S(1)}, bf16[256,256]{1,0:T(8,128)(2,1)}, u32[]{:S(2)}, u32[]{:S(2)}) collective-permute-start(bf16[256,256]{1,0:T(8,128)(2,1)S(1)} %get-tuple-element.721), channel_id=1, source_target_pairs={{128,0},{256,128},{384,256},{129,1},{257,129},{385,257},{130,2},{2... | collective-permute-start | bytes 393224 | tf_op jit(solution)/shard_map/while/body/eval_jaxpr/ppermute | solution.py:15
  318.0 2.2 copy-start.1
  326.7 7.2 %collective-permute-start = (bf16[256,256]{1,0:T(8,128)(2,1)S(1)}, bf16[256,256]{1,0:T(8,128)(2,1)}, u32[]{:S(2)}, u32[]{:S(2)}) collective-permute-start(bf16[256,256]{1,0:T(8,128)(2,1)S(1)} %get-tuple-element.721), channel_id=1, source_target_pairs={{128,0},{256,128},{384,256},{129,1},{257,129},{385,257},{130,2},{2... | collective-permute-start | bytes 393224 | tf_op jit(solution)/shard_map/while/body/eval_jaxpr/ppermute | solution.py:15
  336.0 2.2 copy-start.1
  344.7 7.0 %collective-permute-start = (bf16[256,256]{1,0:T(8,128)(2,1)S(1)}, bf16[256,256]{1,0:T(8,128)(2,1)}, u32[]{:S(2)}, u32[]{:S(2)}) collective-permute-start(bf16[256,256]{1,0:T(8,128)(2,1)S(1)} %get-tuple-element.721), channel_id=1, source_target_pairs={{128,0},{256,128},{384,256},{129,1},{257,129},{385,257},{130,2},{2... | collective-permute-start | bytes 393224 | tf_op jit(solution)/shard_map/while/body/eval_jaxpr/ppermute | solution.py:15
  351.7 4.8 %copy-start.7 = (s32[64]{0:T(128)S(1)}, s32[64]{0:T(128)}, u32[]{:S(2)}) copy-start(s32[64]{0:T(128)} %fusion.12) | copy-start | bytes 772
  366.1 30.4 %all-to-all-start.2 = ((bf16[16,128,128]{2,1,0:T(8,128)(2,1)}), bf16[16,128,128]{2,1,0:T(8,128)(2,1)}, u32[]{:S(2)}, u32[]{:S(2)}) async-start(bf16[16,128,128]{2,1,0:T(8,128)(2,1)} %convert_element_type.116), calls=%async_computation.2 | async-start | bytes 1048576 | tf_op jit(solution)/shard_map/all_to_all | solution.py:210
  382.0 21.7 %copy-start.3 = (bf16[2304,256]{1,0:T(8,128)(2,1)S(1)}, bf16[2304,256]{1,0:T(8,128)(2,1)}, u32[]{:S(2)}) copy-start(bf16[2304,256]{1,0:T(8,128)(2,1)} %get-tuple-element.378) | copy-start | bytes 3538948
  396.6 26.3 %all-to-all-start.3 = ((bf16[16,128,128]{2,1,0:T(8,128)(2,1)}), bf16[16,128,128]{2,1,0:T(8,128)(2,1)S(1)}, u32[]{:S(2)}, u32[]{:S(2)}) async-start(bf16[16,128,128]{2,1,0:T(8,128)(2,1)} %convert_element_type.122), calls=%async_computation.3 | async-start | bytes 1048576 | tf_op jit(solution)/shard_map/all_to_all | solution.py:217
  422.8 0.8 copy-start.4
  423.6 42.0 %all-to-all-start.1 = ((bf16[16,128,256]{2,1,0:T(8,128)(2,1)}), bf16[16,128,256]{2,1,0:T(8,128)(2,1)S(1)}, u32[]{:S(2)}, u32[]{:S(2)}) async-start(bf16[16,128,256]{2,1,0:T(8,128)(2,1)} %bitcast.42), calls=%async_computation.1 | async-start | bytes 2097152 | tf_op jit(solution)/shard_map/all_to_all | solution.py:193

commit v13 on v6

--- a/solution.py
+++ b/solution.py
@@ -66,7 +66,7 @@
     query_rows = (head_input.astype(jnp.float32) * gain_row).astype(jnp.bfloat16)
     blocked_keys = head_keys.reshape(block_count, block_rows, local_kv, HEAD_FEATURES)
     blocked_values = head_values.reshape(block_count, block_rows, local_kv, HEAD_FEATURES)
-    per_turn = 4
+    per_turn = 2
     unit_count = block_count // per_turn
     turn_rows = per_turn * block_rows
     token_rows = turn_rows // ctx_count
@@ -179,11 +179,8 @@
     pick = (target_labels[None, :] == jnp.arange(block_count)[:, None]).astype(jnp.float32)
 
     def gathered(slots):
-        return jnp.dot(
-            pick,
-            slots.reshape(slot_count * listed, block_rows * slot_width),
-            precision=lax.Precision.HIGHEST,
-        )
+        pieces = slots.reshape(slot_count * listed, block_rows, slot_width)
+        return jnp.einsum("jb,brc->jrc", pick, pieces, precision=lax.Precision.HIGHEST)
 
     key_acc = gathered(key_slots)
     value_acc = gathered(value_slots)

time: 465 us -> 452 us (0.972)
  waiting for transfers between devices: 279 us -> 253 us
  other arithmetic: 25.8 us -> 34.5 us
  local copies, waits for them, and re-layouts: 73.4 us -> 67.4 us
    all_to_all x1, waiting for transfers between devices: 35.6 us -> 19.4 us  [shards(): lax.all_to_all(result_heads[:total_rows], 'ctx', split_axis=0, concat_axi...]
    all_to_all x1, waiting for transfers between devices: 24.7 us -> 11 us  [shards(): lax.all_to_all(key_acc.reshape(total_rows, slot_width).astype(jnp.bfloat1...]
    reshape x2 -> x0, local copies, waits for them, and re-layouts: 13.6 us -> none  [gathered(): slots.reshape(slot_count * listed, block_rows * slot_width)]
    all_to_all x1, waiting for transfers between devices: 10.2 us -> 18 us  [shards(): lax.all_to_all(value_acc.reshape(total_rows, slot_width).astype(jnp.bfloa...]
    gather x4 -> x8, local copies, waits for them, and re-layouts: 6.76 us -> 13.1 us  [attend(): blocked_keys[lists_now]]
    all_to_all x1, starting transfers between devices: 13.2 us -> 7.19 us  [shards(): lax.all_to_all(value_acc.reshape(total_rows, slot_width).astype(jnp.bfloa...]
    ppermute x7 -> x11, starting transfers between devices: 8.96 us -> 14.1 us  [passed_along(): return lax.ppermute(block, axis, route)]
    ppermute x7 -> x11, waiting for transfers between devices: 68.9 us -> 65.1 us  [passed_along(): return lax.ppermute(block, axis, route)]
  transfers between devices with their start and end apart: 11 -> 15, of which waited for: 11 -> 15; matrix products, arithmetic and copies ran while one was open for 6% -> 5% of each run, Pallas kernels for 0% -> 0%
where the time goes in v13:
time: 452 us; the launch traced here: 448 us
  waiting for transfers between devices  253 us (56%)
  local copies, waits for them, and re-layouts  67.4 us (15%)
  starting transfers between devices  55.7 us (12%)
  other arithmetic  34.5 us (8%)
  matrix products  24.9 us (6%)
  blocking collectives  10.9 us (2%)
    all_to_all x1, waiting for transfers between devices, shards(): lax.all_to_all(packed, 'ctx', split_axis=1, concat_axis=0, tiled=True)  139 us
    ppermute x11, waiting for transfers between devices, passed_along(): return lax.ppermute(block, axis, route)  65.1 us
    all_to_all x1, waiting for transfers between devices, shards(): lax.all_to_all(result_heads[:total_rows], 'ctx', split_axis=0, concat_axi...  19.4 us
    all_to_all x1, waiting for transfers between devices, shards(): lax.all_to_all(value_acc.reshape(total_rows, slot_width).astype(jnp.bfloa...  18 us
    all_to_all x1, starting transfers between devices, shards(): lax.all_to_all(packed, 'ctx', split_axis=1, concat_axis=0, tiled=True)  15.4 us
    ppermute x11, starting transfers between devices, passed_along(): return lax.ppermute(block, axis, route)  14.1 us
    gather x8, local copies, waits for them, and re-layouts, attend(): blocked_keys[lists_now]  13.1 us
    dot_general x2, matrix products, gathered(): jnp.einsum('jb,brc->jrc', pick, pieces, precision=lax.Precision.HIGHEST)  12.8 us
  transfers between devices with their start and end apart: 15, of which 15 were waited for; matrix products, arithmetic and copies ran while one was open for 5% of the time, Pallas kernels for 0%

profile of v13, /device:TPU:6, one launch (start us, length us, event | category | flops | bytes accessed | tf_op | source)
XLA Modules:
  0.0 448.5 jit_solution(13676503309987335867)
XLA Ops:
  5.0 1.5 copy.181
  7.5 1.9 pad_maximum_fusion
  9.3 15.4 %all-to-all-start = ((bf16[128,16,768]{2,0,1:T(8,128)(2,1)}), bf16[128,16,768]{2,0,1:T(8,128)(2,1)}, u32[]{:S(2)}, u32[]{:S(2)}) async-start(bf16[128,16,768]{2,0,1:T(8,128)(2,1)} %pad_maximum_fusion), calls=%async_computation | async-start | bytes 6291456 | tf_op jit(solution)/shard_map/all_to_all | solution.py:60
  24.9 139.2 %all-to-all-done = bf16[128,16,768]{2,0,1:T(8,128)(2,1)} async-done(((bf16[128,16,768]{2,0,1:T(8,128)(2,1)}), bf16[128,16,768]{2,0,1:T(8,128)(2,1)}, u32[]{:S(2)}, u32[]{:S(2)}) %all-to-all-start) | async-done | bytes 3145760 | tf_op jit(solution)/shard_map/all_to_all | solution.py:60
  164.2 3.0 fusion.29
  167.2 2.1 fusion.28
  169.3 2.4 multiply_convert_fusion.2
  171.7 2.6 broadcast_in_dim.34.clone
  174.3 2.7 broadcast_in_dim.34.clone2
  178.1 165.1 %while.24 = (s32[]{:T(128)}, bf16[256,256]{1,0:T(8,128)(2,1)S(1)}, bf16[2304,256]{1,0:T(8,128)(2,1)}, f32[18,512,128]{2,1,0:T(8,128)}, f32[18,512,128]{2,1,0:T(8...) while((s32[]{:T(128)}, bf16[256,256]{1,0:T(8,128)(2,1)S(1)}, ...), condition=%wide.region_7.8_spmd.clone, body=%wide.region_0.7_spmd.clone.sunk | while | flops 340590400 | bytes 19562376 | solution.py:172
  180.0 1.3 collective-permute-start
  181.5 1.1 constant_dynamic-update-slice_fusion.6
  182.6 4.2 collective-permute-done
  188.6 1.3 collective-permute-start
  190.1 1.1 constant_dynamic-update-slice_fusion.6
  191.2 4.2 collective-permute-done
  197.3 1.3 collective-permute-start
  198.8 1.1 constant_dynamic-update-slice_fusion.6
  199.9 21.4 %collective-permute-done = bf16[256,256]{1,0:T(8,128)(2,1)S(1)} collective-permute-done((bf16[256,256]{1,0:T(8,128)(2,1)S(1)}, bf16[256,256]{1,0:T(8,128)(2,1)S(1)}, u32[]{:S(2)}, u32[]{:S(2)}) %collective-permute-start) | collective-permute-done | bytes 131104 | tf_op jit(solution)/shard_map/while/body/eval_jaxpr/ppermute | solution.py:15
  222.2 6.6 %conditional.3 = (f32[256,256]{1,0:T(8,128)S(1)}, f32[2,512,128]{1,2,0:T(8,128)S(1)}, f32[2,512,128]{2,1,0:T(8,128)S(1)}, f32[256]{0:T(256)S(1)}) conditional(s32[]{:T(128)} %convert_element_type.157, () %tuple.85, (s32[]{:T(128)}, s32[16,4]{1,0:T(8,128)S(1)}, bf16[16,128,1,128]{3,1,0,2:T(8,128)(2,1)}, bf16[2048,256]{1,0:T(8,128)(2,1)}, ...), branch_computations={%region_1.1_spmd, %region_2.6_spmd} | conditional | flops 340131104 | bytes 14839144 | solution.py:148
  223.5 1.6 gather_fusion
  229.5 1.3 collective-permute-start
  231.1 1.1 constant_dynamic-update-slice_fusion.6
  232.2 4.2 collective-permute-done
  237.3 6.6 %conditional.3 = (f32[256,256]{1,0:T(8,128)S(1)}, f32[2,512,128]{1,2,0:T(8,128)S(1)}, f32[2,512,128]{2,1,0:T(8,128)S(1)}, f32[256]{0:T(256)S(1)}) conditional(s32[]{:T(128)} %convert_element_type.157, () %tuple.85, (s32[]{:T(128)}, s32[16,4]{1,0:T(8,128)S(1)}, bf16[16,128,1,128]{3,1,0,2:T(8,128)(2,1)}, bf16[2048,256]{1,0:T(8,128)(2,1)}, ...), branch_computations={%region_1.1_spmd, %region_2.6_spmd} | conditional | flops 340131104 | bytes 14839144 | solution.py:148
  238.6 1.6 gather_fusion
  244.7 1.3 collective-permute-start
  246.2 1.1 constant_dynamic-update-slice_fusion.6
  247.2 4.3 collective-permute-done
  252.4 6.6 %conditional.3 = (f32[256,256]{1,0:T(8,128)S(1)}, f32[2,512,128]{1,2,0:T(8,128)S(1)}, f32[2,512,128]{2,1,0:T(8,128)S(1)}, f32[256]{0:T(256)S(1)}) conditional(s32[]{:T(128)} %convert_element_type.157, () %tuple.85, (s32[]{:T(128)}, s32[16,4]{1,0:T(8,128)S(1)}, bf16[16,128,1,128]{3,1,0,2:T(8,128)(2,1)}, bf16[2048,256]{1,0:T(8,128)(2,1)}, ...), branch_computations={%region_1.1_spmd, %region_2.6_spmd} | conditional | flops 340131104 | bytes 14839144 | solution.py:148
  253.7 1.6 gather_fusion
  259.8 1.3 collective-permute-start
  262.3 4.3 collective-permute-done
  267.5 6.6 %conditional.3 = (f32[256,256]{1,0:T(8,128)S(1)}, f32[2,512,128]{1,2,0:T(8,128)S(1)}, f32[2,512,128]{2,1,0:T(8,128)S(1)}, f32[256]{0:T(256)S(1)}) conditional(s32[]{:T(128)} %convert_element_type.157, () %tuple.85, (s32[]{:T(128)}, s32[16,4]{1,0:T(8,128)S(1)}, bf16[16,128,1,128]{3,1,0,2:T(8,128)(2,1)}, bf16[2048,256]{1,0:T(8,128)(2,1)}, ...), branch_computations={%region_1.1_spmd, %region_2.6_spmd} | conditional | flops 340131104 | bytes 14839144 | solution.py:148
  268.8 1.6 gather_fusion
  274.8 1.3 collective-permute-start
  277.4 4.3 collective-permute-done
  282.6 6.6 %conditional.3 = (f32[256,256]{1,0:T(8,128)S(1)}, f32[2,512,128]{1,2,0:T(8,128)S(1)}, f32[2,512,128]{2,1,0:T(8,128)S(1)}, f32[256]{0:T(256)S(1)}) conditional(s32[]{:T(128)} %convert_element_type.157, () %tuple.85, (s32[]{:T(128)}, s32[16,4]{1,0:T(8,128)S(1)}, bf16[16,128,1,128]{3,1,0,2:T(8,128)(2,1)}, bf16[2048,256]{1,0:T(8,128)(2,1)}, ...), branch_computations={%region_1.1_spmd, %region_2.6_spmd} | conditional | flops 340131104 | bytes 14839144 | solution.py:148
  283.9 1.6 gather_fusion
  290.0 1.3 collective-permute-start
  292.5 4.3 collective-permute-done
  297.7 6.6 %conditional.3 = (f32[256,256]{1,0:T(8,128)S(1)}, f32[2,512,128]{1,2,0:T(8,128)S(1)}, f32[2,512,128]{2,1,0:T(8,128)S(1)}, f32[256]{0:T(256)S(1)}) conditional(s32[]{:T(128)} %convert_element_type.157, () %tuple.85, (s32[]{:T(128)}, s32[16,4]{1,0:T(8,128)S(1)}, bf16[16,128,1,128]{3,1,0,2:T(8,128)(2,1)}, bf16[2048,256]{1,0:T(8,128)(2,1)}, ...), branch_computations={%region_1.1_spmd, %region_2.6_spmd} | conditional | flops 340131104 | bytes 14839144 | solution.py:148
  299.0 1.6 gather_fusion
  305.1 1.3 collective-permute-start
  307.6 4.3 collective-permute-done
  312.9 6.6 %conditional.3 = (f32[256,256]{1,0:T(8,128)S(1)}, f32[2,512,128]{1,2,0:T(8,128)S(1)}, f32[2,512,128]{2,1,0:T(8,128)S(1)}, f32[256]{0:T(256)S(1)}) conditional(s32[]{:T(128)} %convert_element_type.157, () %tuple.85, (s32[]{:T(128)}, s32[16,4]{1,0:T(8,128)S(1)}, bf16[16,128,1,128]{3,1,0,2:T(8,128)(2,1)}, bf16[2048,256]{1,0:T(8,128)(2,1)}, ...), branch_computations={%region_1.1_spmd, %region_2.6_spmd} | conditional | flops 340131104 | bytes 14839144 | solution.py:148
  314.1 1.6 gather_fusion
  320.2 1.3 collective-permute-start
  321.7 1.1 constant_dynamic-update-slice_fusion.6
  322.8 5.4 %collective-permute-done = bf16[256,256]{1,0:T(8,128)(2,1)S(1)} collective-permute-done((bf16[256,256]{1,0:T(8,128)(2,1)S(1)}, bf16[256,256]{1,0:T(8,128)(2,1)S(1)}, u32[]{:S(2)}, u32[]{:S(2)}) %collective-permute-start) | collective-permute-done | bytes 131104 | tf_op jit(solution)/shard_map/while/body/eval_jaxpr/ppermute | solution.py:15
  329.1 6.6 %conditional.3 = (f32[256,256]{1,0:T(8,128)S(1)}, f32[2,512,128]{1,2,0:T(8,128)S(1)}, f32[2,512,128]{2,1,0:T(8,128)S(1)}, f32[256]{0:T(256)S(1)}) conditional(s32[]{:T(128)} %convert_element_type.157, () %tuple.85, (s32[]{:T(128)}, s32[16,4]{1,0:T(8,128)S(1)}, bf16[16,128,1,128]{3,1,0,2:T(8,128)(2,1)}, bf16[2048,256]{1,0:T(8,128)(2,1)}, ...), branch_computations={%region_1.1_spmd, %region_2.6_spmd} | conditional | flops 340131104 | bytes 14839144 | solution.py:148
  330.3 1.6 gather_fusion
  336.4 1.3 collective-permute-start
  338.9 4.3 collective-permute-done
  343.2 6.4 %fusion.16 = bf16[16,128,128]{2,0,1:T(8,128)(2,1)S(1)} fusion(f32[72,128,128]{2,1,0:T(8,128)} %bitcast.105, s32[72]{0:T(128)S(1)} %concatenate.7), kind=kOutput, calls=%fused_computation.41 | convolution fusion | flops 226755712 | bytes 5243168 | tf_op jit(solution)/shard_map/jb,brc->jrc/dot_general | solution.py:183
  350.6 8.3 %all-to-all-start.2 = ((bf16[16,128,128]{2,1,0:T(8,128)(2,1)}), bf16[16,128,128]{2,1,0:T(8,128)(2,1)S(1)}, u32[]{:S(2)}, u32[]{:S(2)}) async-start(bf16[16,128,128]{2,1,0:T(8,128)(2,1)} %copy.161), calls=%async_computation.2 | async-start | bytes 1048576 | tf_op jit(solution)/shard_map/all_to_all | solution.py:188
  358.8 6.4 %fusion.19 = bf16[16,128,128]{2,0,1:T(8,128)(2,1)S(1)} fusion(f32[72,128,128]{2,1,0:T(8,128)} %bitcast.106, s32[72]{0:T(128)S(1)} %concatenate.7), kind=kOutput, calls=%fused_computation.42 | convolution fusion | flops 226755712 | bytes 5243168 | tf_op jit(solution)/shard_map/jb,brc->jrc/dot_general | solution.py:183
  366.2 11.0 %all-to-all-done.2 = bf16[16,128,128]{2,1,0:T(8,128)(2,1)S(1)} async-done(((bf16[16,128,128]{2,1,0:T(8,128)(2,1)}), bf16[16,128,128]{2,1,0:T(8,128)(2,1)S(1)}, u32[]{:S(2)}, u32[]{:S(2)}) %all-to-all-start.2) | async-done | bytes 524320 | tf_op jit(solution)/shard_map/all_to_all | solution.py:188
  377.2 7.2 %all-to-all-start.3 = ((bf16[16,128,128]{2,1,0:T(8,128)(2,1)}), bf16[16,128,128]{2,1,0:T(8,128)(2,1)S(1)}, u32[]{:S(2)}, u32[]{:S(2)}) async-start(bf16[16,128,128]{2,1,0:T(8,128)(2,1)} %copy.164), calls=%async_computation.3 | async-start | bytes 1048576 | tf_op jit(solution)/shard_map/all_to_all | solution.py:195
  385.5 18.0 %all-to-all-done.3 = bf16[16,128,128]{2,1,0:T(8,128)(2,1)S(1)} async-done(((bf16[16,128,128]{2,1,0:T(8,128)(2,1)}), bf16[16,128,128]{2,1,0:T(8,128)(2,1)S(1)}, u32[]{:S(2)}, u32[]{:S(2)}) %all-to-all-start.3) | async-done | bytes 524320 | tf_op jit(solution)/shard_map/all_to_all | solution.py:195
  403.4 10.8 %all-to-all-start.1 = ((bf16[16,128,256]{2,1,0:T(8,128)(2,1)}), bf16[16,128,256]{2,1,0:T(8,128)(2,1)S(1)}, u32[]{:S(2)}, u32[]{:S(2)}) async-start(bf16[16,128,256]{2,1,0:T(8,128)(2,1)} %bitcast.36), calls=%async_computation.1 | async-start | bytes 2097152 | tf_op jit(solution)/shard_map/all_to_all | solution.py:174
  414.2 10.9 %psum.7 = f32[1,256]{1,0:T(1,128)} all-reduce(f32[1,256]{1,0:T(1,128)S(1)} %bitcast.123), channel_id=1, replica_groups=mesh['section'=4,'ctx'=16,'dp'=8] {'dp'}, use_global_device_ids=true, to_apply=%region_10.11 | all-reduce | flops 256 | bytes 2048 | tf_op jit(solution)/shard_map/psum | solution.py:215
  427.0 19.4 %all-to-all-done.1 = bf16[16,128,256]{2,1,0:T(8,128)(2,1)S(1)} async-done(((bf16[16,128,256]{2,1,0:T(8,128)(2,1)}), bf16[16,128,256]{2,1,0:T(8,128)(2,1)S(1)}, u32[]{:S(2)}, u32[]{:S(2)}) %all-to-all-start.1) | async-done | bytes 1048608 | tf_op jit(solution)/shard_map/all_to_all | solution.py:174
  447.1 1.3 copy.166
  (234 shorter events, 77.3 us)
Async XLA Ops:
  0.6 6.2 %copy-start.1 = (bf16[1,128,4096]{2,1,0:T(8,128)(2,1)S(1)}, bf16[1,128,4096]{2,1,0:T(8,128)(2,1)}, u32[]{:S(2)}) copy-start(bf16[1,128,4096]{2,1,0:T(8,128)(2,1)} %param.17) | copy-start | bytes 3145732
  9.3 15.4 %copy-start.3 = (s32[16,4]{0,1:T(4,128)S(1)}, s32[16,4]{0,1:T(4,128)}, u32[]{:S(2)}) copy-start(s32[16,4]{0,1:T(4,128)} %param.18) | copy-start | bytes 772
  9.3 154.8 %all-to-all-start = ((bf16[128,16,768]{2,0,1:T(8,128)(2,1)}), bf16[128,16,768]{2,0,1:T(8,128)(2,1)}, u32[]{:S(2)}, u32[]{:S(2)}) async-start(bf16[128,16,768]{2,0,1:T(8,128)(2,1)} %pad_maximum_fusion), calls=%async_computation | async-start | bytes 6291456 | tf_op jit(solution)/shard_map/all_to_all | solution.py:60
  24.7 144.6 %copy-start.2 = (f32[1,256]{1,0:T(1,128)S(1)}, f32[1,256]{1,0:T(1,128)}, u32[]{:S(2)}) copy-start(f32[1,256]{1,0:T(1,128)} %param.16) | copy-start | bytes 3076
  180.0 6.8 %collective-permute-start = (bf16[256,256]{1,0:T(8,128)(2,1)S(1)}, bf16[256,256]{1,0:T(8,128)(2,1)S(1)}, u32[]{:S(2)}, u32[]{:S(2)}) collective-permute-start(bf16[256,256]{1,0:T(8,128)(2,1)S(1)} %get-tuple-element.723), channel_id=1, source_target_pairs={{128,0},{256,128},{384,256},{129,1},{257,129},{385,257},{130,2},{2... | collective-permute-start | bytes 393224 | tf_op jit(solution)/shard_map/while/body/eval_jaxpr/ppermute | solution.py:15
  188.6 6.8 %collective-permute-start = (bf16[256,256]{1,0:T(8,128)(2,1)S(1)}, bf16[256,256]{1,0:T(8,128)(2,1)S(1)}, u32[]{:S(2)}, u32[]{:S(2)}) collective-permute-start(bf16[256,256]{1,0:T(8,128)(2,1)S(1)} %get-tuple-element.723), channel_id=1, source_target_pairs={{128,0},{256,128},{384,256},{129,1},{257,129},{385,257},{130,2},{2... | collective-permute-start | bytes 393224 | tf_op jit(solution)/shard_map/while/body/eval_jaxpr/ppermute | solution.py:15
  197.3 24.0 %collective-permute-start = (bf16[256,256]{1,0:T(8,128)(2,1)S(1)}, bf16[256,256]{1,0:T(8,128)(2,1)S(1)}, u32[]{:S(2)}, u32[]{:S(2)}) collective-permute-start(bf16[256,256]{1,0:T(8,128)(2,1)S(1)} %get-tuple-element.723), channel_id=1, source_target_pairs={{128,0},{256,128},{384,256},{129,1},{257,129},{385,257},{130,2},{2... | collective-permute-start | bytes 393224 | tf_op jit(solution)/shard_map/while/body/eval_jaxpr/ppermute | solution.py:15
  229.5 6.8 %collective-permute-start = (bf16[256,256]{1,0:T(8,128)(2,1)S(1)}, bf16[256,256]{1,0:T(8,128)(2,1)S(1)}, u32[]{:S(2)}, u32[]{:S(2)}) collective-permute-start(bf16[256,256]{1,0:T(8,128)(2,1)S(1)} %get-tuple-element.723), channel_id=1, source_target_pairs={{128,0},{256,128},{384,256},{129,1},{257,129},{385,257},{130,2},{2... | collective-permute-start | bytes 393224 | tf_op jit(solution)/shard_map/while/body/eval_jaxpr/ppermute | solution.py:15
  244.7 6.8 %collective-permute-start = (bf16[256,256]{1,0:T(8,128)(2,1)S(1)}, bf16[256,256]{1,0:T(8,128)(2,1)S(1)}, u32[]{:S(2)}, u32[]{:S(2)}) collective-permute-start(bf16[256,256]{1,0:T(8,128)(2,1)S(1)} %get-tuple-element.723), channel_id=1, source_target_pairs={{128,0},{256,128},{384,256},{129,1},{257,129},{385,257},{130,2},{2... | collective-permute-start | bytes 393224 | tf_op jit(solution)/shard_map/while/body/eval_jaxpr/ppermute | solution.py:15
  259.8 6.8 %collective-permute-start = (bf16[256,256]{1,0:T(8,128)(2,1)S(1)}, bf16[256,256]{1,0:T(8,128)(2,1)S(1)}, u32[]{:S(2)}, u32[]{:S(2)}) collective-permute-start(bf16[256,256]{1,0:T(8,128)(2,1)S(1)} %get-tuple-element.723), channel_id=1, source_target_pairs={{128,0},{256,128},{384,256},{129,1},{257,129},{385,257},{130,2},{2... | collective-permute-start | bytes 393224 | tf_op jit(solution)/shard_map/while/body/eval_jaxpr/ppermute | solution.py:15
  274.8 6.8 %collective-permute-start = (bf16[256,256]{1,0:T(8,128)(2,1)S(1)}, bf16[256,256]{1,0:T(8,128)(2,1)S(1)}, u32[]{:S(2)}, u32[]{:S(2)}) collective-permute-start(bf16[256,256]{1,0:T(8,128)(2,1)S(1)} %get-tuple-element.723), channel_id=1, source_target_pairs={{128,0},{256,128},{384,256},{129,1},{257,129},{385,257},{130,2},{2... | collective-permute-start | bytes 393224 | tf_op jit(solution)/shard_map/while/body/eval_jaxpr/ppermute | solution.py:15
  290.0 6.8 %collective-permute-start = (bf16[256,256]{1,0:T(8,128)(2,1)S(1)}, bf16[256,256]{1,0:T(8,128)(2,1)S(1)}, u32[]{:S(2)}, u32[]{:S(2)}) collective-permute-start(bf16[256,256]{1,0:T(8,128)(2,1)S(1)} %get-tuple-element.723), channel_id=1, source_target_pairs={{128,0},{256,128},{384,256},{129,1},{257,129},{385,257},{130,2},{2... | collective-permute-start | bytes 393224 | tf_op jit(solution)/shard_map/while/body/eval_jaxpr/ppermute | solution.py:15
  305.1 6.8 %collective-permute-start = (bf16[256,256]{1,0:T(8,128)(2,1)S(1)}, bf16[256,256]{1,0:T(8,128)(2,1)S(1)}, u32[]{:S(2)}, u32[]{:S(2)}) collective-permute-start(bf16[256,256]{1,0:T(8,128)(2,1)S(1)} %get-tuple-element.723), channel_id=1, source_target_pairs={{128,0},{256,128},{384,256},{129,1},{257,129},{385,257},{130,2},{2... | collective-permute-start | bytes 393224 | tf_op jit(solution)/shard_map/while/body/eval_jaxpr/ppermute | solution.py:15
  320.2 8.0 %collective-permute-start = (bf16[256,256]{1,0:T(8,128)(2,1)S(1)}, bf16[256,256]{1,0:T(8,128)(2,1)S(1)}, u32[]{:S(2)}, u32[]{:S(2)}) collective-permute-start(bf16[256,256]{1,0:T(8,128)(2,1)S(1)} %get-tuple-element.723), channel_id=1, source_target_pairs={{128,0},{256,128},{384,256},{129,1},{257,129},{385,257},{130,2},{2... | collective-permute-start | bytes 393224 | tf_op jit(solution)/shard_map/while/body/eval_jaxpr/ppermute | solution.py:15
  336.4 6.8 %collective-permute-start = (bf16[256,256]{1,0:T(8,128)(2,1)S(1)}, bf16[256,256]{1,0:T(8,128)(2,1)S(1)}, u32[]{:S(2)}, u32[]{:S(2)}) collective-permute-start(bf16[256,256]{1,0:T(8,128)(2,1)S(1)} %get-tuple-element.723), channel_id=1, source_target_pairs={{128,0},{256,128},{384,256},{129,1},{257,129},{385,257},{130,2},{2... | collective-permute-start | bytes 393224 | tf_op jit(solution)/shard_map/while/body/eval_jaxpr/ppermute | solution.py:15
  349.6 34.8 %copy-start = (bf16[2304,256]{1,0:T(8,128)(2,1)S(1)}, bf16[2304,256]{1,0:T(8,128)(2,1)}, u32[]{:S(2)}) copy-start(bf16[2304,256]{1,0:T(8,128)(2,1)} %get-tuple-element.378) | copy-start | bytes 3538948
  350.6 26.6 %all-to-all-start.2 = ((bf16[16,128,128]{2,1,0:T(8,128)(2,1)}), bf16[16,128,128]{2,1,0:T(8,128)(2,1)S(1)}, u32[]{:S(2)}, u32[]{:S(2)}) async-start(bf16[16,128,128]{2,1,0:T(8,128)(2,1)} %copy.161), calls=%async_computation.2 | async-start | bytes 1048576 | tf_op jit(solution)/shard_map/all_to_all | solution.py:188
  377.2 26.2 %all-to-all-start.3 = ((bf16[16,128,128]{2,1,0:T(8,128)(2,1)}), bf16[16,128,128]{2,1,0:T(8,128)(2,1)S(1)}, u32[]{:S(2)}, u32[]{:S(2)}) async-start(bf16[16,128,128]{2,1,0:T(8,128)(2,1)} %copy.164), calls=%async_computation.3 | async-start | bytes 1048576 | tf_op jit(solution)/shard_map/all_to_all | solution.py:195
  403.4 43.0 %all-to-all-start.1 = ((bf16[16,128,256]{2,1,0:T(8,128)(2,1)}), bf16[16,128,256]{2,1,0:T(8,128)(2,1)S(1)}, u32[]{:S(2)}, u32[]{:S(2)}) async-start(bf16[16,128,256]{2,1,0:T(8,128)(2,1)} %bitcast.36), calls=%async_computation.1 | async-start | bytes 2097152 | tf_op jit(solution)/shard_map/all_to_all | solution.py:174

commit v14 on v13

--- a/solution.py
+++ b/solution.py
@@ -184,22 +184,21 @@
 
     key_acc = gathered(key_slots)
     value_acc = gathered(value_slots)
-    key_back, value_back = (
-        lax.all_to_all(
-            key_acc.reshape(total_rows, slot_width).astype(jnp.bfloat16),
-            "ctx",
-            split_axis=0,
-            concat_axis=1,
-            tiled=True,
-        ).astype(jnp.float32),
-        lax.all_to_all(
-            value_acc.reshape(total_rows, slot_width).astype(jnp.bfloat16),
-            "ctx",
-            split_axis=0,
-            concat_axis=1,
-            tiled=True,
-        ).astype(jnp.float32),
-    )
+    kv_back = lax.all_to_all(
+        jnp.concatenate(
+            [
+                key_acc.reshape(total_rows, slot_width),
+                value_acc.reshape(total_rows, slot_width),
+            ],
+            axis=1,
+        ).astype(jnp.bfloat16),
+        "ctx",
+        split_axis=0,
+        concat_axis=1,
+        tiled=True,
+    ).astype(jnp.float32).reshape(tok_local, ctx_count, 2, slot_width)
+    key_back = kv_back[:, :, 0].reshape(tok_local, ctx_count * slot_width)
+    value_back = kv_back[:, :, 1].reshape(tok_local, ctx_count * slot_width)
     key_out = (
         key_back.reshape(tok_local, kv_heads, repeats, HEAD_FEATURES)
         .sum(axis=2)

time: 452 us -> 454 us (level)
  starting transfers between devices: 55.7 us -> 46.5 us
  waiting for transfers between devices: 253 us -> 261 us
    all_to_all x2 -> x1, waiting for transfers between devices: 29 us -> 36.9 us  [shards(): lax.all_to_all(jnp.concatenate([key_acc.reshape(total_rows, slot_width),...]
    all_to_all x2 -> x1, starting transfers between devices: 15.4 us -> 8.19 us  [shards(): lax.all_to_all(jnp.concatenate([key_acc.reshape(total_rows, slot_width),...]
  transfers between devices with their start and end apart: 15 -> 14, of which waited for: 15 -> 14; matrix products, arithmetic and copies ran while one was open for 5% -> 6% of each run, Pallas kernels for 0% -> 0%
where the time goes in v14:
time: 454 us; the launch traced here: 451 us
  waiting for transfers between devices  261 us (57%)
  local copies, waits for them, and re-layouts  69.9 us (15%)
  starting transfers between devices  46.5 us (10%)
  other arithmetic  37.3 us (8%)
  matrix products  23 us (5%)
  blocking collectives  11.1 us (2%)
    all_to_all x1, waiting for transfers between devices, shards(): lax.all_to_all(packed, 'ctx', split_axis=1, concat_axis=0, tiled=True)  139 us
    ppermute x11, waiting for transfers between devices, passed_along(): return lax.ppermute(block, axis, route)  65.1 us
    all_to_all x1, waiting for transfers between devices, shards(): lax.all_to_all(jnp.concatenate([key_acc.reshape(total_rows, slot_width),...  36.9 us
    all_to_all x1, waiting for transfers between devices, shards(): lax.all_to_all(result_heads[:total_rows], 'ctx', split_axis=0, concat_axi...  19.6 us
    all_to_all x1, starting transfers between devices, shards(): lax.all_to_all(packed, 'ctx', split_axis=1, concat_axis=0, tiled=True)  15.3 us
    ppermute x11, starting transfers between devices, passed_along(): return lax.ppermute(block, axis, route)  14.1 us
    gather x8, local copies, waits for them, and re-layouts, attend(): blocked_keys[lists_now]  13.1 us
    dynamic_update_slice x11, local copies, waits for them, and re-layouts, turn_step(): lax.dynamic_update_slice_in_dim(value_slots, value_part, target * per_tur...  11.9 us
  transfers between devices with their start and end apart: 14, of which 14 were waited for; matrix products, arithmetic and copies ran while one was open for 6% of the time, Pallas kernels for 0%

profile of v14, /device:TPU:6, one launch (start us, length us, event | category | flops | bytes accessed | tf_op | source)
XLA Modules:
  0.0 450.8 jit_solution(13599828017014279701)
XLA Ops:
  5.0 1.5 copy.179
  7.5 1.8 pad_maximum_fusion
  9.3 15.3 %all-to-all-start = ((bf16[128,16,768]{2,0,1:T(8,128)(2,1)}), bf16[128,16,768]{2,0,1:T(8,128)(2,1)S(1)}, u32[]{:S(2)}, u32[]{:S(2)}) async-start(bf16[128,16,768]{2,0,1:T(8,128)(2,1)} %pad_maximum_fusion), calls=%async_computation | async-start | bytes 6291456 | tf_op jit(solution)/shard_map/all_to_all | solution.py:60
  24.9 139.2 %all-to-all-done = bf16[128,16,768]{2,0,1:T(8,128)(2,1)S(1)} async-done(((bf16[128,16,768]{2,0,1:T(8,128)(2,1)}), bf16[128,16,768]{2,0,1:T(8,128)(2,1)S(1)}, u32[]{:S(2)}, u32[]{:S(2)}) %all-to-all-start) | async-done | bytes 3145760 | tf_op jit(solution)/shard_map/all_to_all | solution.py:60
  164.0 1.1 fusion.29
  165.1 1.2 fusion.28
  166.3 1.2 multiply_convert_fusion.2
  167.6 2.6 broadcast_in_dim.34.clone
  170.2 2.7 broadcast_in_dim.34.clone2
  174.0 165.1 %while.24 = (s32[]{:T(128)}, bf16[256,256]{1,0:T(8,128)(2,1)S(1)}, bf16[2304,256]{1,0:T(8,128)(2,1)}, f32[18,512,128]{2,1,0:T(8,128)}, f32[18,512,128]{2,1,0:T(8...) while((s32[]{:T(128)}, bf16[256,256]{1,0:T(8,128)(2,1)S(1)}, ...), condition=%wide.region_7.8_spmd.clone, body=%wide.region_0.7_spmd.clone.sunk | while | flops 340590400 | bytes 19562376 | solution.py:172
  175.8 1.3 collective-permute-start
  178.4 4.2 collective-permute-done
  184.4 1.3 collective-permute-start
  187.0 4.2 collective-permute-done
  193.1 1.3 collective-permute-start
  195.7 21.4 %collective-permute-done = bf16[256,256]{1,0:T(8,128)(2,1)S(1)} collective-permute-done((bf16[256,256]{1,0:T(8,128)(2,1)S(1)}, bf16[256,256]{1,0:T(8,128)(2,1)S(1)}, u32[]{:S(2)}, u32[]{:S(2)}) %collective-permute-start) | collective-permute-done | bytes 131104 | tf_op jit(solution)/shard_map/while/body/eval_jaxpr/ppermute | solution.py:15
  218.0 6.6 %conditional.3 = (f32[256,256]{1,0:T(8,128)S(1)}, f32[2,512,128]{1,2,0:T(8,128)S(1)}, f32[2,512,128]{2,1,0:T(8,128)S(1)}, f32[256]{0:T(256)S(1)}) conditional(s32[]{:T(128)} %convert_element_type.137, () %tuple.86, (s32[]{:T(128)}, s32[16,4]{1,0:T(8,128)S(1)}, bf16[16,128,1,128]{3,1,0,2:T(8,128)(2,1)}, bf16[2048,256]{1,0:T(8,128)(2,1)}, ...), branch_computations={%region_1.1_spmd, %region_2.6_spmd} | conditional | flops 340131104 | bytes 14839144 | solution.py:148
  219.3 1.6 gather_fusion
  225.3 1.3 collective-permute-start
  227.9 4.3 collective-permute-done
  233.1 6.6 %conditional.3 = (f32[256,256]{1,0:T(8,128)S(1)}, f32[2,512,128]{1,2,0:T(8,128)S(1)}, f32[2,512,128]{2,1,0:T(8,128)S(1)}, f32[256]{0:T(256)S(1)}) conditional(s32[]{:T(128)} %convert_element_type.137, () %tuple.86, (s32[]{:T(128)}, s32[16,4]{1,0:T(8,128)S(1)}, bf16[16,128,1,128]{3,1,0,2:T(8,128)(2,1)}, bf16[2048,256]{1,0:T(8,128)(2,1)}, ...), branch_computations={%region_1.1_spmd, %region_2.6_spmd} | conditional | flops 340131104 | bytes 14839144 | solution.py:148
  234.4 1.6 gather_fusion
  240.4 1.3 collective-permute-start
  243.0 4.3 collective-permute-done
  248.2 6.6 %conditional.3 = (f32[256,256]{1,0:T(8,128)S(1)}, f32[2,512,128]{1,2,0:T(8,128)S(1)}, f32[2,512,128]{2,1,0:T(8,128)S(1)}, f32[256]{0:T(256)S(1)}) conditional(s32[]{:T(128)} %convert_element_type.137, () %tuple.86, (s32[]{:T(128)}, s32[16,4]{1,0:T(8,128)S(1)}, bf16[16,128,1,128]{3,1,0,2:T(8,128)(2,1)}, bf16[2048,256]{1,0:T(8,128)(2,1)}, ...), branch_computations={%region_1.1_spmd, %region_2.6_spmd} | conditional | flops 340131104 | bytes 14839144 | solution.py:148
  249.5 1.6 gather_fusion
  255.5 1.3 collective-permute-start
  258.1 4.3 collective-permute-done
  263.3 6.6 %conditional.3 = (f32[256,256]{1,0:T(8,128)S(1)}, f32[2,512,128]{1,2,0:T(8,128)S(1)}, f32[2,512,128]{2,1,0:T(8,128)S(1)}, f32[256]{0:T(256)S(1)}) conditional(s32[]{:T(128)} %convert_element_type.137, () %tuple.86, (s32[]{:T(128)}, s32[16,4]{1,0:T(8,128)S(1)}, bf16[16,128,1,128]{3,1,0,2:T(8,128)(2,1)}, bf16[2048,256]{1,0:T(8,128)(2,1)}, ...), branch_computations={%region_1.1_spmd, %region_2.6_spmd} | conditional | flops 340131104 | bytes 14839144 | solution.py:148
  264.6 1.6 gather_fusion
  270.6 1.3 collective-permute-start
  272.2 1.1 constant_dynamic-update-slice_fusion.6
  273.3 4.2 collective-permute-done
  278.4 6.6 %conditional.3 = (f32[256,256]{1,0:T(8,128)S(1)}, f32[2,512,128]{1,2,0:T(8,128)S(1)}, f32[2,512,128]{2,1,0:T(8,128)S(1)}, f32[256]{0:T(256)S(1)}) conditional(s32[]{:T(128)} %convert_element_type.137, () %tuple.86, (s32[]{:T(128)}, s32[16,4]{1,0:T(8,128)S(1)}, bf16[16,128,1,128]{3,1,0,2:T(8,128)(2,1)}, bf16[2048,256]{1,0:T(8,128)(2,1)}, ...), branch_computations={%region_1.1_spmd, %region_2.6_spmd} | conditional | flops 340131104 | bytes 14839144 | solution.py:148
  279.7 1.6 gather_fusion
  285.7 1.3 collective-permute-start
  288.3 4.3 collective-permute-done
  293.5 6.6 %conditional.3 = (f32[256,256]{1,0:T(8,128)S(1)}, f32[2,512,128]{1,2,0:T(8,128)S(1)}, f32[2,512,128]{2,1,0:T(8,128)S(1)}, f32[256]{0:T(256)S(1)}) conditional(s32[]{:T(128)} %convert_element_type.137, () %tuple.86, (s32[]{:T(128)}, s32[16,4]{1,0:T(8,128)S(1)}, bf16[16,128,1,128]{3,1,0,2:T(8,128)(2,1)}, bf16[2048,256]{1,0:T(8,128)(2,1)}, ...), branch_computations={%region_1.1_spmd, %region_2.6_spmd} | conditional | flops 340131104 | bytes 14839144 | solution.py:148
  294.8 1.6 gather_fusion
  300.8 1.3 collective-permute-start
  303.4 4.3 collective-permute-done
  308.6 6.6 %conditional.3 = (f32[256,256]{1,0:T(8,128)S(1)}, f32[2,512,128]{1,2,0:T(8,128)S(1)}, f32[2,512,128]{2,1,0:T(8,128)S(1)}, f32[256]{0:T(256)S(1)}) conditional(s32[]{:T(128)} %convert_element_type.137, () %tuple.86, (s32[]{:T(128)}, s32[16,4]{1,0:T(8,128)S(1)}, bf16[16,128,1,128]{3,1,0,2:T(8,128)(2,1)}, bf16[2048,256]{1,0:T(8,128)(2,1)}, ...), branch_computations={%region_1.1_spmd, %region_2.6_spmd} | conditional | flops 340131104 | bytes 14839144 | solution.py:148
  309.9 1.6 gather_fusion
  315.9 1.3 collective-permute-start
  317.5 1.1 constant_dynamic-update-slice_fusion.6
  318.6 5.4 %collective-permute-done = bf16[256,256]{1,0:T(8,128)(2,1)S(1)} collective-permute-done((bf16[256,256]{1,0:T(8,128)(2,1)S(1)}, bf16[256,256]{1,0:T(8,128)(2,1)S(1)}, u32[]{:S(2)}, u32[]{:S(2)}) %collective-permute-start) | collective-permute-done | bytes 131104 | tf_op jit(solution)/shard_map/while/body/eval_jaxpr/ppermute | solution.py:15
  324.9 6.6 %conditional.3 = (f32[256,256]{1,0:T(8,128)S(1)}, f32[2,512,128]{1,2,0:T(8,128)S(1)}, f32[2,512,128]{2,1,0:T(8,128)S(1)}, f32[256]{0:T(256)S(1)}) conditional(s32[]{:T(128)} %convert_element_type.137, () %tuple.86, (s32[]{:T(128)}, s32[16,4]{1,0:T(8,128)S(1)}, bf16[16,128,1,128]{3,1,0,2:T(8,128)(2,1)}, bf16[2048,256]{1,0:T(8,128)(2,1)}, ...), branch_computations={%region_1.1_spmd, %region_2.6_spmd} | conditional | flops 340131104 | bytes 14839144 | solution.py:148
  326.1 1.6 gather_fusion
  332.2 1.3 collective-permute-start
  334.8 4.3 collective-permute-done
  339.0 6.6 %fusion.16 = bf16[16,128,128]{2,0,1:T(8,128)(2,1)S(1)} fusion(f32[72,128,128]{2,1,0:T(8,128)} %bitcast.103, s32[72]{0:T(128)S(1)} %concatenate.12), kind=kOutput, calls=%fused_computation.42 | convolution fusion | flops 226755712 | bytes 5243168 | tf_op jit(solution)/shard_map/jb,brc->jrc/dot_general | solution.py:183
  345.6 4.3 fusion.19
  350.1 1.3 copy.159
  351.4 8.2 %all-to-all-start.2 = ((bf16[16,128,256]{2,1,0:T(8,128)(2,1)}), bf16[16,128,256]{2,1,0:T(8,128)(2,1)S(1)}, u32[]{:S(2)}, u32[]{:S(2)}) async-start(bf16[16,128,256]{2,1,0:T(8,128)(2,1)} %copy.159), calls=%async_computation.2 | async-start | bytes 2097152 | tf_op jit(solution)/shard_map/all_to_all | solution.py:187
  360.6 36.9 %all-to-all-done.2 = bf16[16,128,256]{2,1,0:T(8,128)(2,1)S(1)} async-done(((bf16[16,128,256]{2,1,0:T(8,128)(2,1)}), bf16[16,128,256]{2,1,0:T(8,128)(2,1)S(1)}, u32[]{:S(2)}, u32[]{:S(2)}) %all-to-all-start.2) | async-done | bytes 1048608 | tf_op jit(solution)/shard_map/all_to_all | solution.py:187
  397.5 8.9 %all-to-all-start.1 = ((bf16[16,128,256]{2,1,0:T(8,128)(2,1)}), bf16[16,128,256]{2,1,0:T(8,128)(2,1)S(1)}, u32[]{:S(2)}, u32[]{:S(2)}) async-start(bf16[16,128,256]{2,1,0:T(8,128)(2,1)} %bitcast.36), calls=%async_computation.1 | async-start | bytes 2097152 | tf_op jit(solution)/shard_map/all_to_all | solution.py:174
  406.4 11.1 %psum.7 = f32[1,256]{1,0:T(1,128)} all-reduce(f32[1,256]{1,0:T(1,128)S(1)} %bitcast.125), channel_id=1, replica_groups=mesh['section'=4,'ctx'=16,'dp'=8] {'dp'}, use_global_device_ids=true, to_apply=%region_10.11 | all-reduce | flops 256 | bytes 2048 | tf_op jit(solution)/shard_map/psum | solution.py:214
  417.5 1.5 convert_bitcast_fusion
  419.0 2.3 reshape.141
  421.3 3.6 fusion.30
  424.9 1.3 reduce_sum.45
  427.1 1.3 reduce_sum.46
  429.3 19.6 %all-to-all-done.1 = bf16[16,128,256]{2,1,0:T(8,128)(2,1)S(1)} async-done(((bf16[16,128,256]{2,1,0:T(8,128)(2,1)}), bf16[16,128,256]{2,1,0:T(8,128)(2,1)S(1)}, u32[]{:S(2)}, u32[]{:S(2)}) %all-to-all-start.1) | async-done | bytes 1048608 | tf_op jit(solution)/shard_map/all_to_all | solution.py:174
  449.5 1.3 copy.162
  (241 shorter events, 79.8 us)
Async XLA Ops:
  0.6 6.2 %copy-start.4 = (bf16[1,128,4096]{2,1,0:T(8,128)(2,1)S(1)}, bf16[1,128,4096]{2,1,0:T(8,128)(2,1)}, u32[]{:S(2)}) copy-start(bf16[1,128,4096]{2,1,0:T(8,128)(2,1)} %param.17) | copy-start | bytes 3145732
  9.3 15.4 %copy-start.6 = (s32[16,4]{0,1:T(4,128)S(1)}, s32[16,4]{0,1:T(4,128)}, u32[]{:S(2)}) copy-start(s32[16,4]{0,1:T(4,128)} %param.18) | copy-start | bytes 772
  9.3 154.7 %all-to-all-start = ((bf16[128,16,768]{2,0,1:T(8,128)(2,1)}), bf16[128,16,768]{2,0,1:T(8,128)(2,1)S(1)}, u32[]{:S(2)}, u32[]{:S(2)}) async-start(bf16[128,16,768]{2,0,1:T(8,128)(2,1)} %pad_maximum_fusion), calls=%async_computation | async-start | bytes 6291456 | tf_op jit(solution)/shard_map/all_to_all | solution.py:60
  24.6 141.7 %copy-start.5 = (f32[1,256]{1,0:T(1,128)S(1)}, f32[1,256]{1,0:T(1,128)}, u32[]{:S(2)}) copy-start(f32[1,256]{1,0:T(1,128)} %param.16) | copy-start | bytes 3076
  165.1 7.7 %copy-start.1 = (bf16[2048,256]{1,0:T(8,128)(2,1)}, bf16[2048,256]{1,0:T(8,128)(2,1)S(1)}, u32[]{:S(2)}) copy-start(bf16[2048,256]{1,0:T(8,128)(2,1)S(1)} %get-tuple-element.754) | copy-start | bytes 3145732
  167.5 6.4 %copy-start.2 = (bf16[2048,128]{1,0:T(8,128)(2,1)S(1)}, bf16[2048,128]{1,0:T(8,128)(2,1)}, u32[]{:S(2)}) copy-start(bf16[2048,128]{1,0:T(8,128)(2,1)} %get-tuple-element.377) | copy-start | bytes 1572868
  175.8 6.8 %collective-permute-start = (bf16[256,256]{1,0:T(8,128)(2,1)S(1)}, bf16[256,256]{1,0:T(8,128)(2,1)S(1)}, u32[]{:S(2)}, u32[]{:S(2)}) collective-permute-start(bf16[256,256]{1,0:T(8,128)(2,1)S(1)} %get-tuple-element.725), channel_id=1, source_target_pairs={{128,0},{256,128},{384,256},{129,1},{257,129},{385,257},{130,2},{2... | collective-permute-start | bytes 393224 | tf_op jit(solution)/shard_map/while/body/eval_jaxpr/ppermute | solution.py:15
  184.4 6.8 %collective-permute-start = (bf16[256,256]{1,0:T(8,128)(2,1)S(1)}, bf16[256,256]{1,0:T(8,128)(2,1)S(1)}, u32[]{:S(2)}, u32[]{:S(2)}) collective-permute-start(bf16[256,256]{1,0:T(8,128)(2,1)S(1)} %get-tuple-element.725), channel_id=1, source_target_pairs={{128,0},{256,128},{384,256},{129,1},{257,129},{385,257},{130,2},{2... | collective-permute-start | bytes 393224 | tf_op jit(solution)/shard_map/while/body/eval_jaxpr/ppermute | solution.py:15
  193.1 24.0 %collective-permute-start = (bf16[256,256]{1,0:T(8,128)(2,1)S(1)}, bf16[256,256]{1,0:T(8,128)(2,1)S(1)}, u32[]{:S(2)}, u32[]{:S(2)}) collective-permute-start(bf16[256,256]{1,0:T(8,128)(2,1)S(1)} %get-tuple-element.725), channel_id=1, source_target_pairs={{128,0},{256,128},{384,256},{129,1},{257,129},{385,257},{130,2},{2... | collective-permute-start | bytes 393224 | tf_op jit(solution)/shard_map/while/body/eval_jaxpr/ppermute | solution.py:15
  225.3 6.8 %collective-permute-start = (bf16[256,256]{1,0:T(8,128)(2,1)S(1)}, bf16[256,256]{1,0:T(8,128)(2,1)S(1)}, u32[]{:S(2)}, u32[]{:S(2)}) collective-permute-start(bf16[256,256]{1,0:T(8,128)(2,1)S(1)} %get-tuple-element.725), channel_id=1, source_target_pairs={{128,0},{256,128},{384,256},{129,1},{257,129},{385,257},{130,2},{2... | collective-permute-start | bytes 393224 | tf_op jit(solution)/shard_map/while/body/eval_jaxpr/ppermute | solution.py:15
  240.4 6.8 %collective-permute-start = (bf16[256,256]{1,0:T(8,128)(2,1)S(1)}, bf16[256,256]{1,0:T(8,128)(2,1)S(1)}, u32[]{:S(2)}, u32[]{:S(2)}) collective-permute-start(bf16[256,256]{1,0:T(8,128)(2,1)S(1)} %get-tuple-element.725), channel_id=1, source_target_pairs={{128,0},{256,128},{384,256},{129,1},{257,129},{385,257},{130,2},{2... | collective-permute-start | bytes 393224 | tf_op jit(solution)/shard_map/while/body/eval_jaxpr/ppermute | solution.py:15
  255.5 6.8 %collective-permute-start = (bf16[256,256]{1,0:T(8,128)(2,1)S(1)}, bf16[256,256]{1,0:T(8,128)(2,1)S(1)}, u32[]{:S(2)}, u32[]{:S(2)}) collective-permute-start(bf16[256,256]{1,0:T(8,128)(2,1)S(1)} %get-tuple-element.725), channel_id=1, source_target_pairs={{128,0},{256,128},{384,256},{129,1},{257,129},{385,257},{130,2},{2... | collective-permute-start | bytes 393224 | tf_op jit(solution)/shard_map/while/body/eval_jaxpr/ppermute | solution.py:15
  270.6 6.8 %collective-permute-start = (bf16[256,256]{1,0:T(8,128)(2,1)S(1)}, bf16[256,256]{1,0:T(8,128)(2,1)S(1)}, u32[]{:S(2)}, u32[]{:S(2)}) collective-permute-start(bf16[256,256]{1,0:T(8,128)(2,1)S(1)} %get-tuple-element.725), channel_id=1, source_target_pairs={{128,0},{256,128},{384,256},{129,1},{257,129},{385,257},{130,2},{2... | collective-permute-start | bytes 393224 | tf_op jit(solution)/shard_map/while/body/eval_jaxpr/ppermute | solution.py:15
  285.7 6.8 %collective-permute-start = (bf16[256,256]{1,0:T(8,128)(2,1)S(1)}, bf16[256,256]{1,0:T(8,128)(2,1)S(1)}, u32[]{:S(2)}, u32[]{:S(2)}) collective-permute-start(bf16[256,256]{1,0:T(8,128)(2,1)S(1)} %get-tuple-element.725), channel_id=1, source_target_pairs={{128,0},{256,128},{384,256},{129,1},{257,129},{385,257},{130,2},{2... | collective-permute-start | bytes 393224 | tf_op jit(solution)/shard_map/while/body/eval_jaxpr/ppermute | solution.py:15
  300.8 6.8 %collective-permute-start = (bf16[256,256]{1,0:T(8,128)(2,1)S(1)}, bf16[256,256]{1,0:T(8,128)(2,1)S(1)}, u32[]{:S(2)}, u32[]{:S(2)}) collective-permute-start(bf16[256,256]{1,0:T(8,128)(2,1)S(1)} %get-tuple-element.725), channel_id=1, source_target_pairs={{128,0},{256,128},{384,256},{129,1},{257,129},{385,257},{130,2},{2... | collective-permute-start | bytes 393224 | tf_op jit(solution)/shard_map/while/body/eval_jaxpr/ppermute | solution.py:15
  315.9 8.0 %collective-permute-start = (bf16[256,256]{1,0:T(8,128)(2,1)S(1)}, bf16[256,256]{1,0:T(8,128)(2,1)S(1)}, u32[]{:S(2)}, u32[]{:S(2)}) collective-permute-start(bf16[256,256]{1,0:T(8,128)(2,1)S(1)} %get-tuple-element.725), channel_id=1, source_target_pairs={{128,0},{256,128},{384,256},{129,1},{257,129},{385,257},{130,2},{2... | collective-permute-start | bytes 393224 | tf_op jit(solution)/shard_map/while/body/eval_jaxpr/ppermute | solution.py:15
  332.2 6.8 %collective-permute-start = (bf16[256,256]{1,0:T(8,128)(2,1)S(1)}, bf16[256,256]{1,0:T(8,128)(2,1)S(1)}, u32[]{:S(2)}, u32[]{:S(2)}) collective-permute-start(bf16[256,256]{1,0:T(8,128)(2,1)S(1)} %get-tuple-element.725), channel_id=1, source_target_pairs={{128,0},{256,128},{384,256},{129,1},{257,129},{385,257},{130,2},{2... | collective-permute-start | bytes 393224 | tf_op jit(solution)/shard_map/while/body/eval_jaxpr/ppermute | solution.py:15
  339.0 6.6 %copy-start = (f32[18,512,128]{2,1,0:T(8,128)S(1)}, f32[18,512,128]{2,1,0:T(8,128)}, u32[]{:S(2)}) copy-start(f32[18,512,128]{2,1,0:T(8,128)} %get-tuple-element.380) | copy-start | bytes 14155780
  345.6 14.0 %copy-start.3 = (bf16[2304,256]{1,0:T(8,128)(2,1)S(1)}, bf16[2304,256]{1,0:T(8,128)(2,1)}, u32[]{:S(2)}) copy-start(bf16[2304,256]{1,0:T(8,128)(2,1)} %get-tuple-element.378) | copy-start | bytes 3538948
  351.4 46.1 %all-to-all-start.2 = ((bf16[16,128,256]{2,1,0:T(8,128)(2,1)}), bf16[16,128,256]{2,1,0:T(8,128)(2,1)S(1)}, u32[]{:S(2)}, u32[]{:S(2)}) async-start(bf16[16,128,256]{2,1,0:T(8,128)(2,1)} %copy.159), calls=%async_computation.2 | async-start | bytes 2097152 | tf_op jit(solution)/shard_map/all_to_all | solution.py:187
  397.5 51.4 %all-to-all-start.1 = ((bf16[16,128,256]{2,1,0:T(8,128)(2,1)}), bf16[16,128,256]{2,1,0:T(8,128)(2,1)S(1)}, u32[]{:S(2)}, u32[]{:S(2)}) async-start(bf16[16,128,256]{2,1,0:T(8,128)(2,1)} %bitcast.36), calls=%async_computation.1 | async-start | bytes 2097152 | tf_op jit(solution)/shard_map/all_to_all | solution.py:174
